TPU v7x, 32 devices: a whole 2x2x4 slice. The times are simulated.
32 devices in a mesh: member: 2 (over y), vocab: 16 (over z, x, core).
Axes of the slice: x: 2, y: 2, z: 4, core: 2. Of those that a mesh axis runs over, the one named last changes fastest.
Arguments:
- hidden: bfloat16 [2, 512, 2048], P('member', None, 'vocab'), as said below
- norm_gain: bfloat16 [2, 2048], P('member', 'vocab'), may hold values from 0.5 to 1.5
- head: bfloat16 [2, 2048, 64128], P('member', None, 'vocab'), as said below
- pool_weight: float32 [2], P('member'), may hold values from 0.25 to 1
Outputs:
- log_probs: float32 [512, 64128], P('member', 'vocab')
- agreement: float32 [512], P('member')
Inputs may be any that keep to these rules, and one draw needn't show every extreme that they name: `hidden`: finite values; every member's row has a root mean square over its 2048 features between 0.1 and 100. `head`: finite values, each at most 60 in magnitude, so that a row's logits may reach about a thousand in magnitude.
All inputs are finite; a program needn't handle non-finite values.
Results may differ from a plain program's by a relative error of at most 0.00052.
Values may be sent and summed in bfloat16 or wider, within the bound.
No kernel may reach another device: no remote copies, remote signals or barrier semaphores. Data moves between devices by JAX's collectives and lax.ppermute only.
A program may use at most 128 MiB of HBM per device.

v0:
```python
import jax
import jax.numpy as jnp
from jax import lax
from jax.sharding import PartitionSpec as P

epsilon = 1e-05


def softmax_offset(values, first_pass):
    local_peak = jnp.max(values, axis=1)
    if first_pass:
        row_peak = lax.pmax(local_peak, "vocab")
        summed = lax.psum(jnp.sum(jnp.exp(values - row_peak[:, None]), axis=1), "vocab")
    else:
        row_peak = lax.pmax(local_peak, "vocab")
        summed = lax.psum(jnp.sum(jnp.exp(values - row_peak[:, None]), axis=1), "vocab")
    return row_peak + jnp.log(summed)


def on_device(hidden, norm_gain, head, pool_weight):
    states = hidden[0]
    weights = head[0]
    row_count = states.shape[0]
    narrowed = states.astype(jnp.float32)
    squares = lax.psum(jnp.sum(narrowed * narrowed, axis=1), "vocab")
    width_all = narrowed.shape[1] * lax.axis_size("vocab")
    scaling = lax.rsqrt(squares / width_all + epsilon)[:, None]
    normed = (narrowed * scaling * norm_gain.astype(jnp.float32)).astype(jnp.bfloat16)
    logits = jnp.dot(
        lax.all_gather(normed, "vocab", axis=1, tiled=True),
        weights,
        preferred_element_type=jnp.float32,
    )
    member_lse = softmax_offset(logits, True)
    weighted = pool_weight[0] * (logits - member_lse[:, None])
    share = row_count // lax.axis_size("member")
    pooled_all = lax.psum(weighted, "member")
    kept_rows = lax.dynamic_slice_in_dim(pooled_all, lax.axis_index("member") * share, share, 0)
    agreement = softmax_offset(kept_rows, False)
    return (kept_rows - agreement[:, None], agreement)


def solution(mesh):
    in_specs = (
        P("member", None, "vocab"),
        P("member", "vocab"),
        P("member", None, "vocab"),
        P("member"),
    )
    out_specs = (P("member", "vocab"), P("member"))
    return jax.shard_map(
        on_device, mesh=mesh, in_specs=in_specs, out_specs=out_specs, check_vma=False
    )
```

profile of v0, /device:TPU:0, one launch (start us, length us, event | category | flops | bytes accessed | tf_op | source)
XLA Modules:
  0.0 442.6 jit_solution(5408095204166017930)
XLA Ops:
  7.2 0.0 all-gather.2.cloned.1.call-start
  7.2 1.1 fusion.2
  8.3 34.9 %psum.28 = f32[512]{0:T(512)S(1)} all-reduce(f32[512]{0:T(512)S(1)} %fusion.2), channel_id=1, replica_groups=mesh['member'=2,'vocab'=16] {'vocab'}, use_global_device_ids=true, to_apply=%region_1.0 | all-reduce | flops 512 | bytes 4096 | tf_op jit(solution)/shard_map/psum | solution.py:25
  43.2 0.7 bitcast_convert_fusion
  43.8 1.7 fusion.4
  45.5 0.0 all-gather.2.cloned.1.call-update
  45.6 0.0 all-reduce.2.cloned.1.call-start
  46.3 37.9 %all-gather.2.cloned.1.call-done = bf16[512,2048]{1,0:T(8,128)(2,1)} async-done(((bf16[512,128]{1,0:T(8,128)(2,1)}), bf16[512,2048]{1,0:T(8,128)(2,1)}) %all-gather.2.cloned.1.call-update) | async-done | bytes 2097168 | tf_op jit(solution)/shard_map/all_gather | solution.py:30
  84.2 14.4 %fusion.5 = (f32[512]{0:T(512)S(1)}, f32[512,4008]{0,1:T(8,128)}) fusion(bf16[512,2048]{1,0:T(8,128)(2,1)} %all-gather.2.cloned.1.call-done, bf16[1,2048,4008]{1,2,0:T(8,128)(2,1)} %param.6), kind=kOutput, calls=%fused_computation.16 | convolution fusion | flops 8407436800 | bytes 26724352 | tf_op jit(solution)/shard_map/dot_general | solution.py:29
  98.6 31.6 %pmax.14 = f32[512]{0:T(512)S(1)} all-reduce(f32[512]{0:T(512)S(1)} %get-tuple-element.2), channel_id=1, replica_groups=mesh['member'=2,'vocab'=16] {'vocab'}, use_global_device_ids=true, to_apply=%region_3.0 | all-reduce | flops 512 | bytes 4096 | tf_op jit(solution)/shard_map/pmax | solution.py:12
  130.1 4.5 %exponential_reduce_fusion = f32[512]{0:T(512)S(1)} fusion(f32[512,4008]{0,1:T(8,128)} %get-tuple-element.3, f32[512]{0:T(512)S(1)} %pmax.14), kind=kLoop, calls=%fused_computation.3 | loop fusion | flops 4103680 | bytes 8212480 | tf_op jit(solution)/shard_map/reduce_sum | solution.py:13
  134.6 29.5 %psum.29 = f32[512]{0:T(512)S(1)} all-reduce(f32[512]{0:T(512)S(1)} %exponential_reduce_fusion), channel_id=1, replica_groups=mesh['member'=2,'vocab'=16] {'vocab'}, use_global_device_ids=true, to_apply=%region_5.0 | all-reduce | flops 512 | bytes 4096 | tf_op jit(solution)/shard_map/psum | solution.py:13
  164.1 7.6 %subtract_multiply_fusion = f32[512,4008]{0,1:T(8,128)} fusion(f32[512,4008]{0,1:T(8,128)} %get-tuple-element.3, f32[512]{0:T(512)S(1)} %log_add_fusion, f32[]{:T(128)} %bitcast.14), kind=kLoop, calls=%fused_computation.2 | loop fusion | flops 4104192 | bytes 16418820 | tf_op jit(solution)/shard_map/mul | solution.py:35
  171.7 0.0 all-reduce.2.cloned.1.call-update
  171.7 191.5 %all-reduce.2.cloned.1.call-done = f32[512,4008]{0,1:T(8,128)} async-done(((f32[512,4008]{0,1:T(8,128)}), f32[512,4008]{0,1:T(8,128)}) %all-reduce.2.cloned.1.call-update) | async-done | bytes 8208400 | tf_op jit(solution)/shard_map/psum | solution.py:37
  363.2 2.7 dynamic-slice_reduce_fusion
  365.9 33.1 %pmax.15 = f32[256]{0:T(256)S(1)} all-reduce(f32[256]{0:T(256)S(1)} %dynamic-slice_reduce_fusion), channel_id=1, replica_groups=mesh['member'=2,'vocab'=16] {'vocab'}, use_global_device_ids=true, to_apply=%region_8.0 | all-reduce | flops 256 | bytes 2048 | tf_op jit(solution)/shard_map/pmax | solution.py:15
  399.1 2.8 exponential_reduce_fusion.1
  401.9 29.5 %psum.31 = f32[256]{0:T(256)S(1)} all-reduce(f32[256]{0:T(256)S(1)} %exponential_reduce_fusion.1), channel_id=1, replica_groups=mesh['member'=2,'vocab'=16] {'vocab'}, use_global_device_ids=true, to_apply=%region_10.0 | all-reduce | flops 256 | bytes 2048 | tf_op jit(solution)/shard_map/psum | solution.py:16
  431.4 0.0 copy-start
  431.4 4.4 dynamic-slice_subtract_fusion
  435.8 0.0 copy-done
  (3 shorter events, 0.0 us)
Async XLA Ops:
  7.2 77.0 %all-gather.2.cloned.1.call-start = ((), (), s32[]{:S(2)}) async-start(), calls=%async_computation | async-start | bytes 2228224 | tf_op jit(solution)/shard_map/all_gather | solution.py:30
  45.6 317.7 %all-reduce.2.cloned.1.call-start = ((), (), s32[]{:S(2)}) async-start(), calls=%async_computation.1 | async-start | bytes 16416768 | tf_op jit(solution)/shard_map/psum | solution.py:37
  431.4 4.4 copy-start
Sparse Core Ops, SparseCore 0:
  45.7 38.4 all-gather.1
  171.8 191.3 all-reduce.1
where the time goes:
time: 443 us
  waiting for transfers between devices  229 us (52%)
  blocking collectives  159 us (36%)
  other arithmetic  25.4 us (6%)
  between operations  14.7 us (3%)
  matrix products  14.4 us (3%)
    psum x1, waiting for transfers between devices, on_device(): pooled_all = lax.psum(weighted, 'member')  192 us
    pmax x2, blocking collectives, softmax_offset(): row_peak = lax.pmax(local_peak, 'vocab')  64.7 us
    psum x2, blocking collectives, softmax_offset(): lax.psum(jnp.sum(jnp.exp(values - row_peak[:, None]), axis=1), 'vocab')  59 us
    all_gather x1, waiting for transfers between devices, on_device(): lax.all_gather(normed, 'vocab', axis=1, tiled=True)  37.9 us
    psum x1, blocking collectives, on_device(): squares = lax.psum(jnp.sum(narrowed * narrowed, axis=1), 'vocab')  34.9 us
    dot_general x1, matrix products, on_device(): jnp.dot(lax.all_gather(normed, 'vocab', axis=1, tiled=True), weights, pre...  14.4 us
  transfers between devices with their start and end apart: 2, of which 2 were waited for; matrix products, arithmetic and copies ran while one was open for 0% of the time, Pallas kernels for 0%

commit v1 on v0

v1 whole, which is shorter than its diff:
```python
import jax
import jax.numpy as jnp
from jax import lax
from jax.sharding import PartitionSpec as P

epsilon = 1e-05


def combine_stats(stats):
    peaks = stats[:, 0, :]
    sums = stats[:, 1, :]
    row_peak = jnp.max(peaks, axis=0)
    summed = jnp.sum(sums * jnp.exp(peaks - row_peak[None, :]), axis=0)
    return row_peak, summed


def local_stats(values):
    local_peak = jnp.max(values, axis=1)
    local_sum = jnp.sum(jnp.exp(values - local_peak[:, None]), axis=1)
    return jnp.stack([local_peak, local_sum])


def on_device(hidden, norm_gain, head, pool_weight):
    members = lax.axis_size("member")
    shards = lax.axis_size("vocab")
    me = lax.axis_index("member")
    states = hidden[0]
    row_count, width = states.shape
    share = row_count // members
    weights = head[0]
    vocab_local = weights.shape[1]

    packed = jnp.concatenate([states, norm_gain], axis=0)
    gathered = lax.all_gather(packed, "vocab", axis=0, tiled=False)
    full_states = gathered[:, :row_count, :].astype(jnp.float32)
    gain = gathered[:, row_count, :].astype(jnp.float32)
    width_all = width * shards
    mean_square = jnp.sum(full_states * full_states, axis=(0, 2)) / width_all
    scaling = lax.rsqrt(mean_square + epsilon)
    normed = (full_states * scaling[None, :, None] * gain[:, None, :]).astype(jnp.bfloat16)
    normed = jnp.transpose(normed, (1, 0, 2)).reshape(row_count, width_all)
    logits = jnp.dot(normed, weights, preferred_element_type=jnp.float32)

    w = pool_weight[0]
    own = w * lax.dynamic_slice_in_dim(logits, me * share, share, 0)
    pooled_raw = own
    for shift in range(1, members):
        target = (me + shift) % members
        outgoing = w * lax.dynamic_slice_in_dim(logits, target * share, share, 0)
        perm = [(g, (g + shift) % members) for g in range(members)]
        pooled_raw = pooled_raw + lax.ppermute(outgoing, "member", perm)

    member_stats = lax.all_gather(local_stats(logits), "vocab", axis=0, tiled=False)
    peak, summed = combine_stats(member_stats)
    member_lse = peak + jnp.log(summed)
    offsets = lax.all_gather(w * member_lse, "member", axis=0, tiled=False)
    offset = jnp.sum(lax.dynamic_slice_in_dim(offsets, me * share, share, 1), axis=0)

    pooled = pooled_raw - offset[:, None]
    pooled_stats = lax.all_gather(local_stats(pooled), "vocab", axis=0, tiled=False)
    peak, summed = combine_stats(pooled_stats)
    agreement = peak + jnp.log(summed)
    return (pooled - agreement[:, None], agreement)


def solution(mesh):
    in_specs = (
        P("member", None, "vocab"),
        P("member", "vocab"),
        P("member", None, "vocab"),
        P("member"),
    )
    out_specs = (P("member", "vocab"), P("member"))
    return jax.shard_map(
        on_device, mesh=mesh, in_specs=in_specs, out_specs=out_specs, check_vma=False
    )
```

time: 443 us -> 204 us (0.46)
  waiting for transfers between devices: 229 us -> 45.5 us
  blocking collectives: 159 us -> 104 us
  local copies, waits for them, and re-layouts: 0.01 us -> 8.32 us
  other arithmetic: 25.4 us -> 17.5 us
    psum x1 -> x0, waiting for transfers between devices: 192 us -> none  [on_device(): pooled_all = lax.psum(weighted, 'member')]
    all_gather x0 -> x3, blocking collectives: none -> 104 us  [the longest x1 65.4 us: on_device(): offsets = lax.all_gather(w * member_lse, 'member', axis=0, tiled=False)]
    psum x3 -> x0, blocking collectives: 93.9 us -> none  [the longest x2 59 us: softmax_offset(): lax.psum(jnp.sum(jnp.exp(values - row_peak[:, None]), axis=1), 'vocab')]
    pmax x2 -> x0, blocking collectives: 64.7 us -> none  [softmax_offset(): row_peak = lax.pmax(local_peak, 'vocab')]
    all_gather x1, waiting for transfers between devices: 37.9 us -> 45.5 us  [on_device(): gathered = lax.all_gather(packed, 'vocab', axis=0, tiled=False)]
    mul x2 -> x3, other arithmetic: 8.25 us -> 2.86 us  [the longest x1 2.84 us: on_device(): outgoing = w * lax.dynamic_slice_in_dim(logits, target * share, share, 0)]
    unnamed x2 -> x7, local copies, waits for them, and re-layouts: 0.01 us -> 4.44 us
  transfers between devices with their start and end apart: 2 -> 2, of which waited for: 2 -> 1; matrix products, arithmetic and copies ran while one was open for 0% -> 2% of each run, Pallas kernels for 0% -> 0%
where the time goes in v1:
time: 204 us
  blocking collectives  104 us (51%)
  waiting for transfers between devices  45.5 us (22%)
  other arithmetic  17.5 us (9%)
  between operations  14.8 us (7%)
  matrix products  12.3 us (6%)
  local copies, waits for them, and re-layouts  8.32 us (4%)
    all_gather x1, blocking collectives, on_device(): offsets = lax.all_gather(w * member_lse, 'member', axis=0, tiled=False)  65.4 us
    all_gather x1, waiting for transfers between devices, on_device(): gathered = lax.all_gather(packed, 'vocab', axis=0, tiled=False)  45.5 us
    all_gather x1, blocking collectives, on_device(): lax.all_gather(local_stats(logits), 'vocab', axis=0, tiled=False)  19.5 us
    all_gather x1, blocking collectives, on_device(): lax.all_gather(local_stats(pooled), 'vocab', axis=0, tiled=False)  19.3 us
    dot_general x1, matrix products, on_device(): logits = jnp.dot(normed, weights, preferred_element_type=jnp.float32)  12.3 us
    reduce_sum x2, other arithmetic, local_stats(): local_sum = jnp.sum(jnp.exp(values - local_peak[:, None]), axis=1)  5.25 us
    unnamed x7, local copies, waits for them, and re-layouts  4.44 us
  transfers between devices with their start and end apart: 2, of which 1 were waited for; matrix products, arithmetic and copies ran while one was open for 2% of the time, Pallas kernels for 0%

profile of v1, /device:TPU:0, one launch (start us, length us, event | category | flops | bytes accessed | tf_op | source)
XLA Modules:
  0.0 204.1 jit_solution(11226428174826329725)
XLA Ops:
  7.2 0.0 all-gather.10.cloned.1.call-start
  7.2 1.6 maximum_bitcast_fusion
  8.8 0.0 all-gather.10.cloned.1.call-update
  9.5 45.5 %all-gather.10.cloned.1.call-done = bf16[16,513,128]{2,1,0:T(8,128)(2,1)} async-done(((bf16[1,513,128]{2,1,0:T(8,128)(2,1)}), bf16[16,513,128]{2,1,0:T(8,128)(2,1)}) %all-gather.10.cloned.1.call-update) | async-done | bytes 2101264 | tf_op jit(solution)/shard_map/all_gather | solution.py:34
  55.0 3.1 %slice.24 = bf16[16,512,128]{2,1,0:T(8,128)(2,1)} slice(bf16[16,513,128]{2,1,0:T(8,128)(2,1)} %all-gather.10.cloned.1.call-done), slice={[0:16], [0:512], [0:128]} | slice | bytes 4194304 | tf_op jit(solution)/shard_map/slice | solution.py:35
  58.1 2.9 %copy.24 = bf16[16,512,128]{1,2,0:T(8,128)(2,1)S(1)} copy(bf16[16,512,128]{2,1,0:T(8,128)(2,1)} %slice.24) | data formatting | bytes 4194304
  60.9 0.8 slice.25
  61.7 0.5 fusion.2
  62.2 1.9 fusion.4
  64.1 12.3 %fusion.15 = (f32[512]{0:T(512)S(1)}, f32[512,4008]{0,1:T(8,128)S(1)}) fusion(bf16[512,2048]{0,1:T(8,128)(2,1)} %bitcast.54, bf16[1,2048,4008]{1,2,0:T(8,128)(2,1)} %param.6), kind=kOutput, calls=%fused_computation.36 | convolution fusion | flops 8407436800 | bytes 26724352 | tf_op jit(solution)/shard_map/dot_general | solution.py:42
  76.4 0.0 copy-start
  76.4 2.8 %dynamic-slice_multiply_fusion = f32[256,4008]{0,1:T(8,128)} fusion(f32[512,4008]{0,1:T(8,128)S(1)} %get-tuple-element.11, s32[]{:T(128)S(6)} %select_n.16, f32[]{:T(128)} %bitcast.53), kind=kLoop, calls=%fused_computation.10 | loop fusion | flops 1026048 | bytes 8208392 | tf_op jit(solution)/shard_map/mul | solution.py:49
  79.2 1.6 copy-done
  80.8 1.5 collective-permute-start
  82.3 0.0 copy-start.1
  82.3 4.6 %exponential_reduce_fusion = f32[512]{0:T(512)S(1)} fusion(f32[512,4008]{0,1:T(8,128)} %copy-done, f32[512]{0:T(512)S(1)} %get-tuple-element.10), kind=kLoop, calls=%fused_computation.2 | loop fusion | flops 4103680 | bytes 8212480 | tf_op jit(solution)/shard_map/reduce_sum | solution.py:19
  86.9 19.5 %all-gather.5 = f32[16,2,512]{2,1,0:T(2,128)S(1)} all-gather(f32[1,2,512]{2,1,0:T(2,128)S(1)} %maximum_bitcast_fusion.1), channel_id=3, replica_groups=mesh['member'=2,'vocab'=16] {'vocab'}, dimensions={0}, use_global_device_ids=true | all-gather | bytes 69632 | tf_op jit(solution)/shard_map/all_gather | solution.py:53
  106.4 0.1 fusion.13
  106.6 65.4 %all-gather.6 = f32[2,1,512]{2,1,0:T(1,128)S(1)} all-gather(f32[1,1,512]{2,1,0:T(1,128)S(1)} %bitcast.59), channel_id=4, replica_groups=mesh['member'=2,'vocab'=16] {'member'}, dimensions={0}, use_global_device_ids=true | all-gather | bytes 6144 | tf_op jit(solution)/shard_map/all_gather | solution.py:56
  172.0 0.0 collective-permute-done
  172.0 0.0 copy-done.1
  172.0 3.0 %fusion.12 = (f32[256]{0:T(256)S(1)}, f32[256,4008]{0,1:T(8,128)S(1)}) fusion(f32[256]{0:T(256)S(1)} %dynamic-slice_reduce_fusion, f32[256,4008]{0,1:T(8,128)} %collective-permute-done, f32[512,4008]{0,1:T(8,128)S(1)} %copy-done.1, s32[]{:T(128)S(6)} %select_n.14, f32[]{:T(128)} %bitcast.51), kind=kLoop, calls=%fused_computation.33 | loop fusion | flops 4103936 | bytes 12314632 | tf_op jit(solution)/shard_map/reduce_max | solution.py:18
  175.0 0.6 exponential_reduce_fusion.1
  175.6 19.3 %all-gather.7 = f32[16,2,256]{2,1,0:T(2,128)S(1)} all-gather(f32[1,2,256]{2,1,0:T(2,128)S(1)} %maximum_bitcast_fusion.2), channel_id=5, replica_groups=mesh['member'=2,'vocab'=16] {'vocab'}, dimensions={0}, use_global_device_ids=true | all-gather | bytes 34816 | tf_op jit(solution)/shard_map/all_gather | solution.py:60
  195.0 0.0 copy-start.2
  195.0 2.2 %broadcast_subtract_fusion = f32[256,4008]{0,1:T(8,128)} fusion(f32[256,4008]{0,1:T(8,128)S(1)} %get-tuple-element.3, f32[256]{0:T(256)S(1)} %log_add_fusion), kind=kLoop, calls=%fused_computation.11 | loop fusion | flops 1026048 | bytes 8209408 | tf_op jit(solution)/shard_map/sub | solution.py:63
  197.2 0.0 copy-done.2
  (10 shorter events, 0.2 us)
Async XLA Ops:
  7.2 47.8 %all-gather.10.cloned.1.call-start = ((), (), s32[]{:S(2)}) async-start(), calls=%async_computation | async-start | bytes 2263040 | tf_op jit(solution)/shard_map/all_gather | solution.py:34
  76.4 4.4 %copy-start = (f32[512,4008]{0,1:T(8,128)}, f32[512,4008]{0,1:T(8,128)S(1)}, u32[]{:S(2)}) copy-start(f32[512,4008]{0,1:T(8,128)S(1)} %get-tuple-element.11) | copy-start | bytes 24625156
  80.8 91.2 %collective-permute-start = (f32[256,4008]{0,1:T(8,128)}, f32[256,4008]{0,1:T(8,128)}, u32[]{:S(2)}, u32[]{:S(2)}) collective-permute-start(f32[256,4008]{0,1:T(8,128)} %dynamic-slice_multiply_fusion), channel_id=1, source_target_pairs={{0,16},{16,0},{1,17},{17,1},{2,18},{18,2},{3,19},{19,3},{4,20},{20... | collective-permute-start | bytes 12312584 | tf_op jit(solution)/shard_map/ppermute | solution.py:51
  82.3 89.7 %copy-start.1 = (f32[512,4008]{0,1:T(8,128)S(1)}, f32[512,4008]{0,1:T(8,128)}, u32[]{:S(2)}) copy-start(f32[512,4008]{0,1:T(8,128)} %copy-done) | copy-start | bytes 24625156
  195.0 2.3 %copy-start.2 = (f32[256]{0:T(256)}, f32[256]{0:T(256)S(1)}, u32[]{:S(2)}) copy-start(f32[256]{0:T(256)S(1)} %log_add_fusion) | copy-start | bytes 3076
Sparse Core Ops, SparseCore 0:
  10.7 44.1 all-gather.9

commit v2 on v1

v2 whole, which is shorter than its diff:
```python
import jax
import jax.numpy as jnp
from jax import lax
from jax.sharding import PartitionSpec as P

epsilon = 1e-05
send_pieces = 2


def local_stats(values):
    local_peak = jnp.max(values, axis=1)
    local_sum = jnp.sum(jnp.exp(values - local_peak[:, None]), axis=1)
    return jnp.stack([local_peak, local_sum])


def reduce_stats(stats, axis):
    size = lax.axis_size(axis)
    if size & (size - 1):
        gathered = lax.all_gather(stats, axis, axis=0, tiled=False)
        peak = jnp.max(gathered[:, 0], axis=0)
        summed = jnp.sum(gathered[:, 1] * jnp.exp(gathered[:, 0] - peak[None]), axis=0)
        return peak, summed
    distance = 1
    while distance < size:
        perm = [(a, a ^ distance) for a in range(size)]
        other = lax.ppermute(stats, axis, perm)
        peak = jnp.maximum(stats[0], other[0])
        summed = stats[1] * jnp.exp(stats[0] - peak) + other[1] * jnp.exp(other[0] - peak)
        stats = jnp.stack([peak, summed])
        distance *= 2
    return stats[0], stats[1]


def on_device(hidden, norm_gain, head, pool_weight):
    members = lax.axis_size("member")
    shards = lax.axis_size("vocab")
    me = lax.axis_index("member")
    states = hidden[0]
    row_count, width = states.shape
    share = row_count // members
    weights = head[0]
    width_all = width * shards
    member_weights = lax.all_gather(pool_weight, "member", axis=0, tiled=True)
    member_weights, states = lax.optimization_barrier((member_weights, states))

    def logits_of(first_row, rows):
        piece = lax.dynamic_slice_in_dim(states, first_row, rows, 0)
        packed = jnp.concatenate([piece, norm_gain], axis=0)
        gathered = lax.all_gather(packed, "vocab", axis=0, tiled=False)
        full_states = gathered[:, :rows, :].astype(jnp.float32)
        gain = gathered[:, rows, :].astype(jnp.float32)
        mean_square = jnp.sum(full_states * full_states, axis=(0, 2)) / width_all
        scaling = lax.rsqrt(mean_square + epsilon)
        normed = (full_states * scaling[None, :, None] * gain[:, None, :]).astype(jnp.bfloat16)
        normed = jnp.transpose(normed, (1, 0, 2)).reshape(rows, width_all)
        return jnp.dot(normed, weights, preferred_element_type=jnp.float32)

    sub = share // send_pieces
    received = []
    for shift in range(1, members):
        target = (me + shift) % members
        perm = [(g, (g + shift) % members) for g in range(members)]
        parts = []
        for k in range(send_pieces):
            logits = logits_of(target * share + k * sub, sub)
            parts.append(lax.ppermute(logits, "member", perm))
        received.append((member_weights[(me - shift) % members], parts))
    own_logits = logits_of(me * share, share)
    own_weight = member_weights[me]

    pooled_raw = []
    stats = [[] for _ in range(members + 1)]
    for k in range(send_pieces):
        own = own_logits[k * sub:(k + 1) * sub]
        total = own_weight * own
        stats[0].append(local_stats(own))
        for index, (weight, parts) in enumerate(received):
            total = total + weight * parts[k]
            stats[index + 1].append(local_stats(parts[k]))
        pooled_raw.append(total)
        stats[members].append(local_stats(total))
    stats = jnp.stack([jnp.concatenate(column, axis=1) for column in stats], axis=1)
    peak, summed = reduce_stats(stats, "vocab")
    lse = peak + jnp.log(summed)
    offset = own_weight * lse[0]
    for index, (weight, parts) in enumerate(received):
        offset = offset + weight * lse[index + 1]

    agreement = lse[members] - offset
    pooled = jnp.concatenate(pooled_raw, axis=0) - offset[:, None]
    return (pooled - agreement[:, None], agreement)


def solution(mesh):
    in_specs = (
        P("member", None, "vocab"),
        P("member", "vocab"),
        P("member", None, "vocab"),
        P("member"),
    )
    out_specs = (P("member", "vocab"), P("member"))
    return jax.shard_map(
        on_device, mesh=mesh, in_specs=in_specs, out_specs=out_specs, check_vma=False
    )
```

time: 204 us -> 182 us (0.89)
  blocking collectives: 104 us -> 49.3 us
  matrix products: 12.3 us -> 31 us
  waiting for transfers between devices: 45.5 us -> 50.9 us
  other arithmetic: 17.5 us -> 22.8 us
    all_gather x3 -> x2, blocking collectives: 104 us -> 43.5 us  [logits_of(): gathered = lax.all_gather(packed, 'vocab', axis=0, tiled=False)]
    ppermute x1 -> x6, waiting for transfers between devices: 0.01 us -> 50.9 us  [the longest x2 38 us: on_device(): parts.append(lax.ppermute(logits, 'member', perm))]
    all_gather x1, waiting for transfers between devices: 45.5 us -> 0.01 us  [logits_of(): gathered = lax.all_gather(packed, 'vocab', axis=0, tiled=False)]
    dot_general x1 -> x3, matrix products: 12.3 us -> 31 us  [logits_of(): return jnp.dot(normed, weights, preferred_element_type=jnp.float32)]
    optimization_barrier x0 -> x1, blocking collectives: none -> 5.84 us  [on_device(): member_weights, states = lax.optimization_barrier((member_weights, states))]
    reduce_max x1 -> x4, other arithmetic: 2.95 us -> 8.43 us  [local_stats(): local_peak = jnp.max(values, axis=1)]
    mul x3, other arithmetic: 2.86 us -> 0.01 us  [logits_of(): full_states * scaling[None, :, None] * gain[:, None, :]]
    dynamic_slice x0 -> x3, local copies, waits for them, and re-layouts: none -> 2.28 us  [the longest x2 1.63 us: logits_of(): piece = lax.dynamic_slice_in_dim(states, first_row, rows, 0)]
  transfers between devices with their start and end apart: 2 -> 7, of which waited for: 1 -> 5; matrix products, arithmetic and copies ran while one was open for 2% -> 24% of each run, Pallas kernels for 0% -> 0%
where the time goes in v2:
time: 182 us; the launch traced here: 181 us
  waiting for transfers between devices  50.9 us (28%)
  blocking collectives  49.3 us (27%)
  matrix products  31 us (17%)
  other arithmetic  22.8 us (13%)
  between operations  14.9 us (8%)
  local copies, waits for them, and re-layouts  9.74 us (5%)
  starting transfers between devices  2.36 us (1%)
    all_gather x2, blocking collectives, logits_of(): gathered = lax.all_gather(packed, 'vocab', axis=0, tiled=False)  43.5 us
    ppermute x2, waiting for transfers between devices, on_device(): parts.append(lax.ppermute(logits, 'member', perm))  38 us
    dot_general x3, matrix products, logits_of(): return jnp.dot(normed, weights, preferred_element_type=jnp.float32)  31 us
    ppermute x4, waiting for transfers between devices, reduce_stats(): other = lax.ppermute(stats, axis, perm)  13 us
    reduce_max x4, other arithmetic, local_stats(): local_peak = jnp.max(values, axis=1)  8.43 us
    optimization_barrier x1, blocking collectives, on_device(): member_weights, states = lax.optimization_barrier((member_weights, states))  5.84 us
    reduce_sum x3, other arithmetic, local_stats(): local_sum = jnp.sum(jnp.exp(values - local_peak[:, None]), axis=1)  5.75 us
    unnamed x10, local copies, waits for them, and re-layouts  4.28 us
  transfers between devices with their start and end apart: 7, of which 5 were waited for; matrix products, arithmetic and copies ran while one was open for 24% of the time, Pallas kernels for 0%

profile of v2, /device:TPU:0, one launch (start us, length us, event | category | flops | bytes accessed | tf_op | source)
XLA Modules:
  0.0 181.0 jit_solution(8247871230120377977)
XLA Ops:
  7.9 1.2 dynamic-slice
  9.1 0.8 dynamic-update-slice
  9.9 5.8 %all-reduce = f32[2]{0:T(128)S(1)} all-reduce(f32[2]{0:T(128)S(1)} %dynamic-update-slice), channel_id=1, replica_groups=mesh['member'=2,'vocab'=16] {'member'}, use_global_device_ids=true, to_apply=%add | all-reduce | flops 2 | bytes 16 | tf_op jit(solution)/shard_map/optimization_barrier | solution.py:44
  15.7 0.8 constant_dynamic-slice_fusion.2
  16.6 1.3 maximum_bitcast_fusion
  17.9 0.8 constant_dynamic-slice_fusion.1
  18.7 0.7 fusion.16
  19.3 24.7 %all-gather.4 = bf16[16,129,128]{2,1,0:T(8,128)(2,1)S(1)} all-gather(bf16[1,129,128]{2,1,0:T(8,128)(2,1)S(1)} %get-tuple-element.27), channel_id=3, replica_groups=mesh['member'=2,'vocab'=16] {'vocab'}, dimensions={0}, use_global_device_ids=true | all-gather | bytes 561408 | tf_op jit(solution)/shard_map/all_gather | solution.py:49
  45.0 9.3 %fusion.2 = f32[128,4008]{0,1:T(8,128)} fusion(bf16[128,2048]{0,1:T(8,128)(2,1)S(1)} %bitcast.194, bf16[1,2048,4008]{1,2,0:T(8,128)(2,1)} %param.6), kind=kOutput, calls=%fused_computation.2 | convolution fusion | flops 2101346304 | bytes 18993152 | tf_op jit(solution)/shard_map/dot_general | solution.py:56
  54.4 1.5 collective-permute-start
  55.9 18.8 %all-gather.5 = bf16[16,129,128]{2,1,0:T(8,128)(2,1)S(1)} all-gather(bf16[1,129,128]{2,1,0:T(8,128)(2,1)S(1)} %get-tuple-element.28), channel_id=4, replica_groups=mesh['member'=2,'vocab'=16] {'vocab'}, dimensions={0}, use_global_device_ids=true | all-gather | bytes 561408 | tf_op jit(solution)/shard_map/all_gather | solution.py:49
  75.7 9.3 %fusion = f32[128,4008]{0,1:T(8,128)} fusion(bf16[128,2048]{0,1:T(8,128)(2,1)S(1)} %bitcast.195, bf16[1,2048,4008]{1,2,0:T(8,128)(2,1)} %param.6), kind=kOutput, calls=%fused_computation | convolution fusion | flops 2101346304 | bytes 18993152 | tf_op jit(solution)/shard_map/dot_general | solution.py:56
  85.0 0.6 collective-permute-start.1
  85.5 0.6 fusion.43
  86.2 2.3 %slice.89 = bf16[16,256,128]{2,1,0:T(8,128)(2,1)} slice(bf16[16,257,128]{2,1,0:T(8,128)(2,1)} %all-gather.8.cloned.1.call-done), slice={[0:16], [0:256], [0:128]} | slice | bytes 2097152 | tf_op jit(solution)/shard_map/slice | solution.py:50
  88.5 1.7 copy.38
  90.5 0.8 slice.90
  91.3 1.3 fusion.9
  92.6 12.4 %fusion.4 = f32[256,4008]{0,1:T(8,128)} fusion(bf16[256,2048]{0,1:T(8,128)(2,1)} %bitcast.196, bf16[1,2048,4008]{1,2,0:T(8,128)(2,1)} %param.6), kind=kOutput, calls=%fused_computation.4 | convolution fusion | flops 4202692608 | bytes 21569536 | tf_op jit(solution)/shard_map/dot_general | solution.py:56
  105.0 2.1 %slice_reduce_fusion.1 = f32[128]{0:T(128)S(1)} fusion(f32[256,4008]{0,1:T(8,128)} %fusion.4), kind=kLoop, calls=%fused_computation.22 | loop fusion | flops 512896 | bytes 2052608 | tf_op jit(solution)/shard_map/reduce_max | solution.py:11
  107.6 37.9 %collective-permute-done.1 = f32[128,4008]{0,1:T(8,128)} collective-permute-done((f32[128,4008]{0,1:T(8,128)}, f32[128,4008]{0,1:T(8,128)}, u32[]{:S(2)}, u32[]{:S(2)}) %collective-permute-start.1) | collective-permute-done | bytes 2052128 | tf_op jit(solution)/shard_map/ppermute | solution.py:66
  145.6 2.1 %reduce_max.57 = f32[128]{0:T(128)S(1)} reduce(f32[128,4008]{0,1:T(8,128)} %collective-permute-done.1, f32[]{:T(128)} %constant.47.clone.1), dimensions={1}, to_apply=%region_9.10 | reduce | flops 512896 | bytes 2052612 | tf_op jit(solution)/shard_map/reduce_max | solution.py:11
  147.7 4.6 %exponential_reduce_fusion.5 = (f32[128]{0:T(128)S(1)}, f32[128]{0:T(128)S(1)}, f32[128]{0:T(128)S(1)}, f32[128,4008]{0,1:T(8,128)S(1)}, f32[128]{0:T(128)S(1)}) fusion(f32[256,4008]{0,1:T(8,128)} %fusion.4, f32[128]{0:T(128)S(1)} %slice_reduce_fusion.1, f32[128,4008]{0,1:T(8,128)S(1)} %collective-permute-done, f32[]{:T(128)} %bitcast.8, f32[]{:T(128)} %bitcast.2, ...), kind=kLoop, calls=%fused_computation.18 | loop fusion | flops 4616704 | bytes 8211464 | tf_op jit(solution)/shard_map/reduce_sum | solution.py:12
  152.4 3.7 %fusion.42 = (f32[128]{0:T(128)S(1)}, f32[128,4008]{0,1:T(8,128)S(1)}, f32[128]{0:T(128)S(1)}, f32[128]{0:T(128)S(1)}) fusion(f32[128,4008]{0,1:T(8,128)} %collective-permute-done.1, f32[]{:T(128)} %bitcast.8, f32[256,4008]{0,1:T(8,128)S(1)} %copy-done, f32[]{:T(128)} %bitcast.2, f32[128]{0:T(128)S(1)} %get-tuple-element.7, f32[128]{0:T(128)S(1)} %reduce_max.57), kind=kLoop, calls=%fused_computation.101 | loop fusion | flops 4103808 | bytes 6158856 | tf_op jit(solution)/shard_map/reduce_max | solution.py:11
  156.0 0.6 exponential_reduce_fusion
  156.6 0.6 exponential_reduce_fusion.1
  157.3 1.1 collective-permute-done.2
  158.5 3.6 %collective-permute-done.3 = f32[2,3,256]{2,1,0:T(4,128)S(1)} collective-permute-done((f32[2,3,256]{2,1,0:T(4,128)S(1)}, f32[2,3,256]{2,1,0:T(4,128)S(1)}, u32[]{:S(2)}, u32[]{:S(2)}) %collective-permute-start.3) | collective-permute-done | bytes 6176 | tf_op jit(solution)/shard_map/ppermute | solution.py:26
  162.3 3.6 %collective-permute-done.4 = f32[2,3,256]{2,1,0:T(4,128)S(1)} collective-permute-done((f32[2,3,256]{2,1,0:T(4,128)S(1)}, f32[2,3,256]{2,1,0:T(4,128)S(1)}, u32[]{:S(2)}, u32[]{:S(2)}) %collective-permute-start.4) | collective-permute-done | bytes 6176 | tf_op jit(solution)/shard_map/ppermute | solution.py:26
  166.0 4.5 %collective-permute-done.5 = f32[2,3,256]{2,1,0:T(4,128)S(1)} collective-permute-done((f32[2,3,256]{2,1,0:T(4,128)S(1)}, f32[2,3,256]{2,1,0:T(4,128)S(1)}, u32[]{:S(2)}, u32[]{:S(2)}) %collective-permute-start.5) | collective-permute-done | bytes 6176 | tf_op jit(solution)/shard_map/ppermute | solution.py:26
  170.6 1.3 fusion.40
  171.9 2.3 %fusion.6 = f32[256,4008]{0,1:T(8,128)} fusion(f32[128,4008]{0,1:T(8,128)S(1)} %get-tuple-element.15, f32[128,4008]{0,1:T(8,128)S(1)} %get-tuple-element.18, f32[256]{0:T(256)S(1)} %sub.151, f32[256]{0:T(256)S(1)} %bitcast.200), kind=kLoop, calls=%fused_computation.7 | loop fusion | flops 3078144 | bytes 8210432 | tf_op jit(solution)/shard_map/sub | solution.py:91
  (44 shorter events, 3.3 us)
Async XLA Ops:
  7.2 79.0 %all-gather.8.cloned.1.call-start = ((), (), s32[]{:S(2)}) async-start(), calls=%async_computation | async-start | bytes 1148928 | tf_op jit(solution)/shard_map/all_gather | solution.py:49
  54.4 52.7 %collective-permute-start = (f32[128,4008]{0,1:T(8,128)}, f32[128,4008]{0,1:T(8,128)S(1)}, u32[]{:S(2)}, u32[]{:S(2)}) collective-permute-start(f32[128,4008]{0,1:T(8,128)} %fusion.2), channel_id=1, source_target_pairs={{0,16},{16,0},{1,17},{17,1},{2,18},{18,2},{3,19},{19,3},{4,20},{20... | collective-permute-start | bytes 6156296 | tf_op jit(solution)/shard_map/ppermute | solution.py:66
  85.0 60.6 %collective-permute-start.1 = (f32[128,4008]{0,1:T(8,128)}, f32[128,4008]{0,1:T(8,128)}, u32[]{:S(2)}, u32[]{:S(2)}) collective-permute-start(f32[128,4008]{0,1:T(8,128)} %fusion), channel_id=1, source_target_pairs={{0,16},{16,0},{1,17},{17,1},{2,18},{18,2},{3,19},{19,3},{4,20},{20... | collective-permute-start | bytes 6156296 | tf_op jit(solution)/shard_map/ppermute | solution.py:66
  147.7 4.6 %copy-start = (f32[256,4008]{0,1:T(8,128)S(1)}, f32[256,4008]{0,1:T(8,128)}, u32[]{:S(2)}) copy-start(f32[256,4008]{0,1:T(8,128)} %fusion.4) | copy-start | bytes 12312580
  157.2 1.2 collective-permute-start.2
  158.5 3.7 %collective-permute-start.3 = (f32[2,3,256]{2,1,0:T(4,128)S(1)}, f32[2,3,256]{2,1,0:T(4,128)S(1)}, u32[]{:S(2)}, u32[]{:S(2)}) collective-permute-start(f32[2,3,256]{2,1,0:T(4,128)S(1)} %pad_maximum_fusion.2), channel_id=1, source_target_pairs={{0,2},{1,3},{2,0},{3,1},{4,6},{5,7},{6,4},{7,5},{8,10},{9,11},{10,... | collective-permute-start | bytes 18440 | tf_op jit(solution)/shard_map/ppermute | solution.py:26
  162.2 3.7 %collective-permute-start.4 = (f32[2,3,256]{2,1,0:T(4,128)S(1)}, f32[2,3,256]{2,1,0:T(4,128)S(1)}, u32[]{:S(2)}, u32[]{:S(2)}) collective-permute-start(f32[2,3,256]{2,1,0:T(4,128)S(1)} %pad_maximum_fusion.3), channel_id=1, source_target_pairs={{0,4},{1,5},{2,6},{3,7},{4,0},{5,1},{6,2},{7,3},{8,12},{9,13},{10,... | collective-permute-start | bytes 18440 | tf_op jit(solution)/shard_map/ppermute | solution.py:26
  165.9 4.6 %collective-permute-start.5 = (f32[2,3,256]{2,1,0:T(4,128)S(1)}, f32[2,3,256]{2,1,0:T(4,128)S(1)}, u32[]{:S(2)}, u32[]{:S(2)}) collective-permute-start(f32[2,3,256]{2,1,0:T(4,128)S(1)} %pad_maximum_fusion.4), channel_id=1, source_target_pairs={{0,8},{1,9},{2,10},{3,11},{4,12},{5,13},{6,14},{7,15},{8,0},{9,1},... | collective-permute-start | bytes 18440 | tf_op jit(solution)/shard_map/ppermute | solution.py:26
  171.9 2.3 %copy-start.1 = (f32[256]{0:T(256)}, f32[256]{0:T(256)S(1)}, u32[]{:S(2)}) copy-start(f32[256]{0:T(256)S(1)} %sub.151) | copy-start | bytes 3076
Sparse Core Ops, SparseCore 0:
  18.0 40.8 all-gather.7

commit v3 on v2

--- a/solution.py
+++ b/solution.py
@@ -40,9 +40,6 @@
     share = row_count // members
     weights = head[0]
     width_all = width * shards
-    member_weights = lax.all_gather(pool_weight, "member", axis=0, tiled=True)
-    member_weights, states = lax.optimization_barrier((member_weights, states))
-
     def logits_of(first_row, rows):
         piece = lax.dynamic_slice_in_dim(states, first_row, rows, 0)
         packed = jnp.concatenate([piece, norm_gain], axis=0)
@@ -55,38 +52,46 @@
         normed = jnp.transpose(normed, (1, 0, 2)).reshape(rows, width_all)
         return jnp.dot(normed, weights, preferred_element_type=jnp.float32)
 
+    w = pool_weight[0]
     sub = share // send_pieces
     received = []
+    notes = []
     for shift in range(1, members):
         target = (me + shift) % members
         perm = [(g, (g + shift) % members) for g in range(members)]
         parts = []
+        piece_stats = []
         for k in range(send_pieces):
             logits = logits_of(target * share + k * sub, sub)
-            parts.append(lax.ppermute(logits, "member", perm))
-        received.append((member_weights[(me - shift) % members], parts))
+            parts.append(lax.ppermute(w * logits, "member", perm))
+            piece_stats.append(local_stats(logits))
+        stats_rows = jnp.concatenate(piece_stats, axis=1)
+        note = jnp.concatenate([stats_rows, jnp.broadcast_to(w, (1, share))], axis=0)
+        received.append(parts)
+        notes.append((perm, note))
     own_logits = logits_of(me * share, share)
-    own_weight = member_weights[me]
+    notes, own_logits = lax.optimization_barrier(([note for _, note in notes], own_logits))
+    notes = [lax.ppermute(note, "member", [(g, (g + shift) % members) for g in range(members)])
+             for shift, note in zip(range(1, members), notes)]
 
     pooled_raw = []
-    stats = [[] for _ in range(members + 1)]
+    stats = []
     for k in range(send_pieces):
         own = own_logits[k * sub:(k + 1) * sub]
-        total = own_weight * own
-        stats[0].append(local_stats(own))
-        for index, (weight, parts) in enumerate(received):
-            total = total + weight * parts[k]
-            stats[index + 1].append(local_stats(parts[k]))
+        total = w * own
+        for parts in received:
+            total = total + parts[k]
         pooled_raw.append(total)
-        stats[members].append(local_stats(total))
-    stats = jnp.stack([jnp.concatenate(column, axis=1) for column in stats], axis=1)
+        stats.append(jnp.stack([local_stats(own), local_stats(total)], axis=1))
+    stats = jnp.concatenate(stats, axis=2)
+    stats = jnp.concatenate([stats] + [note[:2, None, :] for note in notes], axis=1)
     peak, summed = reduce_stats(stats, "vocab")
     lse = peak + jnp.log(summed)
-    offset = own_weight * lse[0]
-    for index, (weight, parts) in enumerate(received):
-        offset = offset + weight * lse[index + 1]
+    offset = w * lse[0]
+    for index, note in enumerate(notes):
+        offset = offset + note[2] * lse[index + 2]
 
-    agreement = lse[members] - offset
+    agreement = lse[1] - offset
     pooled = jnp.concatenate(pooled_raw, axis=0) - offset[:, None]
     return (pooled - agreement[:, None], agreement)
 

time: 182 us -> 169 us (0.929)
  blocking collectives: 49.3 us -> 43.8 us
  waiting for transfers between devices: 50.9 us -> 55.9 us
  matrix products: 31 us -> 26.1 us
  local copies, waits for them, and re-layouts: 9.74 us -> 4.9 us
  other arithmetic: 22.8 us -> 18.9 us
    optimization_barrier x1 -> x0, blocking collectives: 5.84 us -> none  [on_device(): member_weights, states = lax.optimization_barrier((member_weights, states))]
    dot_general x3, matrix products: 31 us -> 26.1 us  [logits_of(): return jnp.dot(normed, weights, preferred_element_type=jnp.float32)]
    ppermute x2 -> x3, waiting for transfers between devices: 38 us -> 42.9 us  [the longest x1 42.9 us: on_device(): lax.ppermute(note, 'member', [(g, (g + shift) % members) for g in range(m...]
    reduce_max x4 -> x2, other arithmetic: 8.43 us -> 4.33 us  [local_stats(): local_peak = jnp.max(values, axis=1)]
    unnamed x10 -> x9, local copies, waits for them, and re-layouts: 4.28 us -> 1.92 us
    reduce_sum x3 -> x4, other arithmetic: 5.75 us -> 6.41 us  [local_stats(): local_sum = jnp.sum(jnp.exp(values - local_peak[:, None]), axis=1)]
  transfers between devices with their start and end apart: 7 -> 8, of which waited for: 5 -> 5; matrix products, arithmetic and copies ran while one was open for 24% -> 24% of each run, Pallas kernels for 0% -> 0%
where the time goes in v3:
time: 169 us; the launch traced here: 168 us
  waiting for transfers between devices  55.9 us (33%)
  blocking collectives  43.8 us (26%)
  matrix products  26.1 us (15%)
  other arithmetic  18.9 us (11%)
  between operations  14.9 us (9%)
  local copies, waits for them, and re-layouts  4.9 us (3%)
  starting transfers between devices  3.93 us (2%)
    all_gather x2, blocking collectives, logits_of(): gathered = lax.all_gather(packed, 'vocab', axis=0, tiled=False)  43.8 us
    ppermute x1, waiting for transfers between devices, on_device(): lax.ppermute(note, 'member', [(g, (g + shift) % members) for g in range(m...  42.9 us
    dot_general x3, matrix products, logits_of(): return jnp.dot(normed, weights, preferred_element_type=jnp.float32)  26.1 us
    ppermute x4, waiting for transfers between devices, reduce_stats(): other = lax.ppermute(stats, axis, perm)  13 us
    reduce_sum x4, other arithmetic, local_stats(): local_sum = jnp.sum(jnp.exp(values - local_peak[:, None]), axis=1)  6.41 us
    reduce_max x2, other arithmetic, local_stats(): local_peak = jnp.max(values, axis=1)  4.33 us
  transfers between devices with their start and end apart: 8, of which 5 were waited for; matrix products, arithmetic and copies ran while one was open for 24% of the time, Pallas kernels for 0%

profile of v3, /device:TPU:0, one launch (start us, length us, event | category | flops | bytes accessed | tf_op | source)
XLA Modules:
  0.0 168.4 jit_solution(14553935766301464974)
XLA Ops:
  7.2 0.8 dynamic-slice_bitcast_fusion
  8.1 1.3 maximum_bitcast_fusion
  9.4 0.8 dynamic-slice_bitcast_fusion.2
  10.2 0.7 fusion.16
  10.8 24.8 %all-gather.3 = bf16[16,129,128]{2,1,0:T(8,128)(2,1)S(1)} all-gather(bf16[1,129,128]{2,1,0:T(8,128)(2,1)S(1)} %get-tuple-element.29), channel_id=2, replica_groups=mesh['member'=2,'vocab'=16] {'vocab'}, dimensions={0}, use_global_device_ids=true | all-gather | bytes 561408 | tf_op jit(solution)/shard_map/all_gather | solution.py:46
  37.0 0.3 fusion.12
  37.3 8.1 %fusion.45 = (f32[128]{0:T(128)S(1)}, f32[128,4008]{0,1:T(8,128)S(1)}) fusion(bf16[128,2048]{0,1:T(8,128)(2,1)S(1)} %bitcast.189, bf16[1,2048,4008]{1,2,0:T(8,128)(2,1)} %param.6), kind=kOutput, calls=%fused_computation.109 | convolution fusion | flops 2101859200 | bytes 18993664 | tf_op jit(solution)/shard_map/dot_general | solution.py:53
  45.4 1.8 %broadcast_multiply_fusion.1 = (f32[128,4008]{0,1:T(8,128)}, f32[128]{0:T(128)S(1)}) fusion(f32[128,4008]{0,1:T(8,128)S(1)} %get-tuple-element.34, f32[]{:T(128)} %bitcast.188, f32[128]{0:T(128)S(1)} %get-tuple-element.33), kind=kLoop, calls=%fused_computation.34 | loop fusion | flops 1538944 | bytes 4105220 | tf_op jit(solution)/shard_map/mul | solution.py:66
  47.2 1.6 collective-permute-start
  48.8 19.0 %all-gather.4 = bf16[16,129,128]{2,1,0:T(8,128)(2,1)S(1)} all-gather(bf16[1,129,128]{2,1,0:T(8,128)(2,1)S(1)} %get-tuple-element.30), channel_id=3, replica_groups=mesh['member'=2,'vocab'=16] {'vocab'}, dimensions={0}, use_global_device_ids=true | all-gather | bytes 561408 | tf_op jit(solution)/shard_map/all_gather | solution.py:46
  68.4 0.3 fusion.15
  68.7 8.1 %fusion.44 = (f32[128]{0:T(128)S(1)}, f32[128,4008]{0,1:T(8,128)S(1)}) fusion(bf16[128,2048]{0,1:T(8,128)(2,1)S(1)} %bitcast.190, bf16[1,2048,4008]{1,2,0:T(8,128)(2,1)} %param.6), kind=kOutput, calls=%fused_computation.108 | convolution fusion | flops 2101859200 | bytes 18993664 | tf_op jit(solution)/shard_map/dot_general | solution.py:53
  76.8 1.8 %exponential_reduce_fusion.4 = (f32[128]{0:T(128)S(1)}, f32[128,4008]{0,1:T(8,128)}) fusion(f32[128,4008]{0,1:T(8,128)S(1)} %get-tuple-element.32, f32[128]{0:T(128)S(1)} %get-tuple-element.31, f32[]{:T(128)} %bitcast.186), kind=kLoop, calls=%fused_computation.19 | loop fusion | flops 1538944 | bytes 4105220 | tf_op jit(solution)/shard_map/reduce_sum | solution.py:12
  78.6 0.4 collective-permute-start.1
  79.1 1.2 slice-done
  80.3 0.5 copy.28
  81.2 0.4 copy-done.1
  81.6 0.3 fusion.9
  81.9 9.9 %fusion = f32[256,4008]{0,1:T(8,128)} fusion(bf16[256,2048]{0,1:T(8,128)(2,1)S(1)} %bitcast.191, bf16[1,2048,4008]{1,2,0:T(8,128)(2,1)} %param.6), kind=kOutput, calls=%fused_computation | convolution fusion | flops 4202692608 | bytes 21569536 | tf_op jit(solution)/shard_map/dot_general | solution.py:53
  91.9 1.6 collective-permute-start.2
  93.4 2.1 %slice_reduce_fusion.1 = f32[128]{0:T(128)S(1)} fusion(f32[256,4008]{0,1:T(8,128)} %fusion), kind=kLoop, calls=%fused_computation.22 | loop fusion | flops 512896 | bytes 2052608 | tf_op jit(solution)/shard_map/reduce_max | solution.py:11
  95.6 42.9 %collective-permute-done.2 = f32[3,256]{1,0:T(4,128)S(1)} collective-permute-done((f32[3,256]{1,0:T(4,128)S(1)}, f32[3,256]{1,0:T(4,128)S(1)}, u32[]{:S(2)}, u32[]{:S(2)}) %collective-permute-start.2) | collective-permute-done | bytes 3104 | tf_op jit(solution)/shard_map/ppermute | solution.py:74
  138.5 3.5 %exponential_reduce_fusion.3 = (f32[128]{0:T(128)S(1)}, f32[128]{0:T(128)S(1)}, f32[128]{0:T(128)S(1)}, f32[128,4008]{0,1:T(8,128)S(1)}) fusion(f32[256,4008]{0,1:T(8,128)} %fusion, f32[128]{0:T(128)S(1)} %slice_reduce_fusion.1, f32[128,4008]{0,1:T(8,128)} %collective-permute-done, f32[]{:T(128)} %bitcast.183), kind=kLoop, calls=%fused_computation.16 | loop fusion | flops 3077760 | bytes 8210436 | tf_op jit(solution)/shard_map/reduce_sum | solution.py:12
  142.0 0.4 copy-done
  142.4 2.2 %fusion.43 = (f32[128]{0:T(128)S(1)}, f32[128,4008]{0,1:T(8,128)S(1)}, f32[128]{0:T(128)S(1)}) fusion(f32[128,4008]{0,1:T(8,128)} %collective-permute-done.1, f32[256,4008]{0,1:T(8,128)S(1)} %copy-done, f32[]{:T(128)} %bitcast.187, f32[128]{0:T(128)S(1)} %get-tuple-element.7), kind=kLoop, calls=%fused_computation.107 | loop fusion | flops 2564864 | bytes 6157828 | tf_op jit(solution)/shard_map/reduce_max | solution.py:11
  144.7 0.6 exponential_reduce_fusion
  145.2 0.6 exponential_reduce_fusion.2
  145.9 1.2 collective-permute-done.3
  147.2 3.6 %collective-permute-done.4 = f32[2,3,256]{2,1,0:T(4,128)S(1)} collective-permute-done((f32[2,3,256]{2,1,0:T(4,128)S(1)}, f32[2,3,256]{2,1,0:T(4,128)S(1)}, u32[]{:S(2)}, u32[]{:S(2)}) %collective-permute-start.4) | collective-permute-done | bytes 6176 | tf_op jit(solution)/shard_map/ppermute | solution.py:26
  150.9 3.6 %collective-permute-done.5 = f32[2,3,256]{2,1,0:T(4,128)S(1)} collective-permute-done((f32[2,3,256]{2,1,0:T(4,128)S(1)}, f32[2,3,256]{2,1,0:T(4,128)S(1)}, u32[]{:S(2)}, u32[]{:S(2)}) %collective-permute-start.5) | collective-permute-done | bytes 6176 | tf_op jit(solution)/shard_map/ppermute | solution.py:26
  154.6 4.5 %collective-permute-done.6 = f32[2,3,256]{2,1,0:T(4,128)S(1)} collective-permute-done((f32[2,3,256]{2,1,0:T(4,128)S(1)}, f32[2,3,256]{2,1,0:T(4,128)S(1)}, u32[]{:S(2)}, u32[]{:S(2)}) %collective-permute-start.6) | collective-permute-done | bytes 6176 | tf_op jit(solution)/shard_map/ppermute | solution.py:26
  159.3 2.3 %fusion.6 = f32[256,4008]{0,1:T(8,128)} fusion(f32[128,4008]{0,1:T(8,128)S(1)} %get-tuple-element.15, f32[128,4008]{0,1:T(8,128)S(1)} %get-tuple-element.18, f32[256]{0:T(256)S(1)} %sub.147, f32[256]{0:T(256)S(1)} %bitcast.193), kind=kLoop, calls=%fused_computation.7 | loop fusion | flops 3078144 | bytes 8210432 | tf_op jit(solution)/shard_map/sub | solution.py:96
  (47 shorter events, 2.2 us)
Async XLA Ops:
  7.2 71.9 %all-gather.8.cloned.1.call-start = ((), (), s32[]{:S(2)}) async-start(), calls=%async_computation | async-start | bytes 1148928 | tf_op jit(solution)/shard_map/all_gather | solution.py:46
  47.2 91.3 %collective-permute-start = (f32[128,4008]{0,1:T(8,128)}, f32[128,4008]{0,1:T(8,128)}, u32[]{:S(2)}, u32[]{:S(2)}) collective-permute-start(f32[128,4008]{0,1:T(8,128)} %get-tuple-element.19), channel_id=1, source_target_pairs={{0,16},{16,0},{1,17},{17,1},{2,18},{18,2},{3,19},{19,3},{4,20},{20... | collective-permute-start | bytes 6156296 | tf_op jit(solution)/shard_map/ppermute | solution.py:66
  78.6 63.4 %collective-permute-start.1 = (f32[128,4008]{0,1:T(8,128)}, f32[128,4008]{0,1:T(8,128)}, u32[]{:S(2)}, u32[]{:S(2)}) collective-permute-start(f32[128,4008]{0,1:T(8,128)} %get-tuple-element.22), channel_id=1, source_target_pairs={{0,16},{16,0},{1,17},{17,1},{2,18},{18,2},{3,19},{19,3},{4,20},{20... | collective-permute-start | bytes 6156296 | tf_op jit(solution)/shard_map/ppermute | solution.py:66
  79.1 1.2 slice-start
  80.3 1.2 copy-start.1
  91.9 46.6 %collective-permute-start.2 = (f32[3,256]{1,0:T(4,128)S(1)}, f32[3,256]{1,0:T(4,128)S(1)}, u32[]{:S(2)}, u32[]{:S(2)}) collective-permute-start(f32[3,256]{1,0:T(4,128)S(1)} %fusion.22), channel_id=1, source_target_pairs={{0,16},{16,0},{1,17},{17,1},{2,18},{18,2},{3,19},{19,3},{4,20},{20... | collective-permute-start | bytes 9224 | tf_op jit(solution)/shard_map/ppermute | solution.py:74
  138.5 4.0 %copy-start = (f32[256,4008]{0,1:T(8,128)S(1)}, f32[256,4008]{0,1:T(8,128)}, u32[]{:S(2)}) copy-start(f32[256,4008]{0,1:T(8,128)} %fusion) | copy-start | bytes 12312580
  145.8 1.2 collective-permute-start.3
  147.1 3.7 %collective-permute-start.4 = (f32[2,3,256]{2,1,0:T(4,128)S(1)}, f32[2,3,256]{2,1,0:T(4,128)S(1)}, u32[]{:S(2)}, u32[]{:S(2)}) collective-permute-start(f32[2,3,256]{2,1,0:T(4,128)S(1)} %pad_maximum_fusion.3), channel_id=1, source_target_pairs={{0,2},{1,3},{2,0},{3,1},{4,6},{5,7},{6,4},{7,5},{8,10},{9,11},{10,... | collective-permute-start | bytes 18440 | tf_op jit(solution)/shard_map/ppermute | solution.py:26
  150.8 3.7 %collective-permute-start.5 = (f32[2,3,256]{2,1,0:T(4,128)S(1)}, f32[2,3,256]{2,1,0:T(4,128)S(1)}, u32[]{:S(2)}, u32[]{:S(2)}) collective-permute-start(f32[2,3,256]{2,1,0:T(4,128)S(1)} %pad_maximum_fusion.4), channel_id=1, source_target_pairs={{0,4},{1,5},{2,6},{3,7},{4,0},{5,1},{6,2},{7,3},{8,12},{9,13},{10,... | collective-permute-start | bytes 18440 | tf_op jit(solution)/shard_map/ppermute | solution.py:26
  154.6 4.6 %collective-permute-start.6 = (f32[2,3,256]{2,1,0:T(4,128)S(1)}, f32[2,3,256]{2,1,0:T(4,128)S(1)}, u32[]{:S(2)}, u32[]{:S(2)}) collective-permute-start(f32[2,3,256]{2,1,0:T(4,128)S(1)} %pad_maximum_fusion.5), channel_id=1, source_target_pairs={{0,8},{1,9},{2,10},{3,11},{4,12},{5,13},{6,14},{7,15},{8,0},{9,1},... | collective-permute-start | bytes 18440 | tf_op jit(solution)/shard_map/ppermute | solution.py:26
  159.2 2.3 %copy-start.2 = (f32[256]{0:T(256)}, f32[256]{0:T(256)S(1)}, u32[]{:S(2)}) copy-start(f32[256]{0:T(256)S(1)} %sub.147) | copy-start | bytes 3076
Sparse Core Ops, SparseCore 0:
  10.7 41.0 all-gather.7

commit v4 on v3

--- a/solution.py
+++ b/solution.py
@@ -4,7 +4,6 @@
 from jax.sharding import PartitionSpec as P
 
 epsilon = 1e-05
-send_pieces = 2
 
 
 def local_stats(values):
@@ -40,8 +39,8 @@
     share = row_count // members
     weights = head[0]
     width_all = width * shards
-    def logits_of(first_row, rows):
-        piece = lax.dynamic_slice_in_dim(states, first_row, rows, 0)
+    def logits_of(source, first_row, rows):
+        piece = lax.dynamic_slice_in_dim(source, first_row, rows, 0)
         packed = jnp.concatenate([piece, norm_gain], axis=0)
         gathered = lax.all_gather(packed, "vocab", axis=0, tiled=False)
         full_states = gathered[:, :rows, :].astype(jnp.float32)
@@ -53,34 +52,41 @@
         return jnp.dot(normed, weights, preferred_element_type=jnp.float32)
 
     w = pool_weight[0]
-    sub = share // send_pieces
+    first = share // 4
+    second = (share - first) // 2
+    sizes = [first, second, share - first - second]
+    starts = [sum(sizes[:k]) for k in range(len(sizes))]
     received = []
     notes = []
+    first_logits = None
     for shift in range(1, members):
         target = (me + shift) % members
         perm = [(g, (g + shift) % members) for g in range(members)]
         parts = []
         piece_stats = []
-        for k in range(send_pieces):
-            logits = logits_of(target * share + k * sub, sub)
-            parts.append(lax.ppermute(w * logits, "member", perm))
+        for begin, rows in zip(starts, sizes):
+            logits = logits_of(states, target * share + begin, rows)
+            if first_logits is None:
+                first_logits = logits
+            parts.append(lax.ppermute(logits, "member", perm))
             piece_stats.append(local_stats(logits))
         stats_rows = jnp.concatenate(piece_stats, axis=1)
         note = jnp.concatenate([stats_rows, jnp.broadcast_to(w, (1, share))], axis=0)
         received.append(parts)
-        notes.append((perm, note))
-    own_logits = logits_of(me * share, share)
-    notes, own_logits = lax.optimization_barrier(([note for _, note in notes], own_logits))
+        notes.append(note)
+    first_logits, own_states = lax.optimization_barrier((first_logits, states))
+    own_logits = logits_of(own_states, me * share, share)
+    notes, own_logits = lax.optimization_barrier((notes, own_logits))
     notes = [lax.ppermute(note, "member", [(g, (g + shift) % members) for g in range(members)])
              for shift, note in zip(range(1, members), notes)]
 
     pooled_raw = []
     stats = []
-    for k in range(send_pieces):
-        own = own_logits[k * sub:(k + 1) * sub]
+    for k, (begin, rows) in enumerate(zip(starts, sizes)):
+        own = own_logits[begin:begin + rows]
         total = w * own
-        for parts in received:
-            total = total + parts[k]
+        for parts, note in zip(received, notes):
+            total = total + note[2, begin:begin + rows, None] * parts[k]
         pooled_raw.append(total)
         stats.append(jnp.stack([local_stats(own), local_stats(total)], axis=1))
     stats = jnp.concatenate(stats, axis=2)

time: 169 us -> 186 us (1.10)
  waiting for transfers between devices: 55.9 us -> 16.1 us
  matrix products: 26.1 us -> 47.7 us
  blocking collectives: 43.8 us -> 62.7 us
  local copies, waits for them, and re-layouts: 4.9 us -> 16.7 us
  starting transfers between devices: 3.93 us -> 6.51 us
    ppermute x1, waiting for transfers between devices: 42.9 us -> 5.15 us  [on_device(): lax.ppermute(note, 'member', [(g, (g + shift) % members) for g in range(m...]
    dot_general x3 -> x4, matrix products: 26.1 us -> 47.7 us  [logits_of(): return jnp.dot(normed, weights, preferred_element_type=jnp.float32)]
    all_gather x2 -> x3, blocking collectives: 43.8 us -> 62.7 us  [logits_of(): gathered = lax.all_gather(packed, 'vocab', axis=0, tiled=False)]
    optimization_barrier x0 -> x1, local copies, waits for them, and re-layouts: none -> 5.51 us  [on_device(): notes, own_logits = lax.optimization_barrier((notes, own_logits))]
    unnamed x9 -> x10, local copies, waits for them, and re-layouts: 1.92 us -> 7.31 us
    reduce_max x2 -> x4, other arithmetic: 4.33 us -> 7.08 us  [local_stats(): local_peak = jnp.max(values, axis=1)]
    ppermute x4, starting transfers between devices: 0.28 us -> 2.31 us  [reduce_stats(): other = lax.ppermute(stats, axis, perm)]
    ppermute x4, waiting for transfers between devices: 13 us -> 11 us  [reduce_stats(): other = lax.ppermute(stats, axis, perm)]
  transfers between devices with their start and end apart: 8 -> 9, of which waited for: 5 -> 5; matrix products, arithmetic and copies ran while one was open for 24% -> 33% of each run, Pallas kernels for 0% -> 0%
where the time goes in v4:
time: 186 us; the launch traced here: 185 us
  blocking collectives  62.7 us (34%)
  matrix products  47.7 us (26%)
  other arithmetic  20.5 us (11%)
  local copies, waits for them, and re-layouts  16.7 us (9%)
  waiting for transfers between devices  16.1 us (9%)
  between operations  14.9 us (8%)
  starting transfers between devices  6.51 us (4%)
    all_gather x3, blocking collectives, logits_of(): gathered = lax.all_gather(packed, 'vocab', axis=0, tiled=False)  62.7 us
    dot_general x4, matrix products, logits_of(): return jnp.dot(normed, weights, preferred_element_type=jnp.float32)  47.7 us
    ppermute x4, waiting for transfers between devices, reduce_stats(): other = lax.ppermute(stats, axis, perm)  11 us
    unnamed x10, local copies, waits for them, and re-layouts  7.31 us
    reduce_max x4, other arithmetic, local_stats(): local_peak = jnp.max(values, axis=1)  7.08 us
    reduce_sum x7, other arithmetic, local_stats(): local_sum = jnp.sum(jnp.exp(values - local_peak[:, None]), axis=1)  7.04 us
    optimization_barrier x1, local copies, waits for them, and re-layouts, on_device(): notes, own_logits = lax.optimization_barrier((notes, own_logits))  5.51 us
    ppermute x1, waiting for transfers between devices, on_device(): lax.ppermute(note, 'member', [(g, (g + shift) % members) for g in range(m...  5.15 us
  transfers between devices with their start and end apart: 9, of which 5 were waited for; matrix products, arithmetic and copies ran while one was open for 33% of the time, Pallas kernels for 0%

profile of v4, /device:TPU:0, one launch (start us, length us, event | category | flops | bytes accessed | tf_op | source)
XLA Modules:
  0.0 185.2 jit_solution(10009972254786667496)
XLA Ops:
  7.2 0.7 dynamic-slice_bitcast_fusion.2
  8.0 0.7 maximum_bitcast_fusion.1
  8.6 23.8 %all-gather.4 = bf16[16,65,128]{2,1,0:T(8,128)(2,1)S(1)} all-gather(bf16[1,65,128]{2,1,0:T(8,128)(2,1)S(1)} %maximum_bitcast_fusion.1), channel_id=2, replica_groups=mesh['member'=2,'vocab'=16] {'vocab'}, dimensions={0}, use_global_device_ids=true | all-gather | bytes 282880 | tf_op jit(solution)/shard_map/all_gather | solution.py:45
  32.7 12.0 %fusion.60 = (f32[64]{0:T(128)S(1)}, f32[64,4008]{1,0:T(8,128)}) fusion(bf16[1,2048,4008]{1,2,0:T(8,128)(2,1)} %param.6, f32[16,128]{1,0:T(8,128)S(1)} %bitcast.230, f32[64]{0:T(128)S(1)} %add_rsqrt_fusion.3, bf16[16,65,128]{2,1,0:T(8,128)(2,1)S(1)} %all-gather.4), kind=kOutput, calls=%fused_computation.139 | convolution fusion | flops 1051453888 | bytes 17713920 | tf_op jit(solution)/shard_map/dot_general | solution.py:52
  44.6 1.6 collective-permute-start.1
  46.2 0.6 maximum_bitcast_fusion
  46.9 18.5 %all-gather.5 = bf16[16,97,128]{2,1,0:T(8,128)(2,1)S(1)} all-gather(bf16[1,97,128]{2,1,0:T(8,128)(2,1)S(1)} %get-tuple-element.42), channel_id=3, replica_groups=mesh['member'=2,'vocab'=16] {'vocab'}, dimensions={0}, use_global_device_ids=true | all-gather | bytes 422144 | tf_op jit(solution)/shard_map/all_gather | solution.py:45
  65.6 12.4 %fusion.59 = (f32[96]{0:T(128)S(1)}, f32[96,4008]{1,0:T(8,128)}) fusion(bf16[1,2048,4008]{1,2,0:T(8,128)(2,1)} %param.6, f32[16,128]{1,0:T(8,128)S(1)} %bitcast.231, f32[96]{0:T(128)S(1)} %add_rsqrt_fusion.2, bf16[16,97,128]{2,1,0:T(8,128)(2,1)S(1)} %all-gather.5), kind=kOutput, calls=%fused_computation.138 | convolution fusion | flops 1577180800 | bytes 18358144 | tf_op jit(solution)/shard_map/dot_general | solution.py:52
  78.5 20.3 %all-gather.6 = bf16[16,97,128]{2,1,0:T(8,128)(2,1)S(1)} all-gather(bf16[1,97,128]{2,1,0:T(8,128)(2,1)S(1)} %get-tuple-element.43), channel_id=4, replica_groups=mesh['member'=2,'vocab'=16] {'vocab'}, dimensions={0}, use_global_device_ids=true | all-gather | bytes 422144 | tf_op jit(solution)/shard_map/all_gather | solution.py:45
  99.0 11.0 %fusion.58 = (f32[96]{0:T(128)S(1)}, f32[96,4008]{1,0:T(8,128)S(1)}) fusion(bf16[1,2048,4008]{1,2,0:T(8,128)(2,1)} %param.6, f32[16,128]{1,0:T(8,128)S(1)} %bitcast.232, f32[96]{0:T(128)S(1)} %add_rsqrt_fusion.1, bf16[16,97,128]{2,1,0:T(8,128)(2,1)S(1)} %all-gather.6), kind=kOutput, calls=%fused_computation.137 | convolution fusion | flops 1577180800 | bytes 18358144 | tf_op jit(solution)/shard_map/dot_general | solution.py:52
  109.9 1.8 collective-permute-start.3
  112.4 1.5 exponential_reduce_fusion.8
  114.0 1.8 exponential_reduce_fusion.5
  116.2 2.3 %slice.127 = bf16[16,256,128]{2,1,0:T(8,128)(2,1)} slice(bf16[16,257,128]{2,1,0:T(8,128)(2,1)} %all-gather.10.cloned.1.call-done), slice={[0:16], [0:256], [0:128]} | slice | bytes 2097152 | tf_op jit(solution)/shard_map/slice | solution.py:46
  118.5 1.5 copy.51
  120.3 0.8 slice.128
  121.1 1.3 fusion.11
  122.5 12.4 %fusion = f32[256,4008]{0,1:T(8,128)} fusion(bf16[256,2048]{0,1:T(8,128)(2,1)} %bitcast.228, bf16[1,2048,4008]{1,2,0:T(8,128)(2,1)} %param.6), kind=kOutput, calls=%fused_computation | convolution fusion | flops 4202692608 | bytes 21569536 | tf_op jit(solution)/shard_map/dot_general | solution.py:52
  134.9 5.5 %copy.45 = f32[256,4008]{1,0:T(8,128)} copy(f32[256,4008]{0,1:T(8,128)} %fusion) | data formatting | bytes 8208384 | tf_op jit(solution)/shard_map/optimization_barrier | solution.py:79
  140.6 1.6 slice_reduce_fusion.1
  142.2 1.4 slice_reduce_fusion.2
  143.6 5.1 %collective-permute-done = f32[3,256]{1,0:T(4,128)S(1)} collective-permute-done((f32[3,256]{1,0:T(4,128)S(1)}, f32[3,256]{1,0:T(4,128)S(1)}, u32[]{:S(2)}, u32[]{:S(2)}) %collective-permute-start) | collective-permute-done | bytes 3104 | tf_op jit(solution)/shard_map/ppermute | solution.py:80
  148.8 2.1 %fusion.55 = (f32[64]{0:T(128)S(1)}, f32[64,4008]{1,0:T(8,128)S(1)}, f32[64]{0:T(128)S(1)}) fusion(f32[64,4008]{1,0:T(8,128)} %collective-permute-done.1, f32[64]{0:T(128)S(1)} %slice_bitcast_fusion.4, f32[256,4008]{1,0:T(8,128)} %copy.45, f32[]{:T(128)} %bitcast.223, f32[64]{0:T(128)S(1)} %slice_reduce_fusion.2), kind=kLoop, calls=%fused_computation.134 | loop fusion | flops 1538944 | bytes 3079172 | tf_op jit(solution)/shard_map/reduce_max | solution.py:10
  151.6 2.2 %exponential_reduce_fusion.3 = (f32[96]{0:T(128)S(1)}, f32[96]{0:T(128)S(1)}, f32[96]{0:T(128)S(1)}, f32[96,4008]{1,0:T(8,128)S(1)}) fusion(f32[256,4008]{1,0:T(8,128)S(1)} %copy-done, f32[96]{0:T(128)S(1)} %slice_reduce_fusion.1, f32[96,4008]{1,0:T(8,128)} %collective-permute-done.2, f32[96]{0:T(128)S(1)} %get-tuple-element.40, f32[]{:T(128)} %bitcast.225), kind=kLoop, calls=%fused_computation.18 | loop fusion | flops 2693088 | bytes 6158212 | tf_op jit(solution)/shard_map/reduce_sum | solution.py:11
  154.2 2.0 %fusion.57 = (f32[96]{0:T(128)S(1)}, f32[96,4008]{1,0:T(8,128)S(1)}, f32[96]{0:T(128)S(1)}) fusion(f32[96,4008]{1,0:T(8,128)} %collective-permute-done.3, f32[96]{0:T(128)S(1)} %get-tuple-element.41, f32[256,4008]{1,0:T(8,128)S(1)} %copy-done, f32[]{:T(128)} %bitcast.227, f32[96]{0:T(128)S(1)} %get-tuple-element.19), kind=kLoop, calls=%fused_computation.136 | loop fusion | flops 2308416 | bytes 4618756 | tf_op jit(solution)/shard_map/reduce_max | solution.py:10
  156.8 1.2 collective-permute-done.4
  158.0 2.1 %collective-permute-start.5 = (f32[2,3,256]{2,1,0:T(4,128)S(1)}, f32[2,3,256]{2,1,0:T(4,128)S(1)}, u32[]{:S(2)}, u32[]{:S(2)}) collective-permute-start(f32[2,3,256]{2,1,0:T(4,128)S(1)} %pad_maximum_fusion.3), channel_id=1, source_target_pairs={{0,2},{1,3},{2,0},{3,1},{4,6},{5,7},{6,4},{7,5},{8,10},{9,11},{10,... | collective-permute-start | bytes 18440 | tf_op jit(solution)/shard_map/ppermute | solution.py:25
  160.1 1.6 collective-permute-done.5
  161.8 3.6 %collective-permute-done.6 = f32[2,3,256]{2,1,0:T(4,128)S(1)} collective-permute-done((f32[2,3,256]{2,1,0:T(4,128)S(1)}, f32[2,3,256]{2,1,0:T(4,128)S(1)}, u32[]{:S(2)}, u32[]{:S(2)}) %collective-permute-start.6) | collective-permute-done | bytes 6176 | tf_op jit(solution)/shard_map/ppermute | solution.py:25
  165.6 4.5 %collective-permute-done.7 = f32[2,3,256]{2,1,0:T(4,128)S(1)} collective-permute-done((f32[2,3,256]{2,1,0:T(4,128)S(1)}, f32[2,3,256]{2,1,0:T(4,128)S(1)}, u32[]{:S(2)}, u32[]{:S(2)}) %collective-permute-start.7) | collective-permute-done | bytes 6176 | tf_op jit(solution)/shard_map/ppermute | solution.py:25
  170.2 2.6 %fusion.8 = f32[256,4008]{1,0:T(8,128)} fusion(f32[96,4008]{1,0:T(8,128)S(1)} %get-tuple-element.29, f32[96,4008]{1,0:T(8,128)S(1)} %get-tuple-element.33, f32[64,4008]{1,0:T(8,128)S(1)} %get-tuple-element.25, f32[256]{0:T(256)S(1)} %sub.177, f32[256]{0:T(256)S(1)} %bitcast.234), kind=kLoop, calls=%fused_computation.9 | loop fusion | flops 4104192 | bytes 8210432 | tf_op jit(solution)/shard_map/sub | solution.py:102
  172.7 5.6 %copy.50 = f32[256,4008]{0,1:T(8,128)} copy(f32[256,4008]{1,0:T(8,128)} %fusion.8) | data formatting | bytes 8208384
  (59 shorter events, 4.1 us)
Async XLA Ops:
  7.2 109.1 %all-gather.10.cloned.1.call-start = ((), (), s32[]{:S(2)}) async-start(), calls=%async_computation | async-start | bytes 1148928 | tf_op jit(solution)/shard_map/all_gather | solution.py:45
  32.6 13.6 %copy-start.1 = (bf16[1,512,128]{2,1,0:T(8,128)(2,1)S(1)}, bf16[1,512,128]{2,1,0:T(8,128)(2,1)}, u32[]{:S(2)}) copy-start(bf16[1,512,128]{2,1,0:T(8,128)(2,1)} %param.4) | copy-start | bytes 393220
  32.6 13.6 %copy-start.2 = (bf16[1,128]{1,0:T(2,128)(2,1)S(1)}, bf16[1,128]{1,0:T(2,128)(2,1)}, u32[]{:S(2)}) copy-start(bf16[1,128]{1,0:T(2,128)(2,1)} %param.5) | copy-start | bytes 772
  44.6 104.2 %collective-permute-start.1 = (f32[64,4008]{1,0:T(8,128)}, f32[64,4008]{1,0:T(8,128)}, u32[]{:S(2)}, u32[]{:S(2)}) collective-permute-start(f32[64,4008]{1,0:T(8,128)} %get-tuple-element.49), channel_id=1, source_target_pairs={{0,16},{16,0},{1,17},{17,1},{2,18},{18,2},{3,19},{19,3},{4,20},{20... | collective-permute-start | bytes 3078152 | tf_op jit(solution)/shard_map/ppermute | solution.py:71
  78.0 73.4 %collective-permute-start.2 = (f32[96,4008]{1,0:T(8,128)}, f32[96,4008]{1,0:T(8,128)}, u32[]{:S(2)}, u32[]{:S(2)}) collective-permute-start(f32[96,4008]{1,0:T(8,128)} %get-tuple-element.47), channel_id=1, source_target_pairs={{0,16},{16,0},{1,17},{17,1},{2,18},{18,2},{3,19},{19,3},{4,20},{20... | collective-permute-start | bytes 4617224 | tf_op jit(solution)/shard_map/ppermute | solution.py:71
  109.9 44.3 %collective-permute-start.3 = (f32[96,4008]{1,0:T(8,128)S(1)}, f32[96,4008]{1,0:T(8,128)}, u32[]{:S(2)}, u32[]{:S(2)}) collective-permute-start(f32[96,4008]{1,0:T(8,128)S(1)} %get-tuple-element.45), channel_id=1, source_target_pairs={{0,16},{16,0},{1,17},{17,1},{2,18},{18,2},{3,19},{19,3},{4,20},{20... | collective-permute-start | bytes 4617224 | tf_op jit(solution)/shard_map/ppermute | solution.py:71
  140.4 8.4 %collective-permute-start = (f32[3,256]{1,0:T(4,128)S(1)}, f32[3,256]{1,0:T(4,128)S(1)}, u32[]{:S(2)}, u32[]{:S(2)}) collective-permute-start(f32[3,256]{1,0:T(4,128)S(1)} %fusion.36), channel_id=1, source_target_pairs={{0,16},{16,0},{1,17},{17,1},{2,18},{18,2},{3,19},{19,3},{4,20},{20... | collective-permute-start | bytes 9224 | tf_op jit(solution)/shard_map/ppermute | solution.py:80
  148.8 2.8 %copy-start = (f32[256,4008]{1,0:T(8,128)S(1)}, f32[256,4008]{1,0:T(8,128)}, u32[]{:S(2)}) copy-start(f32[256,4008]{1,0:T(8,128)} %copy.45) | copy-start | bytes 12312580
  156.7 1.2 collective-permute-start.4
  158.0 3.7 %collective-permute-start.5 = (f32[2,3,256]{2,1,0:T(4,128)S(1)}, f32[2,3,256]{2,1,0:T(4,128)S(1)}, u32[]{:S(2)}, u32[]{:S(2)}) collective-permute-start(f32[2,3,256]{2,1,0:T(4,128)S(1)} %pad_maximum_fusion.3), channel_id=1, source_target_pairs={{0,2},{1,3},{2,0},{3,1},{4,6},{5,7},{6,4},{7,5},{8,10},{9,11},{10,... | collective-permute-start | bytes 18440 | tf_op jit(solution)/shard_map/ppermute | solution.py:25
  161.8 3.7 %collective-permute-start.6 = (f32[2,3,256]{2,1,0:T(4,128)S(1)}, f32[2,3,256]{2,1,0:T(4,128)S(1)}, u32[]{:S(2)}, u32[]{:S(2)}) collective-permute-start(f32[2,3,256]{2,1,0:T(4,128)S(1)} %pad_maximum_fusion.4), channel_id=1, source_target_pairs={{0,4},{1,5},{2,6},{3,7},{4,0},{5,1},{6,2},{7,3},{8,12},{9,13},{10,... | collective-permute-start | bytes 18440 | tf_op jit(solution)/shard_map/ppermute | solution.py:25
  165.5 4.6 %collective-permute-start.7 = (f32[2,3,256]{2,1,0:T(4,128)S(1)}, f32[2,3,256]{2,1,0:T(4,128)S(1)}, u32[]{:S(2)}, u32[]{:S(2)}) collective-permute-start(f32[2,3,256]{2,1,0:T(4,128)S(1)} %pad_maximum_fusion.5), channel_id=1, source_target_pairs={{0,8},{1,9},{2,10},{3,11},{4,12},{5,13},{6,14},{7,15},{8,0},{9,1},... | collective-permute-start | bytes 18440 | tf_op jit(solution)/shard_map/ppermute | solution.py:25
  170.2 2.6 %copy-start.3 = (f32[256]{0:T(256)}, f32[256]{0:T(256)S(1)}, u32[]{:S(2)}) copy-start(f32[256]{0:T(256)S(1)} %sub.177) | copy-start | bytes 3076
Sparse Core Ops, SparseCore 0:
  47.0 34.5 all-gather.9

commit v5 on v3

--- a/solution.py
+++ b/solution.py
@@ -31,6 +31,21 @@
     return stats[0], stats[1]
 
 
+def gather_shards(x, axis):
+    size = lax.axis_size(axis)
+    if size & (size - 1):
+        return lax.all_gather(x, axis, axis=0, tiled=False)
+    index = lax.axis_index(axis)
+    block = x[None]
+    distance = 1
+    while distance < size:
+        other = lax.ppermute(block, axis, [(a, a ^ distance) for a in range(size)])
+        lower = (index // distance) % 2 == 0
+        block = jnp.where(lower, jnp.concatenate([block, other]), jnp.concatenate([other, block]))
+        distance *= 2
+    return block
+
+
 def on_device(hidden, norm_gain, head, pool_weight):
     members = lax.axis_size("member")
     shards = lax.axis_size("vocab")
@@ -40,10 +55,10 @@
     share = row_count // members
     weights = head[0]
     width_all = width * shards
-    def logits_of(first_row, rows):
+    def logits_of(first_row, rows, gather):
         piece = lax.dynamic_slice_in_dim(states, first_row, rows, 0)
         packed = jnp.concatenate([piece, norm_gain], axis=0)
-        gathered = lax.all_gather(packed, "vocab", axis=0, tiled=False)
+        gathered = gather(packed)
         full_states = gathered[:, :rows, :].astype(jnp.float32)
         gain = gathered[:, rows, :].astype(jnp.float32)
         mean_square = jnp.sum(full_states * full_states, axis=(0, 2)) / width_all
@@ -62,14 +77,14 @@
         parts = []
         piece_stats = []
         for k in range(send_pieces):
-            logits = logits_of(target * share + k * sub, sub)
+            logits = logits_of(target * share + k * sub, sub, lambda x: gather_shards(x, "vocab"))
             parts.append(lax.ppermute(w * logits, "member", perm))
             piece_stats.append(local_stats(logits))
         stats_rows = jnp.concatenate(piece_stats, axis=1)
         note = jnp.concatenate([stats_rows, jnp.broadcast_to(w, (1, share))], axis=0)
         received.append(parts)
         notes.append((perm, note))
-    own_logits = logits_of(me * share, share)
+    own_logits = logits_of(me * share, share, lambda x: lax.all_gather(x, "vocab", axis=0, tiled=False))
     notes, own_logits = lax.optimization_barrier(([note for _, note in notes], own_logits))
     notes = [lax.ppermute(note, "member", [(g, (g + shift) % members) for g in range(members)])
              for shift, note in zip(range(1, members), notes)]

time: 169 us -> 179 us (1.059)
  blocking collectives: 43.8 us -> 0 us
  waiting for transfers between devices: 55.9 us -> 93.4 us
  starting transfers between devices: 3.93 us -> 20.4 us
    all_gather x2 -> x0, blocking collectives: 43.8 us -> none  [logits_of(): gathered = lax.all_gather(packed, 'vocab', axis=0, tiled=False)]
    ppermute x0 -> x8, waiting for transfers between devices: none -> 26.5 us  [gather_shards(): other = lax.ppermute(block, axis, [(a, a ^ distance) for a in range(size)])]
    ppermute x1, waiting for transfers between devices: 42.9 us -> 59.8 us  [on_device(): lax.ppermute(note, 'member', [(g, (g + shift) % members) for g in range(m...]
    ppermute x0 -> x8, starting transfers between devices: none -> 10.1 us  [gather_shards(): other = lax.ppermute(block, axis, [(a, a ^ distance) for a in range(size)])]
    ppermute x4, starting transfers between devices: 0.28 us -> 6.84 us  [reduce_stats(): other = lax.ppermute(stats, axis, perm)]
    ppermute x4, waiting for transfers between devices: 13 us -> 7.09 us  [reduce_stats(): other = lax.ppermute(stats, axis, perm)]
  transfers between devices with their start and end apart: 8 -> 16, of which waited for: 5 -> 10; matrix products, arithmetic and copies ran while one was open for 24% -> 23% of each run, Pallas kernels for 0% -> 0%
where the time goes in v5:
time: 179 us
  waiting for transfers between devices  93.4 us (52%)
  matrix products  26.2 us (15%)
  starting transfers between devices  20.4 us (11%)
  other arithmetic  18.9 us (11%)
  between operations  15 us (8%)
  local copies, waits for them, and re-layouts  4.89 us (3%)
    ppermute x1, waiting for transfers between devices, on_device(): lax.ppermute(note, 'member', [(g, (g + shift) % members) for g in range(m...  59.8 us
    ppermute x8, waiting for transfers between devices, gather_shards(): other = lax.ppermute(block, axis, [(a, a ^ distance) for a in range(size)])  26.5 us
    dot_general x3, matrix products, logits_of(): return jnp.dot(normed, weights, preferred_element_type=jnp.float32)  26.2 us
    ppermute x8, starting transfers between devices, gather_shards(): other = lax.ppermute(block, axis, [(a, a ^ distance) for a in range(size)])  10.1 us
    ppermute x4, waiting for transfers between devices, reduce_stats(): other = lax.ppermute(stats, axis, perm)  7.09 us
    ppermute x4, starting transfers between devices, reduce_stats(): other = lax.ppermute(stats, axis, perm)  6.84 us
    reduce_sum x4, other arithmetic, local_stats(): local_sum = jnp.sum(jnp.exp(values - local_peak[:, None]), axis=1)  6.42 us
    reduce_max x2, other arithmetic, local_stats(): local_peak = jnp.max(values, axis=1)  4.33 us
  transfers between devices with their start and end apart: 16, of which 10 were waited for; matrix products, arithmetic and copies ran while one was open for 23% of the time, Pallas kernels for 0%

profile of v5, /device:TPU:0, one launch (start us, length us, event | category | flops | bytes accessed | tf_op | source)
XLA Modules:
  0.0 178.7 jit_solution(9774996273644509503)
XLA Ops:
  7.2 0.8 dynamic-slice_bitcast_fusion.2
  9.2 0.8 collective-permute-done.4
  10.0 2.9 %collective-permute-start.5 = (bf16[2,129,128]{2,1,0:T(8,128)(2,1)S(1)}, bf16[2,129,128]{2,1,0:T(8,128)(2,1)S(1)}, u32[]{:S(2)}, u32[]{:S(2)}) collective-permute-start(bf16[2,129,128]{2,1,0:T(8,128)(2,1)S(1)} %maximum_select_fusion.7), channel_id=1, source_target_pairs={{0,2},{1,3},{2,0},{3,1},{4,6},{5,7},{6,4},{7,5},{8,10},{9,11},{10,... | collective-permute-start | bytes 198152 | tf_op jit(solution)/shard_map/ppermute | solution.py:42
  13.1 2.4 %collective-permute-done.5 = bf16[2,129,128]{2,1,0:T(8,128)(2,1)S(1)} collective-permute-done((bf16[2,129,128]{2,1,0:T(8,128)(2,1)S(1)}, bf16[2,129,128]{2,1,0:T(8,128)(2,1)S(1)}, u32[]{:S(2)}, u32[]{:S(2)}) %collective-permute-start.5) | collective-permute-done | bytes 66080 | tf_op jit(solution)/shard_map/ppermute | solution.py:42
  15.5 2.2 %collective-permute-start.6 = (bf16[4,129,128]{2,1,0:T(8,128)(2,1)S(1)}, bf16[4,129,128]{2,1,0:T(8,128)(2,1)S(1)}, u32[]{:S(2)}, u32[]{:S(2)}) collective-permute-start(bf16[4,129,128]{2,1,0:T(8,128)(2,1)S(1)} %maximum_select_fusion.5), channel_id=1, source_target_pairs={{0,4},{1,5},{2,6},{3,7},{4,0},{5,1},{6,2},{7,3},{8,12},{9,13},{10,... | collective-permute-start | bytes 396296 | tf_op jit(solution)/shard_map/ppermute | solution.py:42
  17.7 1.2 collective-permute-start.2
  19.0 3.2 %collective-permute-done.6 = bf16[4,129,128]{2,1,0:T(8,128)(2,1)S(1)} collective-permute-done((bf16[4,129,128]{2,1,0:T(8,128)(2,1)S(1)}, bf16[4,129,128]{2,1,0:T(8,128)(2,1)S(1)}, u32[]{:S(2)}, u32[]{:S(2)}) %collective-permute-start.6) | collective-permute-done | bytes 132128 | tf_op jit(solution)/shard_map/ppermute | solution.py:42
  22.3 3.0 %collective-permute-start.7 = (bf16[8,129,128]{2,1,0:T(8,128)(2,1)S(1)}, bf16[8,129,128]{2,1,0:T(8,128)(2,1)S(1)}, u32[]{:S(2)}, u32[]{:S(2)}) collective-permute-start(bf16[8,129,128]{2,1,0:T(8,128)(2,1)S(1)} %maximum_select_fusion.3), channel_id=1, source_target_pairs={{0,8},{1,9},{2,10},{3,11},{4,12},{5,13},{6,14},{7,15},{8,0},{9,1},... | collective-permute-start | bytes 792584 | tf_op jit(solution)/shard_map/ppermute | solution.py:42
  25.2 0.8 dynamic-slice_bitcast_fusion
  26.1 1.3 maximum_bitcast_fusion
  28.2 16.4 %collective-permute-done.7 = bf16[8,129,128]{2,1,0:T(8,128)(2,1)S(1)} collective-permute-done((bf16[8,129,128]{2,1,0:T(8,128)(2,1)S(1)}, bf16[8,129,128]{2,1,0:T(8,128)(2,1)S(1)}, u32[]{:S(2)}, u32[]{:S(2)}) %collective-permute-start.7) | collective-permute-done | bytes 264224 | tf_op jit(solution)/shard_map/ppermute | solution.py:42
  44.9 3.7 %collective-permute-done.3 = bf16[8,129,128]{2,1,0:T(8,128)(2,1)S(1)} collective-permute-done((bf16[8,129,128]{2,1,0:T(8,128)(2,1)S(1)}, bf16[8,129,128]{2,1,0:T(8,128)(2,1)S(1)}, u32[]{:S(2)}, u32[]{:S(2)}) %collective-permute-start.3) | collective-permute-done | bytes 264224 | tf_op jit(solution)/shard_map/ppermute | solution.py:42
  49.5 8.2 %fusion.44 = (f32[128]{0:T(128)S(1)}, f32[128,4008]{0,1:T(8,128)S(1)}) fusion(bf16[128,2048]{0,1:T(8,128)(2,1)S(1)} %bitcast.182, bf16[1,2048,4008]{1,2,0:T(8,128)(2,1)} %param.6), kind=kOutput, calls=%fused_computation.116 | convolution fusion | flops 2101859200 | bytes 18993664 | tf_op jit(solution)/shard_map/dot_general | solution.py:68
  58.3 1.8 %exponential_reduce_fusion.4 = (f32[128]{0:T(128)S(1)}, f32[128,4008]{0,1:T(8,128)}) fusion(f32[128,4008]{0,1:T(8,128)S(1)} %get-tuple-element.32, f32[128]{0:T(128)S(1)} %get-tuple-element.31, f32[]{:T(128)} %bitcast.178), kind=kLoop, calls=%fused_computation.19 | loop fusion | flops 1538944 | bytes 4105220 | tf_op jit(solution)/shard_map/reduce_sum | solution.py:12
  60.1 1.4 collective-permute-start.9
  61.4 8.1 %fusion.45 = (f32[128]{0:T(128)S(1)}, f32[128,4008]{0,1:T(8,128)S(1)}) fusion(bf16[128,2048]{0,1:T(8,128)(2,1)S(1)} %bitcast.181, bf16[1,2048,4008]{1,2,0:T(8,128)(2,1)} %param.6), kind=kOutput, calls=%fused_computation.117 | convolution fusion | flops 2101859200 | bytes 18993664 | tf_op jit(solution)/shard_map/dot_general | solution.py:68
  69.5 1.8 %broadcast_multiply_fusion.1 = (f32[128,4008]{0,1:T(8,128)}, f32[128]{0:T(128)S(1)}) fusion(f32[128,4008]{0,1:T(8,128)S(1)} %get-tuple-element.34, f32[]{:T(128)} %bitcast.180, f32[128]{0:T(128)S(1)} %get-tuple-element.33), kind=kLoop, calls=%fused_computation.34 | loop fusion | flops 1538944 | bytes 4105220 | tf_op jit(solution)/shard_map/mul | solution.py:81
  72.1 1.2 slice-done
  74.9 9.9 %fusion = f32[256,4008]{0,1:T(8,128)} fusion(bf16[256,2048]{0,1:T(8,128)(2,1)S(1)} %bitcast.183, bf16[1,2048,4008]{1,2,0:T(8,128)(2,1)} %param.6), kind=kOutput, calls=%fused_computation | convolution fusion | flops 4202692608 | bytes 21569536 | tf_op jit(solution)/shard_map/dot_general | solution.py:68
  84.8 1.3 collective-permute-start.10
  86.2 2.1 %slice_reduce_fusion.1 = f32[128]{0:T(128)S(1)} fusion(f32[256,4008]{0,1:T(8,128)} %fusion), kind=kLoop, calls=%fused_computation.22 | loop fusion | flops 512896 | bytes 2052608 | tf_op jit(solution)/shard_map/reduce_max | solution.py:11
  88.3 59.8 %collective-permute-done.10 = f32[3,256]{1,0:T(4,128)S(1)} collective-permute-done((f32[3,256]{1,0:T(4,128)S(1)}, f32[3,256]{1,0:T(4,128)S(1)}, u32[]{:S(2)}, u32[]{:S(2)}) %collective-permute-start.10) | collective-permute-done | bytes 3104 | tf_op jit(solution)/shard_map/ppermute | solution.py:89
  148.1 3.5 %exponential_reduce_fusion.3 = (f32[128]{0:T(128)S(1)}, f32[128]{0:T(128)S(1)}, f32[128]{0:T(128)S(1)}, f32[128,4008]{0,1:T(8,128)S(1)}) fusion(f32[256,4008]{0,1:T(8,128)} %fusion, f32[128]{0:T(128)S(1)} %slice_reduce_fusion.1, f32[128,4008]{0,1:T(8,128)} %collective-permute-done.8, f32[]{:T(128)} %bitcast.175), kind=kLoop, calls=%fused_computation.16 | loop fusion | flops 3077760 | bytes 8210436 | tf_op jit(solution)/shard_map/reduce_sum | solution.py:12
  152.1 2.2 %fusion.43 = (f32[128]{0:T(128)S(1)}, f32[128,4008]{0,1:T(8,128)S(1)}, f32[128]{0:T(128)S(1)}) fusion(f32[128,4008]{0,1:T(8,128)} %collective-permute-done.9, f32[256,4008]{0,1:T(8,128)S(1)} %copy-done, f32[]{:T(128)} %bitcast.179, f32[128]{0:T(128)S(1)} %get-tuple-element.7), kind=kLoop, calls=%fused_computation.115 | loop fusion | flops 2564864 | bytes 6157828 | tf_op jit(solution)/shard_map/reduce_max | solution.py:11
  155.5 1.2 collective-permute-done.11
  156.7 1.1 collective-permute-start.12
  157.8 2.7 %collective-permute-done.12 = f32[2,3,256]{2,1,0:T(4,128)S(1)} collective-permute-done((f32[2,3,256]{2,1,0:T(4,128)S(1)}, f32[2,3,256]{2,1,0:T(4,128)S(1)}, u32[]{:S(2)}, u32[]{:S(2)}) %collective-permute-start.12) | collective-permute-done | bytes 6176 | tf_op jit(solution)/shard_map/ppermute | solution.py:26
  160.5 2.2 %collective-permute-start.13 = (f32[2,3,256]{2,1,0:T(4,128)S(1)}, f32[2,3,256]{2,1,0:T(4,128)S(1)}, u32[]{:S(2)}, u32[]{:S(2)}) collective-permute-start(f32[2,3,256]{2,1,0:T(4,128)S(1)} %pad_maximum_fusion.4), channel_id=1, source_target_pairs={{0,4},{1,5},{2,6},{3,7},{4,0},{5,1},{6,2},{7,3},{8,12},{9,13},{10,... | collective-permute-start | bytes 18440 | tf_op jit(solution)/shard_map/ppermute | solution.py:26
  162.7 1.6 collective-permute-done.13
  164.3 3.5 %collective-permute-start.14 = (f32[2,3,256]{2,1,0:T(4,128)S(1)}, f32[2,3,256]{2,1,0:T(4,128)S(1)}, u32[]{:S(2)}, u32[]{:S(2)}) collective-permute-start(f32[2,3,256]{2,1,0:T(4,128)S(1)} %pad_maximum_fusion.5), channel_id=1, source_target_pairs={{0,8},{1,9},{2,10},{3,11},{4,12},{5,13},{6,14},{7,15},{8,0},{9,1},... | collective-permute-start | bytes 18440 | tf_op jit(solution)/shard_map/ppermute | solution.py:26
  167.8 1.6 collective-permute-done.14
  169.6 2.3 %fusion.6 = f32[256,4008]{0,1:T(8,128)} fusion(f32[128,4008]{0,1:T(8,128)S(1)} %get-tuple-element.15, f32[128,4008]{0,1:T(8,128)S(1)} %get-tuple-element.18, f32[256]{0:T(256)S(1)} %sub.165, f32[256]{0:T(256)S(1)} %bitcast.187), kind=kLoop, calls=%fused_computation.7 | loop fusion | flops 3078144 | bytes 8210432 | tf_op jit(solution)/shard_map/sub | solution.py:111
  (65 shorter events, 7.5 us)
Async XLA Ops:
  7.2 64.9 %all-gather.4.cloned.1.call-start = ((), (), s32[]{:S(2)}) async-start(), calls=%async_computation | async-start | bytes 1148928 | tf_op jit(solution)/shard_map/all_gather | solution.py:87
  8.7 1.3 collective-permute-start.4
  9.1 3.8 %collective-permute-start = (bf16[1,129,128]{2,1,0:T(8,128)(2,1)S(1)}, bf16[1,129,128]{2,1,0:T(8,128)(2,1)S(1)}, u32[]{:S(2)}, u32[]{:S(2)}) collective-permute-start(bf16[1,129,128]{2,1,0:T(8,128)(2,1)S(1)} %get-tuple-element.29), channel_id=1, source_target_pairs={{0,1},{1,0},{2,3},{3,2},{4,5},{5,4},{6,7},{7,6},{8,9},{9,8},{10,11... | collective-permute-start | bytes 99080 | tf_op jit(solution)/shard_map/ppermute | solution.py:42
  10.0 5.4 %collective-permute-start.5 = (bf16[2,129,128]{2,1,0:T(8,128)(2,1)S(1)}, bf16[2,129,128]{2,1,0:T(8,128)(2,1)S(1)}, u32[]{:S(2)}, u32[]{:S(2)}) collective-permute-start(bf16[2,129,128]{2,1,0:T(8,128)(2,1)S(1)} %maximum_select_fusion.7), channel_id=1, source_target_pairs={{0,2},{1,3},{2,0},{3,1},{4,6},{5,7},{6,4},{7,5},{8,10},{9,11},{10,... | collective-permute-start | bytes 198152 | tf_op jit(solution)/shard_map/ppermute | solution.py:42
  12.9 4.8 %collective-permute-start.1 = (bf16[2,129,128]{2,1,0:T(8,128)(2,1)S(1)}, bf16[2,129,128]{2,1,0:T(8,128)(2,1)S(1)}, u32[]{:S(2)}, u32[]{:S(2)}) collective-permute-start(bf16[2,129,128]{2,1,0:T(8,128)(2,1)S(1)} %maximum_select_fusion.6), channel_id=1, source_target_pairs={{0,2},{1,3},{2,0},{3,1},{4,6},{5,7},{6,4},{7,5},{8,10},{9,11},{10,... | collective-permute-start | bytes 198152 | tf_op jit(solution)/shard_map/ppermute | solution.py:42
  15.5 6.7 %collective-permute-start.6 = (bf16[4,129,128]{2,1,0:T(8,128)(2,1)S(1)}, bf16[4,129,128]{2,1,0:T(8,128)(2,1)S(1)}, u32[]{:S(2)}, u32[]{:S(2)}) collective-permute-start(bf16[4,129,128]{2,1,0:T(8,128)(2,1)S(1)} %maximum_select_fusion.5), channel_id=1, source_target_pairs={{0,4},{1,5},{2,6},{3,7},{4,0},{5,1},{6,2},{7,3},{8,12},{9,13},{10,... | collective-permute-start | bytes 396296 | tf_op jit(solution)/shard_map/ppermute | solution.py:42
  17.7 10.3 %collective-permute-start.2 = (bf16[4,129,128]{2,1,0:T(8,128)(2,1)S(1)}, bf16[4,129,128]{2,1,0:T(8,128)(2,1)S(1)}, u32[]{:S(2)}, u32[]{:S(2)}) collective-permute-start(bf16[4,129,128]{2,1,0:T(8,128)(2,1)S(1)} %maximum_select_fusion.4), channel_id=1, source_target_pairs={{0,4},{1,5},{2,6},{3,7},{4,0},{5,1},{6,2},{7,3},{8,12},{9,13},{10,... | collective-permute-start | bytes 396296 | tf_op jit(solution)/shard_map/ppermute | solution.py:42
  22.3 22.4 %collective-permute-start.7 = (bf16[8,129,128]{2,1,0:T(8,128)(2,1)S(1)}, bf16[8,129,128]{2,1,0:T(8,128)(2,1)S(1)}, u32[]{:S(2)}, u32[]{:S(2)}) collective-permute-start(bf16[8,129,128]{2,1,0:T(8,128)(2,1)S(1)} %maximum_select_fusion.3), channel_id=1, source_target_pairs={{0,8},{1,9},{2,10},{3,11},{4,12},{5,13},{6,14},{7,15},{8,0},{9,1},... | collective-permute-start | bytes 792584 | tf_op jit(solution)/shard_map/ppermute | solution.py:42
  28.1 20.5 %collective-permute-start.3 = (bf16[8,129,128]{2,1,0:T(8,128)(2,1)S(1)}, bf16[8,129,128]{2,1,0:T(8,128)(2,1)S(1)}, u32[]{:S(2)}, u32[]{:S(2)}) collective-permute-start(bf16[8,129,128]{2,1,0:T(8,128)(2,1)S(1)} %maximum_select_fusion.2), channel_id=1, source_target_pairs={{0,8},{1,9},{2,10},{3,11},{4,12},{5,13},{6,14},{7,15},{8,0},{9,1},... | collective-permute-start | bytes 792584 | tf_op jit(solution)/shard_map/ppermute | solution.py:42
  60.1 91.6 %collective-permute-start.9 = (f32[128,4008]{0,1:T(8,128)}, f32[128,4008]{0,1:T(8,128)}, u32[]{:S(2)}, u32[]{:S(2)}) collective-permute-start(f32[128,4008]{0,1:T(8,128)} %get-tuple-element.22), channel_id=1, source_target_pairs={{0,16},{16,0},{1,17},{17,1},{2,18},{18,2},{3,19},{19,3},{4,20},{20... | collective-permute-start | bytes 6156296 | tf_op jit(solution)/shard_map/ppermute | solution.py:81
  71.3 76.8 %collective-permute-start.8 = (f32[128,4008]{0,1:T(8,128)}, f32[128,4008]{0,1:T(8,128)}, u32[]{:S(2)}, u32[]{:S(2)}) collective-permute-start(f32[128,4008]{0,1:T(8,128)} %get-tuple-element.19), channel_id=1, source_target_pairs={{0,16},{16,0},{1,17},{17,1},{2,18},{18,2},{3,19},{19,3},{4,20},{20... | collective-permute-start | bytes 6156296 | tf_op jit(solution)/shard_map/ppermute | solution.py:81
  72.1 1.2 slice-start
  73.3 1.2 copy-start.1
  84.8 63.3 %collective-permute-start.10 = (f32[3,256]{1,0:T(4,128)S(1)}, f32[3,256]{1,0:T(4,128)S(1)}, u32[]{:S(2)}, u32[]{:S(2)}) collective-permute-start(f32[3,256]{1,0:T(4,128)S(1)} %fusion.24), channel_id=1, source_target_pairs={{0,16},{16,0},{1,17},{17,1},{2,18},{18,2},{3,19},{19,3},{4,20},{20... | collective-permute-start | bytes 9224 | tf_op jit(solution)/shard_map/ppermute | solution.py:89
  148.1 4.0 %copy-start = (f32[256,4008]{0,1:T(8,128)S(1)}, f32[256,4008]{0,1:T(8,128)}, u32[]{:S(2)}) copy-start(f32[256,4008]{0,1:T(8,128)} %fusion) | copy-start | bytes 12312580
  155.5 1.2 collective-permute-start.11
  156.7 3.7 %collective-permute-start.12 = (f32[2,3,256]{2,1,0:T(4,128)S(1)}, f32[2,3,256]{2,1,0:T(4,128)S(1)}, u32[]{:S(2)}, u32[]{:S(2)}) collective-permute-start(f32[2,3,256]{2,1,0:T(4,128)S(1)} %pad_maximum_fusion.3), channel_id=1, source_target_pairs={{0,2},{1,3},{2,0},{3,1},{4,6},{5,7},{6,4},{7,5},{8,10},{9,11},{10,... | collective-permute-start | bytes 18440 | tf_op jit(solution)/shard_map/ppermute | solution.py:26
  160.5 3.8 %collective-permute-start.13 = (f32[2,3,256]{2,1,0:T(4,128)S(1)}, f32[2,3,256]{2,1,0:T(4,128)S(1)}, u32[]{:S(2)}, u32[]{:S(2)}) collective-permute-start(f32[2,3,256]{2,1,0:T(4,128)S(1)} %pad_maximum_fusion.4), channel_id=1, source_target_pairs={{0,4},{1,5},{2,6},{3,7},{4,0},{5,1},{6,2},{7,3},{8,12},{9,13},{10,... | collective-permute-start | bytes 18440 | tf_op jit(solution)/shard_map/ppermute | solution.py:26
  164.3 5.2 %collective-permute-start.14 = (f32[2,3,256]{2,1,0:T(4,128)S(1)}, f32[2,3,256]{2,1,0:T(4,128)S(1)}, u32[]{:S(2)}, u32[]{:S(2)}) collective-permute-start(f32[2,3,256]{2,1,0:T(4,128)S(1)} %pad_maximum_fusion.5), channel_id=1, source_target_pairs={{0,8},{1,9},{2,10},{3,11},{4,12},{5,13},{6,14},{7,15},{8,0},{9,1},... | collective-permute-start | bytes 18440 | tf_op jit(solution)/shard_map/ppermute | solution.py:26
  169.5 2.3 %copy-start.2 = (f32[256]{0:T(256)}, f32[256]{0:T(256)S(1)}, u32[]{:S(2)}) copy-start(f32[256]{0:T(256)S(1)} %sub.165) | copy-start | bytes 3076
Sparse Core Ops, SparseCore 0:
  27.5 40.3 all-gather.3

commit v6 on v3

--- a/solution.py
+++ b/solution.py
@@ -69,7 +69,8 @@
         note = jnp.concatenate([stats_rows, jnp.broadcast_to(w, (1, share))], axis=0)
         received.append(parts)
         notes.append((perm, note))
-    own_logits = logits_of(me * share, share)
+    own_logits = jnp.concatenate(
+        [logits_of(me * share + k * sub, sub) for k in range(send_pieces)], axis=0)
     notes, own_logits = lax.optimization_barrier(([note for _, note in notes], own_logits))
     notes = [lax.ppermute(note, "member", [(g, (g + shift) % members) for g in range(members)])
              for shift, note in zip(range(1, members), notes)]

time: 169 us -> 153 us (0.905)
  waiting for transfers between devices: 55.9 us -> 12.9 us
  blocking collectives: 43.8 us -> 83.1 us
  between operations: 14.9 us -> 1.56 us
  matrix products: 26.1 us -> 32.3 us
  other arithmetic: 18.9 us -> 15.4 us
  local copies, waits for them, and re-layouts: 4.9 us -> 2.21 us
    ppermute x1, waiting for transfers between devices: 42.9 us -> 1.55 us  [on_device(): lax.ppermute(note, 'member', [(g, (g + shift) % members) for g in range(m...]
    all_gather x2 -> x4, blocking collectives: 43.8 us -> 83.1 us  [logits_of(): gathered = lax.all_gather(packed, 'vocab', axis=0, tiled=False)]
    dot_general x3 -> x4, matrix products: 26.1 us -> 32.3 us  [logits_of(): return jnp.dot(normed, weights, preferred_element_type=jnp.float32)]
  transfers between devices with their start and end apart: 8 -> 7, of which waited for: 5 -> 5; matrix products, arithmetic and copies ran while one was open for 24% -> 21% of each run, Pallas kernels for 0% -> 0%
where the time goes in v6:
time: 153 us
  blocking collectives  83.1 us (54%)
  matrix products  32.3 us (21%)
  other arithmetic  15.4 us (10%)
  waiting for transfers between devices  12.9 us (8%)
  starting transfers between devices  5.57 us (4%)
  local copies, waits for them, and re-layouts  2.21 us (1%)
  between operations  1.56 us (1%)
    all_gather x4, blocking collectives, logits_of(): gathered = lax.all_gather(packed, 'vocab', axis=0, tiled=False)  83.1 us
    dot_general x4, matrix products, logits_of(): return jnp.dot(normed, weights, preferred_element_type=jnp.float32)  32.3 us
    ppermute x4, waiting for transfers between devices, reduce_stats(): other = lax.ppermute(stats, axis, perm)  11.3 us
    reduce_sum x4, other arithmetic, local_stats(): local_sum = jnp.sum(jnp.exp(values - local_peak[:, None]), axis=1)  5 us
  transfers between devices with their start and end apart: 7, of which 5 were waited for; matrix products, arithmetic and copies ran while one was open for 21% of the time, Pallas kernels for 0%

profile of v6, /device:TPU:0, one launch (start us, length us, event | category | flops | bytes accessed | tf_op | source)
XLA Modules:
  0.0 153.0 jit_solution(1305088769536814159)
XLA Ops:
  0.7 0.8 dynamic-slice_bitcast_fusion.1
  1.5 0.7 fusion.23
  2.2 24.7 %all-gather.5 = bf16[16,129,128]{2,1,0:T(8,128)(2,1)S(1)} all-gather(bf16[1,129,128]{2,1,0:T(8,128)(2,1)S(1)} %get-tuple-element.32), channel_id=3, replica_groups=mesh['member'=2,'vocab'=16] {'vocab'}, dimensions={0}, use_global_device_ids=true | all-gather | bytes 561408 | tf_op jit(solution)/shard_map/all_gather | solution.py:46
  28.2 0.3 fusion.14
  28.5 8.1 %fusion.52 = (f32[128]{0:T(128)S(1)}, f32[128,4008]{0,1:T(8,128)S(1)}) fusion(bf16[128,2048]{0,1:T(8,128)(2,1)S(1)} %bitcast.206, bf16[1,2048,4008]{1,2,0:T(8,128)(2,1)} %param.6), kind=kOutput, calls=%fused_computation.123 | convolution fusion | flops 2101859200 | bytes 18993664 | tf_op jit(solution)/shard_map/dot_general | solution.py:53
  36.6 1.8 %exponential_reduce_fusion.4 = (f32[128]{0:T(128)S(1)}, f32[128,4008]{0,1:T(8,128)}) fusion(f32[128,4008]{0,1:T(8,128)S(1)} %get-tuple-element.36, f32[128]{0:T(128)S(1)} %get-tuple-element.35, f32[]{:T(128)} %bitcast.201), kind=kLoop, calls=%fused_computation.17 | loop fusion | flops 1538944 | bytes 4105220 | tf_op jit(solution)/shard_map/reduce_sum | solution.py:12
  38.4 1.5 collective-permute-start.1
  39.9 18.8 %all-gather.4 = bf16[16,129,128]{2,1,0:T(8,128)(2,1)S(1)} all-gather(bf16[1,129,128]{2,1,0:T(8,128)(2,1)S(1)} %get-tuple-element.34), channel_id=2, replica_groups=mesh['member'=2,'vocab'=16] {'vocab'}, dimensions={0}, use_global_device_ids=true | all-gather | bytes 561408 | tf_op jit(solution)/shard_map/all_gather | solution.py:46
  59.3 0.3 fusion.11
  59.7 8.1 %fusion.53 = (f32[128]{0:T(128)S(1)}, f32[128,4008]{0,1:T(8,128)S(1)}) fusion(bf16[128,2048]{0,1:T(8,128)(2,1)S(1)} %bitcast.207, bf16[1,2048,4008]{1,2,0:T(8,128)(2,1)} %param.6), kind=kOutput, calls=%fused_computation.124 | convolution fusion | flops 2101859200 | bytes 18993664 | tf_op jit(solution)/shard_map/dot_general | solution.py:53
  67.8 1.8 %broadcast_multiply_fusion.1 = (f32[128,4008]{0,1:T(8,128)}, f32[128]{0:T(128)S(1)}) fusion(f32[128,4008]{0,1:T(8,128)S(1)} %get-tuple-element.38, f32[]{:T(128)} %bitcast.203, f32[128]{0:T(128)S(1)} %get-tuple-element.37), kind=kLoop, calls=%fused_computation.42 | loop fusion | flops 1538944 | bytes 4105220 | tf_op jit(solution)/shard_map/mul | solution.py:66
  69.5 0.5 collective-permute-start
  70.0 20.5 %all-gather.6 = bf16[16,129,128]{2,1,0:T(8,128)(2,1)S(1)} all-gather(bf16[1,129,128]{2,1,0:T(8,128)(2,1)S(1)} %get-tuple-element.31), channel_id=4, replica_groups=mesh['member'=2,'vocab'=16] {'vocab'}, dimensions={0}, use_global_device_ids=true | all-gather | bytes 561408 | tf_op jit(solution)/shard_map/all_gather | solution.py:46
  90.5 19.2 %all-gather.7 = bf16[16,129,128]{2,1,0:T(8,128)(2,1)S(1)} all-gather(bf16[1,129,128]{2,1,0:T(8,128)(2,1)S(1)} %get-tuple-element.33), channel_id=5, replica_groups=mesh['member'=2,'vocab'=16] {'vocab'}, dimensions={0}, use_global_device_ids=true | all-gather | bytes 561408 | tf_op jit(solution)/shard_map/all_gather | solution.py:46
  110.4 0.3 copy.36
  111.0 0.3 fusion.20
  111.3 8.1 %fusion = f32[128,4008]{0,1:T(8,128)S(1)} fusion(bf16[128,2048]{0,1:T(8,128)(2,1)S(1)} %bitcast.204, bf16[1,2048,4008]{1,2,0:T(8,128)(2,1)} %param.6), kind=kOutput, calls=%fused_computation | convolution fusion | flops 2101346304 | bytes 18993152 | tf_op jit(solution)/shard_map/dot_general | solution.py:53
  119.4 0.3 fusion.17
  119.7 8.1 %fusion.2 = f32[128,4008]{0,1:T(8,128)S(1)} fusion(bf16[128,2048]{0,1:T(8,128)(2,1)S(1)} %bitcast.205, bf16[1,2048,4008]{1,2,0:T(8,128)(2,1)} %param.6), kind=kOutput, calls=%fused_computation.2 | convolution fusion | flops 2101346304 | bytes 18993152 | tf_op jit(solution)/shard_map/dot_general | solution.py:53
  128.1 1.6 %collective-permute-start.2 = (f32[3,256]{1,0:T(4,128)S(1)}, f32[3,256]{1,0:T(4,128)S(1)}, u32[]{:S(2)}, u32[]{:S(2)}) collective-permute-start(f32[3,256]{1,0:T(4,128)S(1)} %fusion.29), channel_id=1, source_target_pairs={{0,16},{16,0},{1,17},{17,1},{2,18},{18,2},{3,19},{19,3},{4,20},{20... | collective-permute-start | bytes 9224 | tf_op jit(solution)/shard_map/ppermute | solution.py:75
  129.7 0.5 slice_reduce_fusion.1
  130.2 1.6 %collective-permute-done.2 = f32[3,256]{1,0:T(4,128)S(1)} collective-permute-done((f32[3,256]{1,0:T(4,128)S(1)}, f32[3,256]{1,0:T(4,128)S(1)}, u32[]{:S(2)}, u32[]{:S(2)}) %collective-permute-start.2) | collective-permute-done | bytes 3104 | tf_op jit(solution)/shard_map/ppermute | solution.py:75
  131.8 2.1 %exponential_reduce_fusion.3 = (f32[128]{0:T(128)S(1)}, f32[128]{0:T(128)S(1)}, f32[128]{0:T(128)S(1)}, f32[128,4008]{0,1:T(8,128)S(1)}) fusion(f32[256,4008]{0,1:T(8,128)S(1)} %pad_maximum_fusion, f32[128]{0:T(128)S(1)} %slice_reduce_fusion.1, f32[128,4008]{0,1:T(8,128)} %collective-permute-done, f32[]{:T(128)} %bitcast.198), kind=kLoop, calls=%fused_computation.14 | loop fusion | flops 3077760 | bytes 8210436 | tf_op jit(solution)/shard_map/reduce_sum | solution.py:12
  134.0 2.2 %fusion.51 = (f32[128]{0:T(128)S(1)}, f32[128,4008]{0,1:T(8,128)S(1)}, f32[128]{0:T(128)S(1)}) fusion(f32[128,4008]{0,1:T(8,128)} %collective-permute-done.1, f32[256,4008]{0,1:T(8,128)S(1)} %pad_maximum_fusion, f32[]{:T(128)} %bitcast.202, f32[128]{0:T(128)S(1)} %get-tuple-element.7), kind=kLoop, calls=%fused_computation.122 | loop fusion | flops 2564864 | bytes 6157828 | tf_op jit(solution)/shard_map/reduce_max | solution.py:11
  136.1 0.6 exponential_reduce_fusion
  136.7 0.6 exponential_reduce_fusion.2
  137.4 1.2 collective-permute-done.3
  138.6 1.7 %collective-permute-start.4 = (f32[2,3,256]{2,1,0:T(4,128)S(1)}, f32[2,3,256]{2,1,0:T(4,128)S(1)}, u32[]{:S(2)}, u32[]{:S(2)}) collective-permute-start(f32[2,3,256]{2,1,0:T(4,128)S(1)} %pad_maximum_fusion.6), channel_id=1, source_target_pairs={{0,2},{1,3},{2,0},{3,1},{4,6},{5,7},{6,4},{7,5},{8,10},{9,11},{10,... | collective-permute-start | bytes 18440 | tf_op jit(solution)/shard_map/ppermute | solution.py:26
  140.3 2.0 %collective-permute-done.4 = f32[2,3,256]{2,1,0:T(4,128)S(1)} collective-permute-done((f32[2,3,256]{2,1,0:T(4,128)S(1)}, f32[2,3,256]{2,1,0:T(4,128)S(1)}, u32[]{:S(2)}, u32[]{:S(2)}) %collective-permute-start.4) | collective-permute-done | bytes 6176 | tf_op jit(solution)/shard_map/ppermute | solution.py:26
  142.4 3.6 %collective-permute-done.5 = f32[2,3,256]{2,1,0:T(4,128)S(1)} collective-permute-done((f32[2,3,256]{2,1,0:T(4,128)S(1)}, f32[2,3,256]{2,1,0:T(4,128)S(1)}, u32[]{:S(2)}, u32[]{:S(2)}) %collective-permute-start.5) | collective-permute-done | bytes 6176 | tf_op jit(solution)/shard_map/ppermute | solution.py:26
  146.1 4.5 %collective-permute-done.6 = f32[2,3,256]{2,1,0:T(4,128)S(1)} collective-permute-done((f32[2,3,256]{2,1,0:T(4,128)S(1)}, f32[2,3,256]{2,1,0:T(4,128)S(1)}, u32[]{:S(2)}, u32[]{:S(2)}) %collective-permute-start.6) | collective-permute-done | bytes 6176 | tf_op jit(solution)/shard_map/ppermute | solution.py:26
  150.7 2.3 %fusion.8 = f32[256,4008]{0,1:T(8,128)} fusion(f32[128,4008]{0,1:T(8,128)S(1)} %get-tuple-element.15, f32[128,4008]{0,1:T(8,128)S(1)} %get-tuple-element.18, f32[256]{0:T(256)S(1)} %sub.147, f32[256]{0:T(256)S(1)} %bitcast.209), kind=kLoop, calls=%fused_computation.10 | loop fusion | flops 3078144 | bytes 8210432 | tf_op jit(solution)/shard_map/sub | solution.py:97
  (48 shorter events, 2.9 us)
Async XLA Ops:
  38.4 95.6 %collective-permute-start.1 = (f32[128,4008]{0,1:T(8,128)}, f32[128,4008]{0,1:T(8,128)}, u32[]{:S(2)}, u32[]{:S(2)}) collective-permute-start(f32[128,4008]{0,1:T(8,128)} %get-tuple-element.22), channel_id=1, source_target_pairs={{0,16},{16,0},{1,17},{17,1},{2,18},{18,2},{3,19},{19,3},{4,20},{20... | collective-permute-start | bytes 6156296 | tf_op jit(solution)/shard_map/ppermute | solution.py:66
  69.5 62.3 %collective-permute-start = (f32[128,4008]{0,1:T(8,128)}, f32[128,4008]{0,1:T(8,128)}, u32[]{:S(2)}, u32[]{:S(2)}) collective-permute-start(f32[128,4008]{0,1:T(8,128)} %get-tuple-element.19), channel_id=1, source_target_pairs={{0,16},{16,0},{1,17},{17,1},{2,18},{18,2},{3,19},{19,3},{4,20},{20... | collective-permute-start | bytes 6156296 | tf_op jit(solution)/shard_map/ppermute | solution.py:66
  128.1 3.7 %collective-permute-start.2 = (f32[3,256]{1,0:T(4,128)S(1)}, f32[3,256]{1,0:T(4,128)S(1)}, u32[]{:S(2)}, u32[]{:S(2)}) collective-permute-start(f32[3,256]{1,0:T(4,128)S(1)} %fusion.29), channel_id=1, source_target_pairs={{0,16},{16,0},{1,17},{17,1},{2,18},{18,2},{3,19},{19,3},{4,20},{20... | collective-permute-start | bytes 9224 | tf_op jit(solution)/shard_map/ppermute | solution.py:75
  137.3 1.2 collective-permute-start.3
  138.6 3.7 %collective-permute-start.4 = (f32[2,3,256]{2,1,0:T(4,128)S(1)}, f32[2,3,256]{2,1,0:T(4,128)S(1)}, u32[]{:S(2)}, u32[]{:S(2)}) collective-permute-start(f32[2,3,256]{2,1,0:T(4,128)S(1)} %pad_maximum_fusion.6), channel_id=1, source_target_pairs={{0,2},{1,3},{2,0},{3,1},{4,6},{5,7},{6,4},{7,5},{8,10},{9,11},{10,... | collective-permute-start | bytes 18440 | tf_op jit(solution)/shard_map/ppermute | solution.py:26
  142.3 3.7 %collective-permute-start.5 = (f32[2,3,256]{2,1,0:T(4,128)S(1)}, f32[2,3,256]{2,1,0:T(4,128)S(1)}, u32[]{:S(2)}, u32[]{:S(2)}) collective-permute-start(f32[2,3,256]{2,1,0:T(4,128)S(1)} %pad_maximum_fusion.7), channel_id=1, source_target_pairs={{0,4},{1,5},{2,6},{3,7},{4,0},{5,1},{6,2},{7,3},{8,12},{9,13},{10,... | collective-permute-start | bytes 18440 | tf_op jit(solution)/shard_map/ppermute | solution.py:26
  146.0 4.6 %collective-permute-start.6 = (f32[2,3,256]{2,1,0:T(4,128)S(1)}, f32[2,3,256]{2,1,0:T(4,128)S(1)}, u32[]{:S(2)}, u32[]{:S(2)}) collective-permute-start(f32[2,3,256]{2,1,0:T(4,128)S(1)} %pad_maximum_fusion.8), channel_id=1, source_target_pairs={{0,8},{1,9},{2,10},{3,11},{4,12},{5,13},{6,14},{7,15},{8,0},{9,1},... | collective-permute-start | bytes 18440 | tf_op jit(solution)/shard_map/ppermute | solution.py:26
  150.7 2.3 %copy-start = (f32[256]{0:T(256)}, f32[256]{0:T(256)S(1)}, u32[]{:S(2)}) copy-start(f32[256]{0:T(256)S(1)} %sub.147) | copy-start | bytes 3076

commit v7 on v3

v7 whole, which is shorter than its diff:
```python
import jax
import jax.numpy as jnp
from jax import lax
from jax.sharding import PartitionSpec as P

epsilon = 1e-05
send_pieces = 2
gather_rows = 255


def local_stats(values):
    local_peak = jnp.max(values, axis=1)
    local_sum = jnp.sum(jnp.exp(values - local_peak[:, None]), axis=1)
    return jnp.stack([local_peak, local_sum])


def reduce_stats(stats, axis):
    size = lax.axis_size(axis)
    if size & (size - 1):
        gathered = lax.all_gather(stats, axis, axis=0, tiled=False)
        peak = jnp.max(gathered[:, 0], axis=0)
        summed = jnp.sum(gathered[:, 1] * jnp.exp(gathered[:, 0] - peak[None]), axis=0)
        return peak, summed
    distance = 1
    while distance < size:
        perm = [(a, a ^ distance) for a in range(size)]
        other = lax.ppermute(stats, axis, perm)
        peak = jnp.maximum(stats[0], other[0])
        summed = stats[1] * jnp.exp(stats[0] - peak) + other[1] * jnp.exp(other[0] - peak)
        stats = jnp.stack([peak, summed])
        distance *= 2
    return stats[0], stats[1]


def on_device(hidden, norm_gain, head, pool_weight):
    members = lax.axis_size("member")
    shards = lax.axis_size("vocab")
    me = lax.axis_index("member")
    states = hidden[0]
    row_count, width = states.shape
    share = row_count // members
    weights = head[0]
    width_all = width * shards
    w = pool_weight[0]
    sub = share // send_pieces

    blocks = []
    for shift in range(1, members):
        target = (me + shift) % members
        for k in range(send_pieces):
            blocks.append(lax.dynamic_slice_in_dim(states, target * share + k * sub, sub, 0))
    blocks.append(lax.dynamic_slice_in_dim(states, me * share, share, 0))
    ordered = jnp.concatenate(blocks, axis=0)

    bounds = [0, sub]
    while bounds[-1] < row_count:
        bounds.append(min(bounds[-1] + gather_rows, row_count))
    gain = None

    def normalize(lo, hi, source):
        nonlocal gain
        packed = source[lo:hi]
        if gain is None:
            packed = jnp.concatenate([packed, norm_gain], axis=0)
        gathered = lax.all_gather(packed, "vocab", axis=0, tiled=False)
        if gain is None:
            gain = gathered[:, hi - lo, :].astype(jnp.float32)
        full_states = gathered[:, :hi - lo, :].astype(jnp.float32)
        mean_square = jnp.sum(full_states * full_states, axis=(0, 2)) / width_all
        scaling = lax.rsqrt(mean_square + epsilon)
        piece = (full_states * scaling[None, :, None] * gain[:, None, :]).astype(jnp.bfloat16)
        return jnp.transpose(piece, (1, 0, 2)).reshape(hi - lo, width_all)

    first_normed = normalize(bounds[0], bounds[1], ordered)
    first_logits = jnp.dot(first_normed, weights, preferred_element_type=jnp.float32)
    first_sent = w * first_logits
    first_sent, ordered = lax.optimization_barrier((first_sent, ordered))
    normed = jnp.concatenate(
        [first_normed] + [normalize(lo, hi, ordered) for lo, hi in zip(bounds[1:-1], bounds[2:])], axis=0)

    def logits_of(lo, rows):
        return jnp.dot(normed[lo:lo + rows], weights, preferred_element_type=jnp.float32)

    received = []
    sent = []
    for shift in range(1, members):
        perm = [(g, (g + shift) % members) for g in range(members)]
        parts = []
        for k in range(send_pieces):
            if shift == 1 and k == 0:
                logits, outgoing = first_logits, first_sent
            else:
                logits = logits_of(((shift - 1) * send_pieces + k) * sub, sub)
                outgoing = w * logits
            parts.append(lax.ppermute(outgoing, "member", perm))
            sent.append(logits)
        received.append(parts)
    own_logits = logits_of(row_count - share, share)

    sent, own_logits = lax.optimization_barrier((sent, own_logits))
    notes = []
    for shift in range(1, members):
        piece_stats = [local_stats(x) for x in sent[(shift - 1) * send_pieces:shift * send_pieces]]
        note = jnp.concatenate(
            [jnp.concatenate(piece_stats, axis=1), jnp.broadcast_to(w, (1, share))], axis=0)
        perm = [(g, (g + shift) % members) for g in range(members)]
        notes.append(lax.ppermute(note, "member", perm))

    def piece_terms(k):
        own = own_logits[k * sub:(k + 1) * sub]
        total = w * own
        for parts in received:
            total = total + parts[k]
        return total, jnp.concatenate([local_stats(own), local_stats(total)], axis=1)

    def flat_lse(stats):
        peak, summed = reduce_stats(stats[:, None, :], "vocab")
        return (peak + jnp.log(summed))[0]

    early = [piece_terms(k) for k in range(send_pieces - 1)]
    early_lse = flat_lse(jnp.concatenate([stats for _, stats in early], axis=1))
    last_parts = [parts[-1] for parts in received]
    last_parts, early_lse = lax.optimization_barrier((last_parts, early_lse))
    for parts, part in zip(received, last_parts):
        parts[-1] = part
    last_total, last_stats = piece_terms(send_pieces - 1)
    tail = jnp.concatenate([last_stats] + [note[:2] for note in notes], axis=1)
    tail_lse = flat_lse(tail)

    own_lse = []
    pooled_lse = []
    for k in range(send_pieces - 1):
        own_lse.append(early_lse[2 * k * sub:(2 * k + 1) * sub])
        pooled_lse.append(early_lse[(2 * k + 1) * sub:(2 * k + 2) * sub])
    own_lse.append(tail_lse[:sub])
    pooled_lse.append(tail_lse[sub:2 * sub])
    offset = w * jnp.concatenate(own_lse)
    for index, note in enumerate(notes):
        lo = 2 * sub + index * share
        offset = offset + note[2] * tail_lse[lo:lo + share]

    agreement = jnp.concatenate(pooled_lse) - offset
    pooled_raw = jnp.concatenate([total for total, _ in early] + [last_total], axis=0)
    pooled = pooled_raw - offset[:, None]
    return (pooled - agreement[:, None], agreement)


def solution(mesh):
    in_specs = (
        P("member", None, "vocab"),
        P("member", "vocab"),
        P("member", None, "vocab"),
        P("member"),
    )
    out_specs = (P("member", "vocab"), P("member"))
    return jax.shard_map(
        on_device, mesh=mesh, in_specs=in_specs, out_specs=out_specs, check_vma=False
    )
```

time: 169 us -> 159 us (0.941)
  waiting for transfers between devices: 55.9 us -> 22.8 us
  blocking collectives: 43.8 us -> 67.4 us
  between operations: 14.9 us -> 1.54 us
  matrix products: 26.1 us -> 34.4 us
  local copies, waits for them, and re-layouts: 4.9 us -> 7.06 us
  other arithmetic: 18.9 us -> 20.7 us
    ppermute x3, waiting for transfers between devices: 42.9 us -> 0.02 us  [the longest x1 0.01 us: on_device(): notes.append(lax.ppermute(note, 'member', perm))]
    all_gather x2 -> x3, blocking collectives: 43.8 us -> 67.4 us  [normalize(): gathered = lax.all_gather(packed, 'vocab', axis=0, tiled=False)]
    ppermute x4 -> x8, waiting for transfers between devices: 13 us -> 22.8 us  [reduce_stats(): other = lax.ppermute(stats, axis, perm)]
    dot_general x3, matrix products: 26.1 us -> 34.4 us  [the longest x2 24.9 us: logits_of(): jnp.dot(normed[lo:lo + rows], weights, preferred_element_type=jnp.float32)]
    reduce_max x2 -> x5, other arithmetic: 4.33 us -> 9.09 us  [local_stats(): local_peak = jnp.max(values, axis=1)]
    reshape x0 -> x1, local copies, waits for them, and re-layouts: none -> 2.18 us  [normalize(): return jnp.transpose(piece, (1, 0, 2)).reshape(hi - lo, width_all)]
    reduce_sum x4, other arithmetic: 6.41 us -> 4.56 us  [local_stats(): local_sum = jnp.sum(jnp.exp(values - local_peak[:, None]), axis=1)]
    mul x4 -> x2, other arithmetic: 1.8 us -> 0.01 us  [the longest x1 0.01 us: on_device(): offset = offset + note[2] * tail_lse[lo:lo + share]]
  transfers between devices with their start and end apart: 8 -> 11, of which waited for: 5 -> 8; matrix products, arithmetic and copies ran while one was open for 24% -> 28% of each run, Pallas kernels for 0% -> 0%
where the time goes in v7:
time: 159 us
  blocking collectives  67.4 us (42%)
  matrix products  34.4 us (22%)
  waiting for transfers between devices  22.8 us (14%)
  other arithmetic  20.7 us (13%)
  local copies, waits for them, and re-layouts  7.06 us (4%)
  starting transfers between devices  4.81 us (3%)
    all_gather x3, blocking collectives, normalize(): gathered = lax.all_gather(packed, 'vocab', axis=0, tiled=False)  67.4 us
    dot_general x2, matrix products, logits_of(): jnp.dot(normed[lo:lo + rows], weights, preferred_element_type=jnp.float32)  24.9 us
    ppermute x8, waiting for transfers between devices, reduce_stats(): other = lax.ppermute(stats, axis, perm)  22.8 us
    dot_general x1, matrix products, on_device(): jnp.dot(first_normed, weights, preferred_element_type=jnp.float32)  9.54 us
    reduce_max x5, other arithmetic, local_stats(): local_peak = jnp.max(values, axis=1)  9.09 us
    reduce_sum x4, other arithmetic, local_stats(): local_sum = jnp.sum(jnp.exp(values - local_peak[:, None]), axis=1)  4.56 us
  transfers between devices with their start and end apart: 11, of which 8 were waited for; matrix products, arithmetic and copies ran while one was open for 28% of the time, Pallas kernels for 0%

profile of v7, /device:TPU:0, one launch (start us, length us, event | category | flops | bytes accessed | tf_op | source)
XLA Modules:
  0.0 158.7 jit_solution(172158791161958452)
XLA Ops:
  0.7 0.8 dynamic-slice_bitcast_fusion.1
  1.4 0.7 maximum_bitcast_fusion
  2.1 24.7 %all-gather.3 = bf16[16,129,128]{2,1,0:T(8,128)(2,1)S(1)} all-gather(bf16[1,129,128]{2,1,0:T(8,128)(2,1)S(1)} %maximum_bitcast_fusion), channel_id=2, replica_groups=mesh['member'=2,'vocab'=16] {'vocab'}, dimensions={0}, use_global_device_ids=true | all-gather | bytes 561408 | tf_op jit(solution)/shard_map/all_gather | solution.py:65
  27.5 0.9 dynamic-slice_bitcast_fusion
  29.3 9.5 %broadcast_multiply_fusion.1 = (f32[128,4008]{0,1:T(8,128)}, f32[128,4008]{0,1:T(8,128)S(1)}) fusion(f32[]{:T(128)} %bitcast.190, bf16[128,2048]{0,1:T(8,128)(2,1)S(1)} %bitcast.197, bf16[1,2048,4008]{1,2,0:T(8,128)(2,1)} %param.6), kind=kOutput, calls=%fused_computation.36 | convolution fusion | flops 2101859328 | bytes 21045252 | tf_op jit(solution)/shard_map/dot_general | solution.py:75
  38.8 1.5 collective-permute-start
  40.4 21.9 %all-gather.4 = bf16[16,255,128]{2,1,0:T(8,128)(2,1)} all-gather(bf16[1,255,128]{2,1,0:T(8,128)(2,1)S(1)} %slice_bitcast_fusion), channel_id=3, replica_groups=mesh['member'=2,'vocab'=16] {'vocab'}, dimensions={0}, use_global_device_ids=true | all-gather | bytes 1109760 | tf_op jit(solution)/shard_map/all_gather | solution.py:65
  62.3 1.5 copy.26
  64.4 0.9 slice.163
  65.3 12.2 %broadcast_multiply_fusion = (f32[128,4008]{0,1:T(8,128)}, f32[128,4008]{0,1:T(8,128)}) fusion(f32[]{:T(128)} %bitcast.193, bf16[128,2048]{0,1:T(8,128)(2,1)} %bitcast.196, bf16[1,2048,4008]{1,2,0:T(8,128)(2,1)} %param.6), kind=kOutput, calls=%fused_computation.35 | convolution fusion | flops 2101859328 | bytes 21045252 | tf_op jit(solution)/shard_map/dot_general | solution.py:82
  78.0 20.9 %all-gather.5 = bf16[16,129,128]{2,1,0:T(8,128)(2,1)S(1)} all-gather(bf16[1,129,128]{2,1,0:T(8,128)(2,1)S(1)} %slice_bitcast_fusion.1), channel_id=4, replica_groups=mesh['member'=2,'vocab'=16] {'vocab'}, dimensions={0}, use_global_device_ids=true | all-gather | bytes 561408 | tf_op jit(solution)/shard_map/all_gather | solution.py:65
  99.1 1.0 fusion.17
  100.1 2.2 %copy.29 = bf16[129,16,128]{0,2,1:T(8,128)(2,1)} copy(bf16[129,16,128]{2,0,1:T(8,128)(2,1)} %fusion.17) | data formatting | bytes 1056768 | tf_op jit(solution)/shard_map/reshape | solution.py:72
  102.3 1.3 fusion.8
  103.6 12.7 %fusion = f32[256,4008]{0,1:T(8,128)} fusion(bf16[1,2048,4008]{1,2,0:T(8,128)(2,1)} %param.6, bf16[129,2048]{0,1:T(8,128)(2,1)} %bitcast.198, bf16[255,2048]{0,1:T(8,128)(2,1)} %bitcast.199), kind=kOutput, calls=%fused_computation | convolution fusion | flops 4204789760 | bytes 22093824 | tf_op jit(solution)/shard_map/dot_general | solution.py:82
  116.8 2.1 %reduce_max.59 = f32[128]{0:T(128)S(1)} reduce(f32[128,4008]{0,1:T(8,128)} %get-tuple-element.15, f32[]{:T(128)} %constant.46.clone.1), dimensions={1}, to_apply=%region_13.14 | reduce | flops 512896 | bytes 2052612 | tf_op jit(solution)/shard_map/reduce_max | solution.py:12
  118.9 2.1 %slice_reduce_fusion = f32[128]{0:T(128)S(1)} fusion(f32[256,4008]{0,1:T(8,128)} %fusion), kind=kLoop, calls=%fused_computation.21 | loop fusion | flops 512896 | bytes 2052608 | tf_op jit(solution)/shard_map/reduce_max | solution.py:12
  121.1 2.9 %exponential_reduce_fusion.3 = (f32[128]{0:T(128)S(1)}, f32[128]{0:T(128)S(1)}) fusion(f32[256,4008]{0,1:T(8,128)} %fusion, f32[128]{0:T(128)S(1)} %slice_reduce_fusion), kind=kLoop, calls=%fused_computation.16 | loop fusion | flops 1538816 | bytes 4105728 | tf_op jit(solution)/shard_map/reduce_sum | solution.py:13
  124.4 2.2 %fusion.56 = (f32[128]{0:T(128)S(1)}, f32[128,4008]{0,1:T(8,128)S(1)}, f32[128]{0:T(128)S(1)}) fusion(f32[128,4008]{0,1:T(8,128)} %collective-permute-done, f32[256,4008]{0,1:T(8,128)S(1)} %copy-done, f32[]{:T(128)} %bitcast.195, f32[128]{0:T(128)S(1)} %get-tuple-element.17), kind=kLoop, calls=%fused_computation.120 | loop fusion | flops 2564864 | bytes 6157828 | tf_op jit(solution)/shard_map/reduce_max | solution.py:12
  127.6 0.8 collective-permute-done.2
  128.6 0.6 exponential_reduce_fusion
  129.1 3.0 %collective-permute-done.3 = f32[2,1,256]{2,1,0:T(1,128)S(1)} collective-permute-done((f32[2,1,256]{2,1,0:T(1,128)S(1)}, f32[2,1,256]{2,1,0:T(1,128)S(1)}, u32[]{:S(2)}, u32[]{:S(2)}) %collective-permute-start.3) | collective-permute-done | bytes 2080 | tf_op jit(solution)/shard_map/ppermute | solution.py:27
  132.2 1.7 %collective-permute-start.6 = (f32[3,256]{1,0:T(4,128)S(1)}, f32[3,256]{1,0:T(4,128)S(1)}, u32[]{:S(2)}, u32[]{:S(2)}) collective-permute-start(f32[3,256]{1,0:T(4,128)S(1)} %fusion.18), channel_id=1, source_target_pairs={{0,16},{16,0},{1,17},{17,1},{2,18},{18,2},{3,19},{19,3},{4,20},{20... | collective-permute-start | bytes 9224 | tf_op jit(solution)/shard_map/ppermute | solution.py:107
  133.9 1.9 %collective-permute-done.4 = f32[2,1,256]{2,1,0:T(1,128)S(1)} collective-permute-done((f32[2,1,256]{2,1,0:T(1,128)S(1)}, f32[2,1,256]{2,1,0:T(1,128)S(1)}, u32[]{:S(2)}, u32[]{:S(2)}) %collective-permute-start.4) | collective-permute-done | bytes 2080 | tf_op jit(solution)/shard_map/ppermute | solution.py:27
  135.9 4.4 %collective-permute-done.5 = f32[2,1,256]{2,1,0:T(1,128)S(1)} collective-permute-done((f32[2,1,256]{2,1,0:T(1,128)S(1)}, f32[2,1,256]{2,1,0:T(1,128)S(1)}, u32[]{:S(2)}, u32[]{:S(2)}) %collective-permute-start.5) | collective-permute-done | bytes 2080 | tf_op jit(solution)/shard_map/ppermute | solution.py:27
  140.4 2.1 %fusion.53 = (f32[128]{0:T(128)S(1)}, f32[128,4008]{0,1:T(8,128)S(1)}) fusion(f32[128,4008]{0,1:T(8,128)} %collective-permute-done.1, f32[256,4008]{0,1:T(8,128)S(1)} %copy-done, f32[]{:T(128)} %bitcast.194), kind=kLoop, calls=%fused_computation.119 | loop fusion | flops 1538944 | bytes 6156804 | tf_op jit(solution)/shard_map/reduce_max | solution.py:12
  142.5 0.6 exponential_reduce_fusion.2
  143.2 1.1 collective-permute-done.7
  144.5 3.5 %collective-permute-done.8 = f32[2,1,512]{2,1,0:T(1,128)S(1)} collective-permute-done((f32[2,1,512]{2,1,0:T(1,128)S(1)}, f32[2,1,512]{2,1,0:T(1,128)S(1)}, u32[]{:S(2)}, u32[]{:S(2)}) %collective-permute-start.8) | collective-permute-done | bytes 4128 | tf_op jit(solution)/shard_map/ppermute | solution.py:27
  148.2 3.5 %collective-permute-done.9 = f32[2,1,512]{2,1,0:T(1,128)S(1)} collective-permute-done((f32[2,1,512]{2,1,0:T(1,128)S(1)}, f32[2,1,512]{2,1,0:T(1,128)S(1)}, u32[]{:S(2)}, u32[]{:S(2)}) %collective-permute-start.9) | collective-permute-done | bytes 4128 | tf_op jit(solution)/shard_map/ppermute | solution.py:27
  151.9 4.5 %collective-permute-done.10 = f32[2,1,512]{2,1,0:T(1,128)S(1)} collective-permute-done((f32[2,1,512]{2,1,0:T(1,128)S(1)}, f32[2,1,512]{2,1,0:T(1,128)S(1)}, u32[]{:S(2)}, u32[]{:S(2)}) %collective-permute-start.10) | collective-permute-done | bytes 4128 | tf_op jit(solution)/shard_map/ppermute | solution.py:27
  156.4 2.3 %fusion.6 = f32[256,4008]{0,1:T(8,128)} fusion(f32[128,4008]{0,1:T(8,128)S(1)} %get-tuple-element.25, f32[128,4008]{0,1:T(8,128)S(1)} %get-tuple-element.31, f32[256]{0:T(256)S(1)} %get-tuple-element.18, f32[256]{0:T(256)S(1)} %get-tuple-element.19), kind=kLoop, calls=%fused_computation.7 | loop fusion | flops 3078144 | bytes 8210432 | tf_op jit(solution)/shard_map/sub | solution.py:145
  (59 shorter events, 5.4 us)
Async XLA Ops:
  38.8 85.1 %collective-permute-start = (f32[128,4008]{0,1:T(8,128)}, f32[128,4008]{0,1:T(8,128)}, u32[]{:S(2)}, u32[]{:S(2)}) collective-permute-start(f32[128,4008]{0,1:T(8,128)} %get-tuple-element.11), channel_id=1, source_target_pairs={{0,16},{16,0},{1,17},{17,1},{2,18},{18,2},{3,19},{19,3},{4,20},{20... | collective-permute-start | bytes 6156296 | tf_op jit(solution)/shard_map/ppermute | solution.py:95
  77.5 62.9 %collective-permute-start.1 = (f32[128,4008]{0,1:T(8,128)}, f32[128,4008]{0,1:T(8,128)}, u32[]{:S(2)}, u32[]{:S(2)}) collective-permute-start(f32[128,4008]{0,1:T(8,128)} %get-tuple-element.45), channel_id=1, source_target_pairs={{0,16},{16,0},{1,17},{17,1},{2,18},{18,2},{3,19},{19,3},{4,20},{20... | collective-permute-start | bytes 6156296 | tf_op jit(solution)/shard_map/ppermute | solution.py:95
  121.1 3.4 %copy-start = (f32[256,4008]{0,1:T(8,128)S(1)}, f32[256,4008]{0,1:T(8,128)}, u32[]{:S(2)}) copy-start(f32[256,4008]{0,1:T(8,128)} %fusion) | copy-start | bytes 12312580
  126.6 2.0 %copy-start.1 = (f32[128,4008]{0,1:T(8,128)S(1)}, f32[128,4008]{0,1:T(8,128)}, u32[]{:S(2)}) copy-start(f32[128,4008]{0,1:T(8,128)} %get-tuple-element.15) | copy-start | bytes 6156292
  127.2 1.2 collective-permute-start.2
  128.5 3.7 %collective-permute-start.3 = (f32[2,1,256]{2,1,0:T(1,128)S(1)}, f32[2,1,256]{2,1,0:T(1,128)S(1)}, u32[]{:S(2)}, u32[]{:S(2)}) collective-permute-start(f32[2,1,256]{2,1,0:T(1,128)S(1)} %pad_maximum_fusion.7), channel_id=1, source_target_pairs={{0,2},{1,3},{2,0},{3,1},{4,6},{5,7},{6,4},{7,5},{8,10},{9,11},{10,... | collective-permute-start | bytes 6152 | tf_op jit(solution)/shard_map/ppermute | solution.py:27
  132.1 3.7 %collective-permute-start.4 = (f32[2,1,256]{2,1,0:T(1,128)S(1)}, f32[2,1,256]{2,1,0:T(1,128)S(1)}, u32[]{:S(2)}, u32[]{:S(2)}) collective-permute-start(f32[2,1,256]{2,1,0:T(1,128)S(1)} %pad_maximum_fusion.8), channel_id=1, source_target_pairs={{0,4},{1,5},{2,6},{3,7},{4,0},{5,1},{6,2},{7,3},{8,12},{9,13},{10,... | collective-permute-start | bytes 6152 | tf_op jit(solution)/shard_map/ppermute | solution.py:27
  132.2 3.7 %collective-permute-start.6 = (f32[3,256]{1,0:T(4,128)S(1)}, f32[3,256]{1,0:T(4,128)S(1)}, u32[]{:S(2)}, u32[]{:S(2)}) collective-permute-start(f32[3,256]{1,0:T(4,128)S(1)} %fusion.18), channel_id=1, source_target_pairs={{0,16},{16,0},{1,17},{17,1},{2,18},{18,2},{3,19},{19,3},{4,20},{20... | collective-permute-start | bytes 9224 | tf_op jit(solution)/shard_map/ppermute | solution.py:107
  135.8 4.5 %collective-permute-start.5 = (f32[2,1,256]{2,1,0:T(1,128)S(1)}, f32[2,1,256]{2,1,0:T(1,128)S(1)}, u32[]{:S(2)}, u32[]{:S(2)}) collective-permute-start(f32[2,1,256]{2,1,0:T(1,128)S(1)} %pad_maximum_fusion.9), channel_id=1, source_target_pairs={{0,8},{1,9},{2,10},{3,11},{4,12},{5,13},{6,14},{7,15},{8,0},{9,1},... | collective-permute-start | bytes 6152 | tf_op jit(solution)/shard_map/ppermute | solution.py:27
  143.1 1.2 collective-permute-start.7
  144.4 3.7 %collective-permute-start.8 = (f32[2,1,512]{2,1,0:T(1,128)S(1)}, f32[2,1,512]{2,1,0:T(1,128)S(1)}, u32[]{:S(2)}, u32[]{:S(2)}) collective-permute-start(f32[2,1,512]{2,1,0:T(1,128)S(1)} %pad_maximum_fusion.4), channel_id=1, source_target_pairs={{0,2},{1,3},{2,0},{3,1},{4,6},{5,7},{6,4},{7,5},{8,10},{9,11},{10,... | collective-permute-start | bytes 12296 | tf_op jit(solution)/shard_map/ppermute | solution.py:27
  148.1 3.7 %collective-permute-start.9 = (f32[2,1,512]{2,1,0:T(1,128)S(1)}, f32[2,1,512]{2,1,0:T(1,128)S(1)}, u32[]{:S(2)}, u32[]{:S(2)}) collective-permute-start(f32[2,1,512]{2,1,0:T(1,128)S(1)} %pad_maximum_fusion.5), channel_id=1, source_target_pairs={{0,4},{1,5},{2,6},{3,7},{4,0},{5,1},{6,2},{7,3},{8,12},{9,13},{10,... | collective-permute-start | bytes 12296 | tf_op jit(solution)/shard_map/ppermute | solution.py:27
  151.8 4.6 %collective-permute-start.10 = (f32[2,1,512]{2,1,0:T(1,128)S(1)}, f32[2,1,512]{2,1,0:T(1,128)S(1)}, u32[]{:S(2)}, u32[]{:S(2)}) collective-permute-start(f32[2,1,512]{2,1,0:T(1,128)S(1)} %pad_maximum_fusion.6), channel_id=1, source_target_pairs={{0,8},{1,9},{2,10},{3,11},{4,12},{5,13},{6,14},{7,15},{8,0},{9,1},... | collective-permute-start | bytes 12296 | tf_op jit(solution)/shard_map/ppermute | solution.py:27
  156.4 2.3 %copy-start.2 = (f32[256]{0:T(256)}, f32[256]{0:T(256)S(1)}, u32[]{:S(2)}) copy-start(f32[256]{0:T(256)S(1)} %get-tuple-element.18) | copy-start | bytes 3076

commit v8 on v7

--- a/solution.py
+++ b/solution.py
@@ -5,7 +5,6 @@
 
 epsilon = 1e-05
 send_pieces = 2
-gather_rows = 255
 
 
 def local_stats(values):
@@ -43,59 +42,50 @@
     width_all = width * shards
     w = pool_weight[0]
     sub = share // send_pieces
-
-    blocks = []
-    for shift in range(1, members):
-        target = (me + shift) % members
-        for k in range(send_pieces):
-            blocks.append(lax.dynamic_slice_in_dim(states, target * share + k * sub, sub, 0))
-    blocks.append(lax.dynamic_slice_in_dim(states, me * share, share, 0))
-    ordered = jnp.concatenate(blocks, axis=0)
-
-    bounds = [0, sub]
-    while bounds[-1] < row_count:
-        bounds.append(min(bounds[-1] + gather_rows, row_count))
     gain = None
 
-    def normalize(lo, hi, source):
+    def normalize(pieces):
         nonlocal gain
-        packed = source[lo:hi]
-        if gain is None:
-            packed = jnp.concatenate([packed, norm_gain], axis=0)
+        packed = jnp.concatenate(pieces + ([norm_gain] if gain is None else []), axis=0)
+        rows = sum(piece.shape[0] for piece in pieces)
         gathered = lax.all_gather(packed, "vocab", axis=0, tiled=False)
         if gain is None:
-            gain = gathered[:, hi - lo, :].astype(jnp.float32)
-        full_states = gathered[:, :hi - lo, :].astype(jnp.float32)
+            gain = gathered[:, rows, :].astype(jnp.float32)
+        full_states = gathered[:, :rows, :].astype(jnp.float32)
         mean_square = jnp.sum(full_states * full_states, axis=(0, 2)) / width_all
         scaling = lax.rsqrt(mean_square + epsilon)
-        piece = (full_states * scaling[None, :, None] * gain[:, None, :]).astype(jnp.bfloat16)
-        return jnp.transpose(piece, (1, 0, 2)).reshape(hi - lo, width_all)
+        normed = (full_states * scaling[None, :, None] * gain[:, None, :]).astype(jnp.bfloat16)
+        return jnp.transpose(normed, (1, 0, 2)).reshape(rows, width_all)
 
-    first_normed = normalize(bounds[0], bounds[1], ordered)
-    first_logits = jnp.dot(first_normed, weights, preferred_element_type=jnp.float32)
-    first_sent = w * first_logits
-    first_sent, ordered = lax.optimization_barrier((first_sent, ordered))
-    normed = jnp.concatenate(
-        [first_normed] + [normalize(lo, hi, ordered) for lo, hi in zip(bounds[1:-1], bounds[2:])], axis=0)
+    source = [states]
 
-    def logits_of(lo, rows):
-        return jnp.dot(normed[lo:lo + rows], weights, preferred_element_type=jnp.float32)
+    def rows_of(first_row, rows):
+        return lax.dynamic_slice_in_dim(source[0], first_row, rows, 0)
 
     received = []
     sent = []
+    own_head = None
     for shift in range(1, members):
+        target = (me + shift) % members
         perm = [(g, (g + shift) % members) for g in range(members)]
         parts = []
         for k in range(send_pieces):
-            if shift == 1 and k == 0:
-                logits, outgoing = first_logits, first_sent
-            else:
-                logits = logits_of(((shift - 1) * send_pieces + k) * sub, sub)
-                outgoing = w * logits
+            pieces = [rows_of(target * share + k * sub, sub)]
+            last = shift == members - 1 and k == send_pieces - 1
+            if last:
+                pieces.append(rows_of(me * share, 1))
+            normed = normalize(pieces)
+            if last:
+                own_head = normed[sub:]
+            logits = jnp.dot(normed[:sub], weights, preferred_element_type=jnp.float32)
+            outgoing = w * logits
+            if not sent:
+                outgoing, source[0] = lax.optimization_barrier((outgoing, states))
             parts.append(lax.ppermute(outgoing, "member", perm))
             sent.append(logits)
         received.append(parts)
-    own_logits = logits_of(row_count - share, share)
+    own_normed = jnp.concatenate([own_head, normalize([rows_of(me * share + 1, share - 1)])], axis=0)
+    own_logits = jnp.dot(own_normed, weights, preferred_element_type=jnp.float32)
 
     sent, own_logits = lax.optimization_barrier((sent, own_logits))
     notes = []
@@ -124,8 +114,7 @@
     for parts, part in zip(received, last_parts):
         parts[-1] = part
     last_total, last_stats = piece_terms(send_pieces - 1)
-    tail = jnp.concatenate([last_stats] + [note[:2] for note in notes], axis=1)
-    tail_lse = flat_lse(tail)
+    tail_lse = flat_lse(jnp.concatenate([last_stats] + [note[:2] for note in notes], axis=1))
 
     own_lse = []
     pooled_lse = []

time: 159 us -> 158 us (level)
  matrix products: 34.4 us -> 32.4 us
    reshape x1 -> x0, local copies, waits for them, and re-layouts: 2.18 us -> none  [normalize(): return jnp.transpose(piece, (1, 0, 2)).reshape(hi - lo, width_all)]
    dot_general x3, matrix products: 34.4 us -> 32.4 us  [the longest x2 19.7 us: on_device(): logits = jnp.dot(normed[:sub], weights, preferred_element_type=jnp.float32)]
    unnamed x9 -> x12, local copies, waits for them, and re-layouts: 0.8 us -> 2.66 us
    dynamic_slice x2 -> x3, local copies, waits for them, and re-layouts: 1.64 us -> 0.01 us  [rows_of(): return lax.dynamic_slice_in_dim(source[0], first_row, rows, 0)]
  transfers between devices with their start and end apart: 11 -> 11, of which waited for: 8 -> 8; matrix products, arithmetic and copies ran while one was open for 28% -> 26% of each run, Pallas kernels for 0% -> 0%
where the time goes in v8:
time: 158 us; the launch traced here: 157 us
  blocking collectives  68.5 us (43%)
  matrix products  32.4 us (21%)
  waiting for transfers between devices  23 us (15%)
  other arithmetic  19.8 us (13%)
  local copies, waits for them, and re-layouts  7.58 us (5%)
  starting transfers between devices  4.6 us (3%)
    all_gather x3, blocking collectives, normalize(): gathered = lax.all_gather(packed, 'vocab', axis=0, tiled=False)  68.5 us
    ppermute x8, waiting for transfers between devices, reduce_stats(): other = lax.ppermute(stats, axis, perm)  23 us
    dot_general x2, matrix products, on_device(): logits = jnp.dot(normed[:sub], weights, preferred_element_type=jnp.float32)  19.7 us
    dot_general x1, matrix products, on_device(): jnp.dot(own_normed, weights, preferred_element_type=jnp.float32)  12.7 us
    reduce_max x5, other arithmetic, local_stats(): local_peak = jnp.max(values, axis=1)  9.12 us
    reduce_sum x4, other arithmetic, local_stats(): local_sum = jnp.sum(jnp.exp(values - local_peak[:, None]), axis=1)  4.56 us
  transfers between devices with their start and end apart: 11, of which 8 were waited for; matrix products, arithmetic and copies ran while one was open for 26% of the time, Pallas kernels for 0%

profile of v8, /device:TPU:0, one launch (start us, length us, event | category | flops | bytes accessed | tf_op | source)
XLA Modules:
  0.0 157.4 jit_solution(13181948478138063616)
XLA Ops:
  0.7 0.9 copy-done
  1.5 0.7 maximum_bitcast_fusion
  2.2 24.7 %all-gather.3 = bf16[16,129,128]{2,1,0:T(8,128)(2,1)S(1)} all-gather(bf16[1,129,128]{2,1,0:T(8,128)(2,1)S(1)} %maximum_bitcast_fusion), channel_id=2, replica_groups=mesh['member'=2,'vocab'=16] {'vocab'}, dimensions={0}, use_global_device_ids=true | all-gather | bytes 561408 | tf_op jit(solution)/shard_map/all_gather | solution.py:51
  28.5 9.5 %broadcast_multiply_fusion.1 = (f32[128,4008]{0,1:T(8,128)}, f32[128,4008]{0,1:T(8,128)S(1)}) fusion(f32[]{:T(128)} %bitcast.182, bf16[128,2048]{0,1:T(8,128)(2,1)S(1)} %bitcast.192, bf16[1,2048,4008]{1,2,0:T(8,128)(2,1)} %param.6), kind=kOutput, calls=%fused_computation.38 | convolution fusion | flops 2101859328 | bytes 21045252 | tf_op jit(solution)/shard_map/dot_general | solution.py:80
  38.1 1.5 collective-permute-start
  39.6 20.2 %all-gather.4 = bf16[16,129,128]{2,1,0:T(8,128)(2,1)} all-gather(bf16[1,129,128]{2,1,0:T(8,128)(2,1)S(1)} %maximum_bitcast_fusion.1), channel_id=3, replica_groups=mesh['member'=2,'vocab'=16] {'vocab'}, dimensions={0}, use_global_device_ids=true | all-gather | bytes 561408 | tf_op jit(solution)/shard_map/all_gather | solution.py:51
  59.8 1.4 copy.12
  61.9 1.0 copy-done.3
  63.0 10.2 %broadcast_multiply_fusion = (f32[128,4008]{0,1:T(8,128)}, f32[128,4008]{0,1:T(8,128)}) fusion(f32[]{:T(128)} %bitcast.185, bf16[128,2048]{0,1:T(8,128)(2,1)S(1)} %bitcast.191, bf16[1,2048,4008]{1,2,0:T(8,128)(2,1)} %param.6), kind=kOutput, calls=%fused_computation.37 | convolution fusion | flops 2101859328 | bytes 21045252 | tf_op jit(solution)/shard_map/dot_general | solution.py:80
  73.7 23.6 %all-gather.5 = bf16[16,255,128]{2,1,0:T(8,128)(2,1)} all-gather(bf16[1,255,128]{2,1,0:T(8,128)(2,1)S(1)} %dynamic-slice_bitcast_fusion), channel_id=4, replica_groups=mesh['member'=2,'vocab'=16] {'vocab'}, dimensions={0}, use_global_device_ids=true | all-gather | bytes 1109760 | tf_op jit(solution)/shard_map/all_gather | solution.py:51
  97.3 1.5 copy.13
  99.1 1.9 %slice.160 = bf16[1,16,128]{0,2,1:T(8,128)(2,1)} slice(bf16[129,16,128]{0,2,1:T(8,128)(2,1)} %copy-done.3), slice={[128:129], [0:16], [0:128]} | slice | bytes 8192 | tf_op jit(solution)/shard_map/slice | solution.py:79
  101.0 1.3 fusion.11
  102.3 12.7 %fusion = f32[256,4008]{0,1:T(8,128)} fusion(bf16[1,2048,4008]{1,2,0:T(8,128)(2,1)} %param.6, bf16[255,2048]{0,1:T(8,128)(2,1)} %bitcast.193, bf16[1,2048]{0,1:T(8,128)(2,1)} %bitcast.194), kind=kOutput, calls=%fused_computation | convolution fusion | flops 4204789760 | bytes 21569536 | tf_op jit(solution)/shard_map/dot_general | solution.py:88
  115.5 2.1 %reduce_max.59 = f32[128]{0:T(128)S(1)} reduce(f32[128,4008]{0,1:T(8,128)} %get-tuple-element.15, f32[]{:T(128)} %constant.46.clone.1), dimensions={1}, to_apply=%region_13.14 | reduce | flops 512896 | bytes 2052612 | tf_op jit(solution)/shard_map/reduce_max | solution.py:11
  117.6 2.1 %slice_reduce_fusion = f32[128]{0:T(128)S(1)} fusion(f32[256,4008]{0,1:T(8,128)} %fusion), kind=kLoop, calls=%fused_computation.26 | loop fusion | flops 512896 | bytes 2052608 | tf_op jit(solution)/shard_map/reduce_max | solution.py:11
  119.7 2.9 %exponential_reduce_fusion.3 = (f32[128]{0:T(128)S(1)}, f32[128]{0:T(128)S(1)}) fusion(f32[256,4008]{0,1:T(8,128)} %fusion, f32[128]{0:T(128)S(1)} %slice_reduce_fusion), kind=kLoop, calls=%fused_computation.21 | loop fusion | flops 1538816 | bytes 4105728 | tf_op jit(solution)/shard_map/reduce_sum | solution.py:12
  123.1 2.2 %fusion.57 = (f32[128]{0:T(128)S(1)}, f32[128,4008]{0,1:T(8,128)S(1)}, f32[128]{0:T(128)S(1)}) fusion(f32[128,4008]{0,1:T(8,128)} %collective-permute-done, f32[256,4008]{0,1:T(8,128)S(1)} %copy-done.1, f32[]{:T(128)} %bitcast.187, f32[128]{0:T(128)S(1)} %get-tuple-element.17), kind=kLoop, calls=%fused_computation.119 | loop fusion | flops 2564864 | bytes 6157828 | tf_op jit(solution)/shard_map/reduce_max | solution.py:11
  125.3 0.6 exponential_reduce_fusion.4
  126.3 0.8 collective-permute-done.2
  127.3 0.6 exponential_reduce_fusion
  127.8 3.0 %collective-permute-done.3 = f32[2,1,256]{2,1,0:T(1,128)S(1)} collective-permute-done((f32[2,1,256]{2,1,0:T(1,128)S(1)}, f32[2,1,256]{2,1,0:T(1,128)S(1)}, u32[]{:S(2)}, u32[]{:S(2)}) %collective-permute-start.3) | collective-permute-done | bytes 2080 | tf_op jit(solution)/shard_map/ppermute | solution.py:26
  130.9 1.6 %collective-permute-start.6 = (f32[3,256]{1,0:T(4,128)S(1)}, f32[3,256]{1,0:T(4,128)S(1)}, u32[]{:S(2)}, u32[]{:S(2)}) collective-permute-start(f32[3,256]{1,0:T(4,128)S(1)} %fusion.20), channel_id=1, source_target_pairs={{0,16},{16,0},{1,17},{17,1},{2,18},{18,2},{3,19},{19,3},{4,20},{20... | collective-permute-start | bytes 9224 | tf_op jit(solution)/shard_map/ppermute | solution.py:97
  132.5 2.0 %collective-permute-done.4 = f32[2,1,256]{2,1,0:T(1,128)S(1)} collective-permute-done((f32[2,1,256]{2,1,0:T(1,128)S(1)}, f32[2,1,256]{2,1,0:T(1,128)S(1)}, u32[]{:S(2)}, u32[]{:S(2)}) %collective-permute-start.4) | collective-permute-done | bytes 2080 | tf_op jit(solution)/shard_map/ppermute | solution.py:26
  134.6 4.4 %collective-permute-done.5 = f32[2,1,256]{2,1,0:T(1,128)S(1)} collective-permute-done((f32[2,1,256]{2,1,0:T(1,128)S(1)}, f32[2,1,256]{2,1,0:T(1,128)S(1)}, u32[]{:S(2)}, u32[]{:S(2)}) %collective-permute-start.5) | collective-permute-done | bytes 2080 | tf_op jit(solution)/shard_map/ppermute | solution.py:26
  139.1 2.1 %fusion.54 = (f32[128]{0:T(128)S(1)}, f32[128,4008]{0,1:T(8,128)S(1)}) fusion(f32[128,4008]{0,1:T(8,128)} %collective-permute-done.1, f32[256,4008]{0,1:T(8,128)S(1)} %copy-done.1, f32[]{:T(128)} %bitcast.186), kind=kLoop, calls=%fused_computation.118 | loop fusion | flops 1538944 | bytes 6156804 | tf_op jit(solution)/shard_map/reduce_max | solution.py:11
  141.2 0.6 exponential_reduce_fusion.2
  141.9 1.1 collective-permute-done.7
  143.1 3.6 %collective-permute-done.8 = f32[2,1,512]{2,1,0:T(1,128)S(1)} collective-permute-done((f32[2,1,512]{2,1,0:T(1,128)S(1)}, f32[2,1,512]{2,1,0:T(1,128)S(1)}, u32[]{:S(2)}, u32[]{:S(2)}) %collective-permute-start.8) | collective-permute-done | bytes 4128 | tf_op jit(solution)/shard_map/ppermute | solution.py:26
  146.8 3.6 %collective-permute-done.9 = f32[2,1,512]{2,1,0:T(1,128)S(1)} collective-permute-done((f32[2,1,512]{2,1,0:T(1,128)S(1)}, f32[2,1,512]{2,1,0:T(1,128)S(1)}, u32[]{:S(2)}, u32[]{:S(2)}) %collective-permute-start.9) | collective-permute-done | bytes 4128 | tf_op jit(solution)/shard_map/ppermute | solution.py:26
  150.5 4.5 %collective-permute-done.10 = f32[2,1,512]{2,1,0:T(1,128)S(1)} collective-permute-done((f32[2,1,512]{2,1,0:T(1,128)S(1)}, f32[2,1,512]{2,1,0:T(1,128)S(1)}, u32[]{:S(2)}, u32[]{:S(2)}) %collective-permute-start.10) | collective-permute-done | bytes 4128 | tf_op jit(solution)/shard_map/ppermute | solution.py:26
  155.1 2.3 %fusion.6 = f32[256,4008]{0,1:T(8,128)} fusion(f32[128,4008]{0,1:T(8,128)S(1)} %get-tuple-element.25, f32[128,4008]{0,1:T(8,128)S(1)} %get-tuple-element.31, f32[256]{0:T(256)S(1)} %get-tuple-element.18, f32[256]{0:T(256)S(1)} %get-tuple-element.19), kind=kLoop, calls=%fused_computation.7 | loop fusion | flops 3078144 | bytes 8210432 | tf_op jit(solution)/shard_map/sub | solution.py:134
  (62 shorter events, 4.9 us)
Async XLA Ops:
  0.6 0.9 copy-start
  38.1 84.5 %collective-permute-start = (f32[128,4008]{0,1:T(8,128)}, f32[128,4008]{0,1:T(8,128)}, u32[]{:S(2)}, u32[]{:S(2)}) collective-permute-start(f32[128,4008]{0,1:T(8,128)} %get-tuple-element.11), channel_id=1, source_target_pairs={{0,16},{16,0},{1,17},{17,1},{2,18},{18,2},{3,19},{19,3},{4,20},{20... | collective-permute-start | bytes 6156296 | tf_op jit(solution)/shard_map/ppermute | solution.py:84
  61.9 1.0 copy-start.3
  73.2 65.9 %collective-permute-start.1 = (f32[128,4008]{0,1:T(8,128)}, f32[128,4008]{0,1:T(8,128)}, u32[]{:S(2)}, u32[]{:S(2)}) collective-permute-start(f32[128,4008]{0,1:T(8,128)} %get-tuple-element.43), channel_id=1, source_target_pairs={{0,16},{16,0},{1,17},{17,1},{2,18},{18,2},{3,19},{19,3},{4,20},{20... | collective-permute-start | bytes 6156296 | tf_op jit(solution)/shard_map/ppermute | solution.py:84
  119.7 3.4 %copy-start.1 = (f32[256,4008]{0,1:T(8,128)S(1)}, f32[256,4008]{0,1:T(8,128)}, u32[]{:S(2)}) copy-start(f32[256,4008]{0,1:T(8,128)} %fusion) | copy-start | bytes 12312580
  125.3 1.9 %copy-start.2 = (f32[128,4008]{0,1:T(8,128)S(1)}, f32[128,4008]{0,1:T(8,128)}, u32[]{:S(2)}) copy-start(f32[128,4008]{0,1:T(8,128)} %get-tuple-element.15) | copy-start | bytes 6156292
  125.9 1.2 collective-permute-start.2
  127.1 3.7 %collective-permute-start.3 = (f32[2,1,256]{2,1,0:T(1,128)S(1)}, f32[2,1,256]{2,1,0:T(1,128)S(1)}, u32[]{:S(2)}, u32[]{:S(2)}) collective-permute-start(f32[2,1,256]{2,1,0:T(1,128)S(1)} %pad_maximum_fusion.4), channel_id=1, source_target_pairs={{0,2},{1,3},{2,0},{3,1},{4,6},{5,7},{6,4},{7,5},{8,10},{9,11},{10,... | collective-permute-start | bytes 6152 | tf_op jit(solution)/shard_map/ppermute | solution.py:26
  130.8 3.7 %collective-permute-start.4 = (f32[2,1,256]{2,1,0:T(1,128)S(1)}, f32[2,1,256]{2,1,0:T(1,128)S(1)}, u32[]{:S(2)}, u32[]{:S(2)}) collective-permute-start(f32[2,1,256]{2,1,0:T(1,128)S(1)} %pad_maximum_fusion.5), channel_id=1, source_target_pairs={{0,4},{1,5},{2,6},{3,7},{4,0},{5,1},{6,2},{7,3},{8,12},{9,13},{10,... | collective-permute-start | bytes 6152 | tf_op jit(solution)/shard_map/ppermute | solution.py:26
  130.9 3.7 %collective-permute-start.6 = (f32[3,256]{1,0:T(4,128)S(1)}, f32[3,256]{1,0:T(4,128)S(1)}, u32[]{:S(2)}, u32[]{:S(2)}) collective-permute-start(f32[3,256]{1,0:T(4,128)S(1)} %fusion.20), channel_id=1, source_target_pairs={{0,16},{16,0},{1,17},{17,1},{2,18},{18,2},{3,19},{19,3},{4,20},{20... | collective-permute-start | bytes 9224 | tf_op jit(solution)/shard_map/ppermute | solution.py:97
  134.5 4.5 %collective-permute-start.5 = (f32[2,1,256]{2,1,0:T(1,128)S(1)}, f32[2,1,256]{2,1,0:T(1,128)S(1)}, u32[]{:S(2)}, u32[]{:S(2)}) collective-permute-start(f32[2,1,256]{2,1,0:T(1,128)S(1)} %pad_maximum_fusion.6), channel_id=1, source_target_pairs={{0,8},{1,9},{2,10},{3,11},{4,12},{5,13},{6,14},{7,15},{8,0},{9,1},... | collective-permute-start | bytes 6152 | tf_op jit(solution)/shard_map/ppermute | solution.py:26
  141.8 1.2 collective-permute-start.7
  143.0 3.7 %collective-permute-start.8 = (f32[2,1,512]{2,1,0:T(1,128)S(1)}, f32[2,1,512]{2,1,0:T(1,128)S(1)}, u32[]{:S(2)}, u32[]{:S(2)}) collective-permute-start(f32[2,1,512]{2,1,0:T(1,128)S(1)} %pad_maximum_fusion.1), channel_id=1, source_target_pairs={{0,2},{1,3},{2,0},{3,1},{4,6},{5,7},{6,4},{7,5},{8,10},{9,11},{10,... | collective-permute-start | bytes 12296 | tf_op jit(solution)/shard_map/ppermute | solution.py:26
  146.7 3.7 %collective-permute-start.9 = (f32[2,1,512]{2,1,0:T(1,128)S(1)}, f32[2,1,512]{2,1,0:T(1,128)S(1)}, u32[]{:S(2)}, u32[]{:S(2)}) collective-permute-start(f32[2,1,512]{2,1,0:T(1,128)S(1)} %pad_maximum_fusion.2), channel_id=1, source_target_pairs={{0,4},{1,5},{2,6},{3,7},{4,0},{5,1},{6,2},{7,3},{8,12},{9,13},{10,... | collective-permute-start | bytes 12296 | tf_op jit(solution)/shard_map/ppermute | solution.py:26
  150.4 4.6 %collective-permute-start.10 = (f32[2,1,512]{2,1,0:T(1,128)S(1)}, f32[2,1,512]{2,1,0:T(1,128)S(1)}, u32[]{:S(2)}, u32[]{:S(2)}) collective-permute-start(f32[2,1,512]{2,1,0:T(1,128)S(1)} %pad_maximum_fusion.3), channel_id=1, source_target_pairs={{0,8},{1,9},{2,10},{3,11},{4,12},{5,13},{6,14},{7,15},{8,0},{9,1},... | collective-permute-start | bytes 12296 | tf_op jit(solution)/shard_map/ppermute | solution.py:26
  155.1 2.3 %copy-start.4 = (f32[256]{0:T(256)}, f32[256]{0:T(256)S(1)}, u32[]{:S(2)}) copy-start(f32[256]{0:T(256)S(1)} %get-tuple-element.18) | copy-start | bytes 3076

commit v9 on v6

--- a/solution.py
+++ b/solution.py
@@ -20,14 +20,24 @@
         peak = jnp.max(gathered[:, 0], axis=0)
         summed = jnp.sum(gathered[:, 1] * jnp.exp(gathered[:, 0] - peak[None]), axis=0)
         return peak, summed
-    distance = 1
-    while distance < size:
-        perm = [(a, a ^ distance) for a in range(size)]
-        other = lax.ppermute(stats, axis, perm)
-        peak = jnp.maximum(stats[0], other[0])
-        summed = stats[1] * jnp.exp(stats[0] - peak) + other[1] * jnp.exp(other[0] - peak)
+    stride = 1
+    while stride < size:
+        radix = 4 if stride * 4 <= size else 2
+        others = [
+            lax.ppermute(stats, axis, [(a, a ^ (j * stride)) for a in range(size)])
+            for j in range(1, radix)
+        ]
+        values = [stats] + others
+        peak = values[0][0]
+        for value in values[1:]:
+            peak = jnp.maximum(peak, value[0])
+        terms = [value[1] * jnp.exp(value[0] - peak) for value in values]
+        if radix == 4:
+            summed = (terms[0] + terms[1]) + (terms[2] + terms[3])
+        else:
+            summed = terms[0] + terms[1]
         stats = jnp.stack([peak, summed])
-        distance *= 2
+        stride *= radix
     return stats[0], stats[1]
 
 

time: 153 us -> 150 us (0.980)
  waiting for transfers between devices: 12.9 us -> 5.44 us
  starting transfers between devices: 5.57 us -> 10 us
    ppermute x4 -> x6, waiting for transfers between devices: 11.3 us -> 3.88 us  [reduce_stats(): lax.ppermute(stats, axis, [(a, a ^ j * stride) for a in range(size)])]
    ppermute x4 -> x6, starting transfers between devices: 1.95 us -> 6.38 us  [reduce_stats(): lax.ppermute(stats, axis, [(a, a ^ j * stride) for a in range(size)])]
  transfers between devices with their start and end apart: 7 -> 9, of which waited for: 5 -> 5; matrix products, arithmetic and copies ran while one was open for 21% -> 21% of each run, Pallas kernels for 0% -> 0%
where the time goes in v9:
time: 150 us
  blocking collectives  83.1 us (55%)
  matrix products  32.3 us (22%)
  other arithmetic  15.4 us (10%)
  starting transfers between devices  10 us (7%)
  waiting for transfers between devices  5.44 us (4%)
  local copies, waits for them, and re-layouts  2.21 us (1%)
  between operations  1.53 us (1%)
    all_gather x4, blocking collectives, logits_of(): gathered = lax.all_gather(packed, 'vocab', axis=0, tiled=False)  83.1 us
    dot_general x4, matrix products, logits_of(): return jnp.dot(normed, weights, preferred_element_type=jnp.float32)  32.3 us
    ppermute x6, starting transfers between devices, reduce_stats(): lax.ppermute(stats, axis, [(a, a ^ j * stride) for a in range(size)])  6.38 us
    reduce_sum x4, other arithmetic, local_stats(): local_sum = jnp.sum(jnp.exp(values - local_peak[:, None]), axis=1)  5 us
    ppermute x6, waiting for transfers between devices, reduce_stats(): lax.ppermute(stats, axis, [(a, a ^ j * stride) for a in range(size)])  3.88 us
  transfers between devices with their start and end apart: 9, of which 5 were waited for; matrix products, arithmetic and copies ran while one was open for 21% of the time, Pallas kernels for 0%

profile of v9, /device:TPU:0, one launch (start us, length us, event | category | flops | bytes accessed | tf_op | source)
XLA Modules:
  0.0 150.0 jit_solution(2973940082352301632)
XLA Ops:
  0.7 0.8 dynamic-slice_bitcast_fusion.1
  1.5 0.7 fusion.23
  2.2 24.7 %all-gather.5 = bf16[16,129,128]{2,1,0:T(8,128)(2,1)S(1)} all-gather(bf16[1,129,128]{2,1,0:T(8,128)(2,1)S(1)} %get-tuple-element.28), channel_id=3, replica_groups=mesh['member'=2,'vocab'=16] {'vocab'}, dimensions={0}, use_global_device_ids=true | all-gather | bytes 561408 | tf_op jit(solution)/shard_map/all_gather | solution.py:56
  28.2 0.3 fusion.14
  28.5 8.1 %fusion.51 = (f32[128]{0:T(128)S(1)}, f32[128,4008]{0,1:T(8,128)S(1)}) fusion(bf16[128,2048]{0,1:T(8,128)(2,1)S(1)} %bitcast.218, bf16[1,2048,4008]{1,2,0:T(8,128)(2,1)} %param.6), kind=kOutput, calls=%fused_computation.119 | convolution fusion | flops 2101859200 | bytes 18993664 | tf_op jit(solution)/shard_map/dot_general | solution.py:63
  36.6 1.8 %exponential_reduce_fusion.4 = (f32[128]{0:T(128)S(1)}, f32[128,4008]{0,1:T(8,128)}) fusion(f32[128,4008]{0,1:T(8,128)S(1)} %get-tuple-element.32, f32[128]{0:T(128)S(1)} %get-tuple-element.31, f32[]{:T(128)} %bitcast.213), kind=kLoop, calls=%fused_computation.17 | loop fusion | flops 1538944 | bytes 4105220 | tf_op jit(solution)/shard_map/reduce_sum | solution.py:12
  38.4 1.5 %collective-permute-start.1 = (f32[128,4008]{0,1:T(8,128)}, f32[128,4008]{0,1:T(8,128)}, u32[]{:S(2)}, u32[]{:S(2)}) collective-permute-start(f32[128,4008]{0,1:T(8,128)} %get-tuple-element.20), channel_id=1, source_target_pairs={{0,16},{16,0},{1,17},{17,1},{2,18},{18,2},{3,19},{19,3},{4,20},{20... | collective-permute-start | bytes 6156296 | tf_op jit(solution)/shard_map/ppermute | solution.py:76
  39.9 18.8 %all-gather.4 = bf16[16,129,128]{2,1,0:T(8,128)(2,1)S(1)} all-gather(bf16[1,129,128]{2,1,0:T(8,128)(2,1)S(1)} %get-tuple-element.30), channel_id=2, replica_groups=mesh['member'=2,'vocab'=16] {'vocab'}, dimensions={0}, use_global_device_ids=true | all-gather | bytes 561408 | tf_op jit(solution)/shard_map/all_gather | solution.py:56
  59.3 0.3 fusion.11
  59.7 8.1 %fusion.52 = (f32[128]{0:T(128)S(1)}, f32[128,4008]{0,1:T(8,128)S(1)}) fusion(bf16[128,2048]{0,1:T(8,128)(2,1)S(1)} %bitcast.219, bf16[1,2048,4008]{1,2,0:T(8,128)(2,1)} %param.6), kind=kOutput, calls=%fused_computation.120 | convolution fusion | flops 2101859200 | bytes 18993664 | tf_op jit(solution)/shard_map/dot_general | solution.py:63
  67.8 1.8 %broadcast_multiply_fusion.1 = (f32[128,4008]{0,1:T(8,128)}, f32[128]{0:T(128)S(1)}) fusion(f32[128,4008]{0,1:T(8,128)S(1)} %get-tuple-element.34, f32[]{:T(128)} %bitcast.215, f32[128]{0:T(128)S(1)} %get-tuple-element.33), kind=kLoop, calls=%fused_computation.42 | loop fusion | flops 1538944 | bytes 4105220 | tf_op jit(solution)/shard_map/mul | solution.py:76
  69.5 0.5 collective-permute-start
  70.0 20.5 %all-gather.6 = bf16[16,129,128]{2,1,0:T(8,128)(2,1)S(1)} all-gather(bf16[1,129,128]{2,1,0:T(8,128)(2,1)S(1)} %get-tuple-element.27), channel_id=4, replica_groups=mesh['member'=2,'vocab'=16] {'vocab'}, dimensions={0}, use_global_device_ids=true | all-gather | bytes 561408 | tf_op jit(solution)/shard_map/all_gather | solution.py:56
  90.5 19.2 %all-gather.7 = bf16[16,129,128]{2,1,0:T(8,128)(2,1)S(1)} all-gather(bf16[1,129,128]{2,1,0:T(8,128)(2,1)S(1)} %get-tuple-element.29), channel_id=5, replica_groups=mesh['member'=2,'vocab'=16] {'vocab'}, dimensions={0}, use_global_device_ids=true | all-gather | bytes 561408 | tf_op jit(solution)/shard_map/all_gather | solution.py:56
  111.3 8.1 %fusion = f32[128,4008]{0,1:T(8,128)S(1)} fusion(bf16[128,2048]{0,1:T(8,128)(2,1)S(1)} %bitcast.216, bf16[1,2048,4008]{1,2,0:T(8,128)(2,1)} %param.6), kind=kOutput, calls=%fused_computation | convolution fusion | flops 2101346304 | bytes 18993152 | tf_op jit(solution)/shard_map/dot_general | solution.py:63
  119.7 8.1 %fusion.2 = f32[128,4008]{0,1:T(8,128)S(1)} fusion(bf16[128,2048]{0,1:T(8,128)(2,1)S(1)} %bitcast.217, bf16[1,2048,4008]{1,2,0:T(8,128)(2,1)} %param.6), kind=kOutput, calls=%fused_computation.2 | convolution fusion | flops 2101346304 | bytes 18993152 | tf_op jit(solution)/shard_map/dot_general | solution.py:63
  128.1 1.6 %collective-permute-start.2 = (f32[3,256]{1,0:T(4,128)S(1)}, f32[3,256]{1,0:T(4,128)S(1)}, u32[]{:S(2)}, u32[]{:S(2)}) collective-permute-start(f32[3,256]{1,0:T(4,128)S(1)} %fusion.33), channel_id=1, source_target_pairs={{0,16},{16,0},{1,17},{17,1},{2,18},{18,2},{3,19},{19,3},{4,20},{20... | collective-permute-start | bytes 9224 | tf_op jit(solution)/shard_map/ppermute | solution.py:85
  129.7 0.5 slice_reduce_fusion.1
  130.2 1.6 %collective-permute-done.2 = f32[3,256]{1,0:T(4,128)S(1)} collective-permute-done((f32[3,256]{1,0:T(4,128)S(1)}, f32[3,256]{1,0:T(4,128)S(1)}, u32[]{:S(2)}, u32[]{:S(2)}) %collective-permute-start.2) | collective-permute-done | bytes 3104 | tf_op jit(solution)/shard_map/ppermute | solution.py:85
  131.8 2.1 %exponential_reduce_fusion.3 = (f32[128]{0:T(128)S(1)}, f32[128]{0:T(128)S(1)}, f32[128]{0:T(128)S(1)}, f32[128,4008]{0,1:T(8,128)S(1)}) fusion(f32[256,4008]{0,1:T(8,128)S(1)} %pad_maximum_fusion, f32[128]{0:T(128)S(1)} %slice_reduce_fusion.1, f32[128,4008]{0,1:T(8,128)} %collective-permute-done, f32[]{:T(128)} %bitcast.210), kind=kLoop, calls=%fused_computation.14 | loop fusion | flops 3077760 | bytes 8210436 | tf_op jit(solution)/shard_map/reduce_sum | solution.py:12
  134.0 2.2 %fusion.50 = (f32[128]{0:T(128)S(1)}, f32[128,4008]{0,1:T(8,128)S(1)}, f32[128]{0:T(128)S(1)}) fusion(f32[128,4008]{0,1:T(8,128)} %collective-permute-done.1, f32[256,4008]{0,1:T(8,128)S(1)} %pad_maximum_fusion, f32[]{:T(128)} %bitcast.214, f32[128]{0:T(128)S(1)} %get-tuple-element.7), kind=kLoop, calls=%fused_computation.118 | loop fusion | flops 2564864 | bytes 6157828 | tf_op jit(solution)/shard_map/reduce_max | solution.py:11
  136.1 0.6 exponential_reduce_fusion
  136.7 0.6 exponential_reduce_fusion.2
  137.3 0.5 collective-permute-start.5
  137.8 1.3 collective-permute-start.4
  139.2 1.2 collective-permute-done.5
  140.4 1.0 collective-permute-done.4
  141.5 0.6 collective-permute-start.8
  142.2 3.8 %collective-permute-start.6 = (f32[2,3,256]{2,1,0:T(4,128)S(1)}, f32[2,3,256]{2,1,0:T(4,128)S(1)}, u32[]{:S(2)}, u32[]{:S(2)}) collective-permute-start(f32[2,3,256]{2,1,0:T(4,128)S(1)} %pad_maximum_fusion.6), channel_id=1, source_target_pairs={{0,4},{1,5},{2,6},{3,7},{4,0},{5,1},{6,2},{7,3},{8,12},{9,13},{10,... | collective-permute-start | bytes 18440 | tf_op jit(solution)/shard_map/ppermute | solution.py:27
  146.0 1.1 collective-permute-done.8
  147.0 0.6 collective-permute-done.6
  147.7 2.3 %fusion.8 = f32[256,4008]{0,1:T(8,128)} fusion(f32[128,4008]{0,1:T(8,128)S(1)} %get-tuple-element.13, f32[128,4008]{0,1:T(8,128)S(1)} %get-tuple-element.16, f32[256]{0:T(256)S(1)} %sub.133, f32[256]{0:T(256)S(1)} %bitcast.221), kind=kLoop, calls=%fused_computation.10 | loop fusion | flops 3078144 | bytes 8210432 | tf_op jit(solution)/shard_map/sub | solution.py:107
  (48 shorter events, 3.8 us)
Async XLA Ops:
  38.4 95.6 %collective-permute-start.1 = (f32[128,4008]{0,1:T(8,128)}, f32[128,4008]{0,1:T(8,128)}, u32[]{:S(2)}, u32[]{:S(2)}) collective-permute-start(f32[128,4008]{0,1:T(8,128)} %get-tuple-element.20), channel_id=1, source_target_pairs={{0,16},{16,0},{1,17},{17,1},{2,18},{18,2},{3,19},{19,3},{4,20},{20... | collective-permute-start | bytes 6156296 | tf_op jit(solution)/shard_map/ppermute | solution.py:76
  69.5 62.3 %collective-permute-start = (f32[128,4008]{0,1:T(8,128)}, f32[128,4008]{0,1:T(8,128)}, u32[]{:S(2)}, u32[]{:S(2)}) collective-permute-start(f32[128,4008]{0,1:T(8,128)} %get-tuple-element.17), channel_id=1, source_target_pairs={{0,16},{16,0},{1,17},{17,1},{2,18},{18,2},{3,19},{19,3},{4,20},{20... | collective-permute-start | bytes 6156296 | tf_op jit(solution)/shard_map/ppermute | solution.py:76
  128.1 3.7 %collective-permute-start.2 = (f32[3,256]{1,0:T(4,128)S(1)}, f32[3,256]{1,0:T(4,128)S(1)}, u32[]{:S(2)}, u32[]{:S(2)}) collective-permute-start(f32[3,256]{1,0:T(4,128)S(1)} %fusion.33), channel_id=1, source_target_pairs={{0,16},{16,0},{1,17},{17,1},{2,18},{18,2},{3,19},{19,3},{4,20},{20... | collective-permute-start | bytes 9224 | tf_op jit(solution)/shard_map/ppermute | solution.py:85
  137.3 3.1 %collective-permute-start.5 = (f32[2,3,256]{2,1,0:T(4,128)S(1)}, f32[2,3,256]{2,1,0:T(4,128)S(1)}, u32[]{:S(2)}, u32[]{:S(2)}) collective-permute-start(f32[2,3,256]{2,1,0:T(4,128)S(1)} %pad_maximum_fusion.5), channel_id=1, source_target_pairs={{0,3},{1,2},{2,1},{3,0},{4,7},{5,6},{6,5},{7,4},{8,11},{9,10},{10,... | collective-permute-start | bytes 18440 | tf_op jit(solution)/shard_map/ppermute | solution.py:27
  137.8 3.7 %collective-permute-start.4 = (f32[2,3,256]{2,1,0:T(4,128)S(1)}, f32[2,3,256]{2,1,0:T(4,128)S(1)}, u32[]{:S(2)}, u32[]{:S(2)}) collective-permute-start(f32[2,3,256]{2,1,0:T(4,128)S(1)} %pad_maximum_fusion.5), channel_id=1, source_target_pairs={{0,2},{1,3},{2,0},{3,1},{4,6},{5,7},{6,4},{7,5},{8,10},{9,11},{10,... | collective-permute-start | bytes 18440 | tf_op jit(solution)/shard_map/ppermute | solution.py:27
  139.1 2.3 %collective-permute-start.3 = (f32[2,3,256]{2,1,0:T(4,128)S(1)}, f32[2,3,256]{2,1,0:T(4,128)S(1)}, u32[]{:S(2)}, u32[]{:S(2)}) collective-permute-start(f32[2,3,256]{2,1,0:T(4,128)S(1)} %pad_maximum_fusion.5), channel_id=1, source_target_pairs={{0,1},{1,0},{2,3},{3,2},{4,5},{5,4},{6,7},{7,6},{8,9},{9,8},{10,11... | collective-permute-start | bytes 18440 | tf_op jit(solution)/shard_map/ppermute | solution.py:27
  141.5 5.5 %collective-permute-start.8 = (f32[2,3,256]{2,1,0:T(4,128)S(1)}, f32[2,3,256]{2,1,0:T(4,128)S(1)}, u32[]{:S(2)}, u32[]{:S(2)}) collective-permute-start(f32[2,3,256]{2,1,0:T(4,128)S(1)} %pad_maximum_fusion.6), channel_id=1, source_target_pairs={{0,12},{1,13},{2,14},{3,15},{4,8},{5,9},{6,10},{7,11},{8,4},{9,5},... | collective-permute-start | bytes 18440 | tf_op jit(solution)/shard_map/ppermute | solution.py:27
  142.2 4.9 %collective-permute-start.7 = (f32[2,3,256]{2,1,0:T(4,128)S(1)}, f32[2,3,256]{2,1,0:T(4,128)S(1)}, u32[]{:S(2)}, u32[]{:S(2)}) collective-permute-start(f32[2,3,256]{2,1,0:T(4,128)S(1)} %pad_maximum_fusion.6), channel_id=1, source_target_pairs={{0,8},{1,9},{2,10},{3,11},{4,12},{5,13},{6,14},{7,15},{8,0},{9,1},... | collective-permute-start | bytes 18440 | tf_op jit(solution)/shard_map/ppermute | solution.py:27
  142.2 5.4 %collective-permute-start.6 = (f32[2,3,256]{2,1,0:T(4,128)S(1)}, f32[2,3,256]{2,1,0:T(4,128)S(1)}, u32[]{:S(2)}, u32[]{:S(2)}) collective-permute-start(f32[2,3,256]{2,1,0:T(4,128)S(1)} %pad_maximum_fusion.6), channel_id=1, source_target_pairs={{0,4},{1,5},{2,6},{3,7},{4,0},{5,1},{6,2},{7,3},{8,12},{9,13},{10,... | collective-permute-start | bytes 18440 | tf_op jit(solution)/shard_map/ppermute | solution.py:27
  147.7 2.3 %copy-start = (f32[256]{0:T(256)}, f32[256]{0:T(256)S(1)}, u32[]{:S(2)}) copy-start(f32[256]{0:T(256)S(1)} %sub.133) | copy-start | bytes 3076

commit v10 on v9

--- a/solution.py
+++ b/solution.py
@@ -50,7 +50,7 @@
     share = row_count // members
     weights = head[0]
     width_all = width * shards
-    def logits_of(first_row, rows):
+    def normed_of(first_row, rows):
         piece = lax.dynamic_slice_in_dim(states, first_row, rows, 0)
         packed = jnp.concatenate([piece, norm_gain], axis=0)
         gathered = lax.all_gather(packed, "vocab", axis=0, tiled=False)
@@ -59,8 +59,10 @@
         mean_square = jnp.sum(full_states * full_states, axis=(0, 2)) / width_all
         scaling = lax.rsqrt(mean_square + epsilon)
         normed = (full_states * scaling[None, :, None] * gain[:, None, :]).astype(jnp.bfloat16)
-        normed = jnp.transpose(normed, (1, 0, 2)).reshape(rows, width_all)
-        return jnp.dot(normed, weights, preferred_element_type=jnp.float32)
+        return jnp.transpose(normed, (1, 0, 2)).reshape(rows, width_all)
+
+    def logits_of(first_row, rows):
+        return jnp.dot(normed_of(first_row, rows), weights, preferred_element_type=jnp.float32)
 
     w = pool_weight[0]
     sub = share // send_pieces
@@ -79,8 +81,9 @@
         note = jnp.concatenate([stats_rows, jnp.broadcast_to(w, (1, share))], axis=0)
         received.append(parts)
         notes.append((perm, note))
-    own_logits = jnp.concatenate(
-        [logits_of(me * share + k * sub, sub) for k in range(send_pieces)], axis=0)
+    own_normed = jnp.concatenate(
+        [normed_of(me * share + k * sub, sub) for k in range(send_pieces)], axis=0)
+    own_logits = jnp.dot(own_normed, weights, preferred_element_type=jnp.float32)
     notes, own_logits = lax.optimization_barrier(([note for _, note in notes], own_logits))
     notes = [lax.ppermute(note, "member", [(g, (g + shift) % members) for g in range(members)])
              for shift, note in zip(range(1, members), notes)]

time: 150 us -> 150 us (level)
  matrix products: 32.3 us -> 26.1 us
  other arithmetic: 15.4 us -> 18.2 us
  waiting for transfers between devices: 5.44 us -> 7.86 us
    dot_general x4 -> x3, matrix products: 32.3 us -> 26.1 us  [the longest x2 16.1 us: logits_of(): jnp.dot(normed_of(first_row, rows), weights, preferred_element_type=jnp.f...]
    ppermute x1, waiting for transfers between devices: 1.55 us -> 4.36 us  [on_device(): lax.ppermute(note, 'member', [(g, (g + shift) % members) for g in range(m...]
    reduce_max x2, other arithmetic: 2.72 us -> 4.33 us  [local_stats(): local_peak = jnp.max(values, axis=1)]
  transfers between devices with their start and end apart: 9 -> 9, of which waited for: 5 -> 5; matrix products, arithmetic and copies ran while one was open for 21% -> 19% of each run, Pallas kernels for 0% -> 0%
where the time goes in v10:
time: 150 us; the launch traced here: 149 us
  blocking collectives  83.1 us (55%)
  matrix products  26.1 us (17%)
  other arithmetic  18.2 us (12%)
  starting transfers between devices  9.91 us (7%)
  waiting for transfers between devices  7.86 us (5%)
  local copies, waits for them, and re-layouts  2.64 us (2%)
  between operations  1.54 us (1%)
    all_gather x4, blocking collectives, normed_of(): gathered = lax.all_gather(packed, 'vocab', axis=0, tiled=False)  83.1 us
    dot_general x2, matrix products, logits_of(): jnp.dot(normed_of(first_row, rows), weights, preferred_element_type=jnp.f...  16.1 us
    dot_general x1, matrix products, on_device(): jnp.dot(own_normed, weights, preferred_element_type=jnp.float32)  9.95 us
    reduce_sum x4, other arithmetic, local_stats(): local_sum = jnp.sum(jnp.exp(values - local_peak[:, None]), axis=1)  6.41 us
    ppermute x6, starting transfers between devices, reduce_stats(): lax.ppermute(stats, axis, [(a, a ^ j * stride) for a in range(size)])  6.36 us
    ppermute x1, waiting for transfers between devices, on_device(): lax.ppermute(note, 'member', [(g, (g + shift) % members) for g in range(m...  4.36 us
    reduce_max x2, other arithmetic, local_stats(): local_peak = jnp.max(values, axis=1)  4.33 us
    ppermute x6, waiting for transfers between devices, reduce_stats(): lax.ppermute(stats, axis, [(a, a ^ j * stride) for a in range(size)])  3.5 us
  transfers between devices with their start and end apart: 9, of which 5 were waited for; matrix products, arithmetic and copies ran while one was open for 19% of the time, Pallas kernels for 0%

profile of v10, /device:TPU:0, one launch (start us, length us, event | category | flops | bytes accessed | tf_op | source)
XLA Modules:
  0.0 149.3 jit_solution(9143156757499976943)
XLA Ops:
  0.7 0.8 dynamic-slice_bitcast_fusion.1
  1.5 0.7 fusion.24
  2.2 24.7 %all-gather.5 = bf16[16,129,128]{2,1,0:T(8,128)(2,1)S(1)} all-gather(bf16[1,129,128]{2,1,0:T(8,128)(2,1)S(1)} %get-tuple-element.28), channel_id=3, replica_groups=mesh['member'=2,'vocab'=16] {'vocab'}, dimensions={0}, use_global_device_ids=true | all-gather | bytes 561408 | tf_op jit(solution)/shard_map/all_gather | solution.py:56
  28.2 0.3 fusion.12
  28.5 8.1 %fusion.53 = (f32[128]{0:T(128)S(1)}, f32[128,4008]{0,1:T(8,128)S(1)}) fusion(bf16[128,2048]{0,1:T(8,128)(2,1)S(1)} %bitcast.212, bf16[1,2048,4008]{1,2,0:T(8,128)(2,1)} %param.6), kind=kOutput, calls=%fused_computation.120 | convolution fusion | flops 2101859200 | bytes 18993664 | tf_op jit(solution)/shard_map/dot_general | solution.py:65
  36.6 1.8 %exponential_reduce_fusion.4 = (f32[128]{0:T(128)S(1)}, f32[128,4008]{0,1:T(8,128)}) fusion(f32[128,4008]{0,1:T(8,128)S(1)} %get-tuple-element.32, f32[128]{0:T(128)S(1)} %get-tuple-element.31, f32[]{:T(128)} %bitcast.209), kind=kLoop, calls=%fused_computation.14 | loop fusion | flops 1538944 | bytes 4105220 | tf_op jit(solution)/shard_map/reduce_sum | solution.py:12
  38.4 1.5 %collective-permute-start.1 = (f32[128,4008]{0,1:T(8,128)}, f32[128,4008]{0,1:T(8,128)}, u32[]{:S(2)}, u32[]{:S(2)}) collective-permute-start(f32[128,4008]{0,1:T(8,128)} %get-tuple-element.20), channel_id=1, source_target_pairs={{0,16},{16,0},{1,17},{17,1},{2,18},{18,2},{3,19},{19,3},{4,20},{20... | collective-permute-start | bytes 6156296 | tf_op jit(solution)/shard_map/ppermute | solution.py:78
  39.9 18.8 %all-gather.4 = bf16[16,129,128]{2,1,0:T(8,128)(2,1)S(1)} all-gather(bf16[1,129,128]{2,1,0:T(8,128)(2,1)S(1)} %get-tuple-element.30), channel_id=2, replica_groups=mesh['member'=2,'vocab'=16] {'vocab'}, dimensions={0}, use_global_device_ids=true | all-gather | bytes 561408 | tf_op jit(solution)/shard_map/all_gather | solution.py:56
  59.4 0.3 fusion.9
  59.7 8.1 %fusion.54 = (f32[128]{0:T(128)S(1)}, f32[128,4008]{0,1:T(8,128)S(1)}) fusion(bf16[128,2048]{0,1:T(8,128)(2,1)S(1)} %bitcast.213, bf16[1,2048,4008]{1,2,0:T(8,128)(2,1)} %param.6), kind=kOutput, calls=%fused_computation.121 | convolution fusion | flops 2101859200 | bytes 18993664 | tf_op jit(solution)/shard_map/dot_general | solution.py:65
  67.8 1.8 %broadcast_multiply_fusion.1 = (f32[128,4008]{0,1:T(8,128)}, f32[128]{0:T(128)S(1)}) fusion(f32[128,4008]{0,1:T(8,128)S(1)} %get-tuple-element.34, f32[]{:T(128)} %bitcast.211, f32[128]{0:T(128)S(1)} %get-tuple-element.33), kind=kLoop, calls=%fused_computation.42 | loop fusion | flops 1538944 | bytes 4105220 | tf_op jit(solution)/shard_map/mul | solution.py:78
  69.6 0.5 collective-permute-start
  70.1 20.5 %all-gather.6 = bf16[16,129,128]{2,1,0:T(8,128)(2,1)S(1)} all-gather(bf16[1,129,128]{2,1,0:T(8,128)(2,1)S(1)} %get-tuple-element.27), channel_id=4, replica_groups=mesh['member'=2,'vocab'=16] {'vocab'}, dimensions={0}, use_global_device_ids=true | all-gather | bytes 561408 | tf_op jit(solution)/shard_map/all_gather | solution.py:56
  91.2 19.1 %all-gather.7 = bf16[16,129,128]{2,1,0:T(8,128)(2,1)S(1)} all-gather(bf16[1,129,128]{2,1,0:T(8,128)(2,1)S(1)} %get-tuple-element.29), channel_id=5, replica_groups=mesh['member'=2,'vocab'=16] {'vocab'}, dimensions={0}, use_global_device_ids=true | all-gather | bytes 561408 | tf_op jit(solution)/shard_map/all_gather | solution.py:56
  111.0 0.3 fusion.15
  111.7 9.9 %fusion = f32[256,4008]{0,1:T(8,128)} fusion(bf16[1,2048,4008]{1,2,0:T(8,128)(2,1)} %param.6, bf16[128,2048]{0,1:T(8,128)(2,1)S(1)} %bitcast.215, bf16[128,2048]{0,1:T(8,128)(2,1)S(1)} %bitcast.214), kind=kOutput, calls=%fused_computation | convolution fusion | flops 4204789760 | bytes 21569536 | tf_op jit(solution)/shard_map/dot_general | solution.py:86
  121.6 1.5 %collective-permute-start.2 = (f32[3,256]{1,0:T(4,128)S(1)}, f32[3,256]{1,0:T(4,128)S(1)}, u32[]{:S(2)}, u32[]{:S(2)}) collective-permute-start(f32[3,256]{1,0:T(4,128)S(1)} %fusion.34), channel_id=1, source_target_pairs={{0,16},{16,0},{1,17},{17,1},{2,18},{18,2},{3,19},{19,3},{4,20},{20... | collective-permute-start | bytes 9224 | tf_op jit(solution)/shard_map/ppermute | solution.py:88
  123.2 2.1 %slice_reduce_fusion.1 = f32[128]{0:T(128)S(1)} fusion(f32[256,4008]{0,1:T(8,128)} %fusion), kind=kLoop, calls=%fused_computation.17 | loop fusion | flops 512896 | bytes 2052608 | tf_op jit(solution)/shard_map/reduce_max | solution.py:11
  125.3 4.4 %collective-permute-done.2 = f32[3,256]{1,0:T(4,128)S(1)} collective-permute-done((f32[3,256]{1,0:T(4,128)S(1)}, f32[3,256]{1,0:T(4,128)S(1)}, u32[]{:S(2)}, u32[]{:S(2)}) %collective-permute-start.2) | collective-permute-done | bytes 3104 | tf_op jit(solution)/shard_map/ppermute | solution.py:88
  129.7 3.5 %exponential_reduce_fusion.3 = (f32[128]{0:T(128)S(1)}, f32[128]{0:T(128)S(1)}, f32[128]{0:T(128)S(1)}, f32[128,4008]{0,1:T(8,128)S(1)}) fusion(f32[256,4008]{0,1:T(8,128)} %fusion, f32[128]{0:T(128)S(1)} %slice_reduce_fusion.1, f32[128,4008]{0,1:T(8,128)} %collective-permute-done, f32[]{:T(128)} %bitcast.206), kind=kLoop, calls=%fused_computation.11 | loop fusion | flops 3077760 | bytes 8210436 | tf_op jit(solution)/shard_map/reduce_sum | solution.py:12
  133.2 0.4 copy-done
  133.6 2.2 %fusion.52 = (f32[128]{0:T(128)S(1)}, f32[128,4008]{0,1:T(8,128)S(1)}, f32[128]{0:T(128)S(1)}) fusion(f32[128,4008]{0,1:T(8,128)} %collective-permute-done.1, f32[256,4008]{0,1:T(8,128)S(1)} %copy-done, f32[]{:T(128)} %bitcast.210, f32[128]{0:T(128)S(1)} %get-tuple-element.7), kind=kLoop, calls=%fused_computation.119 | loop fusion | flops 2564864 | bytes 6157828 | tf_op jit(solution)/shard_map/reduce_max | solution.py:11
  135.9 0.6 exponential_reduce_fusion
  136.4 0.6 exponential_reduce_fusion.2
  137.1 1.2 collective-permute-start.4
  138.3 0.6 collective-permute-start.3
  138.9 1.2 collective-permute-done.5
  140.2 0.7 collective-permute-done.4
  141.1 4.2 %collective-permute-start.6 = (f32[2,3,256]{2,1,0:T(4,128)S(1)}, f32[2,3,256]{2,1,0:T(4,128)S(1)}, u32[]{:S(2)}, u32[]{:S(2)}) collective-permute-start(f32[2,3,256]{2,1,0:T(4,128)S(1)} %pad_maximum_fusion.5), channel_id=1, source_target_pairs={{0,4},{1,5},{2,6},{3,7},{4,0},{5,1},{6,2},{7,3},{8,12},{9,13},{10,... | collective-permute-start | bytes 18440 | tf_op jit(solution)/shard_map/ppermute | solution.py:27
  145.3 1.1 collective-permute-done.8
  146.4 0.6 collective-permute-done.6
  147.0 2.3 %fusion.6 = f32[256,4008]{0,1:T(8,128)} fusion(f32[128,4008]{0,1:T(8,128)S(1)} %get-tuple-element.13, f32[128,4008]{0,1:T(8,128)S(1)} %get-tuple-element.16, f32[256]{0:T(256)S(1)} %sub.133, f32[256]{0:T(256)S(1)} %bitcast.217), kind=kLoop, calls=%fused_computation.7 | loop fusion | flops 3078144 | bytes 8210432 | tf_op jit(solution)/shard_map/sub | solution.py:110
  (48 shorter events, 3.4 us)
Async XLA Ops:
  38.4 94.8 %collective-permute-start.1 = (f32[128,4008]{0,1:T(8,128)}, f32[128,4008]{0,1:T(8,128)}, u32[]{:S(2)}, u32[]{:S(2)}) collective-permute-start(f32[128,4008]{0,1:T(8,128)} %get-tuple-element.20), channel_id=1, source_target_pairs={{0,16},{16,0},{1,17},{17,1},{2,18},{18,2},{3,19},{19,3},{4,20},{20... | collective-permute-start | bytes 6156296 | tf_op jit(solution)/shard_map/ppermute | solution.py:78
  69.6 60.1 %collective-permute-start = (f32[128,4008]{0,1:T(8,128)}, f32[128,4008]{0,1:T(8,128)}, u32[]{:S(2)}, u32[]{:S(2)}) collective-permute-start(f32[128,4008]{0,1:T(8,128)} %get-tuple-element.17), channel_id=1, source_target_pairs={{0,16},{16,0},{1,17},{17,1},{2,18},{18,2},{3,19},{19,3},{4,20},{20... | collective-permute-start | bytes 6156296 | tf_op jit(solution)/shard_map/ppermute | solution.py:78
  121.6 8.0 %collective-permute-start.2 = (f32[3,256]{1,0:T(4,128)S(1)}, f32[3,256]{1,0:T(4,128)S(1)}, u32[]{:S(2)}, u32[]{:S(2)}) collective-permute-start(f32[3,256]{1,0:T(4,128)S(1)} %fusion.34), channel_id=1, source_target_pairs={{0,16},{16,0},{1,17},{17,1},{2,18},{18,2},{3,19},{19,3},{4,20},{20... | collective-permute-start | bytes 9224 | tf_op jit(solution)/shard_map/ppermute | solution.py:88
  129.7 4.0 %copy-start = (f32[256,4008]{0,1:T(8,128)S(1)}, f32[256,4008]{0,1:T(8,128)}, u32[]{:S(2)}) copy-start(f32[256,4008]{0,1:T(8,128)} %fusion) | copy-start | bytes 12312580
  137.0 3.1 %collective-permute-start.5 = (f32[2,3,256]{2,1,0:T(4,128)S(1)}, f32[2,3,256]{2,1,0:T(4,128)S(1)}, u32[]{:S(2)}, u32[]{:S(2)}) collective-permute-start(f32[2,3,256]{2,1,0:T(4,128)S(1)} %pad_maximum_fusion.4), channel_id=1, source_target_pairs={{0,3},{1,2},{2,1},{3,0},{4,7},{5,6},{6,5},{7,4},{8,11},{9,10},{10,... | collective-permute-start | bytes 18440 | tf_op jit(solution)/shard_map/ppermute | solution.py:27
  137.1 3.7 %collective-permute-start.4 = (f32[2,3,256]{2,1,0:T(4,128)S(1)}, f32[2,3,256]{2,1,0:T(4,128)S(1)}, u32[]{:S(2)}, u32[]{:S(2)}) collective-permute-start(f32[2,3,256]{2,1,0:T(4,128)S(1)} %pad_maximum_fusion.4), channel_id=1, source_target_pairs={{0,2},{1,3},{2,0},{3,1},{4,6},{5,7},{6,4},{7,5},{8,10},{9,11},{10,... | collective-permute-start | bytes 18440 | tf_op jit(solution)/shard_map/ppermute | solution.py:27
  138.3 2.5 %collective-permute-start.3 = (f32[2,3,256]{2,1,0:T(4,128)S(1)}, f32[2,3,256]{2,1,0:T(4,128)S(1)}, u32[]{:S(2)}, u32[]{:S(2)}) collective-permute-start(f32[2,3,256]{2,1,0:T(4,128)S(1)} %pad_maximum_fusion.4), channel_id=1, source_target_pairs={{0,1},{1,0},{2,3},{3,2},{4,5},{5,4},{6,7},{7,6},{8,9},{9,8},{10,11... | collective-permute-start | bytes 18440 | tf_op jit(solution)/shard_map/ppermute | solution.py:27
  140.9 5.5 %collective-permute-start.8 = (f32[2,3,256]{2,1,0:T(4,128)S(1)}, f32[2,3,256]{2,1,0:T(4,128)S(1)}, u32[]{:S(2)}, u32[]{:S(2)}) collective-permute-start(f32[2,3,256]{2,1,0:T(4,128)S(1)} %pad_maximum_fusion.5), channel_id=1, source_target_pairs={{0,12},{1,13},{2,14},{3,15},{4,8},{5,9},{6,10},{7,11},{8,4},{9,5},... | collective-permute-start | bytes 18440 | tf_op jit(solution)/shard_map/ppermute | solution.py:27
  140.9 5.4 %collective-permute-start.7 = (f32[2,3,256]{2,1,0:T(4,128)S(1)}, f32[2,3,256]{2,1,0:T(4,128)S(1)}, u32[]{:S(2)}, u32[]{:S(2)}) collective-permute-start(f32[2,3,256]{2,1,0:T(4,128)S(1)} %pad_maximum_fusion.5), channel_id=1, source_target_pairs={{0,8},{1,9},{2,10},{3,11},{4,12},{5,13},{6,14},{7,15},{8,0},{9,1},... | collective-permute-start | bytes 18440 | tf_op jit(solution)/shard_map/ppermute | solution.py:27
  141.1 5.8 %collective-permute-start.6 = (f32[2,3,256]{2,1,0:T(4,128)S(1)}, f32[2,3,256]{2,1,0:T(4,128)S(1)}, u32[]{:S(2)}, u32[]{:S(2)}) collective-permute-start(f32[2,3,256]{2,1,0:T(4,128)S(1)} %pad_maximum_fusion.5), channel_id=1, source_target_pairs={{0,4},{1,5},{2,6},{3,7},{4,0},{5,1},{6,2},{7,3},{8,12},{9,13},{10,... | collective-permute-start | bytes 18440 | tf_op jit(solution)/shard_map/ppermute | solution.py:27
  147.0 2.3 %copy-start.1 = (f32[256]{0:T(256)}, f32[256]{0:T(256)S(1)}, u32[]{:S(2)}) copy-start(f32[256]{0:T(256)S(1)} %sub.133) | copy-start | bytes 3076

commit v11 on v10

--- a/solution.py
+++ b/solution.py
@@ -72,19 +72,22 @@
         target = (me + shift) % members
         perm = [(g, (g + shift) % members) for g in range(members)]
         parts = []
-        piece_stats = []
+        sent = []
         for k in range(send_pieces):
             logits = logits_of(target * share + k * sub, sub)
             parts.append(lax.ppermute(w * logits, "member", perm))
-            piece_stats.append(local_stats(logits))
-        stats_rows = jnp.concatenate(piece_stats, axis=1)
-        note = jnp.concatenate([stats_rows, jnp.broadcast_to(w, (1, share))], axis=0)
+            sent.append(logits)
         received.append(parts)
-        notes.append((perm, note))
+        notes.append(sent)
     own_normed = jnp.concatenate(
         [normed_of(me * share + k * sub, sub) for k in range(send_pieces)], axis=0)
     own_logits = jnp.dot(own_normed, weights, preferred_element_type=jnp.float32)
-    notes, own_logits = lax.optimization_barrier(([note for _, note in notes], own_logits))
+    notes, own_logits = lax.optimization_barrier((notes, own_logits))
+    notes = [
+        jnp.concatenate([jnp.concatenate([local_stats(x) for x in sent], axis=1),
+                         jnp.broadcast_to(w, (1, share))], axis=0)
+        for sent in notes
+    ]
     notes = [lax.ppermute(note, "member", [(g, (g + shift) % members) for g in range(members)])
              for shift, note in zip(range(1, members), notes)]
 

time: 150 us -> 154 us (1.027)
  matrix products: 26.1 us -> 32.1 us
  waiting for transfers between devices: 7.86 us -> 5.45 us
    dot_general x2, matrix products: 16.1 us -> 19.8 us  [logits_of(): jnp.dot(normed_of(first_row, rows), weights, preferred_element_type=jnp.f...]
    ppermute x1, waiting for transfers between devices: 4.36 us -> 1.55 us  [on_device(): lax.ppermute(note, 'member', [(g, (g + shift) % members) for g in range(m...]
    dot_general x1, matrix products: 9.95 us -> 12.3 us  [on_device(): jnp.dot(own_normed, weights, preferred_element_type=jnp.float32)]
    mul x1 -> x0, other arithmetic: 1.79 us -> none  [on_device(): parts.append(lax.ppermute(w * logits, 'member', perm))]
    reduce_max x2 -> x4, other arithmetic: 4.33 us -> 5.41 us  [local_stats(): local_peak = jnp.max(values, axis=1)]
  transfers between devices with their start and end apart: 9 -> 9, of which waited for: 5 -> 5; matrix products, arithmetic and copies ran while one was open for 19% -> 24% of each run, Pallas kernels for 0% -> 0%
where the time goes in v11:
time: 154 us
  blocking collectives  83.1 us (54%)
  matrix products  32.1 us (21%)
  other arithmetic  17.4 us (11%)
  starting transfers between devices  9.98 us (6%)
  waiting for transfers between devices  5.45 us (4%)
  local copies, waits for them, and re-layouts  4.16 us (3%)
    all_gather x4, blocking collectives, normed_of(): gathered = lax.all_gather(packed, 'vocab', axis=0, tiled=False)  83.1 us
    dot_general x2, matrix products, logits_of(): jnp.dot(normed_of(first_row, rows), weights, preferred_element_type=jnp.f...  19.8 us
    dot_general x1, matrix products, on_device(): jnp.dot(own_normed, weights, preferred_element_type=jnp.float32)  12.3 us
    ppermute x6, starting transfers between devices, reduce_stats(): lax.ppermute(stats, axis, [(a, a ^ j * stride) for a in range(size)])  6.38 us
    reduce_sum x4, other arithmetic, local_stats(): local_sum = jnp.sum(jnp.exp(values - local_peak[:, None]), axis=1)  5.56 us
    reduce_max x4, other arithmetic, local_stats(): local_peak = jnp.max(values, axis=1)  5.41 us
    ppermute x6, waiting for transfers between devices, reduce_stats(): lax.ppermute(stats, axis, [(a, a ^ j * stride) for a in range(size)])  3.89 us
  transfers between devices with their start and end apart: 9, of which 5 were waited for; matrix products, arithmetic and copies ran while one was open for 24% of the time, Pallas kernels for 0%

profile of v11, /device:TPU:0, one launch (start us, length us, event | category | flops | bytes accessed | tf_op | source)
XLA Modules:
  0.0 153.7 jit_solution(8857187761420390060)
XLA Ops:
  0.7 0.8 dynamic-slice_bitcast_fusion.1
  1.5 0.7 fusion.24
  2.2 24.7 %all-gather.4 = bf16[16,129,128]{2,1,0:T(8,128)(2,1)S(1)} all-gather(bf16[1,129,128]{2,1,0:T(8,128)(2,1)S(1)} %get-tuple-element.28), channel_id=2, replica_groups=mesh['member'=2,'vocab'=16] {'vocab'}, dimensions={0}, use_global_device_ids=true | all-gather | bytes 561408 | tf_op jit(solution)/shard_map/all_gather | solution.py:56
  28.5 9.5 %broadcast_multiply_fusion.1 = (f32[128,4008]{0,1:T(8,128)}, f32[128,4008]{0,1:T(8,128)S(1)}) fusion(f32[]{:T(128)} %bitcast.219, bf16[128,2048]{0,1:T(8,128)(2,1)S(1)} %bitcast.220, bf16[1,2048,4008]{1,2,0:T(8,128)(2,1)} %param.6), kind=kOutput, calls=%fused_computation.42 | convolution fusion | flops 2101859328 | bytes 21045252 | tf_op jit(solution)/shard_map/dot_general | solution.py:65
  38.1 1.5 collective-permute-start
  39.6 18.8 %all-gather.5 = bf16[16,129,128]{2,1,0:T(8,128)(2,1)S(1)} all-gather(bf16[1,129,128]{2,1,0:T(8,128)(2,1)S(1)} %get-tuple-element.26), channel_id=3, replica_groups=mesh['member'=2,'vocab'=16] {'vocab'}, dimensions={0}, use_global_device_ids=true | all-gather | bytes 561408 | tf_op jit(solution)/shard_map/all_gather | solution.py:56
  59.4 10.3 %broadcast_multiply_fusion = (f32[128,4008]{0,1:T(8,128)}, f32[128,4008]{0,1:T(8,128)}) fusion(f32[]{:T(128)} %bitcast.217, bf16[128,2048]{0,1:T(8,128)(2,1)S(1)} %bitcast.221, bf16[1,2048,4008]{1,2,0:T(8,128)(2,1)} %param.6), kind=kOutput, calls=%fused_computation.41 | convolution fusion | flops 2101859328 | bytes 21045252 | tf_op jit(solution)/shard_map/dot_general | solution.py:65
  70.2 20.5 %all-gather.6 = bf16[16,129,128]{2,1,0:T(8,128)(2,1)S(1)} all-gather(bf16[1,129,128]{2,1,0:T(8,128)(2,1)S(1)} %get-tuple-element.25), channel_id=4, replica_groups=mesh['member'=2,'vocab'=16] {'vocab'}, dimensions={0}, use_global_device_ids=true | all-gather | bytes 561408 | tf_op jit(solution)/shard_map/all_gather | solution.py:56
  90.8 19.2 %all-gather.7 = bf16[16,129,128]{2,1,0:T(8,128)(2,1)S(1)} all-gather(bf16[1,129,128]{2,1,0:T(8,128)(2,1)S(1)} %get-tuple-element.27), channel_id=5, replica_groups=mesh['member'=2,'vocab'=16] {'vocab'}, dimensions={0}, use_global_device_ids=true | all-gather | bytes 561408 | tf_op jit(solution)/shard_map/all_gather | solution.py:56
  109.9 0.8 slice.129
  111.4 1.4 copy.62
  113.1 1.2 fusion.15
  114.6 12.3 %fusion = f32[256,4008]{0,1:T(8,128)} fusion(bf16[1,2048,4008]{1,2,0:T(8,128)(2,1)} %param.6, bf16[128,2048]{0,1:T(8,128)(2,1)S(1)} %bitcast.223, bf16[128,2048]{0,1:T(8,128)(2,1)} %bitcast.222), kind=kOutput, calls=%fused_computation | convolution fusion | flops 4204789760 | bytes 21569536 | tf_op jit(solution)/shard_map/dot_general | solution.py:84
  126.8 0.5 reduce_max.58
  127.4 2.1 %reduce_max.59 = f32[128]{0:T(128)S(1)} reduce(f32[128,4008]{0,1:T(8,128)} %get-tuple-element.7, f32[]{:T(128)} %constant.45.clone.1), dimensions={1}, to_apply=%region_14.15 | reduce | flops 512896 | bytes 2052612 | tf_op jit(solution)/shard_map/reduce_max | solution.py:11
  129.5 2.3 %exponential_reduce_fusion = (f32[128]{0:T(128)S(1)}, f32[128]{0:T(128)S(1)}) fusion(f32[128,4008]{0,1:T(8,128)} %get-tuple-element.7, f32[128]{0:T(128)S(1)} %reduce_max.59, f32[128,4008]{0,1:T(8,128)S(1)} %get-tuple-element.6, f32[128]{0:T(128)S(1)} %reduce_max.58), kind=kLoop, calls=%fused_computation.8 | loop fusion | flops 2051840 | bytes 4106240 | tf_op jit(solution)/shard_map/reduce_sum | solution.py:12
  131.8 1.6 %collective-permute-start.2 = (f32[3,256]{1,0:T(4,128)S(1)}, f32[3,256]{1,0:T(4,128)S(1)}, u32[]{:S(2)}, u32[]{:S(2)}) collective-permute-start(f32[3,256]{1,0:T(4,128)S(1)} %fusion.40), channel_id=1, source_target_pairs={{0,16},{16,0},{1,17},{17,1},{2,18},{18,2},{3,19},{19,3},{4,20},{20... | collective-permute-start | bytes 9224 | tf_op jit(solution)/shard_map/ppermute | solution.py:91
  133.4 0.5 slice_reduce_fusion.1
  133.9 1.6 %collective-permute-done.2 = f32[3,256]{1,0:T(4,128)S(1)} collective-permute-done((f32[3,256]{1,0:T(4,128)S(1)}, f32[3,256]{1,0:T(4,128)S(1)}, u32[]{:S(2)}, u32[]{:S(2)}) %collective-permute-start.2) | collective-permute-done | bytes 3104 | tf_op jit(solution)/shard_map/ppermute | solution.py:91
  135.5 2.2 %exponential_reduce_fusion.5 = (f32[128]{0:T(128)S(1)}, f32[128]{0:T(128)S(1)}, f32[128]{0:T(128)S(1)}, f32[128,4008]{0,1:T(8,128)S(1)}) fusion(f32[256,4008]{0,1:T(8,128)S(1)} %copy-done, f32[128]{0:T(128)S(1)} %slice_reduce_fusion.1, f32[128,4008]{0,1:T(8,128)} %collective-permute-done, f32[]{:T(128)} %bitcast.214), kind=kLoop, calls=%fused_computation.13 | loop fusion | flops 3077760 | bytes 8210436 | tf_op jit(solution)/shard_map/reduce_sum | solution.py:12
  137.7 0.6 exponential_reduce_fusion.4
  138.2 2.2 %fusion.55 = (f32[128]{0:T(128)S(1)}, f32[128,4008]{0,1:T(8,128)S(1)}, f32[128]{0:T(128)S(1)}) fusion(f32[128,4008]{0,1:T(8,128)} %collective-permute-done.1, f32[256,4008]{0,1:T(8,128)S(1)} %copy-done, f32[]{:T(128)} %bitcast.218, f32[128]{0:T(128)S(1)} %get-tuple-element.9), kind=kLoop, calls=%fused_computation.123 | loop fusion | flops 2564864 | bytes 6157828 | tf_op jit(solution)/shard_map/reduce_max | solution.py:11
  140.4 0.6 exponential_reduce_fusion.2
  141.0 0.5 collective-permute-start.5
  141.6 1.3 collective-permute-start.4
  143.0 1.2 collective-permute-done.5
  144.2 1.1 collective-permute-done.4
  145.3 0.6 collective-permute-start.8
  145.9 3.8 %collective-permute-start.6 = (f32[2,3,256]{2,1,0:T(4,128)S(1)}, f32[2,3,256]{2,1,0:T(4,128)S(1)}, u32[]{:S(2)}, u32[]{:S(2)}) collective-permute-start(f32[2,3,256]{2,1,0:T(4,128)S(1)} %pad_maximum_fusion.4), channel_id=1, source_target_pairs={{0,4},{1,5},{2,6},{3,7},{4,0},{5,1},{6,2},{7,3},{8,12},{9,13},{10,... | collective-permute-start | bytes 18440 | tf_op jit(solution)/shard_map/ppermute | solution.py:27
  149.7 1.1 collective-permute-done.8
  150.8 0.6 collective-permute-done.6
  151.4 2.3 %fusion.6 = f32[256,4008]{0,1:T(8,128)} fusion(f32[128,4008]{0,1:T(8,128)S(1)} %get-tuple-element.15, f32[128,4008]{0,1:T(8,128)S(1)} %get-tuple-element.18, f32[256]{0:T(256)S(1)} %sub.133, f32[256]{0:T(256)S(1)} %bitcast.225), kind=kLoop, calls=%fused_computation.7 | loop fusion | flops 3078144 | bytes 8210432 | tf_op jit(solution)/shard_map/sub | solution.py:113
  (48 shorter events, 4.0 us)
Async XLA Ops:
  38.1 97.4 %collective-permute-start = (f32[128,4008]{0,1:T(8,128)}, f32[128,4008]{0,1:T(8,128)}, u32[]{:S(2)}, u32[]{:S(2)}) collective-permute-start(f32[128,4008]{0,1:T(8,128)} %get-tuple-element.31), channel_id=1, source_target_pairs={{0,16},{16,0},{1,17},{17,1},{2,18},{18,2},{3,19},{19,3},{4,20},{20... | collective-permute-start | bytes 6156296 | tf_op jit(solution)/shard_map/ppermute | solution.py:78
  69.7 68.5 %collective-permute-start.1 = (f32[128,4008]{0,1:T(8,128)}, f32[128,4008]{0,1:T(8,128)}, u32[]{:S(2)}, u32[]{:S(2)}) collective-permute-start(f32[128,4008]{0,1:T(8,128)} %get-tuple-element.29), channel_id=1, source_target_pairs={{0,16},{16,0},{1,17},{17,1},{2,18},{18,2},{3,19},{19,3},{4,20},{20... | collective-permute-start | bytes 6156296 | tf_op jit(solution)/shard_map/ppermute | solution.py:78
  129.5 3.9 %copy-start = (f32[256,4008]{0,1:T(8,128)S(1)}, f32[256,4008]{0,1:T(8,128)}, u32[]{:S(2)}) copy-start(f32[256,4008]{0,1:T(8,128)} %fusion) | copy-start | bytes 12312580
  131.8 3.7 %collective-permute-start.2 = (f32[3,256]{1,0:T(4,128)S(1)}, f32[3,256]{1,0:T(4,128)S(1)}, u32[]{:S(2)}, u32[]{:S(2)}) collective-permute-start(f32[3,256]{1,0:T(4,128)S(1)} %fusion.40), channel_id=1, source_target_pairs={{0,16},{16,0},{1,17},{17,1},{2,18},{18,2},{3,19},{19,3},{4,20},{20... | collective-permute-start | bytes 9224 | tf_op jit(solution)/shard_map/ppermute | solution.py:91
  141.0 3.1 %collective-permute-start.5 = (f32[2,3,256]{2,1,0:T(4,128)S(1)}, f32[2,3,256]{2,1,0:T(4,128)S(1)}, u32[]{:S(2)}, u32[]{:S(2)}) collective-permute-start(f32[2,3,256]{2,1,0:T(4,128)S(1)} %copy.50), channel_id=1, source_target_pairs={{0,3},{1,2},{2,1},{3,0},{4,7},{5,6},{6,5},{7,4},{8,11},{9,10},{10,... | collective-permute-start | bytes 18440 | tf_op jit(solution)/shard_map/ppermute | solution.py:27
  141.6 3.7 %collective-permute-start.4 = (f32[2,3,256]{2,1,0:T(4,128)S(1)}, f32[2,3,256]{2,1,0:T(4,128)S(1)}, u32[]{:S(2)}, u32[]{:S(2)}) collective-permute-start(f32[2,3,256]{2,1,0:T(4,128)S(1)} %copy.50), channel_id=1, source_target_pairs={{0,2},{1,3},{2,0},{3,1},{4,6},{5,7},{6,4},{7,5},{8,10},{9,11},{10,... | collective-permute-start | bytes 18440 | tf_op jit(solution)/shard_map/ppermute | solution.py:27
  142.9 2.4 %collective-permute-start.3 = (f32[2,3,256]{2,1,0:T(4,128)S(1)}, f32[2,3,256]{2,1,0:T(4,128)S(1)}, u32[]{:S(2)}, u32[]{:S(2)}) collective-permute-start(f32[2,3,256]{2,1,0:T(4,128)S(1)} %copy.50), channel_id=1, source_target_pairs={{0,1},{1,0},{2,3},{3,2},{4,5},{5,4},{6,7},{7,6},{8,9},{9,8},{10,11... | collective-permute-start | bytes 18440 | tf_op jit(solution)/shard_map/ppermute | solution.py:27
  145.3 5.5 %collective-permute-start.8 = (f32[2,3,256]{2,1,0:T(4,128)S(1)}, f32[2,3,256]{2,1,0:T(4,128)S(1)}, u32[]{:S(2)}, u32[]{:S(2)}) collective-permute-start(f32[2,3,256]{2,1,0:T(4,128)S(1)} %pad_maximum_fusion.4), channel_id=1, source_target_pairs={{0,12},{1,13},{2,14},{3,15},{4,8},{5,9},{6,10},{7,11},{8,4},{9,5},... | collective-permute-start | bytes 18440 | tf_op jit(solution)/shard_map/ppermute | solution.py:27
  145.9 4.9 %collective-permute-start.7 = (f32[2,3,256]{2,1,0:T(4,128)S(1)}, f32[2,3,256]{2,1,0:T(4,128)S(1)}, u32[]{:S(2)}, u32[]{:S(2)}) collective-permute-start(f32[2,3,256]{2,1,0:T(4,128)S(1)} %pad_maximum_fusion.4), channel_id=1, source_target_pairs={{0,8},{1,9},{2,10},{3,11},{4,12},{5,13},{6,14},{7,15},{8,0},{9,1},... | collective-permute-start | bytes 18440 | tf_op jit(solution)/shard_map/ppermute | solution.py:27
  145.9 5.4 %collective-permute-start.6 = (f32[2,3,256]{2,1,0:T(4,128)S(1)}, f32[2,3,256]{2,1,0:T(4,128)S(1)}, u32[]{:S(2)}, u32[]{:S(2)}) collective-permute-start(f32[2,3,256]{2,1,0:T(4,128)S(1)} %pad_maximum_fusion.4), channel_id=1, source_target_pairs={{0,4},{1,5},{2,6},{3,7},{4,0},{5,1},{6,2},{7,3},{8,12},{9,13},{10,... | collective-permute-start | bytes 18440 | tf_op jit(solution)/shard_map/ppermute | solution.py:27
  151.4 2.3 %copy-start.1 = (f32[256]{0:T(256)}, f32[256]{0:T(256)S(1)}, u32[]{:S(2)}) copy-start(f32[256]{0:T(256)S(1)} %sub.133) | copy-start | bytes 3076

commit v12 on v10

--- a/solution.py
+++ b/solution.py
@@ -74,6 +74,15 @@
         parts = []
         piece_stats = []
         for k in range(send_pieces):
+            if shift == 1 and k == 0:
+                normed = normed_of(target * share, sub)
+                half = weights.shape[1] // 2
+                halves = [jnp.dot(normed, columns, preferred_element_type=jnp.float32)
+                          for columns in (weights[:, :half], weights[:, half:])]
+                sent_halves = [lax.ppermute(w * x, "member", perm) for x in halves]
+                parts.append(jnp.concatenate(sent_halves, axis=1))
+                piece_stats.append(local_stats(jnp.concatenate(halves, axis=1)))
+                continue
             logits = logits_of(target * share + k * sub, sub)
             parts.append(lax.ppermute(w * logits, "member", perm))
             piece_stats.append(local_stats(logits))

time: 150 us -> 151 us (level)
  matrix products: 26.1 us -> 31.6 us
  waiting for transfers between devices: 7.86 us -> 4.86 us
    dot_general x0 -> x2, matrix products: none -> 13.6 us  [on_device(): jnp.dot(normed, columns, preferred_element_type=jnp.float32)]
    dot_general x2 -> x1, matrix products: 16.1 us -> 8.06 us  [logits_of(): jnp.dot(normed_of(first_row, rows), weights, preferred_element_type=jnp.f...]
    ppermute x1, waiting for transfers between devices: 4.36 us -> 0.99 us  [on_device(): lax.ppermute(note, 'member', [(g, (g + shift) % members) for g in range(m...]
    ppermute x0 -> x2, starting transfers between devices: none -> 2.03 us  [on_device(): sent_halves = [lax.ppermute(w * x, 'member', perm) for x in halves]]
    mul x1 -> x0, other arithmetic: 1.79 us -> none  [on_device(): parts.append(lax.ppermute(w * logits, 'member', perm))]
    reduce_sum x4 -> x5, other arithmetic: 6.41 us -> 6.98 us  [local_stats(): local_sum = jnp.sum(jnp.exp(values - local_peak[:, None]), axis=1)]
    reduce_max x2 -> x3, other arithmetic: 4.33 us -> 4.34 us  [local_stats(): local_peak = jnp.max(values, axis=1)]
  transfers between devices with their start and end apart: 9 -> 10, of which waited for: 5 -> 5; matrix products, arithmetic and copies ran while one was open for 19% -> 24% of each run, Pallas kernels for 0% -> 0%
where the time goes in v12:
time: 151 us
  blocking collectives  83.1 us (55%)
  matrix products  31.6 us (21%)
  other arithmetic  17 us (11%)
  starting transfers between devices  10.5 us (7%)
  waiting for transfers between devices  4.86 us (3%)
  local copies, waits for them, and re-layouts  2.41 us (2%)
  between operations  1.52 us (1%)
    all_gather x4, blocking collectives, normed_of(): gathered = lax.all_gather(packed, 'vocab', axis=0, tiled=False)  83.1 us
    dot_general x2, matrix products, on_device(): jnp.dot(normed, columns, preferred_element_type=jnp.float32)  13.6 us
    dot_general x1, matrix products, on_device(): jnp.dot(own_normed, weights, preferred_element_type=jnp.float32)  9.94 us
    dot_general x1, matrix products, logits_of(): jnp.dot(normed_of(first_row, rows), weights, preferred_element_type=jnp.f...  8.06 us
    reduce_sum x5, other arithmetic, local_stats(): local_sum = jnp.sum(jnp.exp(values - local_peak[:, None]), axis=1)  6.98 us
    ppermute x6, starting transfers between devices, reduce_stats(): lax.ppermute(stats, axis, [(a, a ^ j * stride) for a in range(size)])  6.41 us
    reduce_max x3, other arithmetic, local_stats(): local_peak = jnp.max(values, axis=1)  4.34 us
    ppermute x6, waiting for transfers between devices, reduce_stats(): lax.ppermute(stats, axis, [(a, a ^ j * stride) for a in range(size)])  3.85 us
  transfers between devices with their start and end apart: 10, of which 5 were waited for; matrix products, arithmetic and copies ran while one was open for 24% of the time, Pallas kernels for 0%

profile of v12, /device:TPU:0, one launch (start us, length us, event | category | flops | bytes accessed | tf_op | source)
XLA Modules:
  0.0 151.0 jit_solution(7664358872453699469)
XLA Ops:
  0.7 0.8 dynamic-slice_bitcast_fusion.1
  1.5 0.7 fusion.25
  2.2 24.7 %all-gather.4 = bf16[16,129,128]{2,1,0:T(8,128)(2,1)S(1)} all-gather(bf16[1,129,128]{2,1,0:T(8,128)(2,1)S(1)} %get-tuple-element.32), channel_id=2, replica_groups=mesh['member'=2,'vocab'=16] {'vocab'}, dimensions={0}, use_global_device_ids=true | all-gather | bytes 561408 | tf_op jit(solution)/shard_map/all_gather | solution.py:56
  28.5 6.7 %broadcast_multiply_fusion.1 = (f32[128,2004]{0,1:T(8,128)}, f32[128]{0:T(128)S(1)}, f32[128,2004]{0,1:T(8,128)S(1)}) fusion(f32[]{:T(128)} %bitcast.209, bf16[128,2048]{0,1:T(8,128)(2,1)S(1)} %bitcast.215, bf16[2048,4008]{0,1:T(8,128)(2,1)} %bitcast.210), kind=kOutput, calls=%fused_computation.43 | convolution fusion | flops 1051186048 | bytes 10802176 | tf_op jit(solution)/shard_map/dot_general | solution.py:80
  35.2 1.5 %collective-permute-start.1 = (f32[128,2004]{0,1:T(8,128)}, f32[128,2004]{0,1:T(8,128)}, u32[]{:S(2)}, u32[]{:S(2)}) collective-permute-start(f32[128,2004]{0,1:T(8,128)} %get-tuple-element.21), channel_id=1, source_target_pairs={{0,16},{16,0},{1,17},{17,1},{2,18},{18,2},{3,19},{19,3},{4,20},{20... | collective-permute-start | bytes 3078152 | tf_op jit(solution)/shard_map/ppermute | solution.py:82
  36.8 6.9 %broadcast_multiply_fusion.2 = (f32[128,2004]{0,1:T(8,128)}, f32[128]{0:T(128)S(1)}, f32[128,2004]{0,1:T(8,128)}) fusion(f32[]{:T(128)} %bitcast.205, bf16[128,2048]{0,1:T(8,128)(2,1)S(1)} %bitcast.216, bf16[2048,4008]{0,1:T(8,128)(2,1)} %bitcast.211), kind=kOutput, calls=%fused_computation.44 | convolution fusion | flops 1051186048 | bytes 10802176 | tf_op jit(solution)/shard_map/dot_general | solution.py:80
  43.7 0.5 collective-permute-start
  44.2 18.8 %all-gather.5 = bf16[16,129,128]{2,1,0:T(8,128)(2,1)S(1)} all-gather(bf16[1,129,128]{2,1,0:T(8,128)(2,1)S(1)} %get-tuple-element.30), channel_id=3, replica_groups=mesh['member'=2,'vocab'=16] {'vocab'}, dimensions={0}, use_global_device_ids=true | all-gather | bytes 561408 | tf_op jit(solution)/shard_map/all_gather | solution.py:56
  63.7 0.3 fusion.12
  64.0 8.1 %fusion.57 = (f32[128]{0:T(128)S(1)}, f32[128,4008]{0,1:T(8,128)S(1)}) fusion(bf16[128,2048]{0,1:T(8,128)(2,1)S(1)} %bitcast.212, bf16[1,2048,4008]{1,2,0:T(8,128)(2,1)} %param.6), kind=kOutput, calls=%fused_computation.125 | convolution fusion | flops 2101859200 | bytes 18993664 | tf_op jit(solution)/shard_map/dot_general | solution.py:65
  72.1 1.8 %exponential_reduce_fusion.4 = (f32[128]{0:T(128)S(1)}, f32[128,4008]{0,1:T(8,128)}) fusion(f32[128,4008]{0,1:T(8,128)S(1)} %get-tuple-element.34, f32[128]{0:T(128)S(1)} %get-tuple-element.33, f32[]{:T(128)} %bitcast.207), kind=kLoop, calls=%fused_computation.15 | loop fusion | flops 1538944 | bytes 4105220 | tf_op jit(solution)/shard_map/reduce_sum | solution.py:12
  73.9 1.5 %collective-permute-start.2 = (f32[128,4008]{0,1:T(8,128)}, f32[128,4008]{0,1:T(8,128)}, u32[]{:S(2)}, u32[]{:S(2)}) collective-permute-start(f32[128,4008]{0,1:T(8,128)} %get-tuple-element.18), channel_id=1, source_target_pairs={{0,16},{16,0},{1,17},{17,1},{2,18},{18,2},{3,19},{19,3},{4,20},{20... | collective-permute-start | bytes 6156296 | tf_op jit(solution)/shard_map/ppermute | solution.py:87
  75.4 20.5 %all-gather.6 = bf16[16,129,128]{2,1,0:T(8,128)(2,1)S(1)} all-gather(bf16[1,129,128]{2,1,0:T(8,128)(2,1)S(1)} %get-tuple-element.29), channel_id=4, replica_groups=mesh['member'=2,'vocab'=16] {'vocab'}, dimensions={0}, use_global_device_ids=true | all-gather | bytes 561408 | tf_op jit(solution)/shard_map/all_gather | solution.py:56
  95.9 19.2 %all-gather.7 = bf16[16,129,128]{2,1,0:T(8,128)(2,1)S(1)} all-gather(bf16[1,129,128]{2,1,0:T(8,128)(2,1)S(1)} %get-tuple-element.31), channel_id=5, replica_groups=mesh['member'=2,'vocab'=16] {'vocab'}, dimensions={0}, use_global_device_ids=true | all-gather | bytes 561408 | tf_op jit(solution)/shard_map/all_gather | solution.py:56
  117.2 0.6 fusion.6
  117.8 9.9 %fusion.19 = f32[256,4008]{0,1:T(8,128)} fusion(bf16[128,2048]{0,1:T(8,128)(2,1)S(1)} %bitcast.214, bf16[128,2048]{0,1:T(8,128)(2,1)S(1)} %bitcast.213, bf16[1,2048,4008]{1,2,0:T(8,128)(2,1)} %param.6), kind=kOutput, calls=%fused_computation.38 | convolution fusion | flops 4204789760 | bytes 21569536 | tf_op jit(solution)/shard_map/dot_general | solution.py:95
  127.7 0.5 collective-permute-start.3
  128.2 2.1 %slice_reduce_fusion.1 = f32[128]{0:T(128)S(1)} fusion(f32[256,4008]{0,1:T(8,128)} %fusion.19), kind=kLoop, calls=%fused_computation.17 | loop fusion | flops 512896 | bytes 2052608 | tf_op jit(solution)/shard_map/reduce_max | solution.py:11
  130.3 1.0 collective-permute-done.3
  131.4 3.5 %exponential_reduce_fusion.3 = (f32[128]{0:T(128)S(1)}, f32[128]{0:T(128)S(1)}, f32[128]{0:T(128)S(1)}, f32[128,4008]{0,1:T(8,128)S(1)}) fusion(f32[256,4008]{0,1:T(8,128)} %fusion.19, f32[128]{0:T(128)S(1)} %slice_reduce_fusion.1, f32[128,2004]{0,1:T(8,128)} %collective-permute-done.1, f32[128,2004]{0,1:T(8,128)} %collective-permute-done, f32[]{:T(128)} %bitcast.203), kind=kLoop, calls=%fused_computation.13 | loop fusion | flops 3590784 | bytes 8210436 | tf_op jit(solution)/shard_map/reduce_sum | solution.py:12
  134.9 0.6 exponential_reduce_fusion.2
  135.5 2.2 %fusion.56 = (f32[128]{0:T(128)S(1)}, f32[128,4008]{0,1:T(8,128)S(1)}, f32[128]{0:T(128)S(1)}) fusion(f32[128,4008]{0,1:T(8,128)} %collective-permute-done.2, f32[256,4008]{0,1:T(8,128)S(1)} %copy-done, f32[]{:T(128)} %bitcast.208, f32[128]{0:T(128)S(1)} %get-tuple-element.7), kind=kLoop, calls=%fused_computation.124 | loop fusion | flops 2564864 | bytes 6157828 | tf_op jit(solution)/shard_map/reduce_max | solution.py:11
  137.7 0.6 exponential_reduce_fusion
  138.3 0.5 collective-permute-start.6
  138.8 1.3 collective-permute-start.5
  140.3 1.2 collective-permute-done.6
  141.5 1.0 collective-permute-done.5
  142.5 0.6 collective-permute-start.9
  143.2 3.8 %collective-permute-start.7 = (f32[2,3,256]{2,1,0:T(4,128)S(1)}, f32[2,3,256]{2,1,0:T(4,128)S(1)}, u32[]{:S(2)}, u32[]{:S(2)}) collective-permute-start(f32[2,3,256]{2,1,0:T(4,128)S(1)} %pad_maximum_fusion.5), channel_id=1, source_target_pairs={{0,4},{1,5},{2,6},{3,7},{4,0},{5,1},{6,2},{7,3},{8,12},{9,13},{10,... | collective-permute-start | bytes 18440 | tf_op jit(solution)/shard_map/ppermute | solution.py:27
  147.0 1.1 collective-permute-done.9
  148.0 0.6 collective-permute-done.7
  148.7 2.3 %fusion.4 = f32[256,4008]{0,1:T(8,128)} fusion(f32[128,4008]{0,1:T(8,128)S(1)} %get-tuple-element.13, f32[128,4008]{0,1:T(8,128)S(1)} %get-tuple-element.16, f32[256]{0:T(256)S(1)} %sub.133, f32[256]{0:T(256)S(1)} %bitcast.218), kind=kLoop, calls=%fused_computation.5 | loop fusion | flops 3078144 | bytes 8210432 | tf_op jit(solution)/shard_map/sub | solution.py:119
  (54 shorter events, 4.1 us)
Async XLA Ops:
  35.2 96.1 %collective-permute-start.1 = (f32[128,2004]{0,1:T(8,128)}, f32[128,2004]{0,1:T(8,128)}, u32[]{:S(2)}, u32[]{:S(2)}) collective-permute-start(f32[128,2004]{0,1:T(8,128)} %get-tuple-element.21), channel_id=1, source_target_pairs={{0,16},{16,0},{1,17},{17,1},{2,18},{18,2},{3,19},{19,3},{4,20},{20... | collective-permute-start | bytes 3078152 | tf_op jit(solution)/shard_map/ppermute | solution.py:82
  43.7 87.7 %collective-permute-start = (f32[128,2004]{0,1:T(8,128)}, f32[128,2004]{0,1:T(8,128)}, u32[]{:S(2)}, u32[]{:S(2)}) collective-permute-start(f32[128,2004]{0,1:T(8,128)} %get-tuple-element.19), channel_id=1, source_target_pairs={{0,16},{16,0},{1,17},{17,1},{2,18},{18,2},{3,19},{19,3},{4,20},{20... | collective-permute-start | bytes 3078152 | tf_op jit(solution)/shard_map/ppermute | solution.py:82
  73.9 61.6 %collective-permute-start.2 = (f32[128,4008]{0,1:T(8,128)}, f32[128,4008]{0,1:T(8,128)}, u32[]{:S(2)}, u32[]{:S(2)}) collective-permute-start(f32[128,4008]{0,1:T(8,128)} %get-tuple-element.18), channel_id=1, source_target_pairs={{0,16},{16,0},{1,17},{17,1},{2,18},{18,2},{3,19},{19,3},{4,20},{20... | collective-permute-start | bytes 6156296 | tf_op jit(solution)/shard_map/ppermute | solution.py:87
  116.0 1.2 copy-start.1
  127.7 3.6 %collective-permute-start.3 = (f32[3,256]{1,0:T(4,128)S(1)}, f32[3,256]{1,0:T(4,128)S(1)}, u32[]{:S(2)}, u32[]{:S(2)}) collective-permute-start(f32[3,256]{1,0:T(4,128)S(1)} %fusion.35), channel_id=1, source_target_pairs={{0,16},{16,0},{1,17},{17,1},{2,18},{18,2},{3,19},{19,3},{4,20},{20... | collective-permute-start | bytes 9224 | tf_op jit(solution)/shard_map/ppermute | solution.py:97
  131.4 4.1 %copy-start = (f32[256,4008]{0,1:T(8,128)S(1)}, f32[256,4008]{0,1:T(8,128)}, u32[]{:S(2)}) copy-start(f32[256,4008]{0,1:T(8,128)} %fusion.19) | copy-start | bytes 12312580
  138.3 3.1 %collective-permute-start.6 = (f32[2,3,256]{2,1,0:T(4,128)S(1)}, f32[2,3,256]{2,1,0:T(4,128)S(1)}, u32[]{:S(2)}, u32[]{:S(2)}) collective-permute-start(f32[2,3,256]{2,1,0:T(4,128)S(1)} %pad_maximum_fusion.4), channel_id=1, source_target_pairs={{0,3},{1,2},{2,1},{3,0},{4,7},{5,6},{6,5},{7,4},{8,11},{9,10},{10,... | collective-permute-start | bytes 18440 | tf_op jit(solution)/shard_map/ppermute | solution.py:27
  138.8 3.7 %collective-permute-start.5 = (f32[2,3,256]{2,1,0:T(4,128)S(1)}, f32[2,3,256]{2,1,0:T(4,128)S(1)}, u32[]{:S(2)}, u32[]{:S(2)}) collective-permute-start(f32[2,3,256]{2,1,0:T(4,128)S(1)} %pad_maximum_fusion.4), channel_id=1, source_target_pairs={{0,2},{1,3},{2,0},{3,1},{4,6},{5,7},{6,4},{7,5},{8,10},{9,11},{10,... | collective-permute-start | bytes 18440 | tf_op jit(solution)/shard_map/ppermute | solution.py:27
  140.1 2.4 %collective-permute-start.4 = (f32[2,3,256]{2,1,0:T(4,128)S(1)}, f32[2,3,256]{2,1,0:T(4,128)S(1)}, u32[]{:S(2)}, u32[]{:S(2)}) collective-permute-start(f32[2,3,256]{2,1,0:T(4,128)S(1)} %pad_maximum_fusion.4), channel_id=1, source_target_pairs={{0,1},{1,0},{2,3},{3,2},{4,5},{5,4},{6,7},{7,6},{8,9},{9,8},{10,11... | collective-permute-start | bytes 18440 | tf_op jit(solution)/shard_map/ppermute | solution.py:27
  142.5 5.5 %collective-permute-start.9 = (f32[2,3,256]{2,1,0:T(4,128)S(1)}, f32[2,3,256]{2,1,0:T(4,128)S(1)}, u32[]{:S(2)}, u32[]{:S(2)}) collective-permute-start(f32[2,3,256]{2,1,0:T(4,128)S(1)} %pad_maximum_fusion.5), channel_id=1, source_target_pairs={{0,12},{1,13},{2,14},{3,15},{4,8},{5,9},{6,10},{7,11},{8,4},{9,5},... | collective-permute-start | bytes 18440 | tf_op jit(solution)/shard_map/ppermute | solution.py:27
  143.2 4.9 %collective-permute-start.8 = (f32[2,3,256]{2,1,0:T(4,128)S(1)}, f32[2,3,256]{2,1,0:T(4,128)S(1)}, u32[]{:S(2)}, u32[]{:S(2)}) collective-permute-start(f32[2,3,256]{2,1,0:T(4,128)S(1)} %pad_maximum_fusion.5), channel_id=1, source_target_pairs={{0,8},{1,9},{2,10},{3,11},{4,12},{5,13},{6,14},{7,15},{8,0},{9,1},... | collective-permute-start | bytes 18440 | tf_op jit(solution)/shard_map/ppermute | solution.py:27
  143.2 5.4 %collective-permute-start.7 = (f32[2,3,256]{2,1,0:T(4,128)S(1)}, f32[2,3,256]{2,1,0:T(4,128)S(1)}, u32[]{:S(2)}, u32[]{:S(2)}) collective-permute-start(f32[2,3,256]{2,1,0:T(4,128)S(1)} %pad_maximum_fusion.5), channel_id=1, source_target_pairs={{0,4},{1,5},{2,6},{3,7},{4,0},{5,1},{6,2},{7,3},{8,12},{9,13},{10,... | collective-permute-start | bytes 18440 | tf_op jit(solution)/shard_map/ppermute | solution.py:27
  148.7 2.3 %copy-start.2 = (f32[256]{0:T(256)}, f32[256]{0:T(256)S(1)}, u32[]{:S(2)}) copy-start(f32[256]{0:T(256)S(1)} %sub.133) | copy-start | bytes 3076

commit v13 on v12

--- a/solution.py
+++ b/solution.py
@@ -50,48 +50,60 @@
     share = row_count // members
     weights = head[0]
     width_all = width * shards
-    def normed_of(first_row, rows):
-        piece = lax.dynamic_slice_in_dim(states, first_row, rows, 0)
-        packed = jnp.concatenate([piece, norm_gain], axis=0)
+    gain = None
+    source = [states]
+
+    def normed_of(slices):
+        nonlocal gain
+        pieces = [lax.dynamic_slice_in_dim(source[0], lo, rows, 0) for lo, rows in slices]
+        rows = sum(rows for _, rows in slices)
+        packed = jnp.concatenate(pieces + ([norm_gain] if gain is None else []), axis=0)
         gathered = lax.all_gather(packed, "vocab", axis=0, tiled=False)
+        if gain is None:
+            gain = gathered[:, rows, :].astype(jnp.float32)
         full_states = gathered[:, :rows, :].astype(jnp.float32)
-        gain = gathered[:, rows, :].astype(jnp.float32)
         mean_square = jnp.sum(full_states * full_states, axis=(0, 2)) / width_all
         scaling = lax.rsqrt(mean_square + epsilon)
         normed = (full_states * scaling[None, :, None] * gain[:, None, :]).astype(jnp.bfloat16)
         return jnp.transpose(normed, (1, 0, 2)).reshape(rows, width_all)
 
-    def logits_of(first_row, rows):
-        return jnp.dot(normed_of(first_row, rows), weights, preferred_element_type=jnp.float32)
-
     w = pool_weight[0]
     sub = share // send_pieces
     received = []
     notes = []
+    own_first = None
     for shift in range(1, members):
         target = (me + shift) % members
         perm = [(g, (g + shift) % members) for g in range(members)]
         parts = []
         piece_stats = []
         for k in range(send_pieces):
+            slices = [(target * share + k * sub, sub)]
+            last = shift == members - 1 and k == send_pieces - 1
+            if last:
+                slices.append((me * share, 1))
+            normed = normed_of(slices)
+            if last:
+                own_first = normed[sub:]
+                normed = normed[:sub]
             if shift == 1 and k == 0:
-                normed = normed_of(target * share, sub)
                 half = weights.shape[1] // 2
                 halves = [jnp.dot(normed, columns, preferred_element_type=jnp.float32)
                           for columns in (weights[:, :half], weights[:, half:])]
-                sent_halves = [lax.ppermute(w * x, "member", perm) for x in halves]
+                outgoing = [w * x for x in halves]
+                outgoing[0], source[0] = lax.optimization_barrier((outgoing[0], states))
+                sent_halves = [lax.ppermute(x, "member", perm) for x in outgoing]
                 parts.append(jnp.concatenate(sent_halves, axis=1))
                 piece_stats.append(local_stats(jnp.concatenate(halves, axis=1)))
                 continue
-            logits = logits_of(target * share + k * sub, sub)
+            logits = jnp.dot(normed, weights, preferred_element_type=jnp.float32)
             parts.append(lax.ppermute(w * logits, "member", perm))
             piece_stats.append(local_stats(logits))
         stats_rows = jnp.concatenate(piece_stats, axis=1)
         note = jnp.concatenate([stats_rows, jnp.broadcast_to(w, (1, share))], axis=0)
         received.append(parts)
         notes.append((perm, note))
-    own_normed = jnp.concatenate(
-        [normed_of(me * share + k * sub, sub) for k in range(send_pieces)], axis=0)
+    own_normed = jnp.concatenate([own_first, normed_of([(me * share + 1, share - 1)])], axis=0)
     own_logits = jnp.dot(own_normed, weights, preferred_element_type=jnp.float32)
     notes, own_logits = lax.optimization_barrier(([note for _, note in notes], own_logits))
     notes = [lax.ppermute(note, "member", [(g, (g + shift) % members) for g in range(members)])

time: 151 us -> 147 us (0.974)
  blocking collectives: 83.1 us -> 65.6 us
  waiting for transfers between devices: 4.86 us -> 16.5 us
    all_gather x4 -> x3, blocking collectives: 83.1 us -> 65.6 us  [normed_of(): gathered = lax.all_gather(packed, 'vocab', axis=0, tiled=False)]
    ppermute x1, waiting for transfers between devices: 0.99 us -> 13 us  [on_device(): lax.ppermute(note, 'member', [(g, (g + shift) % members) for g in range(m...]
  transfers between devices with their start and end apart: 10 -> 10, of which waited for: 5 -> 5; matrix products, arithmetic and copies ran while one was open for 24% -> 25% of each run, Pallas kernels for 0% -> 0%
where the time goes in v13:
time: 147 us; the launch traced here: 146 us
  blocking collectives  65.6 us (45%)
  matrix products  32.5 us (22%)
  waiting for transfers between devices  16.5 us (11%)
  other arithmetic  16.4 us (11%)
  starting transfers between devices  10.4 us (7%)
  local copies, waits for them, and re-layouts  3.22 us (2%)
  between operations  1.53 us (1%)
    all_gather x3, blocking collectives, normed_of(): gathered = lax.all_gather(packed, 'vocab', axis=0, tiled=False)  65.6 us
    dot_general x2, matrix products, on_device(): jnp.dot(normed, columns, preferred_element_type=jnp.float32)  14 us
    ppermute x1, waiting for transfers between devices, on_device(): lax.ppermute(note, 'member', [(g, (g + shift) % members) for g in range(m...  13 us
    dot_general x1, matrix products, on_device(): jnp.dot(own_normed, weights, preferred_element_type=jnp.float32)  10.1 us
    dot_general x1, matrix products, on_device(): logits = jnp.dot(normed, weights, preferred_element_type=jnp.float32)  8.34 us
    reduce_sum x5, other arithmetic, local_stats(): local_sum = jnp.sum(jnp.exp(values - local_peak[:, None]), axis=1)  6.97 us
    ppermute x6, starting transfers between devices, reduce_stats(): lax.ppermute(stats, axis, [(a, a ^ j * stride) for a in range(size)])  6.36 us
    reduce_max x3, other arithmetic, local_stats(): local_peak = jnp.max(values, axis=1)  4.34 us
  transfers between devices with their start and end apart: 10, of which 5 were waited for; matrix products, arithmetic and copies ran while one was open for 25% of the time, Pallas kernels for 0%

profile of v13, /device:TPU:0, one launch (start us, length us, event | category | flops | bytes accessed | tf_op | source)
XLA Modules:
  0.0 146.2 jit_solution(14247018035634122529)
XLA Ops:
  0.7 0.9 copy-done
  1.5 0.7 maximum_bitcast_fusion
  2.2 24.7 %all-gather.3 = bf16[16,129,128]{2,1,0:T(8,128)(2,1)S(1)} all-gather(bf16[1,129,128]{2,1,0:T(8,128)(2,1)S(1)} %maximum_bitcast_fusion), channel_id=2, replica_groups=mesh['member'=2,'vocab'=16] {'vocab'}, dimensions={0}, use_global_device_ids=true | all-gather | bytes 561408 | tf_op jit(solution)/shard_map/all_gather | solution.py:61
  28.5 7.0 %broadcast_multiply_fusion.1 = (f32[128,2004]{0,1:T(8,128)}, f32[128]{0:T(128)S(1)}, f32[128,2004]{0,1:T(8,128)}) fusion(f32[]{:T(128)} %bitcast.181, bf16[128,2048]{0,1:T(8,128)(2,1)S(1)} %bitcast.190, bf16[2048,4008]{0,1:T(8,128)(2,1)} %bitcast.185), kind=kOutput, calls=%fused_computation.39 | convolution fusion | flops 1051186048 | bytes 10802176 | tf_op jit(solution)/shard_map/dot_general | solution.py:91
  35.6 1.5 %collective-permute-start.1 = (f32[128,2004]{0,1:T(8,128)}, f32[128,2004]{0,1:T(8,128)}, u32[]{:S(2)}, u32[]{:S(2)}) collective-permute-start(f32[128,2004]{0,1:T(8,128)} %get-tuple-element.23), channel_id=1, source_target_pairs={{0,16},{16,0},{1,17},{17,1},{2,18},{18,2},{3,19},{19,3},{4,20},{20... | collective-permute-start | bytes 3078152 | tf_op jit(solution)/shard_map/ppermute | solution.py:95
  37.1 7.0 %fusion.47 = (f32[128]{0:T(128)S(1)}, f32[128,2004]{0,1:T(8,128)}, f32[128,2004]{0,1:T(8,128)}) fusion(f32[]{:T(128)} %bitcast.176, bf16[128,2048]{0,1:T(8,128)(2,1)S(1)} %bitcast.191, bf16[2048,4008]{0,1:T(8,128)(2,1)} %bitcast.186), kind=kOutput, calls=%fused_computation.107 | convolution fusion | flops 1051186048 | bytes 10802176 | tf_op jit(solution)/shard_map/dot_general | solution.py:91
  44.1 0.5 collective-permute-start
  44.6 18.8 %all-gather.4 = bf16[16,129,128]{2,1,0:T(8,128)(2,1)S(1)} all-gather(bf16[1,129,128]{2,1,0:T(8,128)(2,1)S(1)} %maximum_bitcast_fusion.1), channel_id=3, replica_groups=mesh['member'=2,'vocab'=16] {'vocab'}, dimensions={0}, use_global_device_ids=true | all-gather | bytes 561408 | tf_op jit(solution)/shard_map/all_gather | solution.py:61
  63.4 0.5 copy.12
  64.7 8.3 %fusion.48 = (f32[128]{0:T(128)S(1)}, f32[128,4008]{0,1:T(8,128)S(1)}) fusion(bf16[128,2048]{0,1:T(8,128)(2,1)S(1)} %bitcast.188, bf16[1,2048,4008]{1,2,0:T(8,128)(2,1)} %param.6), kind=kOutput, calls=%fused_computation.108 | convolution fusion | flops 2101859200 | bytes 18993664 | tf_op jit(solution)/shard_map/dot_general | solution.py:99
  73.1 1.8 %exponential_reduce_fusion.4 = (f32[128]{0:T(128)S(1)}, f32[128,4008]{0,1:T(8,128)}) fusion(f32[128,4008]{0,1:T(8,128)S(1)} %get-tuple-element.31, f32[128]{0:T(128)S(1)} %get-tuple-element.30, f32[]{:T(128)} %bitcast.179), kind=kLoop, calls=%fused_computation.25 | loop fusion | flops 1538944 | bytes 4105220 | tf_op jit(solution)/shard_map/reduce_sum | solution.py:12
  74.9 1.5 %collective-permute-start.2 = (f32[128,4008]{0,1:T(8,128)}, f32[128,4008]{0,1:T(8,128)}, u32[]{:S(2)}, u32[]{:S(2)}) collective-permute-start(f32[128,4008]{0,1:T(8,128)} %get-tuple-element.22), channel_id=1, source_target_pairs={{0,16},{16,0},{1,17},{17,1},{2,18},{18,2},{3,19},{19,3},{4,20},{20... | collective-permute-start | bytes 6156296 | tf_op jit(solution)/shard_map/ppermute | solution.py:100
  76.4 22.1 %all-gather.5 = bf16[16,255,128]{2,1,0:T(8,128)(2,1)S(1)} all-gather(bf16[1,255,128]{2,1,0:T(8,128)(2,1)S(1)} %dynamic-slice_bitcast_fusion), channel_id=4, replica_groups=mesh['member'=2,'vocab'=16] {'vocab'}, dimensions={0}, use_global_device_ids=true | all-gather | bytes 1109760 | tf_op jit(solution)/shard_map/all_gather | solution.py:61
  98.5 0.5 copy.13
  99.7 0.5 copy-done.3
  100.6 0.6 fusion.12
  101.1 10.1 %fusion.17 = f32[256,4008]{0,1:T(8,128)} fusion(bf16[255,2048]{0,1:T(8,128)(2,1)S(1)} %bitcast.189, bf16[1,2048]{0,1:T(8,128)(2,1)S(1)} %bitcast.187, bf16[1,2048,4008]{1,2,0:T(8,128)(2,1)} %param.6), kind=kOutput, calls=%fused_computation.34 | convolution fusion | flops 4204789760 | bytes 21569536 | tf_op jit(solution)/shard_map/dot_general | solution.py:107
  111.3 0.5 collective-permute-start.3
  111.8 2.1 %slice_reduce_fusion.1 = f32[128]{0:T(128)S(1)} fusion(f32[256,4008]{0,1:T(8,128)} %fusion.17), kind=kLoop, calls=%fused_computation.27 | loop fusion | flops 512896 | bytes 2052608 | tf_op jit(solution)/shard_map/reduce_max | solution.py:11
  113.9 13.0 %collective-permute-done.3 = f32[3,256]{1,0:T(4,128)S(1)} collective-permute-done((f32[3,256]{1,0:T(4,128)S(1)}, f32[3,256]{1,0:T(4,128)S(1)}, u32[]{:S(2)}, u32[]{:S(2)}) %collective-permute-start.3) | collective-permute-done | bytes 3104 | tf_op jit(solution)/shard_map/ppermute | solution.py:109
  126.9 3.5 %exponential_reduce_fusion.3 = (f32[128]{0:T(128)S(1)}, f32[128]{0:T(128)S(1)}, f32[128]{0:T(128)S(1)}, f32[128,4008]{0,1:T(8,128)S(1)}) fusion(f32[256,4008]{0,1:T(8,128)} %fusion.17, f32[128]{0:T(128)S(1)} %slice_reduce_fusion.1, f32[128,2004]{0,1:T(8,128)} %collective-permute-done.1, f32[128,2004]{0,1:T(8,128)} %collective-permute-done, f32[]{:T(128)} %bitcast.175), kind=kLoop, calls=%fused_computation.23 | loop fusion | flops 3590784 | bytes 8210436 | tf_op jit(solution)/shard_map/reduce_sum | solution.py:12
  130.5 0.6 exponential_reduce_fusion.2
  131.1 2.2 %fusion.46 = (f32[128]{0:T(128)S(1)}, f32[128,4008]{0,1:T(8,128)S(1)}, f32[128]{0:T(128)S(1)}) fusion(f32[128,4008]{0,1:T(8,128)} %collective-permute-done.2, f32[256,4008]{0,1:T(8,128)S(1)} %copy-done.1, f32[]{:T(128)} %bitcast.180, f32[128]{0:T(128)S(1)} %get-tuple-element.11), kind=kLoop, calls=%fused_computation.106 | loop fusion | flops 2564864 | bytes 6157828 | tf_op jit(solution)/shard_map/reduce_max | solution.py:11
  133.3 0.6 exponential_reduce_fusion
  134.0 1.2 collective-permute-start.5
  135.2 0.6 collective-permute-start.4
  135.8 1.2 collective-permute-done.6
  137.0 0.7 collective-permute-done.5
  138.0 4.2 %collective-permute-start.7 = (f32[2,3,256]{2,1,0:T(4,128)S(1)}, f32[2,3,256]{2,1,0:T(4,128)S(1)}, u32[]{:S(2)}, u32[]{:S(2)}) collective-permute-start(f32[2,3,256]{2,1,0:T(4,128)S(1)} %pad_maximum_fusion.1), channel_id=1, source_target_pairs={{0,4},{1,5},{2,6},{3,7},{4,0},{5,1},{6,2},{7,3},{8,12},{9,13},{10,... | collective-permute-start | bytes 18440 | tf_op jit(solution)/shard_map/ppermute | solution.py:27
  142.2 1.1 collective-permute-done.9
  143.2 0.6 collective-permute-done.7
  143.9 2.3 %fusion.4 = f32[256,4008]{0,1:T(8,128)} fusion(f32[128,4008]{0,1:T(8,128)S(1)} %get-tuple-element.17, f32[128,4008]{0,1:T(8,128)S(1)} %get-tuple-element.20, f32[256]{0:T(256)S(1)} %sub.133, f32[256]{0:T(256)S(1)} %bitcast.196), kind=kLoop, calls=%fused_computation.5 | loop fusion | flops 3078144 | bytes 8210432 | tf_op jit(solution)/shard_map/sub | solution.py:131
  (52 shorter events, 3.3 us)
Async XLA Ops:
  0.6 0.9 copy-start
  35.6 91.4 %collective-permute-start.1 = (f32[128,2004]{0,1:T(8,128)}, f32[128,2004]{0,1:T(8,128)}, u32[]{:S(2)}, u32[]{:S(2)}) collective-permute-start(f32[128,2004]{0,1:T(8,128)} %get-tuple-element.23), channel_id=1, source_target_pairs={{0,16},{16,0},{1,17},{17,1},{2,18},{18,2},{3,19},{19,3},{4,20},{20... | collective-permute-start | bytes 3078152 | tf_op jit(solution)/shard_map/ppermute | solution.py:95
  44.1 82.8 %collective-permute-start = (f32[128,2004]{0,1:T(8,128)}, f32[128,2004]{0,1:T(8,128)}, u32[]{:S(2)}, u32[]{:S(2)}) collective-permute-start(f32[128,2004]{0,1:T(8,128)} %get-tuple-element.8), channel_id=1, source_target_pairs={{0,16},{16,0},{1,17},{17,1},{2,18},{18,2},{3,19},{19,3},{4,20},{20... | collective-permute-start | bytes 3078152 | tf_op jit(solution)/shard_map/ppermute | solution.py:95
  64.6 11.8 %copy-start.2 = (bf16[129,16,128]{0,2,1:T(8,128)(2,1)}, bf16[129,16,128]{0,2,1:T(8,128)(2,1)S(1)}, u32[]{:S(2)}) copy-start(bf16[129,16,128]{0,2,1:T(8,128)(2,1)S(1)} %fusion.16) | copy-start | bytes 1585156
  74.9 56.2 %collective-permute-start.2 = (f32[128,4008]{0,1:T(8,128)}, f32[128,4008]{0,1:T(8,128)}, u32[]{:S(2)}, u32[]{:S(2)}) collective-permute-start(f32[128,4008]{0,1:T(8,128)} %get-tuple-element.22), channel_id=1, source_target_pairs={{0,16},{16,0},{1,17},{17,1},{2,18},{18,2},{3,19},{19,3},{4,20},{20... | collective-permute-start | bytes 6156296 | tf_op jit(solution)/shard_map/ppermute | solution.py:100
  99.0 1.2 copy-start.3
  99.1 1.5 %copy-start.4 = (f32[128,2004]{0,1:T(8,128)S(1)}, f32[128,2004]{0,1:T(8,128)}, u32[]{:S(2)}) copy-start(f32[128,2004]{0,1:T(8,128)} %get-tuple-element.29) | copy-start | bytes 3078148
  99.4 1.8 %slice-start = ((bf16[129,16,128]{0,2,1:T(8,128)(2,1)}), bf16[1,16,128]{0,2,1:T(8,128)(2,1)S(1)}, s32[]{:S(2)}) async-start(bf16[129,16,128]{0,2,1:T(8,128)(2,1)} %copy-done.2), calls=%async_computation | async-start | bytes 1048576 | tf_op jit(solution)/shard_map/slice | solution.py:87
  111.3 15.6 %collective-permute-start.3 = (f32[3,256]{1,0:T(4,128)S(1)}, f32[3,256]{1,0:T(4,128)S(1)}, u32[]{:S(2)}, u32[]{:S(2)}) collective-permute-start(f32[3,256]{1,0:T(4,128)S(1)} %fusion.29), channel_id=1, source_target_pairs={{0,16},{16,0},{1,17},{17,1},{2,18},{18,2},{3,19},{19,3},{4,20},{20... | collective-permute-start | bytes 9224 | tf_op jit(solution)/shard_map/ppermute | solution.py:109
  126.9 4.1 %copy-start.1 = (f32[256,4008]{0,1:T(8,128)S(1)}, f32[256,4008]{0,1:T(8,128)}, u32[]{:S(2)}) copy-start(f32[256,4008]{0,1:T(8,128)} %fusion.17) | copy-start | bytes 12312580
  133.9 3.1 %collective-permute-start.6 = (f32[2,3,256]{2,1,0:T(4,128)S(1)}, f32[2,3,256]{2,1,0:T(4,128)S(1)}, u32[]{:S(2)}, u32[]{:S(2)}) collective-permute-start(f32[2,3,256]{2,1,0:T(4,128)S(1)} %pad_maximum_fusion), channel_id=1, source_target_pairs={{0,3},{1,2},{2,1},{3,0},{4,7},{5,6},{6,5},{7,4},{8,11},{9,10},{10,... | collective-permute-start | bytes 18440 | tf_op jit(solution)/shard_map/ppermute | solution.py:27
  134.0 3.7 %collective-permute-start.5 = (f32[2,3,256]{2,1,0:T(4,128)S(1)}, f32[2,3,256]{2,1,0:T(4,128)S(1)}, u32[]{:S(2)}, u32[]{:S(2)}) collective-permute-start(f32[2,3,256]{2,1,0:T(4,128)S(1)} %pad_maximum_fusion), channel_id=1, source_target_pairs={{0,2},{1,3},{2,0},{3,1},{4,6},{5,7},{6,4},{7,5},{8,10},{9,11},{10,... | collective-permute-start | bytes 18440 | tf_op jit(solution)/shard_map/ppermute | solution.py:27
  135.2 2.5 %collective-permute-start.4 = (f32[2,3,256]{2,1,0:T(4,128)S(1)}, f32[2,3,256]{2,1,0:T(4,128)S(1)}, u32[]{:S(2)}, u32[]{:S(2)}) collective-permute-start(f32[2,3,256]{2,1,0:T(4,128)S(1)} %pad_maximum_fusion), channel_id=1, source_target_pairs={{0,1},{1,0},{2,3},{3,2},{4,5},{5,4},{6,7},{7,6},{8,9},{9,8},{10,11... | collective-permute-start | bytes 18440 | tf_op jit(solution)/shard_map/ppermute | solution.py:27
  137.7 5.5 %collective-permute-start.9 = (f32[2,3,256]{2,1,0:T(4,128)S(1)}, f32[2,3,256]{2,1,0:T(4,128)S(1)}, u32[]{:S(2)}, u32[]{:S(2)}) collective-permute-start(f32[2,3,256]{2,1,0:T(4,128)S(1)} %pad_maximum_fusion.1), channel_id=1, source_target_pairs={{0,12},{1,13},{2,14},{3,15},{4,8},{5,9},{6,10},{7,11},{8,4},{9,5},... | collective-permute-start | bytes 18440 | tf_op jit(solution)/shard_map/ppermute | solution.py:27
  137.8 5.4 %collective-permute-start.8 = (f32[2,3,256]{2,1,0:T(4,128)S(1)}, f32[2,3,256]{2,1,0:T(4,128)S(1)}, u32[]{:S(2)}, u32[]{:S(2)}) collective-permute-start(f32[2,3,256]{2,1,0:T(4,128)S(1)} %pad_maximum_fusion.1), channel_id=1, source_target_pairs={{0,8},{1,9},{2,10},{3,11},{4,12},{5,13},{6,14},{7,15},{8,0},{9,1},... | collective-permute-start | bytes 18440 | tf_op jit(solution)/shard_map/ppermute | solution.py:27
  138.0 5.8 %collective-permute-start.7 = (f32[2,3,256]{2,1,0:T(4,128)S(1)}, f32[2,3,256]{2,1,0:T(4,128)S(1)}, u32[]{:S(2)}, u32[]{:S(2)}) collective-permute-start(f32[2,3,256]{2,1,0:T(4,128)S(1)} %pad_maximum_fusion.1), channel_id=1, source_target_pairs={{0,4},{1,5},{2,6},{3,7},{4,0},{5,1},{6,2},{7,3},{8,12},{9,13},{10,... | collective-permute-start | bytes 18440 | tf_op jit(solution)/shard_map/ppermute | solution.py:27
  143.9 2.3 %copy-start.5 = (f32[256]{0:T(256)}, f32[256]{0:T(256)S(1)}, u32[]{:S(2)}) copy-start(f32[256]{0:T(256)S(1)} %sub.133) | copy-start | bytes 3076

commit v14 on v13

--- a/solution.py
+++ b/solution.py
@@ -109,25 +109,41 @@
     notes = [lax.ppermute(note, "member", [(g, (g + shift) % members) for g in range(members)])
              for shift, note in zip(range(1, members), notes)]
 
-    pooled_raw = []
-    stats = []
-    for k in range(send_pieces):
+    def piece_terms(k):
         own = own_logits[k * sub:(k + 1) * sub]
         total = w * own
         for parts in received:
             total = total + parts[k]
-        pooled_raw.append(total)
-        stats.append(jnp.stack([local_stats(own), local_stats(total)], axis=1))
-    stats = jnp.concatenate(stats, axis=2)
-    stats = jnp.concatenate([stats] + [note[:2, None, :] for note in notes], axis=1)
-    peak, summed = reduce_stats(stats, "vocab")
-    lse = peak + jnp.log(summed)
-    offset = w * lse[0]
+        return total, jnp.concatenate([local_stats(own), local_stats(total)], axis=1)
+
+    def flat_lse(stats):
+        peak, summed = reduce_stats(stats[:, None, :], "vocab")
+        return (peak + jnp.log(summed))[0]
+
+    early = [piece_terms(k) for k in range(send_pieces - 1)]
+    early_lse = flat_lse(jnp.concatenate([stats for _, stats in early], axis=1))
+    last_parts = [parts[-1] for parts in received]
+    last_parts, early_lse = lax.optimization_barrier((last_parts, early_lse))
+    for parts, part in zip(received, last_parts):
+        parts[-1] = part
+    last_total, last_stats = piece_terms(send_pieces - 1)
+    tail_lse = flat_lse(jnp.concatenate([last_stats] + [note[:2] for note in notes], axis=1))
+
+    own_lse = []
+    pooled_lse = []
+    for k in range(send_pieces - 1):
+        own_lse.append(early_lse[2 * k * sub:(2 * k + 1) * sub])
+        pooled_lse.append(early_lse[(2 * k + 1) * sub:(2 * k + 2) * sub])
+    own_lse.append(tail_lse[:sub])
+    pooled_lse.append(tail_lse[sub:2 * sub])
+    offset = w * jnp.concatenate(own_lse)
     for index, note in enumerate(notes):
-        offset = offset + note[2] * lse[index + 2]
+        lo = 2 * sub + index * share
+        offset = offset + note[2] * tail_lse[lo:lo + share]
 
-    agreement = lse[1] - offset
-    pooled = jnp.concatenate(pooled_raw, axis=0) - offset[:, None]
+    agreement = jnp.concatenate(pooled_lse) - offset
+    pooled_raw = jnp.concatenate([total for total, _ in early] + [last_total], axis=0)
+    pooled = pooled_raw - offset[:, None]
     return (pooled - agreement[:, None], agreement)
 
 

time: 147 us -> 144 us (0.980)
  waiting for transfers between devices: 16.5 us -> 7.88 us
  starting transfers between devices: 10.4 us -> 16.8 us
    ppermute x1, waiting for transfers between devices: 13 us -> 0.49 us  [on_device(): lax.ppermute(note, 'member', [(g, (g + shift) % members) for g in range(m...]
    ppermute x6 -> x12, starting transfers between devices: 6.36 us -> 12.7 us  [reduce_stats(): lax.ppermute(stats, axis, [(a, a ^ j * stride) for a in range(size)])]
    ppermute x6 -> x12, waiting for transfers between devices: 3.5 us -> 7.38 us  [reduce_stats(): lax.ppermute(stats, axis, [(a, a ^ j * stride) for a in range(size)])]
    reduce_max x3 -> x4, other arithmetic: 4.34 us -> 6.41 us  [local_stats(): local_peak = jnp.max(values, axis=1)]
    reduce_sum x5, other arithmetic: 6.97 us -> 5.36 us  [local_stats(): local_sum = jnp.sum(jnp.exp(values - local_peak[:, None]), axis=1)]
  transfers between devices with their start and end apart: 10 -> 16, of which waited for: 5 -> 10; matrix products, arithmetic and copies ran while one was open for 25% -> 26% of each run, Pallas kernels for 0% -> 0%
where the time goes in v14:
time: 144 us
  blocking collectives  65.6 us (46%)
  matrix products  32.6 us (23%)
  other arithmetic  16.9 us (12%)
  starting transfers between devices  16.8 us (12%)
  waiting for transfers between devices  7.88 us (5%)
  local copies, waits for them, and re-layouts  2.76 us (2%)
  between operations  1.53 us (1%)
    all_gather x3, blocking collectives, normed_of(): gathered = lax.all_gather(packed, 'vocab', axis=0, tiled=False)  65.6 us
    dot_general x2, matrix products, on_device(): jnp.dot(normed, columns, preferred_element_type=jnp.float32)  14 us
    ppermute x12, starting transfers between devices, reduce_stats(): lax.ppermute(stats, axis, [(a, a ^ j * stride) for a in range(size)])  12.7 us
    dot_general x1, matrix products, on_device(): jnp.dot(own_normed, weights, preferred_element_type=jnp.float32)  10.2 us
    dot_general x1, matrix products, on_device(): logits = jnp.dot(normed, weights, preferred_element_type=jnp.float32)  8.34 us
    ppermute x12, waiting for transfers between devices, reduce_stats(): lax.ppermute(stats, axis, [(a, a ^ j * stride) for a in range(size)])  7.38 us
    reduce_max x4, other arithmetic, local_stats(): local_peak = jnp.max(values, axis=1)  6.41 us
    reduce_sum x5, other arithmetic, local_stats(): local_sum = jnp.sum(jnp.exp(values - local_peak[:, None]), axis=1)  5.36 us
  transfers between devices with their start and end apart: 16, of which 10 were waited for; matrix products, arithmetic and copies ran while one was open for 26% of the time, Pallas kernels for 0%

profile of v14, /device:TPU:0, one launch (start us, length us, event | category | flops | bytes accessed | tf_op | source)
XLA Modules:
  0.0 144.1 jit_solution(7506007834544685060)
XLA Ops:
  0.7 0.9 copy-done
  1.5 0.7 maximum_bitcast_fusion
  2.2 24.7 %all-gather.3 = bf16[16,129,128]{2,1,0:T(8,128)(2,1)S(1)} all-gather(bf16[1,129,128]{2,1,0:T(8,128)(2,1)S(1)} %maximum_bitcast_fusion), channel_id=2, replica_groups=mesh['member'=2,'vocab'=16] {'vocab'}, dimensions={0}, use_global_device_ids=true | all-gather | bytes 561408 | tf_op jit(solution)/shard_map/all_gather | solution.py:61
  28.5 7.0 %fusion.54 = (f32[128]{0:T(128)S(1)}, f32[128,2004]{0,1:T(8,128)}, f32[128,2004]{0,1:T(8,128)}) fusion(f32[]{:T(128)} %bitcast.229, bf16[128,2048]{0,1:T(8,128)(2,1)S(1)} %bitcast.238, bf16[2048,4008]{0,1:T(8,128)(2,1)} %bitcast.233), kind=kOutput, calls=%fused_computation.125 | convolution fusion | flops 1051186048 | bytes 10802176 | tf_op jit(solution)/shard_map/dot_general | solution.py:91
  35.6 1.5 %collective-permute-start.1 = (f32[128,2004]{0,1:T(8,128)}, f32[128,2004]{0,1:T(8,128)}, u32[]{:S(2)}, u32[]{:S(2)}) collective-permute-start(f32[128,2004]{0,1:T(8,128)} %get-tuple-element.30), channel_id=1, source_target_pairs={{0,16},{16,0},{1,17},{17,1},{2,18},{18,2},{3,19},{19,3},{4,20},{20... | collective-permute-start | bytes 3078152 | tf_op jit(solution)/shard_map/ppermute | solution.py:95
  37.1 7.0 %fusion.55 = (f32[128]{0:T(128)S(1)}, f32[128,2004]{0,1:T(8,128)}, f32[128,2004]{0,1:T(8,128)}) fusion(f32[]{:T(128)} %bitcast.224, bf16[128,2048]{0,1:T(8,128)(2,1)S(1)} %bitcast.239, bf16[2048,4008]{0,1:T(8,128)(2,1)} %bitcast.234), kind=kOutput, calls=%fused_computation.126 | convolution fusion | flops 1051186048 | bytes 10802176 | tf_op jit(solution)/shard_map/dot_general | solution.py:91
  44.6 18.8 %all-gather.4 = bf16[16,129,128]{2,1,0:T(8,128)(2,1)S(1)} all-gather(bf16[1,129,128]{2,1,0:T(8,128)(2,1)S(1)} %maximum_bitcast_fusion.1), channel_id=3, replica_groups=mesh['member'=2,'vocab'=16] {'vocab'}, dimensions={0}, use_global_device_ids=true | all-gather | bytes 561408 | tf_op jit(solution)/shard_map/all_gather | solution.py:61
  64.7 8.3 %fusion.57 = (f32[128]{0:T(128)S(1)}, f32[128,4008]{0,1:T(8,128)S(1)}) fusion(bf16[128,2048]{0,1:T(8,128)(2,1)S(1)} %bitcast.236, bf16[1,2048,4008]{1,2,0:T(8,128)(2,1)} %param.6), kind=kOutput, calls=%fused_computation.128 | convolution fusion | flops 2101859200 | bytes 18993664 | tf_op jit(solution)/shard_map/dot_general | solution.py:99
  73.1 1.8 %exponential_reduce_fusion.4 = (f32[128]{0:T(128)S(1)}, f32[128,4008]{0,1:T(8,128)}) fusion(f32[128,4008]{0,1:T(8,128)S(1)} %get-tuple-element.39, f32[128]{0:T(128)S(1)} %get-tuple-element.38, f32[]{:T(128)} %bitcast.227), kind=kLoop, calls=%fused_computation.25 | loop fusion | flops 1538944 | bytes 4105220 | tf_op jit(solution)/shard_map/reduce_sum | solution.py:12
  74.9 1.5 %collective-permute-start.2 = (f32[128,4008]{0,1:T(8,128)}, f32[128,4008]{0,1:T(8,128)}, u32[]{:S(2)}, u32[]{:S(2)}) collective-permute-start(f32[128,4008]{0,1:T(8,128)} %get-tuple-element.28), channel_id=1, source_target_pairs={{0,16},{16,0},{1,17},{17,1},{2,18},{18,2},{3,19},{19,3},{4,20},{20... | collective-permute-start | bytes 6156296 | tf_op jit(solution)/shard_map/ppermute | solution.py:100
  76.4 22.1 %all-gather.5 = bf16[16,255,128]{2,1,0:T(8,128)(2,1)S(1)} all-gather(bf16[1,255,128]{2,1,0:T(8,128)(2,1)S(1)} %dynamic-slice_bitcast_fusion), channel_id=4, replica_groups=mesh['member'=2,'vocab'=16] {'vocab'}, dimensions={0}, use_global_device_ids=true | all-gather | bytes 1109760 | tf_op jit(solution)/shard_map/all_gather | solution.py:61
  100.1 10.2 %fusion.17 = f32[256,4008]{0,1:T(8,128)} fusion(bf16[255,2048]{0,1:T(8,128)(2,1)S(1)} %bitcast.237, bf16[1,2048]{0,1:T(8,128)(2,1)S(1)} %bitcast.235, bf16[1,2048,4008]{1,2,0:T(8,128)(2,1)} %param.6), kind=kOutput, calls=%fused_computation.34 | convolution fusion | flops 4204789760 | bytes 21569536 | tf_op jit(solution)/shard_map/dot_general | solution.py:107
  110.3 1.9 %fusion.12 = f32[128]{0:T(128)S(1)} fusion(f32[128,2004]{0,1:T(8,128)S(1)} %copy-done.3, f32[128,2004]{0,1:T(8,128)} %get-tuple-element.37, f32[128]{0:T(128)S(1)} %reduce_max.78), kind=kLoop, calls=%fused_computation.18 | loop fusion | flops 1538944 | bytes 2053120 | tf_op jit(solution)/shard_map/reduce_sum | solution.py:12
  112.2 0.6 collective-permute-start.9
  112.8 2.1 %slice_reduce_fusion = f32[128]{0:T(128)S(1)} fusion(f32[256,4008]{0,1:T(8,128)} %fusion.17), kind=kLoop, calls=%fused_computation.26 | loop fusion | flops 512896 | bytes 2052608 | tf_op jit(solution)/shard_map/reduce_max | solution.py:11
  115.5 2.1 %fusion.53 = (f32[128]{0:T(128)S(1)}, f32[128,4008]{0,1:T(8,128)S(1)}, f32[128]{0:T(128)S(1)}) fusion(f32[128,2004]{0,1:T(8,128)} %collective-permute-done.1, f32[128,2004]{0,1:T(8,128)} %collective-permute-done, f32[256,4008]{0,1:T(8,128)S(1)} %copy-done.1, f32[]{:T(128)} %bitcast.223, f32[128]{0:T(128)S(1)} %get-tuple-element.15), kind=kLoop, calls=%fused_computation.124 | loop fusion | flops 3077888 | bytes 6157828 | tf_op jit(solution)/shard_map/reduce_max | solution.py:11
  118.3 1.7 %collective-permute-start.4 = (f32[2,1,256]{2,0,1:T(2,128)S(1)}, f32[2,1,256]{2,0,1:T(2,128)S(1)}, u32[]{:S(2)}, u32[]{:S(2)}) collective-permute-start(f32[2,1,256]{2,0,1:T(2,128)S(1)} %fusion.62), channel_id=1, source_target_pairs={{0,2},{1,3},{2,0},{3,1},{4,6},{5,7},{6,4},{7,5},{8,10},{9,11},{10,... | collective-permute-start | bytes 6152 | tf_op jit(solution)/shard_map/ppermute | solution.py:27
  120.1 1.1 collective-permute-done.5
  121.3 0.7 collective-permute-done.4
  122.0 0.9 collective-permute-start.8
  122.9 3.6 %collective-permute-start.6 = (f32[2,1,256]{2,1,0:T(1,128)S(1)}, f32[2,1,256]{2,1,0:T(1,128)S(1)}, u32[]{:S(2)}, u32[]{:S(2)}) collective-permute-start(f32[2,1,256]{2,1,0:T(1,128)S(1)} %pad_maximum_fusion.2), channel_id=1, source_target_pairs={{0,4},{1,5},{2,6},{3,7},{4,0},{5,1},{6,2},{7,3},{8,12},{9,13},{10,... | collective-permute-start | bytes 6152 | tf_op jit(solution)/shard_map/ppermute | solution.py:27
  127.4 0.6 collective-permute-done.6
  128.0 2.2 %fusion.52 = (f32[128]{0:T(128)S(1)}, f32[128,4008]{0,1:T(8,128)S(1)}) fusion(f32[128,4008]{0,1:T(8,128)} %collective-permute-done.2, f32[256,4008]{0,1:T(8,128)S(1)} %copy-done.1, f32[]{:T(128)} %bitcast.228), kind=kLoop, calls=%fused_computation.123 | loop fusion | flops 1538944 | bytes 6156804 | tf_op jit(solution)/shard_map/reduce_max | solution.py:11
  130.8 1.7 %collective-permute-start.11 = (f32[2,1,512]{2,0,1:T(2,128)S(1)}, f32[2,1,512]{2,0,1:T(2,128)S(1)}, u32[]{:S(2)}, u32[]{:S(2)}) collective-permute-start(f32[2,1,512]{2,0,1:T(2,128)S(1)} %fusion.61), channel_id=1, source_target_pairs={{0,2},{1,3},{2,0},{3,1},{4,6},{5,7},{6,4},{7,5},{8,10},{9,11},{10,... | collective-permute-start | bytes 12296 | tf_op jit(solution)/shard_map/ppermute | solution.py:27
  132.7 1.2 collective-permute-done.12
  133.8 0.7 collective-permute-done.11
  134.5 2.4 %collective-permute-start.15 = (f32[2,1,512]{2,1,0:T(1,128)S(1)}, f32[2,1,512]{2,1,0:T(1,128)S(1)}, u32[]{:S(2)}, u32[]{:S(2)}) collective-permute-start(f32[2,1,512]{2,1,0:T(1,128)S(1)} %pad_maximum_fusion.1), channel_id=1, source_target_pairs={{0,12},{1,13},{2,14},{3,15},{4,8},{5,9},{6,10},{7,11},{8,4},{9,5},... | collective-permute-start | bytes 12296 | tf_op jit(solution)/shard_map/ppermute | solution.py:27
  137.0 1.1 collective-permute-start.14
  138.1 0.9 collective-permute-start.13
  139.0 1.0 collective-permute-done.15
  140.0 1.5 %collective-permute-done.14 = f32[2,1,512]{2,1,0:T(1,128)S(1)} collective-permute-done((f32[2,1,512]{2,1,0:T(1,128)S(1)}, f32[2,1,512]{2,1,0:T(1,128)S(1)}, u32[]{:S(2)}, u32[]{:S(2)}) %collective-permute-start.14) | collective-permute-done | bytes 4128 | tf_op jit(solution)/shard_map/ppermute | solution.py:27
  141.8 2.3 %fusion.4 = f32[256,4008]{0,1:T(8,128)} fusion(f32[128,4008]{0,1:T(8,128)S(1)} %get-tuple-element.21, f32[128,4008]{0,1:T(8,128)S(1)} %get-tuple-element.25, f32[256]{0:T(256)S(1)} %get-tuple-element.16, f32[256]{0:T(256)S(1)} %get-tuple-element.17), kind=kLoop, calls=%fused_computation.5 | loop fusion | flops 3078144 | bytes 8210432 | tf_op jit(solution)/shard_map/sub | solution.py:147
  (66 shorter events, 7.9 us)
Async XLA Ops:
  0.6 0.9 copy-start
  35.6 79.9 %collective-permute-start.1 = (f32[128,2004]{0,1:T(8,128)}, f32[128,2004]{0,1:T(8,128)}, u32[]{:S(2)}, u32[]{:S(2)}) collective-permute-start(f32[128,2004]{0,1:T(8,128)} %get-tuple-element.30), channel_id=1, source_target_pairs={{0,16},{16,0},{1,17},{17,1},{2,18},{18,2},{3,19},{19,3},{4,20},{20... | collective-permute-start | bytes 3078152 | tf_op jit(solution)/shard_map/ppermute | solution.py:95
  44.1 71.4 %collective-permute-start = (f32[128,2004]{0,1:T(8,128)}, f32[128,2004]{0,1:T(8,128)}, u32[]{:S(2)}, u32[]{:S(2)}) collective-permute-start(f32[128,2004]{0,1:T(8,128)} %get-tuple-element.10), channel_id=1, source_target_pairs={{0,16},{16,0},{1,17},{17,1},{2,18},{18,2},{3,19},{19,3},{4,20},{20... | collective-permute-start | bytes 3078152 | tf_op jit(solution)/shard_map/ppermute | solution.py:95
  64.6 11.8 %copy-start.2 = (bf16[129,16,128]{0,2,1:T(8,128)(2,1)}, bf16[129,16,128]{0,2,1:T(8,128)(2,1)S(1)}, u32[]{:S(2)}) copy-start(bf16[129,16,128]{0,2,1:T(8,128)(2,1)S(1)} %fusion.16) | copy-start | bytes 1585156
  74.9 53.2 %collective-permute-start.2 = (f32[128,4008]{0,1:T(8,128)}, f32[128,4008]{0,1:T(8,128)}, u32[]{:S(2)}, u32[]{:S(2)}) collective-permute-start(f32[128,4008]{0,1:T(8,128)} %get-tuple-element.28), channel_id=1, source_target_pairs={{0,16},{16,0},{1,17},{17,1},{2,18},{18,2},{3,19},{19,3},{4,20},{20... | collective-permute-start | bytes 6156296 | tf_op jit(solution)/shard_map/ppermute | solution.py:100
  99.0 1.0 slice-start
  100.1 10.2 %copy-start.3 = (f32[128,2004]{0,1:T(8,128)S(1)}, f32[128,2004]{0,1:T(8,128)}, u32[]{:S(2)}) copy-start(f32[128,2004]{0,1:T(8,128)} %get-tuple-element.40) | copy-start | bytes 3078148
  110.3 4.6 %copy-start.1 = (f32[256,4008]{0,1:T(8,128)S(1)}, f32[256,4008]{0,1:T(8,128)}, u32[]{:S(2)}) copy-start(f32[256,4008]{0,1:T(8,128)} %fusion.17) | copy-start | bytes 12312580
  112.2 14.7 %collective-permute-start.9 = (f32[3,256]{1,0:T(4,128)S(1)}, f32[3,256]{1,0:T(4,128)S(1)}, u32[]{:S(2)}, u32[]{:S(2)}) collective-permute-start(f32[3,256]{1,0:T(4,128)S(1)} %fusion.21), channel_id=1, source_target_pairs={{0,16},{16,0},{1,17},{17,1},{2,18},{18,2},{3,19},{19,3},{4,20},{20... | collective-permute-start | bytes 9224 | tf_op jit(solution)/shard_map/ppermute | solution.py:109
  118.2 3.1 %collective-permute-start.5 = (f32[2,1,256]{2,0,1:T(2,128)S(1)}, f32[2,1,256]{2,0,1:T(2,128)S(1)}, u32[]{:S(2)}, u32[]{:S(2)}) collective-permute-start(f32[2,1,256]{2,0,1:T(2,128)S(1)} %fusion.62), channel_id=1, source_target_pairs={{0,3},{1,2},{2,1},{3,0},{4,7},{5,6},{6,5},{7,4},{8,11},{9,10},{10,... | collective-permute-start | bytes 6152 | tf_op jit(solution)/shard_map/ppermute | solution.py:27
  118.3 3.7 %collective-permute-start.4 = (f32[2,1,256]{2,0,1:T(2,128)S(1)}, f32[2,1,256]{2,0,1:T(2,128)S(1)}, u32[]{:S(2)}, u32[]{:S(2)}) collective-permute-start(f32[2,1,256]{2,0,1:T(2,128)S(1)} %fusion.62), channel_id=1, source_target_pairs={{0,2},{1,3},{2,0},{3,1},{4,6},{5,7},{6,4},{7,5},{8,10},{9,11},{10,... | collective-permute-start | bytes 6152 | tf_op jit(solution)/shard_map/ppermute | solution.py:27
  120.0 2.0 %collective-permute-start.3 = (f32[2,1,256]{2,0,1:T(2,128)S(1)}, f32[2,1,256]{2,0,1:T(2,128)S(1)}, u32[]{:S(2)}, u32[]{:S(2)}) collective-permute-start(f32[2,1,256]{2,0,1:T(2,128)S(1)} %fusion.62), channel_id=1, source_target_pairs={{0,1},{1,0},{2,3},{3,2},{4,5},{5,4},{6,7},{7,6},{8,9},{9,8},{10,11... | collective-permute-start | bytes 6152 | tf_op jit(solution)/shard_map/ppermute | solution.py:27
  122.0 5.4 %collective-permute-start.8 = (f32[2,1,256]{2,1,0:T(1,128)S(1)}, f32[2,1,256]{2,1,0:T(1,128)S(1)}, u32[]{:S(2)}, u32[]{:S(2)}) collective-permute-start(f32[2,1,256]{2,1,0:T(1,128)S(1)} %pad_maximum_fusion.2), channel_id=1, source_target_pairs={{0,12},{1,13},{2,14},{3,15},{4,8},{5,9},{6,10},{7,11},{8,4},{9,5},... | collective-permute-start | bytes 6152 | tf_op jit(solution)/shard_map/ppermute | solution.py:27
  122.9 4.6 %collective-permute-start.7 = (f32[2,1,256]{2,1,0:T(1,128)S(1)}, f32[2,1,256]{2,1,0:T(1,128)S(1)}, u32[]{:S(2)}, u32[]{:S(2)}) collective-permute-start(f32[2,1,256]{2,1,0:T(1,128)S(1)} %pad_maximum_fusion.2), channel_id=1, source_target_pairs={{0,8},{1,9},{2,10},{3,11},{4,12},{5,13},{6,14},{7,15},{8,0},{9,1},... | collective-permute-start | bytes 6152 | tf_op jit(solution)/shard_map/ppermute | solution.py:27
  122.9 5.1 %collective-permute-start.6 = (f32[2,1,256]{2,1,0:T(1,128)S(1)}, f32[2,1,256]{2,1,0:T(1,128)S(1)}, u32[]{:S(2)}, u32[]{:S(2)}) collective-permute-start(f32[2,1,256]{2,1,0:T(1,128)S(1)} %pad_maximum_fusion.2), channel_id=1, source_target_pairs={{0,4},{1,5},{2,6},{3,7},{4,0},{5,1},{6,2},{7,3},{8,12},{9,13},{10,... | collective-permute-start | bytes 6152 | tf_op jit(solution)/shard_map/ppermute | solution.py:27
  130.7 3.1 %collective-permute-start.12 = (f32[2,1,512]{2,0,1:T(2,128)S(1)}, f32[2,1,512]{2,0,1:T(2,128)S(1)}, u32[]{:S(2)}, u32[]{:S(2)}) collective-permute-start(f32[2,1,512]{2,0,1:T(2,128)S(1)} %fusion.61), channel_id=1, source_target_pairs={{0,3},{1,2},{2,1},{3,0},{4,7},{5,6},{6,5},{7,4},{8,11},{9,10},{10,... | collective-permute-start | bytes 12296 | tf_op jit(solution)/shard_map/ppermute | solution.py:27
  130.8 3.7 %collective-permute-start.11 = (f32[2,1,512]{2,0,1:T(2,128)S(1)}, f32[2,1,512]{2,0,1:T(2,128)S(1)}, u32[]{:S(2)}, u32[]{:S(2)}) collective-permute-start(f32[2,1,512]{2,0,1:T(2,128)S(1)} %fusion.61), channel_id=1, source_target_pairs={{0,2},{1,3},{2,0},{3,1},{4,6},{5,7},{6,4},{7,5},{8,10},{9,11},{10,... | collective-permute-start | bytes 12296 | tf_op jit(solution)/shard_map/ppermute | solution.py:27
  132.5 2.0 %collective-permute-start.10 = (f32[2,1,512]{2,0,1:T(2,128)S(1)}, f32[2,1,512]{2,0,1:T(2,128)S(1)}, u32[]{:S(2)}, u32[]{:S(2)}) collective-permute-start(f32[2,1,512]{2,0,1:T(2,128)S(1)} %fusion.61), channel_id=1, source_target_pairs={{0,1},{1,0},{2,3},{3,2},{4,5},{5,4},{6,7},{7,6},{8,9},{9,8},{10,11... | collective-permute-start | bytes 12296 | tf_op jit(solution)/shard_map/ppermute | solution.py:27
  134.5 5.5 %collective-permute-start.15 = (f32[2,1,512]{2,1,0:T(1,128)S(1)}, f32[2,1,512]{2,1,0:T(1,128)S(1)}, u32[]{:S(2)}, u32[]{:S(2)}) collective-permute-start(f32[2,1,512]{2,1,0:T(1,128)S(1)} %pad_maximum_fusion.1), channel_id=1, source_target_pairs={{0,12},{1,13},{2,14},{3,15},{4,8},{5,9},{6,10},{7,11},{8,4},{9,5},... | collective-permute-start | bytes 12296 | tf_op jit(solution)/shard_map/ppermute | solution.py:27
  137.0 4.5 %collective-permute-start.14 = (f32[2,1,512]{2,1,0:T(1,128)S(1)}, f32[2,1,512]{2,1,0:T(1,128)S(1)}, u32[]{:S(2)}, u32[]{:S(2)}) collective-permute-start(f32[2,1,512]{2,1,0:T(1,128)S(1)} %pad_maximum_fusion.1), channel_id=1, source_target_pairs={{0,8},{1,9},{2,10},{3,11},{4,12},{5,13},{6,14},{7,15},{8,0},{9,1},... | collective-permute-start | bytes 12296 | tf_op jit(solution)/shard_map/ppermute | solution.py:27
  138.1 3.6 %collective-permute-start.13 = (f32[2,1,512]{2,1,0:T(1,128)S(1)}, f32[2,1,512]{2,1,0:T(1,128)S(1)}, u32[]{:S(2)}, u32[]{:S(2)}) collective-permute-start(f32[2,1,512]{2,1,0:T(1,128)S(1)} %pad_maximum_fusion.1), channel_id=1, source_target_pairs={{0,4},{1,5},{2,6},{3,7},{4,0},{5,1},{6,2},{7,3},{8,12},{9,13},{10,... | collective-permute-start | bytes 12296 | tf_op jit(solution)/shard_map/ppermute | solution.py:27
  141.8 2.3 %copy-start.4 = (f32[256]{0:T(256)}, f32[256]{0:T(256)S(1)}, u32[]{:S(2)}) copy-start(f32[256]{0:T(256)S(1)} %get-tuple-element.16) | copy-start | bytes 3076

commit v15 on v14

--- a/solution.py
+++ b/solution.py
@@ -87,7 +87,7 @@
                 own_first = normed[sub:]
                 normed = normed[:sub]
             if shift == 1 and k == 0:
-                half = weights.shape[1] // 2
+                half = (weights.shape[1] // 2 + 127) // 128 * 128
                 halves = [jnp.dot(normed, columns, preferred_element_type=jnp.float32)
                           for columns in (weights[:, :half], weights[:, half:])]
                 outgoing = [w * x for x in halves]

time: 144 us -> 181 us (1.26)
  local copies, waits for them, and re-layouts: 2.76 us -> 26.9 us
  other arithmetic: 16.9 us -> 21 us
  waiting for transfers between devices: 7.88 us -> 11.4 us
  matrix products: 32.6 us -> 35.2 us
    optimization_barrier x0 -> x2, local copies, waits for them, and re-layouts: none -> 8.4 us  [the longest x1 5.51 us: on_device(): lax.optimization_barrier(([note for _, note in notes], own_logits))]
    unnamed x12 -> x11, local copies, waits for them, and re-layouts: 1.21 us -> 7.42 us
    ppermute x12, waiting for transfers between devices: 7.38 us -> 11.4 us  [reduce_stats(): lax.ppermute(stats, axis, [(a, a ^ j * stride) for a in range(size)])]
    dot_general x0 -> x2, local copies, waits for them, and re-layouts: none -> 3.64 us  [the longest x1 2.1 us: on_device(): logits = jnp.dot(normed, weights, preferred_element_type=jnp.float32)]
    mul x0 -> x1, other arithmetic: none -> 3.1 us  [on_device(): parts.append(lax.ppermute(w * logits, 'member', perm))]
    mul x0 -> x1, local copies, waits for them, and re-layouts: none -> 2.9 us  [on_device(): parts.append(lax.ppermute(w * logits, 'member', perm))]
    dot_general x1, matrix products: 10.2 us -> 12.7 us  [on_device(): jnp.dot(own_normed, weights, preferred_element_type=jnp.float32)]
  transfers between devices with their start and end apart: 16 -> 16, of which waited for: 10 -> 7; matrix products, arithmetic and copies ran while one was open for 26% -> 33% of each run, Pallas kernels for 0% -> 0%
where the time goes in v15:
time: 181 us; the launch traced here: 180 us
  blocking collectives  66.8 us (37%)
  matrix products  35.2 us (19%)
  local copies, waits for them, and re-layouts  26.9 us (15%)
  other arithmetic  21 us (12%)
  starting transfers between devices  16.9 us (9%)
  waiting for transfers between devices  11.4 us (6%)
    all_gather x3, blocking collectives, normed_of(): gathered = lax.all_gather(packed, 'vocab', axis=0, tiled=False)  66.8 us
    dot_general x2, matrix products, on_device(): jnp.dot(normed, columns, preferred_element_type=jnp.float32)  14.5 us
    ppermute x12, starting transfers between devices, reduce_stats(): lax.ppermute(stats, axis, [(a, a ^ j * stride) for a in range(size)])  12.8 us
    dot_general x1, matrix products, on_device(): jnp.dot(own_normed, weights, preferred_element_type=jnp.float32)  12.7 us
    ppermute x12, waiting for transfers between devices, reduce_stats(): lax.ppermute(stats, axis, [(a, a ^ j * stride) for a in range(size)])  11.4 us
    dot_general x1, matrix products, on_device(): logits = jnp.dot(normed, weights, preferred_element_type=jnp.float32)  8.07 us
    unnamed x11, local copies, waits for them, and re-layouts  7.42 us
    reduce_max x4, other arithmetic, local_stats(): local_peak = jnp.max(values, axis=1)  6.91 us
  transfers between devices with their start and end apart: 16, of which 7 were waited for; matrix products, arithmetic and copies ran while one was open for 33% of the time, Pallas kernels for 0%

profile of v15, /device:TPU:0, one launch (start us, length us, event | category | flops | bytes accessed | tf_op | source)
XLA Modules:
  0.0 179.8 jit_solution(902085546769507404)
XLA Ops:
  2.2 24.7 %all-gather.3 = bf16[16,129,128]{2,1,0:T(8,128)(2,1)S(1)} all-gather(bf16[1,129,128]{2,1,0:T(8,128)(2,1)S(1)} %maximum_bitcast_fusion), channel_id=2, replica_groups=mesh['member'=2,'vocab'=16] {'vocab'}, dimensions={0}, use_global_device_ids=true | all-gather | bytes 561408 | tf_op jit(solution)/shard_map/all_gather | solution.py:61
  28.6 6.8 %fusion.55 = (f32[128]{0:T(128)S(1)}, f32[128,1960]{0,1:T(8,128)}, f32[128,1960]{0,1:T(8,128)}) fusion(f32[]{:T(128)} %bitcast.226, bf16[128,2048]{0,1:T(8,128)(2,1)S(1)} %bitcast.238, bf16[2048,4008]{0,1:T(8,128)(2,1)} %bitcast.233), kind=kOutput, calls=%fused_computation.126 | convolution fusion | flops 1028106112 | bytes 10560512 | tf_op jit(solution)/shard_map/dot_general | solution.py:91
  35.4 1.5 collective-permute-start.1
  36.9 7.7 %fusion.54 = (f32[128]{0:T(128)S(1)}, f32[128,2048]{1,0:T(8,128)}, f32[128,2048]{1,0:T(8,128)}) fusion(f32[]{:T(128)} %bitcast.224, bf16[128,2048]{0,1:T(8,128)(2,1)S(1)} %bitcast.239, bf16[2048,4008]{0,1:T(8,128)(2,1)} %bitcast.234), kind=kOutput, calls=%fused_computation.125 | convolution fusion | flops 1074265984 | bytes 11011072 | tf_op jit(solution)/shard_map/dot_general | solution.py:91
  45.1 18.8 %all-gather.4 = bf16[16,129,128]{2,1,0:T(8,128)(2,1)S(1)} all-gather(bf16[1,129,128]{2,1,0:T(8,128)(2,1)S(1)} %maximum_bitcast_fusion.1), channel_id=3, replica_groups=mesh['member'=2,'vocab'=16] {'vocab'}, dimensions={0}, use_global_device_ids=true | all-gather | bytes 561408 | tf_op jit(solution)/shard_map/all_gather | solution.py:61
  65.2 8.1 %fusion.57 = (f32[128]{0:T(128)S(1)}, f32[128,4008]{0,1:T(8,128)S(1)}) fusion(bf16[128,2048]{0,1:T(8,128)(2,1)S(1)} %bitcast.235, bf16[1,2048,4008]{1,2,0:T(8,128)(2,1)} %param.6), kind=kOutput, calls=%fused_computation.128 | convolution fusion | flops 2101859200 | bytes 18993664 | tf_op jit(solution)/shard_map/dot_general | solution.py:99
  73.3 2.1 %copy.37 = f32[128,4008]{1,0:T(8,128)} copy(f32[128,4008]{0,1:T(8,128)S(1)} %get-tuple-element.46) | data formatting | bytes 4104192 | tf_op jit(solution)/shard_map/dot_general | solution.py:99
  75.4 3.1 %broadcast_multiply_fusion = f32[128,4008]{1,0:T(8,128)} fusion(f32[128,4008]{1,0:T(8,128)} %copy.37, f32[]{:T(128)} %bitcast.228), kind=kLoop, calls=%fused_computation.38 | loop fusion | flops 513024 | bytes 4104196 | tf_op jit(solution)/shard_map/mul | solution.py:100
  78.5 2.9 %copy.38 = f32[128,4008]{0,1:T(8,128)} copy(f32[128,4008]{1,0:T(8,128)} %broadcast_multiply_fusion) | data formatting | bytes 4104192 | tf_op jit(solution)/shard_map/mul | solution.py:100
  81.4 1.5 collective-permute-start.2
  83.8 23.3 %all-gather.5 = bf16[16,255,128]{2,1,0:T(8,128)(2,1)} all-gather(bf16[1,255,128]{2,1,0:T(8,128)(2,1)S(1)} %dynamic-slice_bitcast_fusion), channel_id=4, replica_groups=mesh['member'=2,'vocab'=16] {'vocab'}, dimensions={0}, use_global_device_ids=true | all-gather | bytes 1109760 | tf_op jit(solution)/shard_map/all_gather | solution.py:61
  107.2 1.5 copy.32
  110.4 12.7 %fusion.17 = f32[256,4008]{0,1:T(8,128)} fusion(bf16[255,2048]{0,1:T(8,128)(2,1)} %bitcast.236, bf16[1,2048]{0,1:T(8,128)(2,1)} %bitcast.237, bf16[1,2048,4008]{1,2,0:T(8,128)(2,1)} %param.6), kind=kOutput, calls=%fused_computation.34 | convolution fusion | flops 4204789760 | bytes 21569536 | tf_op jit(solution)/shard_map/dot_general | solution.py:107
  123.0 1.5 copy.30
  126.8 5.5 %copy.34 = f32[256,4008]{1,0:T(8,128)} copy(f32[256,4008]{0,1:T(8,128)} %fusion.17) | data formatting | bytes 8208384 | tf_op jit(solution)/shard_map/optimization_barrier | solution.py:108
  132.3 1.8 slice_reduce_fusion
  134.1 2.7 %exponential_reduce_fusion.1 = (f32[128]{0:T(128)S(1)}, f32[128]{0:T(128)S(1)}) fusion(f32[256,4008]{1,0:T(8,128)} %copy.34, f32[128]{0:T(128)S(1)} %slice_reduce_fusion), kind=kLoop, calls=%fused_computation.21 | loop fusion | flops 1538816 | bytes 4105728 | tf_op jit(solution)/shard_map/reduce_sum | solution.py:12
  136.8 1.5 copy.35
  138.3 2.5 %fusion.53 = (f32[128]{0:T(128)S(1)}, f32[128,4008]{1,0:T(8,128)S(1)}, f32[128]{0:T(128)S(1)}) fusion(f32[128,1960]{1,0:T(8,128)S(1)} %copy.35, f32[128,2048]{1,0:T(8,128)} %collective-permute-done, f32[256,4008]{1,0:T(8,128)} %copy.34, f32[]{:T(128)} %bitcast.223, f32[128]{0:T(128)S(1)} %get-tuple-element.23), kind=kLoop, calls=%fused_computation.124 | loop fusion | flops 3077888 | bytes 6157828 | tf_op jit(solution)/shard_map/reduce_max | solution.py:11
  141.6 1.6 collective-permute-start.5
  143.2 1.8 collective-permute-done.4
  145.1 1.4 collective-permute-start.7
  146.5 3.0 %collective-permute-start.8 = (f32[2,1,256]{2,1,0:T(1,128)S(1)}, f32[2,1,256]{2,1,0:T(1,128)S(1)}, u32[]{:S(2)}, u32[]{:S(2)}) collective-permute-start(f32[2,1,256]{2,1,0:T(1,128)S(1)} %pad_maximum_fusion.2), channel_id=1, source_target_pairs={{0,12},{1,13},{2,14},{3,15},{4,8},{5,9},{6,10},{7,11},{8,4},{9,5},... | collective-permute-start | bytes 6152 | tf_op jit(solution)/shard_map/ppermute | solution.py:27
  149.7 2.2 %collective-permute-done.8 = f32[2,1,256]{2,1,0:T(1,128)S(1)} collective-permute-done((f32[2,1,256]{2,1,0:T(1,128)S(1)}, f32[2,1,256]{2,1,0:T(1,128)S(1)}, u32[]{:S(2)}, u32[]{:S(2)}) %collective-permute-start.8) | collective-permute-done | bytes 2080 | tf_op jit(solution)/shard_map/ppermute | solution.py:27
  151.9 2.9 %copy.39 = f32[128,4008]{1,0:T(8,128)} copy(f32[128,4008]{0,1:T(8,128)} %collective-permute-done.2) | data formatting | bytes 4104192 | tf_op jit(solution)/shard_map/optimization_barrier | solution.py:126
  154.8 2.6 %fusion.52 = (f32[128]{0:T(128)S(1)}, f32[128,4008]{1,0:T(8,128)S(1)}) fusion(f32[128,4008]{1,0:T(8,128)} %copy.39, f32[256,4008]{1,0:T(8,128)} %copy.34, f32[]{:T(128)} %bitcast.229), kind=kLoop, calls=%fused_computation.123 | loop fusion | flops 1538944 | bytes 6156804 | tf_op jit(solution)/shard_map/reduce_max | solution.py:11
  159.9 1.8 collective-permute-done.11
  162.4 3.8 %collective-permute-start.14 = (f32[2,1,512]{2,1,0:T(1,128)S(1)}, f32[2,1,512]{2,1,0:T(1,128)S(1)}, u32[]{:S(2)}, u32[]{:S(2)}) collective-permute-start(f32[2,1,512]{2,1,0:T(1,128)S(1)} %pad_maximum_fusion.1), channel_id=1, source_target_pairs={{0,8},{1,9},{2,10},{3,11},{4,12},{5,13},{6,14},{7,15},{8,0},{9,1},... | collective-permute-start | bytes 12296 | tf_op jit(solution)/shard_map/ppermute | solution.py:27
  166.2 1.6 collective-permute-done.14
  167.8 3.8 %collective-permute-done.15 = f32[2,1,512]{2,1,0:T(1,128)S(1)} collective-permute-done((f32[2,1,512]{2,1,0:T(1,128)S(1)}, f32[2,1,512]{2,1,0:T(1,128)S(1)}, u32[]{:S(2)}, u32[]{:S(2)}) %collective-permute-start.15) | collective-permute-done | bytes 4128 | tf_op jit(solution)/shard_map/ppermute | solution.py:27
  171.7 2.5 %fusion.4 = f32[256,4008]{1,0:T(8,128)} fusion(f32[128,4008]{1,0:T(8,128)S(1)} %get-tuple-element.29, f32[128,4008]{1,0:T(8,128)S(1)} %get-tuple-element.33, f32[256]{0:T(256)S(1)} %get-tuple-element.24, f32[256]{0:T(256)S(1)} %get-tuple-element.25), kind=kLoop, calls=%fused_computation.5 | loop fusion | flops 3078144 | bytes 8210432 | tf_op jit(solution)/shard_map/sub | solution.py:147
  174.3 5.6 %copy.40 = f32[256,4008]{0,1:T(8,128)} copy(f32[256,4008]{1,0:T(8,128)} %fusion.4) | data formatting | bytes 8208384
  (71 shorter events, 13.4 us)
Async XLA Ops:
  0.6 0.9 copy-start
  35.4 101.4 %collective-permute-start.1 = (f32[128,1960]{0,1:T(8,128)}, f32[128,1960]{0,1:T(8,128)}, u32[]{:S(2)}, u32[]{:S(2)}) collective-permute-start(f32[128,1960]{0,1:T(8,128)} %get-tuple-element.38), channel_id=1, source_target_pairs={{0,16},{16,0},{1,17},{17,1},{2,18},{18,2},{3,19},{19,3},{4,20},{20... | collective-permute-start | bytes 3010568 | tf_op jit(solution)/shard_map/ppermute | solution.py:95
  44.6 93.7 %collective-permute-start = (f32[128,2048]{1,0:T(8,128)}, f32[128,2048]{1,0:T(8,128)}, u32[]{:S(2)}, u32[]{:S(2)}) collective-permute-start(f32[128,2048]{1,0:T(8,128)} %get-tuple-element.10), channel_id=1, source_target_pairs={{0,16},{16,0},{1,17},{17,1},{2,18},{18,2},{3,19},{19,3},{4,20},{20... | collective-permute-start | bytes 3145736 | tf_op jit(solution)/shard_map/ppermute | solution.py:95
  81.4 70.5 %collective-permute-start.2 = (f32[128,4008]{0,1:T(8,128)}, f32[128,4008]{0,1:T(8,128)}, u32[]{:S(2)}, u32[]{:S(2)}) collective-permute-start(f32[128,4008]{0,1:T(8,128)} %copy.38), channel_id=1, source_target_pairs={{0,16},{16,0},{1,17},{17,1},{2,18},{18,2},{3,19},{19,3},{4,20},{20... | collective-permute-start | bytes 6156296 | tf_op jit(solution)/shard_map/ppermute | solution.py:100
  124.6 1.2 copy-start.2
  126.2 23.3 %collective-permute-start.9 = (f32[3,256]{1,0:T(4,128)S(1)}, f32[3,256]{1,0:T(4,128)S(1)}, u32[]{:S(2)}, u32[]{:S(2)}) collective-permute-start(f32[3,256]{1,0:T(4,128)S(1)} %fusion.21), channel_id=1, source_target_pairs={{0,16},{16,0},{1,17},{17,1},{2,18},{18,2},{3,19},{19,3},{4,20},{20... | collective-permute-start | bytes 9224 | tf_op jit(solution)/shard_map/ppermute | solution.py:109
  141.3 2.0 %collective-permute-start.3 = (f32[2,1,256]{2,0,1:T(2,128)S(1)}, f32[2,1,256]{2,0,1:T(2,128)S(1)}, u32[]{:S(2)}, u32[]{:S(2)}) collective-permute-start(f32[2,1,256]{2,0,1:T(2,128)S(1)} %fusion.62), channel_id=1, source_target_pairs={{0,1},{1,0},{2,3},{3,2},{4,5},{5,4},{6,7},{7,6},{8,9},{9,8},{10,11... | collective-permute-start | bytes 6152 | tf_op jit(solution)/shard_map/ppermute | solution.py:27
  141.4 3.6 %collective-permute-start.4 = (f32[2,1,256]{2,0,1:T(2,128)S(1)}, f32[2,1,256]{2,0,1:T(2,128)S(1)}, u32[]{:S(2)}, u32[]{:S(2)}) collective-permute-start(f32[2,1,256]{2,0,1:T(2,128)S(1)} %fusion.62), channel_id=1, source_target_pairs={{0,2},{1,3},{2,0},{3,1},{4,6},{5,7},{6,4},{7,5},{8,10},{9,11},{10,... | collective-permute-start | bytes 6152 | tf_op jit(solution)/shard_map/ppermute | solution.py:27
  141.6 3.4 %collective-permute-start.5 = (f32[2,1,256]{2,0,1:T(2,128)S(1)}, f32[2,1,256]{2,0,1:T(2,128)S(1)}, u32[]{:S(2)}, u32[]{:S(2)}) collective-permute-start(f32[2,1,256]{2,0,1:T(2,128)S(1)} %fusion.62), channel_id=1, source_target_pairs={{0,3},{1,2},{2,1},{3,0},{4,7},{5,6},{6,5},{7,4},{8,11},{9,10},{10,... | collective-permute-start | bytes 6152 | tf_op jit(solution)/shard_map/ppermute | solution.py:27
  145.1 4.5 %collective-permute-start.6 = (f32[2,1,256]{2,1,0:T(1,128)S(1)}, f32[2,1,256]{2,1,0:T(1,128)S(1)}, u32[]{:S(2)}, u32[]{:S(2)}) collective-permute-start(f32[2,1,256]{2,1,0:T(1,128)S(1)} %pad_maximum_fusion.2), channel_id=1, source_target_pairs={{0,4},{1,5},{2,6},{3,7},{4,0},{5,1},{6,2},{7,3},{8,12},{9,13},{10,... | collective-permute-start | bytes 6152 | tf_op jit(solution)/shard_map/ppermute | solution.py:27
  145.1 4.5 %collective-permute-start.7 = (f32[2,1,256]{2,1,0:T(1,128)S(1)}, f32[2,1,256]{2,1,0:T(1,128)S(1)}, u32[]{:S(2)}, u32[]{:S(2)}) collective-permute-start(f32[2,1,256]{2,1,0:T(1,128)S(1)} %pad_maximum_fusion.2), channel_id=1, source_target_pairs={{0,8},{1,9},{2,10},{3,11},{4,12},{5,13},{6,14},{7,15},{8,0},{9,1},... | collective-permute-start | bytes 6152 | tf_op jit(solution)/shard_map/ppermute | solution.py:27
  146.5 5.4 %collective-permute-start.8 = (f32[2,1,256]{2,1,0:T(1,128)S(1)}, f32[2,1,256]{2,1,0:T(1,128)S(1)}, u32[]{:S(2)}, u32[]{:S(2)}) collective-permute-start(f32[2,1,256]{2,1,0:T(1,128)S(1)} %pad_maximum_fusion.2), channel_id=1, source_target_pairs={{0,12},{1,13},{2,14},{3,15},{4,8},{5,9},{6,10},{7,11},{8,4},{9,5},... | collective-permute-start | bytes 6152 | tf_op jit(solution)/shard_map/ppermute | solution.py:27
  157.9 2.0 %collective-permute-start.10 = (f32[2,1,512]{2,0,1:T(2,128)S(1)}, f32[2,1,512]{2,0,1:T(2,128)S(1)}, u32[]{:S(2)}, u32[]{:S(2)}) collective-permute-start(f32[2,1,512]{2,0,1:T(2,128)S(1)} %fusion.61), channel_id=1, source_target_pairs={{0,1},{1,0},{2,3},{3,2},{4,5},{5,4},{6,7},{7,6},{8,9},{9,8},{10,11... | collective-permute-start | bytes 12296 | tf_op jit(solution)/shard_map/ppermute | solution.py:27
  158.0 3.7 %collective-permute-start.11 = (f32[2,1,512]{2,0,1:T(2,128)S(1)}, f32[2,1,512]{2,0,1:T(2,128)S(1)}, u32[]{:S(2)}, u32[]{:S(2)}) collective-permute-start(f32[2,1,512]{2,0,1:T(2,128)S(1)} %fusion.61), channel_id=1, source_target_pairs={{0,2},{1,3},{2,0},{3,1},{4,6},{5,7},{6,4},{7,5},{8,10},{9,11},{10,... | collective-permute-start | bytes 12296 | tf_op jit(solution)/shard_map/ppermute | solution.py:27
  158.7 3.0 %collective-permute-start.12 = (f32[2,1,512]{2,0,1:T(2,128)S(1)}, f32[2,1,512]{2,0,1:T(2,128)S(1)}, u32[]{:S(2)}, u32[]{:S(2)}) collective-permute-start(f32[2,1,512]{2,0,1:T(2,128)S(1)} %fusion.61), channel_id=1, source_target_pairs={{0,3},{1,2},{2,1},{3,0},{4,7},{5,6},{6,5},{7,4},{8,11},{9,10},{10,... | collective-permute-start | bytes 12296 | tf_op jit(solution)/shard_map/ppermute | solution.py:27
  161.8 4.5 %collective-permute-start.13 = (f32[2,1,512]{2,1,0:T(1,128)S(1)}, f32[2,1,512]{2,1,0:T(1,128)S(1)}, u32[]{:S(2)}, u32[]{:S(2)}) collective-permute-start(f32[2,1,512]{2,1,0:T(1,128)S(1)} %pad_maximum_fusion.1), channel_id=1, source_target_pairs={{0,4},{1,5},{2,6},{3,7},{4,0},{5,1},{6,2},{7,3},{8,12},{9,13},{10,... | collective-permute-start | bytes 12296 | tf_op jit(solution)/shard_map/ppermute | solution.py:27
  162.4 5.4 %collective-permute-start.14 = (f32[2,1,512]{2,1,0:T(1,128)S(1)}, f32[2,1,512]{2,1,0:T(1,128)S(1)}, u32[]{:S(2)}, u32[]{:S(2)}) collective-permute-start(f32[2,1,512]{2,1,0:T(1,128)S(1)} %pad_maximum_fusion.1), channel_id=1, source_target_pairs={{0,8},{1,9},{2,10},{3,11},{4,12},{5,13},{6,14},{7,15},{8,0},{9,1},... | collective-permute-start | bytes 12296 | tf_op jit(solution)/shard_map/ppermute | solution.py:27
  166.2 5.4 %collective-permute-start.15 = (f32[2,1,512]{2,1,0:T(1,128)S(1)}, f32[2,1,512]{2,1,0:T(1,128)S(1)}, u32[]{:S(2)}, u32[]{:S(2)}) collective-permute-start(f32[2,1,512]{2,1,0:T(1,128)S(1)} %pad_maximum_fusion.1), channel_id=1, source_target_pairs={{0,12},{1,13},{2,14},{3,15},{4,8},{5,9},{6,10},{7,11},{8,4},{9,5},... | collective-permute-start | bytes 12296 | tf_op jit(solution)/shard_map/ppermute | solution.py:27
  171.7 2.6 %copy-start.3 = (f32[256]{0:T(256)}, f32[256]{0:T(256)S(1)}, u32[]{:S(2)}) copy-start(f32[256]{0:T(256)S(1)} %get-tuple-element.24) | copy-start | bytes 3076
  171.7 8.1 %copy-start.1 = (bf16[1,512,128]{2,1,0:T(8,128)(2,1)S(1)}, bf16[1,512,128]{2,1,0:T(8,128)(2,1)}, u32[]{:S(2)}) copy-start(bf16[1,512,128]{2,1,0:T(8,128)(2,1)} %param.4) | copy-start | bytes 393220

commit v16 on v14

--- a/solution.py
+++ b/solution.py
@@ -102,12 +102,9 @@
         stats_rows = jnp.concatenate(piece_stats, axis=1)
         note = jnp.concatenate([stats_rows, jnp.broadcast_to(w, (1, share))], axis=0)
         received.append(parts)
-        notes.append((perm, note))
+        notes.append(lax.ppermute(note, "member", perm))
     own_normed = jnp.concatenate([own_first, normed_of([(me * share + 1, share - 1)])], axis=0)
     own_logits = jnp.dot(own_normed, weights, preferred_element_type=jnp.float32)
-    notes, own_logits = lax.optimization_barrier(([note for _, note in notes], own_logits))
-    notes = [lax.ppermute(note, "member", [(g, (g + shift) % members) for g in range(members)])
-             for shift, note in zip(range(1, members), notes)]
 
     def piece_terms(k):
         own = own_logits[k * sub:(k + 1) * sub]

time: 144 us -> 147 us (1.021)
  other arithmetic: 16.9 us -> 19.1 us
    reduce_sum x5, other arithmetic: 5.36 us -> 7.56 us  [local_stats(): local_sum = jnp.sum(jnp.exp(values - local_peak[:, None]), axis=1)]
  transfers between devices with their start and end apart: 16 -> 16, of which waited for: 10 -> 9; matrix products, arithmetic and copies ran while one was open for 26% -> 27% of each run, Pallas kernels for 0% -> 0%
where the time goes in v16:
time: 147 us
  blocking collectives  65.5 us (45%)
  matrix products  32.5 us (22%)
  other arithmetic  19.1 us (13%)
  starting transfers between devices  17 us (12%)
  waiting for transfers between devices  8.05 us (5%)
  local copies, waits for them, and re-layouts  3.24 us (2%)
  between operations  1.54 us (1%)
    all_gather x3, blocking collectives, normed_of(): gathered = lax.all_gather(packed, 'vocab', axis=0, tiled=False)  65.5 us
    dot_general x2, matrix products, on_device(): jnp.dot(normed, columns, preferred_element_type=jnp.float32)  14 us
    ppermute x12, starting transfers between devices, reduce_stats(): lax.ppermute(stats, axis, [(a, a ^ j * stride) for a in range(size)])  12.9 us
    dot_general x1, matrix products, on_device(): jnp.dot(own_normed, weights, preferred_element_type=jnp.float32)  10.1 us
    dot_general x1, matrix products, on_device(): logits = jnp.dot(normed, weights, preferred_element_type=jnp.float32)  8.37 us
    ppermute x12, waiting for transfers between devices, reduce_stats(): lax.ppermute(stats, axis, [(a, a ^ j * stride) for a in range(size)])  8.04 us
    reduce_sum x5, other arithmetic, local_stats(): local_sum = jnp.sum(jnp.exp(values - local_peak[:, None]), axis=1)  7.56 us
    reduce_max x4, other arithmetic, local_stats(): local_peak = jnp.max(values, axis=1)  6.39 us
  transfers between devices with their start and end apart: 16, of which 9 were waited for; matrix products, arithmetic and copies ran while one was open for 27% of the time, Pallas kernels for 0%

profile of v16, /device:TPU:0, one launch (start us, length us, event | category | flops | bytes accessed | tf_op | source)
XLA Modules:
  0.0 146.9 jit_solution(8244086315412951520)
XLA Ops:
  0.7 0.9 copy-done
  1.5 0.7 maximum_bitcast_fusion
  2.2 24.7 %all-gather.3 = bf16[16,129,128]{2,1,0:T(8,128)(2,1)S(1)} all-gather(bf16[1,129,128]{2,1,0:T(8,128)(2,1)S(1)} %maximum_bitcast_fusion), channel_id=2, replica_groups=mesh['member'=2,'vocab'=16] {'vocab'}, dimensions={0}, use_global_device_ids=true | all-gather | bytes 561408 | tf_op jit(solution)/shard_map/all_gather | solution.py:61
  28.5 7.1 %fusion.54 = (f32[128]{0:T(128)S(1)}, f32[128,2004]{0,1:T(8,128)}, f32[128,2004]{0,1:T(8,128)}) fusion(f32[]{:T(128)} %bitcast.229, bf16[128,2048]{0,1:T(8,128)(2,1)S(1)} %bitcast.238, bf16[2048,4008]{0,1:T(8,128)(2,1)} %bitcast.233), kind=kOutput, calls=%fused_computation.125 | convolution fusion | flops 1051186048 | bytes 10802176 | tf_op jit(solution)/shard_map/dot_general | solution.py:91
  35.6 1.5 %collective-permute-start.1 = (f32[128,2004]{0,1:T(8,128)}, f32[128,2004]{0,1:T(8,128)}, u32[]{:S(2)}, u32[]{:S(2)}) collective-permute-start(f32[128,2004]{0,1:T(8,128)} %get-tuple-element.26), channel_id=1, source_target_pairs={{0,16},{16,0},{1,17},{17,1},{2,18},{18,2},{3,19},{19,3},{4,20},{20... | collective-permute-start | bytes 3078152 | tf_op jit(solution)/shard_map/ppermute | solution.py:95
  37.1 7.0 %fusion.55 = (f32[128]{0:T(128)S(1)}, f32[128,2004]{0,1:T(8,128)}, f32[128,2004]{0,1:T(8,128)}) fusion(f32[]{:T(128)} %bitcast.224, bf16[128,2048]{0,1:T(8,128)(2,1)S(1)} %bitcast.239, bf16[2048,4008]{0,1:T(8,128)(2,1)} %bitcast.234), kind=kOutput, calls=%fused_computation.126 | convolution fusion | flops 1051186048 | bytes 10802176 | tf_op jit(solution)/shard_map/dot_general | solution.py:91
  44.6 18.8 %all-gather.4 = bf16[16,129,128]{2,1,0:T(8,128)(2,1)S(1)} all-gather(bf16[1,129,128]{2,1,0:T(8,128)(2,1)S(1)} %maximum_bitcast_fusion.1), channel_id=3, replica_groups=mesh['member'=2,'vocab'=16] {'vocab'}, dimensions={0}, use_global_device_ids=true | all-gather | bytes 561408 | tf_op jit(solution)/shard_map/all_gather | solution.py:61
  64.7 8.4 %fusion.57 = (f32[128]{0:T(128)S(1)}, f32[128,4008]{0,1:T(8,128)S(1)}) fusion(bf16[128,2048]{0,1:T(8,128)(2,1)S(1)} %bitcast.236, bf16[1,2048,4008]{1,2,0:T(8,128)(2,1)} %param.6), kind=kOutput, calls=%fused_computation.128 | convolution fusion | flops 2101859200 | bytes 18993664 | tf_op jit(solution)/shard_map/dot_general | solution.py:99
  73.1 1.8 %fusion.12 = f32[128]{0:T(128)S(1)} fusion(f32[128,2004]{0,1:T(8,128)S(1)} %copy-done.3, f32[128,2004]{0,1:T(8,128)} %get-tuple-element.33, f32[128]{0:T(128)S(1)} %reduce_max.82), kind=kLoop, calls=%fused_computation.19 | loop fusion | flops 1538944 | bytes 2053120 | tf_op jit(solution)/shard_map/reduce_sum | solution.py:12
  74.9 1.8 %exponential_reduce_fusion = (f32[128]{0:T(128)S(1)}, f32[128,4008]{0,1:T(8,128)}) fusion(f32[128,4008]{0,1:T(8,128)S(1)} %get-tuple-element.35, f32[128]{0:T(128)S(1)} %get-tuple-element.34, f32[]{:T(128)} %bitcast.227), kind=kLoop, calls=%fused_computation.20 | loop fusion | flops 1538944 | bytes 4105220 | tf_op jit(solution)/shard_map/reduce_sum | solution.py:12
  76.7 1.6 %collective-permute-start.9 = (f32[3,256]{1,0:T(4,128)S(1)}, f32[3,256]{1,0:T(4,128)S(1)}, u32[]{:S(2)}, u32[]{:S(2)}) collective-permute-start(f32[3,256]{1,0:T(4,128)S(1)} %fusion.21), channel_id=1, source_target_pairs={{0,16},{16,0},{1,17},{17,1},{2,18},{18,2},{3,19},{19,3},{4,20},{20... | collective-permute-start | bytes 9224 | tf_op jit(solution)/shard_map/ppermute | solution.py:105
  78.8 22.0 %all-gather.5 = bf16[16,255,128]{2,1,0:T(8,128)(2,1)S(1)} all-gather(bf16[1,255,128]{2,1,0:T(8,128)(2,1)S(1)} %dynamic-slice_bitcast_fusion), channel_id=4, replica_groups=mesh['member'=2,'vocab'=16] {'vocab'}, dimensions={0}, use_global_device_ids=true | all-gather | bytes 1109760 | tf_op jit(solution)/shard_map/all_gather | solution.py:61
  102.4 10.1 %fusion.17 = f32[256,4008]{0,1:T(8,128)} fusion(bf16[255,2048]{0,1:T(8,128)(2,1)S(1)} %bitcast.237, bf16[1,2048]{0,1:T(8,128)(2,1)S(1)} %bitcast.235, bf16[1,2048,4008]{1,2,0:T(8,128)(2,1)} %param.6), kind=kOutput, calls=%fused_computation.34 | convolution fusion | flops 4204789760 | bytes 21569536 | tf_op jit(solution)/shard_map/dot_general | solution.py:107
  112.5 2.1 %slice_reduce_fusion = f32[128]{0:T(128)S(1)} fusion(f32[256,4008]{0,1:T(8,128)} %fusion.17), kind=kLoop, calls=%fused_computation.26 | loop fusion | flops 512896 | bytes 2052608 | tf_op jit(solution)/shard_map/reduce_max | solution.py:11
  114.7 2.9 %exponential_reduce_fusion.2 = (f32[128]{0:T(128)S(1)}, f32[128]{0:T(128)S(1)}) fusion(f32[256,4008]{0,1:T(8,128)} %fusion.17, f32[128]{0:T(128)S(1)} %slice_reduce_fusion), kind=kLoop, calls=%fused_computation.22 | loop fusion | flops 1538816 | bytes 4105728 | tf_op jit(solution)/shard_map/reduce_sum | solution.py:12
  118.0 2.1 %fusion.53 = (f32[128]{0:T(128)S(1)}, f32[128,4008]{0,1:T(8,128)S(1)}, f32[128]{0:T(128)S(1)}) fusion(f32[128,2004]{0,1:T(8,128)} %collective-permute-done.1, f32[128,2004]{0,1:T(8,128)} %collective-permute-done, f32[256,4008]{0,1:T(8,128)S(1)} %copy-done.1, f32[]{:T(128)} %bitcast.223, f32[128]{0:T(128)S(1)} %get-tuple-element.11), kind=kLoop, calls=%fused_computation.124 | loop fusion | flops 3077888 | bytes 6157828 | tf_op jit(solution)/shard_map/reduce_max | solution.py:11
  121.2 1.6 %collective-permute-start.4 = (f32[2,1,256]{2,0,1:T(2,128)S(1)}, f32[2,1,256]{2,0,1:T(2,128)S(1)}, u32[]{:S(2)}, u32[]{:S(2)}) collective-permute-start(f32[2,1,256]{2,0,1:T(2,128)S(1)} %fusion.62), channel_id=1, source_target_pairs={{0,2},{1,3},{2,0},{3,1},{4,6},{5,7},{6,4},{7,5},{8,10},{9,11},{10,... | collective-permute-start | bytes 6152 | tf_op jit(solution)/shard_map/ppermute | solution.py:27
  122.8 1.0 collective-permute-done.5
  123.8 1.0 collective-permute-done.4
  124.8 0.8 collective-permute-start.8
  125.6 3.7 %collective-permute-start.6 = (f32[2,1,256]{2,1,0:T(1,128)S(1)}, f32[2,1,256]{2,1,0:T(1,128)S(1)}, u32[]{:S(2)}, u32[]{:S(2)}) collective-permute-start(f32[2,1,256]{2,1,0:T(1,128)S(1)} %pad_maximum_fusion.2), channel_id=1, source_target_pairs={{0,4},{1,5},{2,6},{3,7},{4,0},{5,1},{6,2},{7,3},{8,12},{9,13},{10,... | collective-permute-start | bytes 6152 | tf_op jit(solution)/shard_map/ppermute | solution.py:27
  129.3 1.0 collective-permute-done.8
  130.9 2.1 %fusion.52 = (f32[128]{0:T(128)S(1)}, f32[128,4008]{0,1:T(8,128)S(1)}) fusion(f32[128,4008]{0,1:T(8,128)} %collective-permute-done.2, f32[256,4008]{0,1:T(8,128)S(1)} %copy-done.1, f32[]{:T(128)} %bitcast.228), kind=kLoop, calls=%fused_computation.123 | loop fusion | flops 1538944 | bytes 6156804 | tf_op jit(solution)/shard_map/reduce_max | solution.py:11
  133.6 1.7 %collective-permute-start.11 = (f32[2,1,512]{2,0,1:T(2,128)S(1)}, f32[2,1,512]{2,0,1:T(2,128)S(1)}, u32[]{:S(2)}, u32[]{:S(2)}) collective-permute-start(f32[2,1,512]{2,0,1:T(2,128)S(1)} %fusion.61), channel_id=1, source_target_pairs={{0,2},{1,3},{2,0},{3,1},{4,6},{5,7},{6,4},{7,5},{8,10},{9,11},{10,... | collective-permute-start | bytes 12296 | tf_op jit(solution)/shard_map/ppermute | solution.py:27
  135.5 1.2 collective-permute-done.12
  136.7 0.7 collective-permute-done.11
  137.4 2.4 %collective-permute-start.15 = (f32[2,1,512]{2,1,0:T(1,128)S(1)}, f32[2,1,512]{2,1,0:T(1,128)S(1)}, u32[]{:S(2)}, u32[]{:S(2)}) collective-permute-start(f32[2,1,512]{2,1,0:T(1,128)S(1)} %pad_maximum_fusion.1), channel_id=1, source_target_pairs={{0,12},{1,13},{2,14},{3,15},{4,8},{5,9},{6,10},{7,11},{8,4},{9,5},... | collective-permute-start | bytes 12296 | tf_op jit(solution)/shard_map/ppermute | solution.py:27
  139.8 1.1 collective-permute-start.14
  140.9 0.9 collective-permute-start.13
  141.8 1.0 collective-permute-done.15
  142.8 1.5 collective-permute-done.14
  144.6 2.3 %fusion.4 = f32[256,4008]{0,1:T(8,128)} fusion(f32[128,4008]{0,1:T(8,128)S(1)} %get-tuple-element.17, f32[128,4008]{0,1:T(8,128)S(1)} %get-tuple-element.21, f32[256]{0:T(256)S(1)} %get-tuple-element.12, f32[256]{0:T(256)S(1)} %get-tuple-element.13), kind=kLoop, calls=%fused_computation.5 | loop fusion | flops 3078144 | bytes 8210432 | tf_op jit(solution)/shard_map/sub | solution.py:144
  (66 shorter events, 8.1 us)
Async XLA Ops:
  0.6 0.9 copy-start
  35.6 81.9 %collective-permute-start.1 = (f32[128,2004]{0,1:T(8,128)}, f32[128,2004]{0,1:T(8,128)}, u32[]{:S(2)}, u32[]{:S(2)}) collective-permute-start(f32[128,2004]{0,1:T(8,128)} %get-tuple-element.26), channel_id=1, source_target_pairs={{0,16},{16,0},{1,17},{17,1},{2,18},{18,2},{3,19},{19,3},{4,20},{20... | collective-permute-start | bytes 3078152 | tf_op jit(solution)/shard_map/ppermute | solution.py:95
  44.1 73.5 %collective-permute-start = (f32[128,2004]{0,1:T(8,128)}, f32[128,2004]{0,1:T(8,128)}, u32[]{:S(2)}, u32[]{:S(2)}) collective-permute-start(f32[128,2004]{0,1:T(8,128)} %get-tuple-element.7), channel_id=1, source_target_pairs={{0,16},{16,0},{1,17},{17,1},{2,18},{18,2},{3,19},{19,3},{4,20},{20... | collective-permute-start | bytes 3078152 | tf_op jit(solution)/shard_map/ppermute | solution.py:95
  64.6 14.2 %copy-start.2 = (bf16[129,16,128]{0,2,1:T(8,128)(2,1)}, bf16[129,16,128]{0,2,1:T(8,128)(2,1)S(1)}, u32[]{:S(2)}) copy-start(bf16[129,16,128]{0,2,1:T(8,128)(2,1)S(1)} %fusion.16) | copy-start | bytes 1585156
  64.7 8.4 %copy-start.3 = (f32[128,2004]{0,1:T(8,128)S(1)}, f32[128,2004]{0,1:T(8,128)}, u32[]{:S(2)}) copy-start(f32[128,2004]{0,1:T(8,128)} %get-tuple-element.36) | copy-start | bytes 3078148
  76.7 52.6 %collective-permute-start.9 = (f32[3,256]{1,0:T(4,128)S(1)}, f32[3,256]{1,0:T(4,128)S(1)}, u32[]{:S(2)}, u32[]{:S(2)}) collective-permute-start(f32[3,256]{1,0:T(4,128)S(1)} %fusion.21), channel_id=1, source_target_pairs={{0,16},{16,0},{1,17},{17,1},{2,18},{18,2},{3,19},{19,3},{4,20},{20... | collective-permute-start | bytes 9224 | tf_op jit(solution)/shard_map/ppermute | solution.py:105
  78.3 52.6 %collective-permute-start.2 = (f32[128,4008]{0,1:T(8,128)}, f32[128,4008]{0,1:T(8,128)}, u32[]{:S(2)}, u32[]{:S(2)}) collective-permute-start(f32[128,4008]{0,1:T(8,128)} %get-tuple-element.24), channel_id=1, source_target_pairs={{0,16},{16,0},{1,17},{17,1},{2,18},{18,2},{3,19},{19,3},{4,20},{20... | collective-permute-start | bytes 6156296 | tf_op jit(solution)/shard_map/ppermute | solution.py:100
  101.4 1.0 slice-start
  114.7 3.4 %copy-start.1 = (f32[256,4008]{0,1:T(8,128)S(1)}, f32[256,4008]{0,1:T(8,128)}, u32[]{:S(2)}) copy-start(f32[256,4008]{0,1:T(8,128)} %fusion.17) | copy-start | bytes 12312580
  120.7 3.1 %collective-permute-start.5 = (f32[2,1,256]{2,0,1:T(2,128)S(1)}, f32[2,1,256]{2,0,1:T(2,128)S(1)}, u32[]{:S(2)}, u32[]{:S(2)}) collective-permute-start(f32[2,1,256]{2,0,1:T(2,128)S(1)} %fusion.62), channel_id=1, source_target_pairs={{0,3},{1,2},{2,1},{3,0},{4,7},{5,6},{6,5},{7,4},{8,11},{9,10},{10,... | collective-permute-start | bytes 6152 | tf_op jit(solution)/shard_map/ppermute | solution.py:27
  121.2 3.6 %collective-permute-start.4 = (f32[2,1,256]{2,0,1:T(2,128)S(1)}, f32[2,1,256]{2,0,1:T(2,128)S(1)}, u32[]{:S(2)}, u32[]{:S(2)}) collective-permute-start(f32[2,1,256]{2,0,1:T(2,128)S(1)} %fusion.62), channel_id=1, source_target_pairs={{0,2},{1,3},{2,0},{3,1},{4,6},{5,7},{6,4},{7,5},{8,10},{9,11},{10,... | collective-permute-start | bytes 6152 | tf_op jit(solution)/shard_map/ppermute | solution.py:27
  122.8 2.0 %collective-permute-start.3 = (f32[2,1,256]{2,0,1:T(2,128)S(1)}, f32[2,1,256]{2,0,1:T(2,128)S(1)}, u32[]{:S(2)}, u32[]{:S(2)}) collective-permute-start(f32[2,1,256]{2,0,1:T(2,128)S(1)} %fusion.62), channel_id=1, source_target_pairs={{0,1},{1,0},{2,3},{3,2},{4,5},{5,4},{6,7},{7,6},{8,9},{9,8},{10,11... | collective-permute-start | bytes 6152 | tf_op jit(solution)/shard_map/ppermute | solution.py:27
  124.8 5.4 %collective-permute-start.8 = (f32[2,1,256]{2,1,0:T(1,128)S(1)}, f32[2,1,256]{2,1,0:T(1,128)S(1)}, u32[]{:S(2)}, u32[]{:S(2)}) collective-permute-start(f32[2,1,256]{2,1,0:T(1,128)S(1)} %pad_maximum_fusion.2), channel_id=1, source_target_pairs={{0,12},{1,13},{2,14},{3,15},{4,8},{5,9},{6,10},{7,11},{8,4},{9,5},... | collective-permute-start | bytes 6152 | tf_op jit(solution)/shard_map/ppermute | solution.py:27
  125.6 4.7 %collective-permute-start.7 = (f32[2,1,256]{2,1,0:T(1,128)S(1)}, f32[2,1,256]{2,1,0:T(1,128)S(1)}, u32[]{:S(2)}, u32[]{:S(2)}) collective-permute-start(f32[2,1,256]{2,1,0:T(1,128)S(1)} %pad_maximum_fusion.2), channel_id=1, source_target_pairs={{0,8},{1,9},{2,10},{3,11},{4,12},{5,13},{6,14},{7,15},{8,0},{9,1},... | collective-permute-start | bytes 6152 | tf_op jit(solution)/shard_map/ppermute | solution.py:27
  125.6 5.3 %collective-permute-start.6 = (f32[2,1,256]{2,1,0:T(1,128)S(1)}, f32[2,1,256]{2,1,0:T(1,128)S(1)}, u32[]{:S(2)}, u32[]{:S(2)}) collective-permute-start(f32[2,1,256]{2,1,0:T(1,128)S(1)} %pad_maximum_fusion.2), channel_id=1, source_target_pairs={{0,4},{1,5},{2,6},{3,7},{4,0},{5,1},{6,2},{7,3},{8,12},{9,13},{10,... | collective-permute-start | bytes 6152 | tf_op jit(solution)/shard_map/ppermute | solution.py:27
  133.6 3.1 %collective-permute-start.12 = (f32[2,1,512]{2,0,1:T(2,128)S(1)}, f32[2,1,512]{2,0,1:T(2,128)S(1)}, u32[]{:S(2)}, u32[]{:S(2)}) collective-permute-start(f32[2,1,512]{2,0,1:T(2,128)S(1)} %fusion.61), channel_id=1, source_target_pairs={{0,3},{1,2},{2,1},{3,0},{4,7},{5,6},{6,5},{7,4},{8,11},{9,10},{10,... | collective-permute-start | bytes 12296 | tf_op jit(solution)/shard_map/ppermute | solution.py:27
  133.6 3.7 %collective-permute-start.11 = (f32[2,1,512]{2,0,1:T(2,128)S(1)}, f32[2,1,512]{2,0,1:T(2,128)S(1)}, u32[]{:S(2)}, u32[]{:S(2)}) collective-permute-start(f32[2,1,512]{2,0,1:T(2,128)S(1)} %fusion.61), channel_id=1, source_target_pairs={{0,2},{1,3},{2,0},{3,1},{4,6},{5,7},{6,4},{7,5},{8,10},{9,11},{10,... | collective-permute-start | bytes 12296 | tf_op jit(solution)/shard_map/ppermute | solution.py:27
  135.3 2.0 %collective-permute-start.10 = (f32[2,1,512]{2,0,1:T(2,128)S(1)}, f32[2,1,512]{2,0,1:T(2,128)S(1)}, u32[]{:S(2)}, u32[]{:S(2)}) collective-permute-start(f32[2,1,512]{2,0,1:T(2,128)S(1)} %fusion.61), channel_id=1, source_target_pairs={{0,1},{1,0},{2,3},{3,2},{4,5},{5,4},{6,7},{7,6},{8,9},{9,8},{10,11... | collective-permute-start | bytes 12296 | tf_op jit(solution)/shard_map/ppermute | solution.py:27
  137.4 5.5 %collective-permute-start.15 = (f32[2,1,512]{2,1,0:T(1,128)S(1)}, f32[2,1,512]{2,1,0:T(1,128)S(1)}, u32[]{:S(2)}, u32[]{:S(2)}) collective-permute-start(f32[2,1,512]{2,1,0:T(1,128)S(1)} %pad_maximum_fusion.1), channel_id=1, source_target_pairs={{0,12},{1,13},{2,14},{3,15},{4,8},{5,9},{6,10},{7,11},{8,4},{9,5},... | collective-permute-start | bytes 12296 | tf_op jit(solution)/shard_map/ppermute | solution.py:27
  139.8 4.5 %collective-permute-start.14 = (f32[2,1,512]{2,1,0:T(1,128)S(1)}, f32[2,1,512]{2,1,0:T(1,128)S(1)}, u32[]{:S(2)}, u32[]{:S(2)}) collective-permute-start(f32[2,1,512]{2,1,0:T(1,128)S(1)} %pad_maximum_fusion.1), channel_id=1, source_target_pairs={{0,8},{1,9},{2,10},{3,11},{4,12},{5,13},{6,14},{7,15},{8,0},{9,1},... | collective-permute-start | bytes 12296 | tf_op jit(solution)/shard_map/ppermute | solution.py:27
  140.9 3.6 %collective-permute-start.13 = (f32[2,1,512]{2,1,0:T(1,128)S(1)}, f32[2,1,512]{2,1,0:T(1,128)S(1)}, u32[]{:S(2)}, u32[]{:S(2)}) collective-permute-start(f32[2,1,512]{2,1,0:T(1,128)S(1)} %pad_maximum_fusion.1), channel_id=1, source_target_pairs={{0,4},{1,5},{2,6},{3,7},{4,0},{5,1},{6,2},{7,3},{8,12},{9,13},{10,... | collective-permute-start | bytes 12296 | tf_op jit(solution)/shard_map/ppermute | solution.py:27
  144.6 2.3 %copy-start.4 = (f32[256]{0:T(256)}, f32[256]{0:T(256)S(1)}, u32[]{:S(2)}) copy-start(f32[256]{0:T(256)S(1)} %get-tuple-element.12) | copy-start | bytes 3076

commit v17 on v14

--- a/solution.py
+++ b/solution.py
@@ -22,7 +22,7 @@
         return peak, summed
     stride = 1
     while stride < size:
-        radix = 4 if stride * 4 <= size else 2
+        radix = 4 if stride == 1 and size >= 4 else 2
         others = [
             lax.ppermute(stats, axis, [(a, a ^ (j * stride)) for a in range(size)])
             for j in range(1, radix)

time: 144 us -> 147 us (1.021)
  waiting for transfers between devices: 7.88 us -> 19.2 us
  starting transfers between devices: 16.8 us -> 8.4 us
    ppermute x12 -> x10, waiting for transfers between devices: 7.38 us -> 17.6 us  [reduce_stats(): lax.ppermute(stats, axis, [(a, a ^ j * stride) for a in range(size)])]
    ppermute x12 -> x10, starting transfers between devices: 12.7 us -> 4.28 us  [reduce_stats(): lax.ppermute(stats, axis, [(a, a ^ j * stride) for a in range(size)])]
  transfers between devices with their start and end apart: 16 -> 14, of which waited for: 10 -> 9; matrix products, arithmetic and copies ran while one was open for 26% -> 25% of each run, Pallas kernels for 0% -> 0%
where the time goes in v17:
time: 147 us
  blocking collectives  65.6 us (45%)
  matrix products  32.6 us (22%)
  waiting for transfers between devices  19.2 us (13%)
  other arithmetic  16.9 us (11%)
  starting transfers between devices  8.4 us (6%)
  local copies, waits for them, and re-layouts  2.76 us (2%)
  between operations  1.58 us (1%)
    all_gather x3, blocking collectives, normed_of(): gathered = lax.all_gather(packed, 'vocab', axis=0, tiled=False)  65.6 us
    ppermute x10, waiting for transfers between devices, reduce_stats(): lax.ppermute(stats, axis, [(a, a ^ j * stride) for a in range(size)])  17.6 us
    dot_general x2, matrix products, on_device(): jnp.dot(normed, columns, preferred_element_type=jnp.float32)  14 us
    dot_general x1, matrix products, on_device(): jnp.dot(own_normed, weights, preferred_element_type=jnp.float32)  10.2 us
    dot_general x1, matrix products, on_device(): logits = jnp.dot(normed, weights, preferred_element_type=jnp.float32)  8.34 us
    reduce_max x4, other arithmetic, local_stats(): local_peak = jnp.max(values, axis=1)  6.41 us
    reduce_sum x5, other arithmetic, local_stats(): local_sum = jnp.sum(jnp.exp(values - local_peak[:, None]), axis=1)  5.36 us
    ppermute x10, starting transfers between devices, reduce_stats(): lax.ppermute(stats, axis, [(a, a ^ j * stride) for a in range(size)])  4.28 us
  transfers between devices with their start and end apart: 14, of which 9 were waited for; matrix products, arithmetic and copies ran while one was open for 25% of the time, Pallas kernels for 0%

profile of v17, /device:TPU:0, one launch (start us, length us, event | category | flops | bytes accessed | tf_op | source)
XLA Modules:
  0.0 147.0 jit_solution(10421556955913330976)
XLA Ops:
  0.7 0.9 copy-done
  1.5 0.7 maximum_bitcast_fusion
  2.2 24.7 %all-gather.3 = bf16[16,129,128]{2,1,0:T(8,128)(2,1)S(1)} all-gather(bf16[1,129,128]{2,1,0:T(8,128)(2,1)S(1)} %maximum_bitcast_fusion), channel_id=2, replica_groups=mesh['member'=2,'vocab'=16] {'vocab'}, dimensions={0}, use_global_device_ids=true | all-gather | bytes 561408 | tf_op jit(solution)/shard_map/all_gather | solution.py:61
  28.5 7.0 %fusion.58 = (f32[128]{0:T(128)S(1)}, f32[128,2004]{0,1:T(8,128)}, f32[128,2004]{0,1:T(8,128)}) fusion(f32[]{:T(128)} %bitcast.215, bf16[128,2048]{0,1:T(8,128)(2,1)S(1)} %bitcast.224, bf16[2048,4008]{0,1:T(8,128)(2,1)} %bitcast.219), kind=kOutput, calls=%fused_computation.129 | convolution fusion | flops 1051186048 | bytes 10802176 | tf_op jit(solution)/shard_map/dot_general | solution.py:91
  35.6 1.5 %collective-permute-start.1 = (f32[128,2004]{0,1:T(8,128)}, f32[128,2004]{0,1:T(8,128)}, u32[]{:S(2)}, u32[]{:S(2)}) collective-permute-start(f32[128,2004]{0,1:T(8,128)} %get-tuple-element.30), channel_id=1, source_target_pairs={{0,16},{16,0},{1,17},{17,1},{2,18},{18,2},{3,19},{19,3},{4,20},{20... | collective-permute-start | bytes 3078152 | tf_op jit(solution)/shard_map/ppermute | solution.py:95
  37.1 7.0 %fusion.59 = (f32[128]{0:T(128)S(1)}, f32[128,2004]{0,1:T(8,128)}, f32[128,2004]{0,1:T(8,128)}) fusion(f32[]{:T(128)} %bitcast.210, bf16[128,2048]{0,1:T(8,128)(2,1)S(1)} %bitcast.225, bf16[2048,4008]{0,1:T(8,128)(2,1)} %bitcast.220), kind=kOutput, calls=%fused_computation.130 | convolution fusion | flops 1051186048 | bytes 10802176 | tf_op jit(solution)/shard_map/dot_general | solution.py:91
  44.6 18.8 %all-gather.4 = bf16[16,129,128]{2,1,0:T(8,128)(2,1)S(1)} all-gather(bf16[1,129,128]{2,1,0:T(8,128)(2,1)S(1)} %maximum_bitcast_fusion.1), channel_id=3, replica_groups=mesh['member'=2,'vocab'=16] {'vocab'}, dimensions={0}, use_global_device_ids=true | all-gather | bytes 561408 | tf_op jit(solution)/shard_map/all_gather | solution.py:61
  64.7 8.3 %fusion.61 = (f32[128]{0:T(128)S(1)}, f32[128,4008]{0,1:T(8,128)S(1)}) fusion(bf16[128,2048]{0,1:T(8,128)(2,1)S(1)} %bitcast.222, bf16[1,2048,4008]{1,2,0:T(8,128)(2,1)} %param.6), kind=kOutput, calls=%fused_computation.132 | convolution fusion | flops 2101859200 | bytes 18993664 | tf_op jit(solution)/shard_map/dot_general | solution.py:99
  73.1 1.8 %exponential_reduce_fusion.4 = (f32[128]{0:T(128)S(1)}, f32[128,4008]{0,1:T(8,128)}) fusion(f32[128,4008]{0,1:T(8,128)S(1)} %get-tuple-element.43, f32[128]{0:T(128)S(1)} %get-tuple-element.42, f32[]{:T(128)} %bitcast.213), kind=kLoop, calls=%fused_computation.25 | loop fusion | flops 1538944 | bytes 4105220 | tf_op jit(solution)/shard_map/reduce_sum | solution.py:12
  74.9 1.5 %collective-permute-start.2 = (f32[128,4008]{0,1:T(8,128)}, f32[128,4008]{0,1:T(8,128)}, u32[]{:S(2)}, u32[]{:S(2)}) collective-permute-start(f32[128,4008]{0,1:T(8,128)} %get-tuple-element.28), channel_id=1, source_target_pairs={{0,16},{16,0},{1,17},{17,1},{2,18},{18,2},{3,19},{19,3},{4,20},{20... | collective-permute-start | bytes 6156296 | tf_op jit(solution)/shard_map/ppermute | solution.py:100
  76.4 22.1 %all-gather.5 = bf16[16,255,128]{2,1,0:T(8,128)(2,1)S(1)} all-gather(bf16[1,255,128]{2,1,0:T(8,128)(2,1)S(1)} %dynamic-slice_bitcast_fusion), channel_id=4, replica_groups=mesh['member'=2,'vocab'=16] {'vocab'}, dimensions={0}, use_global_device_ids=true | all-gather | bytes 1109760 | tf_op jit(solution)/shard_map/all_gather | solution.py:61
  100.1 10.2 %fusion.17 = f32[256,4008]{0,1:T(8,128)} fusion(bf16[255,2048]{0,1:T(8,128)(2,1)S(1)} %bitcast.223, bf16[1,2048]{0,1:T(8,128)(2,1)S(1)} %bitcast.221, bf16[1,2048,4008]{1,2,0:T(8,128)(2,1)} %param.6), kind=kOutput, calls=%fused_computation.34 | convolution fusion | flops 4204789760 | bytes 21569536 | tf_op jit(solution)/shard_map/dot_general | solution.py:107
  110.3 1.9 %fusion.12 = f32[128]{0:T(128)S(1)} fusion(f32[128,2004]{0,1:T(8,128)S(1)} %copy-done.3, f32[128,2004]{0,1:T(8,128)} %get-tuple-element.41, f32[128]{0:T(128)S(1)} %reduce_max.78), kind=kLoop, calls=%fused_computation.18 | loop fusion | flops 1538944 | bytes 2053120 | tf_op jit(solution)/shard_map/reduce_sum | solution.py:12
  112.2 2.1 %slice_reduce_fusion = f32[128]{0:T(128)S(1)} fusion(f32[256,4008]{0,1:T(8,128)} %fusion.17), kind=kLoop, calls=%fused_computation.26 | loop fusion | flops 512896 | bytes 2052608 | tf_op jit(solution)/shard_map/reduce_max | solution.py:11
  114.4 0.6 exponential_reduce_fusion.1
  114.9 2.1 %fusion.57 = (f32[128]{0:T(128)S(1)}, f32[128,4008]{0,1:T(8,128)S(1)}, f32[128]{0:T(128)S(1)}) fusion(f32[128,2004]{0,1:T(8,128)} %collective-permute-done.1, f32[128,2004]{0,1:T(8,128)} %collective-permute-done, f32[256,4008]{0,1:T(8,128)S(1)} %copy-done.1, f32[]{:T(128)} %bitcast.209, f32[128]{0:T(128)S(1)} %get-tuple-element.15), kind=kLoop, calls=%fused_computation.128 | loop fusion | flops 3077888 | bytes 6157828 | tf_op jit(solution)/shard_map/reduce_max | solution.py:11
  117.1 0.6 exponential_reduce_fusion.2
  117.9 1.7 %collective-permute-start.4 = (f32[2,1,256]{2,0,1:T(2,128)S(1)}, f32[2,1,256]{2,0,1:T(2,128)S(1)}, u32[]{:S(2)}, u32[]{:S(2)}) collective-permute-start(f32[2,1,256]{2,0,1:T(2,128)S(1)} %fusion.66), channel_id=1, source_target_pairs={{0,2},{1,3},{2,0},{3,1},{4,6},{5,7},{6,4},{7,5},{8,10},{9,11},{10,... | collective-permute-start | bytes 6152 | tf_op jit(solution)/shard_map/ppermute | solution.py:27
  119.7 1.0 collective-permute-done.5
  120.7 0.8 collective-permute-done.4
  121.6 0.6 collective-permute-start.8
  122.2 3.0 %collective-permute-done.6 = f32[2,1,256]{2,1,0:T(1,128)S(1)} collective-permute-done((f32[2,1,256]{2,1,0:T(1,128)S(1)}, f32[2,1,256]{2,1,0:T(1,128)S(1)}, u32[]{:S(2)}, u32[]{:S(2)}) %collective-permute-start.6) | collective-permute-done | bytes 2080 | tf_op jit(solution)/shard_map/ppermute | solution.py:27
  125.3 1.6 %collective-permute-done.8 = f32[3,256]{1,0:T(4,128)S(1)} collective-permute-done((f32[3,256]{1,0:T(4,128)S(1)}, f32[3,256]{1,0:T(4,128)S(1)}, u32[]{:S(2)}, u32[]{:S(2)}) %collective-permute-start.8) | collective-permute-done | bytes 3104 | tf_op jit(solution)/shard_map/ppermute | solution.py:109
  126.9 2.9 %collective-permute-done.7 = f32[2,1,256]{2,1,0:T(1,128)S(1)} collective-permute-done((f32[2,1,256]{2,1,0:T(1,128)S(1)}, f32[2,1,256]{2,1,0:T(1,128)S(1)}, u32[]{:S(2)}, u32[]{:S(2)}) %collective-permute-start.7) | collective-permute-done | bytes 2080 | tf_op jit(solution)/shard_map/ppermute | solution.py:27
  129.8 2.2 %fusion.56 = (f32[128]{0:T(128)S(1)}, f32[128,4008]{0,1:T(8,128)S(1)}) fusion(f32[128,4008]{0,1:T(8,128)} %collective-permute-done.2, f32[256,4008]{0,1:T(8,128)S(1)} %copy-done.1, f32[]{:T(128)} %bitcast.214), kind=kLoop, calls=%fused_computation.127 | loop fusion | flops 1538944 | bytes 6156804 | tf_op jit(solution)/shard_map/reduce_max | solution.py:11
  132.0 0.6 exponential_reduce_fusion
  132.6 1.8 %collective-permute-start.10 = (f32[2,1,512]{2,0,1:T(2,128)S(1)}, f32[2,1,512]{2,0,1:T(2,128)S(1)}, u32[]{:S(2)}, u32[]{:S(2)}) collective-permute-start(f32[2,1,512]{2,0,1:T(2,128)S(1)} %fusion.65), channel_id=1, source_target_pairs={{0,2},{1,3},{2,0},{3,1},{4,6},{5,7},{6,4},{7,5},{8,10},{9,11},{10,... | collective-permute-start | bytes 12296 | tf_op jit(solution)/shard_map/ppermute | solution.py:27
  134.5 1.1 collective-permute-done.11
  135.6 0.7 collective-permute-done.10
  136.4 3.6 %collective-permute-done.12 = f32[2,1,512]{2,1,0:T(1,128)S(1)} collective-permute-done((f32[2,1,512]{2,1,0:T(1,128)S(1)}, f32[2,1,512]{2,1,0:T(1,128)S(1)}, u32[]{:S(2)}, u32[]{:S(2)}) %collective-permute-start.12) | collective-permute-done | bytes 4128 | tf_op jit(solution)/shard_map/ppermute | solution.py:27
  140.1 4.5 %collective-permute-done.13 = f32[2,1,512]{2,1,0:T(1,128)S(1)} collective-permute-done((f32[2,1,512]{2,1,0:T(1,128)S(1)}, f32[2,1,512]{2,1,0:T(1,128)S(1)}, u32[]{:S(2)}, u32[]{:S(2)}) %collective-permute-start.13) | collective-permute-done | bytes 4128 | tf_op jit(solution)/shard_map/ppermute | solution.py:27
  144.7 2.3 %fusion.4 = f32[256,4008]{0,1:T(8,128)} fusion(f32[128,4008]{0,1:T(8,128)S(1)} %get-tuple-element.21, f32[128,4008]{0,1:T(8,128)S(1)} %get-tuple-element.25, f32[256]{0:T(256)S(1)} %get-tuple-element.16, f32[256]{0:T(256)S(1)} %get-tuple-element.17), kind=kLoop, calls=%fused_computation.5 | loop fusion | flops 3078144 | bytes 8210432 | tf_op jit(solution)/shard_map/sub | solution.py:147
  (66 shorter events, 5.3 us)
Async XLA Ops:
  0.6 0.9 copy-start
  35.6 79.4 %collective-permute-start.1 = (f32[128,2004]{0,1:T(8,128)}, f32[128,2004]{0,1:T(8,128)}, u32[]{:S(2)}, u32[]{:S(2)}) collective-permute-start(f32[128,2004]{0,1:T(8,128)} %get-tuple-element.30), channel_id=1, source_target_pairs={{0,16},{16,0},{1,17},{17,1},{2,18},{18,2},{3,19},{19,3},{4,20},{20... | collective-permute-start | bytes 3078152 | tf_op jit(solution)/shard_map/ppermute | solution.py:95
  44.1 70.8 %collective-permute-start = (f32[128,2004]{0,1:T(8,128)}, f32[128,2004]{0,1:T(8,128)}, u32[]{:S(2)}, u32[]{:S(2)}) collective-permute-start(f32[128,2004]{0,1:T(8,128)} %get-tuple-element.10), channel_id=1, source_target_pairs={{0,16},{16,0},{1,17},{17,1},{2,18},{18,2},{3,19},{19,3},{4,20},{20... | collective-permute-start | bytes 3078152 | tf_op jit(solution)/shard_map/ppermute | solution.py:95
  64.6 11.8 %copy-start.2 = (bf16[129,16,128]{0,2,1:T(8,128)(2,1)}, bf16[129,16,128]{0,2,1:T(8,128)(2,1)S(1)}, u32[]{:S(2)}) copy-start(bf16[129,16,128]{0,2,1:T(8,128)(2,1)S(1)} %fusion.16) | copy-start | bytes 1585156
  74.9 55.0 %collective-permute-start.2 = (f32[128,4008]{0,1:T(8,128)}, f32[128,4008]{0,1:T(8,128)}, u32[]{:S(2)}, u32[]{:S(2)}) collective-permute-start(f32[128,4008]{0,1:T(8,128)} %get-tuple-element.28), channel_id=1, source_target_pairs={{0,16},{16,0},{1,17},{17,1},{2,18},{18,2},{3,19},{19,3},{4,20},{20... | collective-permute-start | bytes 6156296 | tf_op jit(solution)/shard_map/ppermute | solution.py:100
  99.0 1.0 slice-start
  100.1 10.2 %copy-start.3 = (f32[128,2004]{0,1:T(8,128)S(1)}, f32[128,2004]{0,1:T(8,128)}, u32[]{:S(2)}) copy-start(f32[128,2004]{0,1:T(8,128)} %get-tuple-element.44) | copy-start | bytes 3078148
  110.3 4.1 %copy-start.1 = (f32[256,4008]{0,1:T(8,128)S(1)}, f32[256,4008]{0,1:T(8,128)}, u32[]{:S(2)}) copy-start(f32[256,4008]{0,1:T(8,128)} %fusion.17) | copy-start | bytes 12312580
  117.6 3.1 %collective-permute-start.5 = (f32[2,1,256]{2,0,1:T(2,128)S(1)}, f32[2,1,256]{2,0,1:T(2,128)S(1)}, u32[]{:S(2)}, u32[]{:S(2)}) collective-permute-start(f32[2,1,256]{2,0,1:T(2,128)S(1)} %fusion.66), channel_id=1, source_target_pairs={{0,3},{1,2},{2,1},{3,0},{4,7},{5,6},{6,5},{7,4},{8,11},{9,10},{10,... | collective-permute-start | bytes 6152 | tf_op jit(solution)/shard_map/ppermute | solution.py:27
  117.9 3.6 %collective-permute-start.4 = (f32[2,1,256]{2,0,1:T(2,128)S(1)}, f32[2,1,256]{2,0,1:T(2,128)S(1)}, u32[]{:S(2)}, u32[]{:S(2)}) collective-permute-start(f32[2,1,256]{2,0,1:T(2,128)S(1)} %fusion.66), channel_id=1, source_target_pairs={{0,2},{1,3},{2,0},{3,1},{4,6},{5,7},{6,4},{7,5},{8,10},{9,11},{10,... | collective-permute-start | bytes 6152 | tf_op jit(solution)/shard_map/ppermute | solution.py:27
  119.7 1.8 %collective-permute-start.3 = (f32[2,1,256]{2,0,1:T(2,128)S(1)}, f32[2,1,256]{2,0,1:T(2,128)S(1)}, u32[]{:S(2)}, u32[]{:S(2)}) collective-permute-start(f32[2,1,256]{2,0,1:T(2,128)S(1)} %fusion.66), channel_id=1, source_target_pairs={{0,1},{1,0},{2,3},{3,2},{4,5},{5,4},{6,7},{7,6},{8,9},{9,8},{10,11... | collective-permute-start | bytes 6152 | tf_op jit(solution)/shard_map/ppermute | solution.py:27
  121.6 3.7 %collective-permute-start.6 = (f32[2,1,256]{2,1,0:T(1,128)S(1)}, f32[2,1,256]{2,1,0:T(1,128)S(1)}, u32[]{:S(2)}, u32[]{:S(2)}) collective-permute-start(f32[2,1,256]{2,1,0:T(1,128)S(1)} %pad_maximum_fusion.3), channel_id=1, source_target_pairs={{0,4},{1,5},{2,6},{3,7},{4,0},{5,1},{6,2},{7,3},{8,12},{9,13},{10,... | collective-permute-start | bytes 6152 | tf_op jit(solution)/shard_map/ppermute | solution.py:27
  121.6 5.3 %collective-permute-start.8 = (f32[3,256]{1,0:T(4,128)S(1)}, f32[3,256]{1,0:T(4,128)S(1)}, u32[]{:S(2)}, u32[]{:S(2)}) collective-permute-start(f32[3,256]{1,0:T(4,128)S(1)} %fusion.21), channel_id=1, source_target_pairs={{0,16},{16,0},{1,17},{17,1},{2,18},{18,2},{3,19},{19,3},{4,20},{20... | collective-permute-start | bytes 9224 | tf_op jit(solution)/shard_map/ppermute | solution.py:109
  125.2 4.5 %collective-permute-start.7 = (f32[2,1,256]{2,1,0:T(1,128)S(1)}, f32[2,1,256]{2,1,0:T(1,128)S(1)}, u32[]{:S(2)}, u32[]{:S(2)}) collective-permute-start(f32[2,1,256]{2,1,0:T(1,128)S(1)} %pad_maximum_fusion.4), channel_id=1, source_target_pairs={{0,8},{1,9},{2,10},{3,11},{4,12},{5,13},{6,14},{7,15},{8,0},{9,1},... | collective-permute-start | bytes 6152 | tf_op jit(solution)/shard_map/ppermute | solution.py:27
  132.5 3.1 %collective-permute-start.11 = (f32[2,1,512]{2,0,1:T(2,128)S(1)}, f32[2,1,512]{2,0,1:T(2,128)S(1)}, u32[]{:S(2)}, u32[]{:S(2)}) collective-permute-start(f32[2,1,512]{2,0,1:T(2,128)S(1)} %fusion.65), channel_id=1, source_target_pairs={{0,3},{1,2},{2,1},{3,0},{4,7},{5,6},{6,5},{7,4},{8,11},{9,10},{10,... | collective-permute-start | bytes 12296 | tf_op jit(solution)/shard_map/ppermute | solution.py:27
  132.6 3.7 %collective-permute-start.10 = (f32[2,1,512]{2,0,1:T(2,128)S(1)}, f32[2,1,512]{2,0,1:T(2,128)S(1)}, u32[]{:S(2)}, u32[]{:S(2)}) collective-permute-start(f32[2,1,512]{2,0,1:T(2,128)S(1)} %fusion.65), channel_id=1, source_target_pairs={{0,2},{1,3},{2,0},{3,1},{4,6},{5,7},{6,4},{7,5},{8,10},{9,11},{10,... | collective-permute-start | bytes 12296 | tf_op jit(solution)/shard_map/ppermute | solution.py:27
  134.4 1.9 %collective-permute-start.9 = (f32[2,1,512]{2,0,1:T(2,128)S(1)}, f32[2,1,512]{2,0,1:T(2,128)S(1)}, u32[]{:S(2)}, u32[]{:S(2)}) collective-permute-start(f32[2,1,512]{2,0,1:T(2,128)S(1)} %fusion.65), channel_id=1, source_target_pairs={{0,1},{1,0},{2,3},{3,2},{4,5},{5,4},{6,7},{7,6},{8,9},{9,8},{10,11... | collective-permute-start | bytes 12296 | tf_op jit(solution)/shard_map/ppermute | solution.py:27
  136.3 3.7 %collective-permute-start.12 = (f32[2,1,512]{2,1,0:T(1,128)S(1)}, f32[2,1,512]{2,1,0:T(1,128)S(1)}, u32[]{:S(2)}, u32[]{:S(2)}) collective-permute-start(f32[2,1,512]{2,1,0:T(1,128)S(1)} %pad_maximum_fusion.1), channel_id=1, source_target_pairs={{0,4},{1,5},{2,6},{3,7},{4,0},{5,1},{6,2},{7,3},{8,12},{9,13},{10,... | collective-permute-start | bytes 12296 | tf_op jit(solution)/shard_map/ppermute | solution.py:27
  140.0 4.6 %collective-permute-start.13 = (f32[2,1,512]{2,1,0:T(1,128)S(1)}, f32[2,1,512]{2,1,0:T(1,128)S(1)}, u32[]{:S(2)}, u32[]{:S(2)}) collective-permute-start(f32[2,1,512]{2,1,0:T(1,128)S(1)} %pad_maximum_fusion.2), channel_id=1, source_target_pairs={{0,8},{1,9},{2,10},{3,11},{4,12},{5,13},{6,14},{7,15},{8,0},{9,1},... | collective-permute-start | bytes 12296 | tf_op jit(solution)/shard_map/ppermute | solution.py:27
  144.7 2.3 %copy-start.4 = (f32[256]{0:T(256)}, f32[256]{0:T(256)S(1)}, u32[]{:S(2)}) copy-start(f32[256]{0:T(256)S(1)} %get-tuple-element.16) | copy-start | bytes 3076

commit v18 on v17

--- a/solution.py
+++ b/solution.py
@@ -22,7 +22,7 @@
         return peak, summed
     stride = 1
     while stride < size:
-        radix = 4 if stride == 1 and size >= 4 else 2
+        radix = min(size // stride, 16)
         others = [
             lax.ppermute(stats, axis, [(a, a ^ (j * stride)) for a in range(size)])
             for j in range(1, radix)
@@ -32,11 +32,9 @@
         for value in values[1:]:
             peak = jnp.maximum(peak, value[0])
         terms = [value[1] * jnp.exp(value[0] - peak) for value in values]
-        if radix == 4:
-            summed = (terms[0] + terms[1]) + (terms[2] + terms[3])
-        else:
-            summed = terms[0] + terms[1]
-        stats = jnp.stack([peak, summed])
+        while len(terms) > 1:
+            terms = [terms[j] + terms[j + 1] for j in range(0, len(terms), 2)]
+        stats = jnp.stack([peak, terms[0]])
         stride *= radix
     return stats[0], stats[1]
 

time: 147 us -> 171 us (1.16)
  starting transfers between devices: 8.4 us -> 41 us
  waiting for transfers between devices: 19.2 us -> 10.3 us
    ppermute x10 -> x30, starting transfers between devices: 4.28 us -> 36.9 us  [reduce_stats(): lax.ppermute(stats, axis, [(a, a ^ j * stride) for a in range(size)])]
    ppermute x10 -> x30, waiting for transfers between devices: 17.6 us -> 6.1 us  [reduce_stats(): lax.ppermute(stats, axis, [(a, a ^ j * stride) for a in range(size)])]
    ppermute x1, waiting for transfers between devices: 1.59 us -> 4.23 us  [on_device(): lax.ppermute(note, 'member', [(g, (g + shift) % members) for g in range(m...]
  transfers between devices with their start and end apart: 14 -> 34, of which waited for: 9 -> 7; matrix products, arithmetic and copies ran while one was open for 25% -> 22% of each run, Pallas kernels for 0% -> 0%
where the time goes in v18:
time: 171 us
  blocking collectives  65.6 us (38%)
  starting transfers between devices  41 us (24%)
  matrix products  32.6 us (19%)
  other arithmetic  16.9 us (10%)
  waiting for transfers between devices  10.3 us (6%)
  local copies, waits for them, and re-layouts  2.76 us (2%)
    all_gather x3, blocking collectives, normed_of(): gathered = lax.all_gather(packed, 'vocab', axis=0, tiled=False)  65.6 us
    ppermute x30, starting transfers between devices, reduce_stats(): lax.ppermute(stats, axis, [(a, a ^ j * stride) for a in range(size)])  36.9 us
    dot_general x2, matrix products, on_device(): jnp.dot(normed, columns, preferred_element_type=jnp.float32)  14.1 us
    dot_general x1, matrix products, on_device(): jnp.dot(own_normed, weights, preferred_element_type=jnp.float32)  10.2 us
    dot_general x1, matrix products, on_device(): logits = jnp.dot(normed, weights, preferred_element_type=jnp.float32)  8.34 us
    reduce_max x4, other arithmetic, local_stats(): local_peak = jnp.max(values, axis=1)  6.41 us
    ppermute x30, waiting for transfers between devices, reduce_stats(): lax.ppermute(stats, axis, [(a, a ^ j * stride) for a in range(size)])  6.1 us
    reduce_sum x5, other arithmetic, local_stats(): local_sum = jnp.sum(jnp.exp(values - local_peak[:, None]), axis=1)  5.38 us
  transfers between devices with their start and end apart: 34, of which 7 were waited for; matrix products, arithmetic and copies ran while one was open for 22% of the time, Pallas kernels for 0%

profile of v18, /device:TPU:0, one launch (start us, length us, event | category | flops | bytes accessed | tf_op | source)
XLA Modules:
  0.0 170.8 jit_solution(16537930543551185345)
XLA Ops:
  2.2 24.7 %all-gather.3 = bf16[16,129,128]{2,1,0:T(8,128)(2,1)S(1)} all-gather(bf16[1,129,128]{2,1,0:T(8,128)(2,1)S(1)} %maximum_bitcast_fusion), channel_id=2, replica_groups=mesh['member'=2,'vocab'=16] {'vocab'}, dimensions={0}, use_global_device_ids=true | all-gather | bytes 561408 | tf_op jit(solution)/shard_map/all_gather | solution.py:59
  28.5 7.1 %fusion.84 = (f32[128]{0:T(128)S(1)}, f32[128,2004]{0,1:T(8,128)}, f32[128,2004]{0,1:T(8,128)}) fusion(f32[]{:T(128)} %bitcast.451, bf16[128,2048]{0,1:T(8,128)(2,1)S(1)} %bitcast.460, bf16[2048,4008]{0,1:T(8,128)(2,1)} %bitcast.455), kind=kOutput, calls=%fused_computation.187 | convolution fusion | flops 1051186048 | bytes 10802176 | tf_op jit(solution)/shard_map/dot_general | solution.py:89
  35.6 1.5 collective-permute-start.1
  37.1 7.0 %fusion.85 = (f32[128]{0:T(128)S(1)}, f32[128,2004]{0,1:T(8,128)}, f32[128,2004]{0,1:T(8,128)}) fusion(f32[]{:T(128)} %bitcast.446, bf16[128,2048]{0,1:T(8,128)(2,1)S(1)} %bitcast.461, bf16[2048,4008]{0,1:T(8,128)(2,1)} %bitcast.456), kind=kOutput, calls=%fused_computation.188 | convolution fusion | flops 1051186048 | bytes 10802176 | tf_op jit(solution)/shard_map/dot_general | solution.py:89
  44.7 18.8 %all-gather.4 = bf16[16,129,128]{2,1,0:T(8,128)(2,1)S(1)} all-gather(bf16[1,129,128]{2,1,0:T(8,128)(2,1)S(1)} %maximum_bitcast_fusion.1), channel_id=3, replica_groups=mesh['member'=2,'vocab'=16] {'vocab'}, dimensions={0}, use_global_device_ids=true | all-gather | bytes 561408 | tf_op jit(solution)/shard_map/all_gather | solution.py:59
  64.8 8.3 %fusion.87 = (f32[128]{0:T(128)S(1)}, f32[128,4008]{0,1:T(8,128)S(1)}) fusion(bf16[128,2048]{0,1:T(8,128)(2,1)S(1)} %bitcast.458, bf16[1,2048,4008]{1,2,0:T(8,128)(2,1)} %param.6), kind=kOutput, calls=%fused_computation.190 | convolution fusion | flops 2101859200 | bytes 18993664 | tf_op jit(solution)/shard_map/dot_general | solution.py:97
  73.1 1.8 %exponential_reduce_fusion.4 = (f32[128]{0:T(128)S(1)}, f32[128,4008]{0,1:T(8,128)}) fusion(f32[128,4008]{0,1:T(8,128)S(1)} %get-tuple-element.35, f32[128]{0:T(128)S(1)} %get-tuple-element.34, f32[]{:T(128)} %bitcast.449), kind=kLoop, calls=%fused_computation.25 | loop fusion | flops 1538944 | bytes 4105220 | tf_op jit(solution)/shard_map/reduce_sum | solution.py:12
  74.9 1.5 collective-permute-start.2
  76.5 22.1 %all-gather.5 = bf16[16,255,128]{2,1,0:T(8,128)(2,1)S(1)} all-gather(bf16[1,255,128]{2,1,0:T(8,128)(2,1)S(1)} %dynamic-slice_bitcast_fusion), channel_id=4, replica_groups=mesh['member'=2,'vocab'=16] {'vocab'}, dimensions={0}, use_global_device_ids=true | all-gather | bytes 1109760 | tf_op jit(solution)/shard_map/all_gather | solution.py:59
  100.1 10.2 %fusion.17 = f32[256,4008]{0,1:T(8,128)} fusion(bf16[255,2048]{0,1:T(8,128)(2,1)S(1)} %bitcast.459, bf16[1,2048]{0,1:T(8,128)(2,1)S(1)} %bitcast.457, bf16[1,2048,4008]{1,2,0:T(8,128)(2,1)} %param.6), kind=kOutput, calls=%fused_computation.34 | convolution fusion | flops 4204789760 | bytes 21569536 | tf_op jit(solution)/shard_map/dot_general | solution.py:105
  110.4 1.9 %fusion.12 = f32[128]{0:T(128)S(1)} fusion(f32[128,2004]{0,1:T(8,128)S(1)} %copy-done.3, f32[128,2004]{0,1:T(8,128)} %get-tuple-element.33, f32[128]{0:T(128)S(1)} %reduce_max.78), kind=kLoop, calls=%fused_computation.18 | loop fusion | flops 1538944 | bytes 2053120 | tf_op jit(solution)/shard_map/reduce_sum | solution.py:12
  112.9 2.1 %slice_reduce_fusion = f32[128]{0:T(128)S(1)} fusion(f32[256,4008]{0,1:T(8,128)} %fusion.17), kind=kLoop, calls=%fused_computation.26 | loop fusion | flops 512896 | bytes 2052608 | tf_op jit(solution)/shard_map/reduce_max | solution.py:11
  115.6 2.1 %fusion.83 = (f32[128]{0:T(128)S(1)}, f32[128,4008]{0,1:T(8,128)S(1)}, f32[128]{0:T(128)S(1)}) fusion(f32[128,2004]{0,1:T(8,128)} %collective-permute-done.1, f32[128,2004]{0,1:T(8,128)} %collective-permute-done, f32[256,4008]{0,1:T(8,128)S(1)} %copy-done.1, f32[]{:T(128)} %bitcast.445, f32[128]{0:T(128)S(1)} %get-tuple-element.15), kind=kLoop, calls=%fused_computation.186 | loop fusion | flops 3077888 | bytes 6157828 | tf_op jit(solution)/shard_map/reduce_max | solution.py:11
  118.7 4.1 %collective-permute-start.16 = (f32[2,1,256]{2,0,1:T(2,128)S(1)}, f32[2,1,256]{2,0,1:T(2,128)S(1)}, u32[]{:S(2)}, u32[]{:S(2)}) collective-permute-start(f32[2,1,256]{2,0,1:T(2,128)S(1)} %fusion.92), channel_id=1, source_target_pairs={{0,14},{1,15},{2,12},{3,13},{4,10},{5,11},{6,8},{7,9},{8,6},{9,7},... | collective-permute-start | bytes 6152 | tf_op jit(solution)/shard_map/ppermute | solution.py:27
  122.7 4.2 %collective-permute-done.18 = f32[3,256]{1,0:T(4,128)S(1)} collective-permute-done((f32[3,256]{1,0:T(4,128)S(1)}, f32[3,256]{1,0:T(4,128)S(1)}, u32[]{:S(2)}, u32[]{:S(2)}) %collective-permute-start.18) | collective-permute-done | bytes 3104 | tf_op jit(solution)/shard_map/ppermute | solution.py:107
  127.0 3.0 %collective-permute-start.12 = (f32[2,1,256]{2,0,1:T(2,128)S(1)}, f32[2,1,256]{2,0,1:T(2,128)S(1)}, u32[]{:S(2)}, u32[]{:S(2)}) collective-permute-start(f32[2,1,256]{2,0,1:T(2,128)S(1)} %fusion.92), channel_id=1, source_target_pairs={{0,10},{1,11},{2,8},{3,9},{4,14},{5,15},{6,12},{7,13},{8,2},{9,3},... | collective-permute-start | bytes 6152 | tf_op jit(solution)/shard_map/ppermute | solution.py:27
  130.4 1.9 %collective-permute-done.14 = f32[2,1,256]{2,0,1:T(2,128)S(1)} collective-permute-done((f32[2,1,256]{2,0,1:T(2,128)S(1)}, f32[2,1,256]{2,0,1:T(2,128)S(1)}, u32[]{:S(2)}, u32[]{:S(2)}) %collective-permute-start.14) | collective-permute-done | bytes 2080 | tf_op jit(solution)/shard_map/ppermute | solution.py:27
  133.2 1.6 collective-permute-start.9
  134.7 1.8 %collective-permute-start.8 = (f32[2,1,256]{2,0,1:T(2,128)S(1)}, f32[2,1,256]{2,0,1:T(2,128)S(1)}, u32[]{:S(2)}, u32[]{:S(2)}) collective-permute-start(f32[2,1,256]{2,0,1:T(2,128)S(1)} %fusion.92), channel_id=1, source_target_pairs={{0,6},{1,7},{2,4},{3,5},{4,2},{5,3},{6,0},{7,1},{8,14},{9,15},{10,... | collective-permute-start | bytes 6152 | tf_op jit(solution)/shard_map/ppermute | solution.py:27
  137.1 2.0 %collective-permute-start.6 = (f32[2,1,256]{2,0,1:T(2,128)S(1)}, f32[2,1,256]{2,0,1:T(2,128)S(1)}, u32[]{:S(2)}, u32[]{:S(2)}) collective-permute-start(f32[2,1,256]{2,0,1:T(2,128)S(1)} %fusion.92), channel_id=1, source_target_pairs={{0,4},{1,5},{2,6},{3,7},{4,0},{5,1},{6,2},{7,3},{8,12},{9,13},{10,... | collective-permute-start | bytes 6152 | tf_op jit(solution)/shard_map/ppermute | solution.py:27
  139.2 1.1 collective-permute-start.4
  142.9 2.2 %fusion.82 = (f32[128]{0:T(128)S(1)}, f32[128,4008]{0,1:T(8,128)S(1)}) fusion(f32[128,4008]{0,1:T(8,128)} %collective-permute-done.2, f32[256,4008]{0,1:T(8,128)S(1)} %copy-done.1, f32[]{:T(128)} %bitcast.450), kind=kLoop, calls=%fused_computation.185 | loop fusion | flops 1538944 | bytes 6156804 | tf_op jit(solution)/shard_map/reduce_max | solution.py:11
  145.6 2.3 %collective-permute-start.33 = (f32[2,1,512]{2,0,1:T(2,128)S(1)}, f32[2,1,512]{2,0,1:T(2,128)S(1)}, u32[]{:S(2)}, u32[]{:S(2)}) collective-permute-start(f32[2,1,512]{2,0,1:T(2,128)S(1)} %fusion.91), channel_id=1, source_target_pairs={{0,15},{1,14},{2,13},{3,12},{4,11},{5,10},{6,9},{7,8},{8,7},{9,6},... | collective-permute-start | bytes 12296 | tf_op jit(solution)/shard_map/ppermute | solution.py:27
  147.9 1.5 collective-permute-start.32
  149.4 2.7 %collective-permute-start.31 = (f32[2,1,512]{2,0,1:T(2,128)S(1)}, f32[2,1,512]{2,0,1:T(2,128)S(1)}, u32[]{:S(2)}, u32[]{:S(2)}) collective-permute-start(f32[2,1,512]{2,0,1:T(2,128)S(1)} %fusion.91), channel_id=1, source_target_pairs={{0,13},{1,12},{2,15},{3,14},{4,9},{5,8},{6,11},{7,10},{8,5},{9,4},... | collective-permute-start | bytes 12296 | tf_op jit(solution)/shard_map/ppermute | solution.py:27
  152.1 1.5 collective-permute-start.30
  153.7 2.8 %collective-permute-start.28 = (f32[2,1,512]{2,0,1:T(2,128)S(1)}, f32[2,1,512]{2,0,1:T(2,128)S(1)}, u32[]{:S(2)}, u32[]{:S(2)}) collective-permute-start(f32[2,1,512]{2,0,1:T(2,128)S(1)} %fusion.91), channel_id=1, source_target_pairs={{0,10},{1,11},{2,8},{3,9},{4,14},{5,15},{6,12},{7,13},{8,2},{9,3},... | collective-permute-start | bytes 12296 | tf_op jit(solution)/shard_map/ppermute | solution.py:27
  157.0 2.9 %collective-permute-start.26 = (f32[2,1,512]{2,0,1:T(2,128)S(1)}, f32[2,1,512]{2,0,1:T(2,128)S(1)}, u32[]{:S(2)}, u32[]{:S(2)}) collective-permute-start(f32[2,1,512]{2,0,1:T(2,128)S(1)} %fusion.91), channel_id=1, source_target_pairs={{0,8},{1,9},{2,10},{3,11},{4,12},{5,13},{6,14},{7,15},{8,0},{9,1},... | collective-permute-start | bytes 12296 | tf_op jit(solution)/shard_map/ppermute | solution.py:27
  160.1 1.7 collective-permute-start.24
  162.3 2.0 %collective-permute-start.22 = (f32[2,1,512]{2,0,1:T(2,128)S(1)}, f32[2,1,512]{2,0,1:T(2,128)S(1)}, u32[]{:S(2)}, u32[]{:S(2)}) collective-permute-start(f32[2,1,512]{2,0,1:T(2,128)S(1)} %fusion.91), channel_id=1, source_target_pairs={{0,4},{1,5},{2,6},{3,7},{4,0},{5,1},{6,2},{7,3},{8,12},{9,13},{10,... | collective-permute-start | bytes 12296 | tf_op jit(solution)/shard_map/ppermute | solution.py:27
  166.2 1.1 collective-permute-done.21
  168.5 2.3 %fusion.4 = f32[256,4008]{0,1:T(8,128)} fusion(f32[128,4008]{0,1:T(8,128)S(1)} %get-tuple-element.19, f32[128,4008]{0,1:T(8,128)S(1)} %get-tuple-element.21, f32[256]{0:T(256)S(1)} %get-tuple-element.16, f32[256]{0:T(256)S(1)} %get-tuple-element.17), kind=kLoop, calls=%fused_computation.5 | loop fusion | flops 3078144 | bytes 8210432 | tf_op jit(solution)/shard_map/sub | solution.py:145
  (98 shorter events, 17.3 us)
Async XLA Ops:
  35.6 79.9 %collective-permute-start.1 = (f32[128,2004]{0,1:T(8,128)}, f32[128,2004]{0,1:T(8,128)}, u32[]{:S(2)}, u32[]{:S(2)}) collective-permute-start(f32[128,2004]{0,1:T(8,128)} %get-tuple-element.26), channel_id=1, source_target_pairs={{0,16},{16,0},{1,17},{17,1},{2,18},{18,2},{3,19},{19,3},{4,20},{20... | collective-permute-start | bytes 3078152 | tf_op jit(solution)/shard_map/ppermute | solution.py:93
  44.1 71.4 %collective-permute-start = (f32[128,2004]{0,1:T(8,128)}, f32[128,2004]{0,1:T(8,128)}, u32[]{:S(2)}, u32[]{:S(2)}) collective-permute-start(f32[128,2004]{0,1:T(8,128)} %get-tuple-element.10), channel_id=1, source_target_pairs={{0,16},{16,0},{1,17},{17,1},{2,18},{18,2},{3,19},{19,3},{4,20},{20... | collective-permute-start | bytes 3078152 | tf_op jit(solution)/shard_map/ppermute | solution.py:93
  74.9 68.0 %collective-permute-start.2 = (f32[128,4008]{0,1:T(8,128)}, f32[128,4008]{0,1:T(8,128)}, u32[]{:S(2)}, u32[]{:S(2)}) collective-permute-start(f32[128,4008]{0,1:T(8,128)} %get-tuple-element.24), channel_id=1, source_target_pairs={{0,16},{16,0},{1,17},{17,1},{2,18},{18,2},{3,19},{19,3},{4,20},{20... | collective-permute-start | bytes 6156296 | tf_op jit(solution)/shard_map/ppermute | solution.py:98
  112.3 14.6 %collective-permute-start.18 = (f32[3,256]{1,0:T(4,128)S(1)}, f32[3,256]{1,0:T(4,128)S(1)}, u32[]{:S(2)}, u32[]{:S(2)}) collective-permute-start(f32[3,256]{1,0:T(4,128)S(1)} %fusion.21), channel_id=1, source_target_pairs={{0,16},{16,0},{1,17},{17,1},{2,18},{18,2},{3,19},{19,3},{4,20},{20... | collective-permute-start | bytes 9224 | tf_op jit(solution)/shard_map/ppermute | solution.py:107
  118.3 8.7 %collective-permute-start.17 = (f32[2,1,256]{2,0,1:T(2,128)S(1)}, f32[2,1,256]{2,0,1:T(2,128)S(1)}, u32[]{:S(2)}, u32[]{:S(2)}) collective-permute-start(f32[2,1,256]{2,0,1:T(2,128)S(1)} %fusion.92), channel_id=1, source_target_pairs={{0,15},{1,14},{2,13},{3,12},{4,11},{5,10},{6,9},{7,8},{8,7},{9,6},... | collective-permute-start | bytes 6152 | tf_op jit(solution)/shard_map/ppermute | solution.py:27
  118.7 8.3 %collective-permute-start.16 = (f32[2,1,256]{2,0,1:T(2,128)S(1)}, f32[2,1,256]{2,0,1:T(2,128)S(1)}, u32[]{:S(2)}, u32[]{:S(2)}) collective-permute-start(f32[2,1,256]{2,0,1:T(2,128)S(1)} %fusion.92), channel_id=1, source_target_pairs={{0,14},{1,15},{2,12},{3,13},{4,10},{5,11},{6,8},{7,9},{8,6},{9,7},... | collective-permute-start | bytes 6152 | tf_op jit(solution)/shard_map/ppermute | solution.py:27
  122.7 7.3 %collective-permute-start.15 = (f32[2,1,256]{2,0,1:T(2,128)S(1)}, f32[2,1,256]{2,0,1:T(2,128)S(1)}, u32[]{:S(2)}, u32[]{:S(2)}) collective-permute-start(f32[2,1,256]{2,0,1:T(2,128)S(1)} %fusion.92), channel_id=1, source_target_pairs={{0,13},{1,12},{2,15},{3,14},{4,9},{5,8},{6,11},{7,10},{8,5},{9,4},... | collective-permute-start | bytes 6152 | tf_op jit(solution)/shard_map/ppermute | solution.py:27
  127.0 5.4 %collective-permute-start.14 = (f32[2,1,256]{2,0,1:T(2,128)S(1)}, f32[2,1,256]{2,0,1:T(2,128)S(1)}, u32[]{:S(2)}, u32[]{:S(2)}) collective-permute-start(f32[2,1,256]{2,0,1:T(2,128)S(1)} %fusion.92), channel_id=1, source_target_pairs={{0,12},{1,13},{2,14},{3,15},{4,8},{5,9},{6,10},{7,11},{8,4},{9,5},... | collective-permute-start | bytes 6152 | tf_op jit(solution)/shard_map/ppermute | solution.py:27
  127.0 6.2 %collective-permute-start.13 = (f32[2,1,256]{2,0,1:T(2,128)S(1)}, f32[2,1,256]{2,0,1:T(2,128)S(1)}, u32[]{:S(2)}, u32[]{:S(2)}) collective-permute-start(f32[2,1,256]{2,0,1:T(2,128)S(1)} %fusion.92), channel_id=1, source_target_pairs={{0,11},{1,10},{2,9},{3,8},{4,15},{5,14},{6,13},{7,12},{8,3},{9,2},... | collective-permute-start | bytes 6152 | tf_op jit(solution)/shard_map/ppermute | solution.py:27
  127.0 7.8 %collective-permute-start.12 = (f32[2,1,256]{2,0,1:T(2,128)S(1)}, f32[2,1,256]{2,0,1:T(2,128)S(1)}, u32[]{:S(2)}, u32[]{:S(2)}) collective-permute-start(f32[2,1,256]{2,0,1:T(2,128)S(1)} %fusion.92), channel_id=1, source_target_pairs={{0,10},{1,11},{2,8},{3,9},{4,14},{5,15},{6,12},{7,13},{8,2},{9,3},... | collective-permute-start | bytes 6152 | tf_op jit(solution)/shard_map/ppermute | solution.py:27
  130.0 6.6 %collective-permute-start.11 = (f32[2,1,256]{2,0,1:T(2,128)S(1)}, f32[2,1,256]{2,0,1:T(2,128)S(1)}, u32[]{:S(2)}, u32[]{:S(2)}) collective-permute-start(f32[2,1,256]{2,0,1:T(2,128)S(1)} %fusion.92), channel_id=1, source_target_pairs={{0,9},{1,8},{2,11},{3,10},{4,13},{5,12},{6,15},{7,14},{8,1},{9,0},... | collective-permute-start | bytes 6152 | tf_op jit(solution)/shard_map/ppermute | solution.py:27
  132.3 4.8 %collective-permute-start.10 = (f32[2,1,256]{2,0,1:T(2,128)S(1)}, f32[2,1,256]{2,0,1:T(2,128)S(1)}, u32[]{:S(2)}, u32[]{:S(2)}) collective-permute-start(f32[2,1,256]{2,0,1:T(2,128)S(1)} %fusion.92), channel_id=1, source_target_pairs={{0,8},{1,9},{2,10},{3,11},{4,12},{5,13},{6,14},{7,15},{8,0},{9,1},... | collective-permute-start | bytes 6152 | tf_op jit(solution)/shard_map/ppermute | solution.py:27
  133.2 5.9 %collective-permute-start.9 = (f32[2,1,256]{2,0,1:T(2,128)S(1)}, f32[2,1,256]{2,0,1:T(2,128)S(1)}, u32[]{:S(2)}, u32[]{:S(2)}) collective-permute-start(f32[2,1,256]{2,0,1:T(2,128)S(1)} %fusion.92), channel_id=1, source_target_pairs={{0,7},{1,6},{2,5},{3,4},{4,3},{5,2},{6,1},{7,0},{8,15},{9,14},{10,... | collective-permute-start | bytes 6152 | tf_op jit(solution)/shard_map/ppermute | solution.py:27
  134.7 4.5 %collective-permute-start.8 = (f32[2,1,256]{2,0,1:T(2,128)S(1)}, f32[2,1,256]{2,0,1:T(2,128)S(1)}, u32[]{:S(2)}, u32[]{:S(2)}) collective-permute-start(f32[2,1,256]{2,0,1:T(2,128)S(1)} %fusion.92), channel_id=1, source_target_pairs={{0,6},{1,7},{2,4},{3,5},{4,2},{5,3},{6,0},{7,1},{8,14},{9,15},{10,... | collective-permute-start | bytes 6152 | tf_op jit(solution)/shard_map/ppermute | solution.py:27
  136.5 3.8 %collective-permute-start.7 = (f32[2,1,256]{2,0,1:T(2,128)S(1)}, f32[2,1,256]{2,0,1:T(2,128)S(1)}, u32[]{:S(2)}, u32[]{:S(2)}) collective-permute-start(f32[2,1,256]{2,0,1:T(2,128)S(1)} %fusion.92), channel_id=1, source_target_pairs={{0,5},{1,4},{2,7},{3,6},{4,1},{5,0},{6,3},{7,2},{8,13},{9,12},{10,... | collective-permute-start | bytes 6152 | tf_op jit(solution)/shard_map/ppermute | solution.py:27
  137.1 3.9 %collective-permute-start.6 = (f32[2,1,256]{2,0,1:T(2,128)S(1)}, f32[2,1,256]{2,0,1:T(2,128)S(1)}, u32[]{:S(2)}, u32[]{:S(2)}) collective-permute-start(f32[2,1,256]{2,0,1:T(2,128)S(1)} %fusion.92), channel_id=1, source_target_pairs={{0,4},{1,5},{2,6},{3,7},{4,0},{5,1},{6,2},{7,3},{8,12},{9,13},{10,... | collective-permute-start | bytes 6152 | tf_op jit(solution)/shard_map/ppermute | solution.py:27
  139.1 3.0 %collective-permute-start.5 = (f32[2,1,256]{2,0,1:T(2,128)S(1)}, f32[2,1,256]{2,0,1:T(2,128)S(1)}, u32[]{:S(2)}, u32[]{:S(2)}) collective-permute-start(f32[2,1,256]{2,0,1:T(2,128)S(1)} %fusion.92), channel_id=1, source_target_pairs={{0,3},{1,2},{2,1},{3,0},{4,7},{5,6},{6,5},{7,4},{8,11},{9,10},{10,... | collective-permute-start | bytes 6152 | tf_op jit(solution)/shard_map/ppermute | solution.py:27
  139.2 3.6 %collective-permute-start.4 = (f32[2,1,256]{2,0,1:T(2,128)S(1)}, f32[2,1,256]{2,0,1:T(2,128)S(1)}, u32[]{:S(2)}, u32[]{:S(2)}) collective-permute-start(f32[2,1,256]{2,0,1:T(2,128)S(1)} %fusion.92), channel_id=1, source_target_pairs={{0,2},{1,3},{2,0},{3,1},{4,6},{5,7},{6,4},{7,5},{8,10},{9,11},{10,... | collective-permute-start | bytes 6152 | tf_op jit(solution)/shard_map/ppermute | solution.py:27
  145.6 8.1 %collective-permute-start.33 = (f32[2,1,512]{2,0,1:T(2,128)S(1)}, f32[2,1,512]{2,0,1:T(2,128)S(1)}, u32[]{:S(2)}, u32[]{:S(2)}) collective-permute-start(f32[2,1,512]{2,0,1:T(2,128)S(1)} %fusion.91), channel_id=1, source_target_pairs={{0,15},{1,14},{2,13},{3,12},{4,11},{5,10},{6,9},{7,8},{8,7},{9,6},... | collective-permute-start | bytes 12296 | tf_op jit(solution)/shard_map/ppermute | solution.py:27
  147.9 8.6 %collective-permute-start.32 = (f32[2,1,512]{2,0,1:T(2,128)S(1)}, f32[2,1,512]{2,0,1:T(2,128)S(1)}, u32[]{:S(2)}, u32[]{:S(2)}) collective-permute-start(f32[2,1,512]{2,0,1:T(2,128)S(1)} %fusion.91), channel_id=1, source_target_pairs={{0,14},{1,15},{2,12},{3,13},{4,10},{5,11},{6,8},{7,9},{8,6},{9,7},... | collective-permute-start | bytes 12296 | tf_op jit(solution)/shard_map/ppermute | solution.py:27
  149.4 7.5 %collective-permute-start.31 = (f32[2,1,512]{2,0,1:T(2,128)S(1)}, f32[2,1,512]{2,0,1:T(2,128)S(1)}, u32[]{:S(2)}, u32[]{:S(2)}) collective-permute-start(f32[2,1,512]{2,0,1:T(2,128)S(1)} %fusion.91), channel_id=1, source_target_pairs={{0,13},{1,12},{2,15},{3,14},{4,9},{5,8},{6,11},{7,10},{8,5},{9,4},... | collective-permute-start | bytes 12296 | tf_op jit(solution)/shard_map/ppermute | solution.py:27
  152.1 7.7 %collective-permute-start.30 = (f32[2,1,512]{2,0,1:T(2,128)S(1)}, f32[2,1,512]{2,0,1:T(2,128)S(1)}, u32[]{:S(2)}, u32[]{:S(2)}) collective-permute-start(f32[2,1,512]{2,0,1:T(2,128)S(1)} %fusion.91), channel_id=1, source_target_pairs={{0,12},{1,13},{2,14},{3,15},{4,8},{5,9},{6,10},{7,11},{8,4},{9,5},... | collective-permute-start | bytes 12296 | tf_op jit(solution)/shard_map/ppermute | solution.py:27
  153.7 6.5 %collective-permute-start.29 = (f32[2,1,512]{2,0,1:T(2,128)S(1)}, f32[2,1,512]{2,0,1:T(2,128)S(1)}, u32[]{:S(2)}, u32[]{:S(2)}) collective-permute-start(f32[2,1,512]{2,0,1:T(2,128)S(1)} %fusion.91), channel_id=1, source_target_pairs={{0,11},{1,10},{2,9},{3,8},{4,15},{5,14},{6,13},{7,12},{8,3},{9,2},... | collective-permute-start | bytes 12296 | tf_op jit(solution)/shard_map/ppermute | solution.py:27
  153.7 8.2 %collective-permute-start.28 = (f32[2,1,512]{2,0,1:T(2,128)S(1)}, f32[2,1,512]{2,0,1:T(2,128)S(1)}, u32[]{:S(2)}, u32[]{:S(2)}) collective-permute-start(f32[2,1,512]{2,0,1:T(2,128)S(1)} %fusion.91), channel_id=1, source_target_pairs={{0,10},{1,11},{2,8},{3,9},{4,14},{5,15},{6,12},{7,13},{8,2},{9,3},... | collective-permute-start | bytes 12296 | tf_op jit(solution)/shard_map/ppermute | solution.py:27
  156.5 5.8 %collective-permute-start.27 = (f32[2,1,512]{2,0,1:T(2,128)S(1)}, f32[2,1,512]{2,0,1:T(2,128)S(1)}, u32[]{:S(2)}, u32[]{:S(2)}) collective-permute-start(f32[2,1,512]{2,0,1:T(2,128)S(1)} %fusion.91), channel_id=1, source_target_pairs={{0,9},{1,8},{2,11},{3,10},{4,13},{5,12},{6,15},{7,14},{8,1},{9,0},... | collective-permute-start | bytes 12296 | tf_op jit(solution)/shard_map/ppermute | solution.py:27
  157.0 7.3 %collective-permute-start.26 = (f32[2,1,512]{2,0,1:T(2,128)S(1)}, f32[2,1,512]{2,0,1:T(2,128)S(1)}, u32[]{:S(2)}, u32[]{:S(2)}) collective-permute-start(f32[2,1,512]{2,0,1:T(2,128)S(1)} %fusion.91), channel_id=1, source_target_pairs={{0,8},{1,9},{2,10},{3,11},{4,12},{5,13},{6,14},{7,15},{8,0},{9,1},... | collective-permute-start | bytes 12296 | tf_op jit(solution)/shard_map/ppermute | solution.py:27
  159.9 4.9 %collective-permute-start.25 = (f32[2,1,512]{2,0,1:T(2,128)S(1)}, f32[2,1,512]{2,0,1:T(2,128)S(1)}, u32[]{:S(2)}, u32[]{:S(2)}) collective-permute-start(f32[2,1,512]{2,0,1:T(2,128)S(1)} %fusion.91), channel_id=1, source_target_pairs={{0,7},{1,6},{2,5},{3,4},{4,3},{5,2},{6,1},{7,0},{8,15},{9,14},{10,... | collective-permute-start | bytes 12296 | tf_op jit(solution)/shard_map/ppermute | solution.py:27
  160.1 5.4 %collective-permute-start.24 = (f32[2,1,512]{2,0,1:T(2,128)S(1)}, f32[2,1,512]{2,0,1:T(2,128)S(1)}, u32[]{:S(2)}, u32[]{:S(2)}) collective-permute-start(f32[2,1,512]{2,0,1:T(2,128)S(1)} %fusion.91), channel_id=1, source_target_pairs={{0,6},{1,7},{2,4},{3,5},{4,2},{5,3},{6,0},{7,1},{8,14},{9,15},{10,... | collective-permute-start | bytes 12296 | tf_op jit(solution)/shard_map/ppermute | solution.py:27
  161.8 4.3 %collective-permute-start.23 = (f32[2,1,512]{2,0,1:T(2,128)S(1)}, f32[2,1,512]{2,0,1:T(2,128)S(1)}, u32[]{:S(2)}, u32[]{:S(2)}) collective-permute-start(f32[2,1,512]{2,0,1:T(2,128)S(1)} %fusion.91), channel_id=1, source_target_pairs={{0,5},{1,4},{2,7},{3,6},{4,1},{5,0},{6,3},{7,2},{8,13},{9,12},{10,... | collective-permute-start | bytes 12296 | tf_op jit(solution)/shard_map/ppermute | solution.py:27
  162.3 3.9 %collective-permute-start.22 = (f32[2,1,512]{2,0,1:T(2,128)S(1)}, f32[2,1,512]{2,0,1:T(2,128)S(1)}, u32[]{:S(2)}, u32[]{:S(2)}) collective-permute-start(f32[2,1,512]{2,0,1:T(2,128)S(1)} %fusion.91), channel_id=1, source_target_pairs={{0,4},{1,5},{2,6},{3,7},{4,0},{5,1},{6,2},{7,3},{8,12},{9,13},{10,... | collective-permute-start | bytes 12296 | tf_op jit(solution)/shard_map/ppermute | solution.py:27
  164.3 3.0 %collective-permute-start.21 = (f32[2,1,512]{2,0,1:T(2,128)S(1)}, f32[2,1,512]{2,0,1:T(2,128)S(1)}, u32[]{:S(2)}, u32[]{:S(2)}) collective-permute-start(f32[2,1,512]{2,0,1:T(2,128)S(1)} %fusion.91), channel_id=1, source_target_pairs={{0,3},{1,2},{2,1},{3,0},{4,7},{5,6},{6,5},{7,4},{8,11},{9,10},{10,... | collective-permute-start | bytes 12296 | tf_op jit(solution)/shard_map/ppermute | solution.py:27
  164.8 3.6 %collective-permute-start.20 = (f32[2,1,512]{2,0,1:T(2,128)S(1)}, f32[2,1,512]{2,0,1:T(2,128)S(1)}, u32[]{:S(2)}, u32[]{:S(2)}) collective-permute-start(f32[2,1,512]{2,0,1:T(2,128)S(1)} %fusion.91), channel_id=1, source_target_pairs={{0,2},{1,3},{2,0},{3,1},{4,6},{5,7},{6,4},{7,5},{8,10},{9,11},{10,... | collective-permute-start | bytes 12296 | tf_op jit(solution)/shard_map/ppermute | solution.py:27
  (8 other events, 36.2 us)

commit v19 on v17

--- a/solution.py
+++ b/solution.py
@@ -20,9 +20,12 @@
         peak = jnp.max(gathered[:, 0], axis=0)
         summed = jnp.sum(gathered[:, 1] * jnp.exp(gathered[:, 0] - peak[None]), axis=0)
         return peak, summed
+    rounds = []
     stride = 1
     while stride < size:
-        radix = 4 if stride == 1 and size >= 4 else 2
+        rounds.append((stride, 4 if stride * 4 <= size else 2))
+        stride *= rounds[-1][1]
+    for stride, radix in reversed(rounds):
         others = [
             lax.ppermute(stats, axis, [(a, a ^ (j * stride)) for a in range(size)])
             for j in range(1, radix)
@@ -37,7 +40,6 @@
         else:
             summed = terms[0] + terms[1]
         stats = jnp.stack([peak, summed])
-        stride *= radix
     return stats[0], stats[1]
 
 

time: 147 us -> 144 us (0.980)
  waiting for transfers between devices: 19.2 us -> 7.88 us
  starting transfers between devices: 8.4 us -> 16.8 us
    ppermute x10 -> x12, waiting for transfers between devices: 17.6 us -> 7.14 us  [reduce_stats(): lax.ppermute(stats, axis, [(a, a ^ j * stride) for a in range(size)])]
    ppermute x10 -> x12, starting transfers between devices: 4.28 us -> 12.7 us  [reduce_stats(): lax.ppermute(stats, axis, [(a, a ^ j * stride) for a in range(size)])]
  transfers between devices with their start and end apart: 14 -> 16, of which waited for: 9 -> 10; matrix products, arithmetic and copies ran while one was open for 25% -> 26% of each run, Pallas kernels for 0% -> 0%
where the time goes in v19:
time: 144 us
  blocking collectives  65.6 us (46%)
  matrix products  32.6 us (23%)
  other arithmetic  16.9 us (12%)
  starting transfers between devices  16.8 us (12%)
  waiting for transfers between devices  7.88 us (5%)
  local copies, waits for them, and re-layouts  2.76 us (2%)
  between operations  1.54 us (1%)
    all_gather x3, blocking collectives, normed_of(): gathered = lax.all_gather(packed, 'vocab', axis=0, tiled=False)  65.6 us
    dot_general x2, matrix products, on_device(): jnp.dot(normed, columns, preferred_element_type=jnp.float32)  14 us
    ppermute x12, starting transfers between devices, reduce_stats(): lax.ppermute(stats, axis, [(a, a ^ j * stride) for a in range(size)])  12.7 us
    dot_general x1, matrix products, on_device(): jnp.dot(own_normed, weights, preferred_element_type=jnp.float32)  10.2 us
    dot_general x1, matrix products, on_device(): logits = jnp.dot(normed, weights, preferred_element_type=jnp.float32)  8.34 us
    ppermute x12, waiting for transfers between devices, reduce_stats(): lax.ppermute(stats, axis, [(a, a ^ j * stride) for a in range(size)])  7.14 us
    reduce_max x4, other arithmetic, local_stats(): local_peak = jnp.max(values, axis=1)  6.41 us
    reduce_sum x5, other arithmetic, local_stats(): local_sum = jnp.sum(jnp.exp(values - local_peak[:, None]), axis=1)  5.36 us
  transfers between devices with their start and end apart: 16, of which 10 were waited for; matrix products, arithmetic and copies ran while one was open for 26% of the time, Pallas kernels for 0%

profile of v19, /device:TPU:0, one launch (start us, length us, event | category | flops | bytes accessed | tf_op | source)
XLA Modules:
  0.0 144.1 jit_solution(952984219612054231)
XLA Ops:
  0.7 0.9 copy-done
  1.5 0.7 maximum_bitcast_fusion
  2.2 24.7 %all-gather.3 = bf16[16,129,128]{2,1,0:T(8,128)(2,1)S(1)} all-gather(bf16[1,129,128]{2,1,0:T(8,128)(2,1)S(1)} %maximum_bitcast_fusion), channel_id=2, replica_groups=mesh['member'=2,'vocab'=16] {'vocab'}, dimensions={0}, use_global_device_ids=true | all-gather | bytes 561408 | tf_op jit(solution)/shard_map/all_gather | solution.py:63
  28.5 7.0 %fusion.54 = (f32[128]{0:T(128)S(1)}, f32[128,2004]{0,1:T(8,128)}, f32[128,2004]{0,1:T(8,128)}) fusion(f32[]{:T(128)} %bitcast.229, bf16[128,2048]{0,1:T(8,128)(2,1)S(1)} %bitcast.238, bf16[2048,4008]{0,1:T(8,128)(2,1)} %bitcast.233), kind=kOutput, calls=%fused_computation.125 | convolution fusion | flops 1051186048 | bytes 10802176 | tf_op jit(solution)/shard_map/dot_general | solution.py:93
  35.6 1.5 %collective-permute-start.1 = (f32[128,2004]{0,1:T(8,128)}, f32[128,2004]{0,1:T(8,128)}, u32[]{:S(2)}, u32[]{:S(2)}) collective-permute-start(f32[128,2004]{0,1:T(8,128)} %get-tuple-element.30), channel_id=1, source_target_pairs={{0,16},{16,0},{1,17},{17,1},{2,18},{18,2},{3,19},{19,3},{4,20},{20... | collective-permute-start | bytes 3078152 | tf_op jit(solution)/shard_map/ppermute | solution.py:97
  37.1 7.0 %fusion.55 = (f32[128]{0:T(128)S(1)}, f32[128,2004]{0,1:T(8,128)}, f32[128,2004]{0,1:T(8,128)}) fusion(f32[]{:T(128)} %bitcast.224, bf16[128,2048]{0,1:T(8,128)(2,1)S(1)} %bitcast.239, bf16[2048,4008]{0,1:T(8,128)(2,1)} %bitcast.234), kind=kOutput, calls=%fused_computation.126 | convolution fusion | flops 1051186048 | bytes 10802176 | tf_op jit(solution)/shard_map/dot_general | solution.py:93
  44.6 18.8 %all-gather.4 = bf16[16,129,128]{2,1,0:T(8,128)(2,1)S(1)} all-gather(bf16[1,129,128]{2,1,0:T(8,128)(2,1)S(1)} %maximum_bitcast_fusion.1), channel_id=3, replica_groups=mesh['member'=2,'vocab'=16] {'vocab'}, dimensions={0}, use_global_device_ids=true | all-gather | bytes 561408 | tf_op jit(solution)/shard_map/all_gather | solution.py:63
  64.7 8.3 %fusion.57 = (f32[128]{0:T(128)S(1)}, f32[128,4008]{0,1:T(8,128)S(1)}) fusion(bf16[128,2048]{0,1:T(8,128)(2,1)S(1)} %bitcast.236, bf16[1,2048,4008]{1,2,0:T(8,128)(2,1)} %param.6), kind=kOutput, calls=%fused_computation.128 | convolution fusion | flops 2101859200 | bytes 18993664 | tf_op jit(solution)/shard_map/dot_general | solution.py:101
  73.1 1.8 %exponential_reduce_fusion.4 = (f32[128]{0:T(128)S(1)}, f32[128,4008]{0,1:T(8,128)}) fusion(f32[128,4008]{0,1:T(8,128)S(1)} %get-tuple-element.39, f32[128]{0:T(128)S(1)} %get-tuple-element.38, f32[]{:T(128)} %bitcast.227), kind=kLoop, calls=%fused_computation.25 | loop fusion | flops 1538944 | bytes 4105220 | tf_op jit(solution)/shard_map/reduce_sum | solution.py:12
  74.9 1.5 %collective-permute-start.2 = (f32[128,4008]{0,1:T(8,128)}, f32[128,4008]{0,1:T(8,128)}, u32[]{:S(2)}, u32[]{:S(2)}) collective-permute-start(f32[128,4008]{0,1:T(8,128)} %get-tuple-element.28), channel_id=1, source_target_pairs={{0,16},{16,0},{1,17},{17,1},{2,18},{18,2},{3,19},{19,3},{4,20},{20... | collective-permute-start | bytes 6156296 | tf_op jit(solution)/shard_map/ppermute | solution.py:102
  76.4 22.1 %all-gather.5 = bf16[16,255,128]{2,1,0:T(8,128)(2,1)S(1)} all-gather(bf16[1,255,128]{2,1,0:T(8,128)(2,1)S(1)} %dynamic-slice_bitcast_fusion), channel_id=4, replica_groups=mesh['member'=2,'vocab'=16] {'vocab'}, dimensions={0}, use_global_device_ids=true | all-gather | bytes 1109760 | tf_op jit(solution)/shard_map/all_gather | solution.py:63
  100.1 10.2 %fusion.17 = f32[256,4008]{0,1:T(8,128)} fusion(bf16[255,2048]{0,1:T(8,128)(2,1)S(1)} %bitcast.237, bf16[1,2048]{0,1:T(8,128)(2,1)S(1)} %bitcast.235, bf16[1,2048,4008]{1,2,0:T(8,128)(2,1)} %param.6), kind=kOutput, calls=%fused_computation.34 | convolution fusion | flops 4204789760 | bytes 21569536 | tf_op jit(solution)/shard_map/dot_general | solution.py:109
  110.3 1.9 %fusion.12 = f32[128]{0:T(128)S(1)} fusion(f32[128,2004]{0,1:T(8,128)S(1)} %copy-done.3, f32[128,2004]{0,1:T(8,128)} %get-tuple-element.37, f32[128]{0:T(128)S(1)} %reduce_max.78), kind=kLoop, calls=%fused_computation.18 | loop fusion | flops 1538944 | bytes 2053120 | tf_op jit(solution)/shard_map/reduce_sum | solution.py:12
  112.2 0.6 collective-permute-start.9
  112.8 2.1 %slice_reduce_fusion = f32[128]{0:T(128)S(1)} fusion(f32[256,4008]{0,1:T(8,128)} %fusion.17), kind=kLoop, calls=%fused_computation.26 | loop fusion | flops 512896 | bytes 2052608 | tf_op jit(solution)/shard_map/reduce_max | solution.py:11
  115.5 2.1 %fusion.53 = (f32[128]{0:T(128)S(1)}, f32[128,4008]{0,1:T(8,128)S(1)}, f32[128]{0:T(128)S(1)}) fusion(f32[128,2004]{0,1:T(8,128)} %collective-permute-done.1, f32[128,2004]{0,1:T(8,128)} %collective-permute-done, f32[256,4008]{0,1:T(8,128)S(1)} %copy-done.1, f32[]{:T(128)} %bitcast.223, f32[128]{0:T(128)S(1)} %get-tuple-element.15), kind=kLoop, calls=%fused_computation.124 | loop fusion | flops 3077888 | bytes 6157828 | tf_op jit(solution)/shard_map/reduce_max | solution.py:11
  118.7 4.0 %collective-permute-start.3 = (f32[2,1,256]{2,0,1:T(2,128)S(1)}, f32[2,1,256]{2,0,1:T(2,128)S(1)}, u32[]{:S(2)}, u32[]{:S(2)}) collective-permute-start(f32[2,1,256]{2,0,1:T(2,128)S(1)} %fusion.62), channel_id=1, source_target_pairs={{0,4},{1,5},{2,6},{3,7},{4,0},{5,1},{6,2},{7,3},{8,12},{9,13},{10,... | collective-permute-start | bytes 6152 | tf_op jit(solution)/shard_map/ppermute | solution.py:30
  122.7 1.0 collective-permute-done.5
  124.3 0.7 collective-permute-start.7
  125.0 1.2 collective-permute-start.6
  126.2 0.7 collective-permute-done.9
  127.3 0.7 collective-permute-done.7
  128.0 2.2 %fusion.52 = (f32[128]{0:T(128)S(1)}, f32[128,4008]{0,1:T(8,128)S(1)}) fusion(f32[128,4008]{0,1:T(8,128)} %collective-permute-done.2, f32[256,4008]{0,1:T(8,128)S(1)} %copy-done.1, f32[]{:T(128)} %bitcast.228), kind=kLoop, calls=%fused_computation.123 | loop fusion | flops 1538944 | bytes 6156804 | tf_op jit(solution)/shard_map/reduce_max | solution.py:11
  130.7 2.4 %collective-permute-start.12 = (f32[2,1,512]{2,0,1:T(2,128)S(1)}, f32[2,1,512]{2,0,1:T(2,128)S(1)}, u32[]{:S(2)}, u32[]{:S(2)}) collective-permute-start(f32[2,1,512]{2,0,1:T(2,128)S(1)} %fusion.61), channel_id=1, source_target_pairs={{0,12},{1,13},{2,14},{3,15},{4,8},{5,9},{6,10},{7,11},{8,4},{9,5},... | collective-permute-start | bytes 12296 | tf_op jit(solution)/shard_map/ppermute | solution.py:30
  133.2 1.1 collective-permute-start.11
  134.3 0.9 collective-permute-start.10
  135.2 1.0 collective-permute-done.12
  136.2 1.5 %collective-permute-done.11 = f32[2,1,512]{2,0,1:T(2,128)S(1)} collective-permute-done((f32[2,1,512]{2,0,1:T(2,128)S(1)}, f32[2,1,512]{2,0,1:T(2,128)S(1)}, u32[]{:S(2)}, u32[]{:S(2)}) %collective-permute-start.11) | collective-permute-done | bytes 4128 | tf_op jit(solution)/shard_map/ppermute | solution.py:30
  138.4 1.5 %collective-permute-start.13 = (f32[2,1,512]{2,1,0:T(1,128)S(1)}, f32[2,1,512]{2,1,0:T(1,128)S(1)}, u32[]{:S(2)}, u32[]{:S(2)}) collective-permute-start(f32[2,1,512]{2,1,0:T(1,128)S(1)} %pad_maximum_fusion.1), channel_id=1, source_target_pairs={{0,1},{1,0},{2,3},{3,2},{4,5},{5,4},{6,7},{7,6},{8,9},{9,8},{10,11... | collective-permute-start | bytes 12296 | tf_op jit(solution)/shard_map/ppermute | solution.py:30
  139.9 1.2 collective-permute-done.15
  141.0 0.7 collective-permute-done.14
  141.8 2.3 %fusion.4 = f32[256,4008]{0,1:T(8,128)} fusion(f32[128,4008]{0,1:T(8,128)S(1)} %get-tuple-element.21, f32[128,4008]{0,1:T(8,128)S(1)} %get-tuple-element.25, f32[256]{0:T(256)S(1)} %get-tuple-element.16, f32[256]{0:T(256)S(1)} %get-tuple-element.17), kind=kLoop, calls=%fused_computation.5 | loop fusion | flops 3078144 | bytes 8210432 | tf_op jit(solution)/shard_map/sub | solution.py:149
  (66 shorter events, 8.4 us)
Async XLA Ops:
  0.6 0.9 copy-start
  35.6 79.9 %collective-permute-start.1 = (f32[128,2004]{0,1:T(8,128)}, f32[128,2004]{0,1:T(8,128)}, u32[]{:S(2)}, u32[]{:S(2)}) collective-permute-start(f32[128,2004]{0,1:T(8,128)} %get-tuple-element.30), channel_id=1, source_target_pairs={{0,16},{16,0},{1,17},{17,1},{2,18},{18,2},{3,19},{19,3},{4,20},{20... | collective-permute-start | bytes 3078152 | tf_op jit(solution)/shard_map/ppermute | solution.py:97
  44.1 71.4 %collective-permute-start = (f32[128,2004]{0,1:T(8,128)}, f32[128,2004]{0,1:T(8,128)}, u32[]{:S(2)}, u32[]{:S(2)}) collective-permute-start(f32[128,2004]{0,1:T(8,128)} %get-tuple-element.10), channel_id=1, source_target_pairs={{0,16},{16,0},{1,17},{17,1},{2,18},{18,2},{3,19},{19,3},{4,20},{20... | collective-permute-start | bytes 3078152 | tf_op jit(solution)/shard_map/ppermute | solution.py:97
  64.6 11.8 %copy-start.2 = (bf16[129,16,128]{0,2,1:T(8,128)(2,1)}, bf16[129,16,128]{0,2,1:T(8,128)(2,1)S(1)}, u32[]{:S(2)}) copy-start(bf16[129,16,128]{0,2,1:T(8,128)(2,1)S(1)} %fusion.16) | copy-start | bytes 1585156
  74.9 53.2 %collective-permute-start.2 = (f32[128,4008]{0,1:T(8,128)}, f32[128,4008]{0,1:T(8,128)}, u32[]{:S(2)}, u32[]{:S(2)}) collective-permute-start(f32[128,4008]{0,1:T(8,128)} %get-tuple-element.28), channel_id=1, source_target_pairs={{0,16},{16,0},{1,17},{17,1},{2,18},{18,2},{3,19},{19,3},{4,20},{20... | collective-permute-start | bytes 6156296 | tf_op jit(solution)/shard_map/ppermute | solution.py:102
  99.0 1.0 slice-start
  100.1 10.2 %copy-start.3 = (f32[128,2004]{0,1:T(8,128)S(1)}, f32[128,2004]{0,1:T(8,128)}, u32[]{:S(2)}) copy-start(f32[128,2004]{0,1:T(8,128)} %get-tuple-element.40) | copy-start | bytes 3078148
  110.3 4.6 %copy-start.1 = (f32[256,4008]{0,1:T(8,128)S(1)}, f32[256,4008]{0,1:T(8,128)}, u32[]{:S(2)}) copy-start(f32[256,4008]{0,1:T(8,128)} %fusion.17) | copy-start | bytes 12312580
  112.2 14.7 %collective-permute-start.9 = (f32[3,256]{1,0:T(4,128)S(1)}, f32[3,256]{1,0:T(4,128)S(1)}, u32[]{:S(2)}, u32[]{:S(2)}) collective-permute-start(f32[3,256]{1,0:T(4,128)S(1)} %fusion.21), channel_id=1, source_target_pairs={{0,16},{16,0},{1,17},{17,1},{2,18},{18,2},{3,19},{19,3},{4,20},{20... | collective-permute-start | bytes 9224 | tf_op jit(solution)/shard_map/ppermute | solution.py:111
  118.2 5.4 %collective-permute-start.5 = (f32[2,1,256]{2,0,1:T(2,128)S(1)}, f32[2,1,256]{2,0,1:T(2,128)S(1)}, u32[]{:S(2)}, u32[]{:S(2)}) collective-permute-start(f32[2,1,256]{2,0,1:T(2,128)S(1)} %fusion.62), channel_id=1, source_target_pairs={{0,12},{1,13},{2,14},{3,15},{4,8},{5,9},{6,10},{7,11},{8,4},{9,5},... | collective-permute-start | bytes 6152 | tf_op jit(solution)/shard_map/ppermute | solution.py:30
  118.3 5.4 %collective-permute-start.4 = (f32[2,1,256]{2,0,1:T(2,128)S(1)}, f32[2,1,256]{2,0,1:T(2,128)S(1)}, u32[]{:S(2)}, u32[]{:S(2)}) collective-permute-start(f32[2,1,256]{2,0,1:T(2,128)S(1)} %fusion.62), channel_id=1, source_target_pairs={{0,8},{1,9},{2,10},{3,11},{4,12},{5,13},{6,14},{7,15},{8,0},{9,1},... | collective-permute-start | bytes 6152 | tf_op jit(solution)/shard_map/ppermute | solution.py:30
  118.7 5.5 %collective-permute-start.3 = (f32[2,1,256]{2,0,1:T(2,128)S(1)}, f32[2,1,256]{2,0,1:T(2,128)S(1)}, u32[]{:S(2)}, u32[]{:S(2)}) collective-permute-start(f32[2,1,256]{2,0,1:T(2,128)S(1)} %fusion.62), channel_id=1, source_target_pairs={{0,4},{1,5},{2,6},{3,7},{4,0},{5,1},{6,2},{7,3},{8,12},{9,13},{10,... | collective-permute-start | bytes 6152 | tf_op jit(solution)/shard_map/ppermute | solution.py:30
  124.3 3.1 %collective-permute-start.8 = (f32[2,1,256]{2,1,0:T(1,128)S(1)}, f32[2,1,256]{2,1,0:T(1,128)S(1)}, u32[]{:S(2)}, u32[]{:S(2)}) collective-permute-start(f32[2,1,256]{2,1,0:T(1,128)S(1)} %pad_maximum_fusion.2), channel_id=1, source_target_pairs={{0,3},{1,2},{2,1},{3,0},{4,7},{5,6},{6,5},{7,4},{8,11},{9,10},{10,... | collective-permute-start | bytes 6152 | tf_op jit(solution)/shard_map/ppermute | solution.py:30
  124.3 3.7 %collective-permute-start.7 = (f32[2,1,256]{2,1,0:T(1,128)S(1)}, f32[2,1,256]{2,1,0:T(1,128)S(1)}, u32[]{:S(2)}, u32[]{:S(2)}) collective-permute-start(f32[2,1,256]{2,1,0:T(1,128)S(1)} %pad_maximum_fusion.2), channel_id=1, source_target_pairs={{0,2},{1,3},{2,0},{3,1},{4,6},{5,7},{6,4},{7,5},{8,10},{9,11},{10,... | collective-permute-start | bytes 6152 | tf_op jit(solution)/shard_map/ppermute | solution.py:30
  125.0 3.0 %collective-permute-start.6 = (f32[2,1,256]{2,1,0:T(1,128)S(1)}, f32[2,1,256]{2,1,0:T(1,128)S(1)}, u32[]{:S(2)}, u32[]{:S(2)}) collective-permute-start(f32[2,1,256]{2,1,0:T(1,128)S(1)} %pad_maximum_fusion.2), channel_id=1, source_target_pairs={{0,1},{1,0},{2,3},{3,2},{4,5},{5,4},{6,7},{7,6},{8,9},{9,8},{10,11... | collective-permute-start | bytes 6152 | tf_op jit(solution)/shard_map/ppermute | solution.py:30
  130.7 5.5 %collective-permute-start.12 = (f32[2,1,512]{2,0,1:T(2,128)S(1)}, f32[2,1,512]{2,0,1:T(2,128)S(1)}, u32[]{:S(2)}, u32[]{:S(2)}) collective-permute-start(f32[2,1,512]{2,0,1:T(2,128)S(1)} %fusion.61), channel_id=1, source_target_pairs={{0,12},{1,13},{2,14},{3,15},{4,8},{5,9},{6,10},{7,11},{8,4},{9,5},... | collective-permute-start | bytes 12296 | tf_op jit(solution)/shard_map/ppermute | solution.py:30
  133.2 4.5 %collective-permute-start.11 = (f32[2,1,512]{2,0,1:T(2,128)S(1)}, f32[2,1,512]{2,0,1:T(2,128)S(1)}, u32[]{:S(2)}, u32[]{:S(2)}) collective-permute-start(f32[2,1,512]{2,0,1:T(2,128)S(1)} %fusion.61), channel_id=1, source_target_pairs={{0,8},{1,9},{2,10},{3,11},{4,12},{5,13},{6,14},{7,15},{8,0},{9,1},... | collective-permute-start | bytes 12296 | tf_op jit(solution)/shard_map/ppermute | solution.py:30
  134.3 3.6 %collective-permute-start.10 = (f32[2,1,512]{2,0,1:T(2,128)S(1)}, f32[2,1,512]{2,0,1:T(2,128)S(1)}, u32[]{:S(2)}, u32[]{:S(2)}) collective-permute-start(f32[2,1,512]{2,0,1:T(2,128)S(1)} %fusion.61), channel_id=1, source_target_pairs={{0,4},{1,5},{2,6},{3,7},{4,0},{5,1},{6,2},{7,3},{8,12},{9,13},{10,... | collective-permute-start | bytes 12296 | tf_op jit(solution)/shard_map/ppermute | solution.py:30
  137.9 3.1 %collective-permute-start.15 = (f32[2,1,512]{2,1,0:T(1,128)S(1)}, f32[2,1,512]{2,1,0:T(1,128)S(1)}, u32[]{:S(2)}, u32[]{:S(2)}) collective-permute-start(f32[2,1,512]{2,1,0:T(1,128)S(1)} %pad_maximum_fusion.1), channel_id=1, source_target_pairs={{0,3},{1,2},{2,1},{3,0},{4,7},{5,6},{6,5},{7,4},{8,11},{9,10},{10,... | collective-permute-start | bytes 12296 | tf_op jit(solution)/shard_map/ppermute | solution.py:30
  138.0 3.7 %collective-permute-start.14 = (f32[2,1,512]{2,1,0:T(1,128)S(1)}, f32[2,1,512]{2,1,0:T(1,128)S(1)}, u32[]{:S(2)}, u32[]{:S(2)}) collective-permute-start(f32[2,1,512]{2,1,0:T(1,128)S(1)} %pad_maximum_fusion.1), channel_id=1, source_target_pairs={{0,2},{1,3},{2,0},{3,1},{4,6},{5,7},{6,4},{7,5},{8,10},{9,11},{10,... | collective-permute-start | bytes 12296 | tf_op jit(solution)/shard_map/ppermute | solution.py:30
  138.4 3.3 %collective-permute-start.13 = (f32[2,1,512]{2,1,0:T(1,128)S(1)}, f32[2,1,512]{2,1,0:T(1,128)S(1)}, u32[]{:S(2)}, u32[]{:S(2)}) collective-permute-start(f32[2,1,512]{2,1,0:T(1,128)S(1)} %pad_maximum_fusion.1), channel_id=1, source_target_pairs={{0,1},{1,0},{2,3},{3,2},{4,5},{5,4},{6,7},{7,6},{8,9},{9,8},{10,11... | collective-permute-start | bytes 12296 | tf_op jit(solution)/shard_map/ppermute | solution.py:30
  141.8 2.3 %copy-start.4 = (f32[256]{0:T(256)}, f32[256]{0:T(256)S(1)}, u32[]{:S(2)}) copy-start(f32[256]{0:T(256)S(1)} %get-tuple-element.16) | copy-start | bytes 3076
